TPU v7x, 32 devices: a whole 2x2x4 slice. The times are simulated.
32 devices in a mesh: tm: 8 (over z, x), state: 4 (over y, core).
Axes of the slice: x: 2, y: 2, z: 4, core: 2. Of those that a mesh axis runs over, the one named last changes fastest.
Arguments:
- obs: bfloat16 [2048, 16, 256], P(('state', 'tm')), may hold values from -6 to 6
- mask: int32 [2048, 16], P(('state', 'tm')), may hold values 0 or 1
- loadings: bfloat16 [2048, 2048], P('state'), may hold values from -0.125 to 0.125
- decay: float32 [16, 2048], P('tm', 'state'), may hold values from 0 to 1, as said below
Outputs:
- smoothed: float32 [2048, 16, 256], P('state', 'tm')
- residual: float32 [2048, 16, 256], P('state', 'tm')
Inputs may be any that keep to these rules, and one draw needn't show every extreme that they name: Every decay lies strictly between 0 and 1.
All inputs are finite; a program needn't handle non-finite values. No bound on the sum of `mask` on one device may be relied on, other than what follows from the above.
Results may differ from a plain program's by a relative error of at most 0.0021.
Values may be sent and summed in bfloat16 or wider, within the bound.
No kernel may reach another device: no remote copies, remote signals or barrier semaphores. Data moves between devices by JAX's collectives and lax.ppermute only.
A program may use at most 64 MiB of HBM per device.

v0:
```python
import jax
import jax.numpy as jnp
from jax import lax
from jax.sharding import PartitionSpec as P


def from_behind(x, axis, by):
    count = lax.axis_size(axis)
    pairs = [(i, i + by) for i in range(count) if 0 <= i + by < count]
    return lax.ppermute(x, axis, pairs)


def local(obs, mask, loadings, decay):
    masked = obs * mask[:, :, None].astype(jnp.bfloat16)
    arrival_flags = lax.all_to_all(masked, "tm", split_axis=1, concat_axis=0, tiled=True)
    step_count = arrival_flags.shape[1]
    member_count = arrival_flags.shape[2]
    row_width = decay.shape[1]
    loading_matrix_block = loadings
    information = lax.psum_scatter(
        jnp.einsum(
            "xd,xme->dme", loading_matrix_block, arrival_flags, preferred_element_type=jnp.float32
        ),
        "state",
        scatter_dimension=0,
        tiled=True,
    )
    zero_state = jnp.zeros((row_width, member_count), jnp.float32)
    unit_rates = jnp.ones((row_width,), jnp.float32)
    partial_state = zero_state
    growth = unit_rates
    filtered_local = []
    reaches = []
    for position in range(step_count):
        decay_row = decay[position]
        partial_state = decay_row[:, None] * partial_state + information[:, position, :]
        growth = growth * decay_row
        filtered_local.append(partial_state)
        reaches.append(growth)

    def forward_turn(hop_index, carried_pair):
        incoming, outgoing = carried_pair
        incoming = from_behind(outgoing, "tm", 1)
        return (incoming, growth[:, None] * incoming + partial_state)

    entering, _ = lax.fori_loop(
        0, lax.axis_size("tm") - 1, forward_turn, (zero_state, partial_state)
    )
    filtered = [
        filtered_local[position] + reaches[position][:, None] * entering
        for position in range(step_count)
    ]
    back_state = zero_state
    carried_span = unit_rates
    back_local = [None] * step_count
    back_spans = [None] * step_count
    for position in reversed(range(step_count)):
        decay_row = decay[position]
        back_state = (
            decay_row[:, None] * back_state
            + (1.0 - decay_row * decay_row)[:, None] * filtered[position]
        )
        carried_span = carried_span * decay_row
        back_local[position] = back_state
        back_spans[position] = carried_span

    def backward_turn(hop_index, carried_pair):
        incoming, outgoing = carried_pair
        incoming = from_behind(outgoing, "tm", -1)
        return (incoming, carried_span[:, None] * incoming + back_state)

    later_state, _ = lax.fori_loop(
        0, lax.axis_size("tm") - 1, backward_turn, (zero_state, back_state)
    )
    smoothed = jnp.stack(
        [
            back_local[position] + back_spans[position][:, None] * later_state
            for position in range(step_count)
        ],
        axis=1,
    )
    rounded = smoothed.astype(jnp.bfloat16)
    loading_matrix_block = loadings
    fitted = jnp.einsum(
        "so,ogy->sgy",
        loading_matrix_block,
        lax.all_gather(rounded, "state", axis=0, tiled=True),
        preferred_element_type=jnp.float32,
    )
    residual = arrival_flags.astype(jnp.float32) - fitted
    return (smoothed, residual)


def solution(mesh):
    return jax.shard_map(
        local,
        mesh=mesh,
        in_specs=(
            P(("state", "tm"), None, None),
            P(("state", "tm"), None),
            P("state", None),
            P("tm", "state"),
        ),
        out_specs=(P("state", "tm", None), P("state", "tm", None)),
        check_vma=False,
    )
```

profile of v0, /device:TPU:0, one launch (start us, length us, event | category | flops | bytes accessed | tf_op | source)
XLA Modules:
  0.0 343.4 jit_solution(9331826668370613463)
XLA Ops:
  9.3 21.6 %all_to_all.18 = bf16[64,16,256]{2,0,1:T(8,128)(2,1)S(1)} all-to-all(bf16[64,16,256]{2,0,1:T(8,128)(2,1)S(1)} %copy_multiply_fusion), channel_id=1, replica_groups=mesh['tm'=8,'state'=4] {'tm'}, dimensions={1} | all-to-all | bytes 1048576 | tf_op jit(solution)/shard_map/all_to_all | solution.py:15
  31.8 3.2 convolution_bitcast_fusion
  35.7 43.0 %reduce-scatter.2.cloned.1.call-done = f32[512,2,256]{0,2,1:T(8,128)} async-done(((f32[2048,2,256]{0,2,1:T(8,128)}), f32[512,2,256]{0,2,1:T(8,128)}) %reduce-scatter.2.cloned.1.call-update) | async-done | bytes 1048592 | tf_op jit(solution)/shard_map/reduce_scatter | solution.py:20
  81.9 101.8 %while.24 = (s32[]{:T(128)}, f32[512,256]{1,0:T(8,128)}, f32[512,256]{1,0:T(8,128)}, f32[512]{0:T(512)S(1)}, f32[512,256]{1,0:T(8,128)S(1)}, /*index=5*/s32[]{:T(128)}) while((s32[]{:T(128)}, f32[512,256]{1,0:T(8,128)}, f32[512,256]{1,0:T(8,128)}, f32[512]{0:T(512)S(1)}, f32[512,256]{1,0:T(8,128)S(1)}, /*index=5*/s32[]{:T(128)}) %tuple.50), condition=%wide.region_2.0_spmd, body=%wide.region_1.0_spmd.sunk | while | flops 262146 | bytes 5769353 | solution.py:46
  81.9 3.4 collective-permute-start
  85.3 11.5 %collective-permute-done = f32[512,256]{1,0:T(8,128)S(1)} collective-permute-done((f32[512,256]{1,0:T(8,128)}, f32[512,256]{1,0:T(8,128)S(1)}, u32[]{:S(2)}, u32[]{:S(2)}) %collective-permute-start) | collective-permute-done | bytes 524320 | tf_op jit(solution)/shard_map/while/body/eval_jaxpr/ppermute | solution.py:10
  97.7 4.3 %collective-permute-start = (f32[512,256]{1,0:T(8,128)}, f32[512,256]{1,0:T(8,128)S(1)}, u32[]{:S(2)}, u32[]{:S(2)}) collective-permute-start(f32[512,256]{1,0:T(8,128)} %get-tuple-element.187), channel_id=1, source_target_pairs={{0,4},{4,8},{8,12},{12,16},{16,20},{20,24},{24,28},{1,5},{5,9},{9,... | collective-permute-start | bytes 1572872 | tf_op jit(solution)/shard_map/while/body/eval_jaxpr/ppermute | solution.py:10
  102.0 10.6 %collective-permute-done = f32[512,256]{1,0:T(8,128)S(1)} collective-permute-done((f32[512,256]{1,0:T(8,128)}, f32[512,256]{1,0:T(8,128)S(1)}, u32[]{:S(2)}, u32[]{:S(2)}) %collective-permute-start) | collective-permute-done | bytes 524320 | tf_op jit(solution)/shard_map/while/body/eval_jaxpr/ppermute | solution.py:10
  113.6 4.3 %collective-permute-start = (f32[512,256]{1,0:T(8,128)}, f32[512,256]{1,0:T(8,128)S(1)}, u32[]{:S(2)}, u32[]{:S(2)}) collective-permute-start(f32[512,256]{1,0:T(8,128)} %get-tuple-element.187), channel_id=1, source_target_pairs={{0,4},{4,8},{8,12},{12,16},{16,20},{20,24},{24,28},{1,5},{5,9},{9,... | collective-permute-start | bytes 1572872 | tf_op jit(solution)/shard_map/while/body/eval_jaxpr/ppermute | solution.py:10
  117.9 9.7 %collective-permute-done = f32[512,256]{1,0:T(8,128)S(1)} collective-permute-done((f32[512,256]{1,0:T(8,128)}, f32[512,256]{1,0:T(8,128)S(1)}, u32[]{:S(2)}, u32[]{:S(2)}) %collective-permute-start) | collective-permute-done | bytes 524320 | tf_op jit(solution)/shard_map/while/body/eval_jaxpr/ppermute | solution.py:10
  128.5 5.2 %collective-permute-start = (f32[512,256]{1,0:T(8,128)}, f32[512,256]{1,0:T(8,128)S(1)}, u32[]{:S(2)}, u32[]{:S(2)}) collective-permute-start(f32[512,256]{1,0:T(8,128)} %get-tuple-element.187), channel_id=1, source_target_pairs={{0,4},{4,8},{8,12},{12,16},{16,20},{20,24},{24,28},{1,5},{5,9},{9,... | collective-permute-start | bytes 1572872 | tf_op jit(solution)/shard_map/while/body/eval_jaxpr/ppermute | solution.py:10
  133.7 8.7 %collective-permute-done = f32[512,256]{1,0:T(8,128)S(1)} collective-permute-done((f32[512,256]{1,0:T(8,128)}, f32[512,256]{1,0:T(8,128)S(1)}, u32[]{:S(2)}, u32[]{:S(2)}) %collective-permute-start) | collective-permute-done | bytes 524320 | tf_op jit(solution)/shard_map/while/body/eval_jaxpr/ppermute | solution.py:10
  143.4 5.2 %collective-permute-start = (f32[512,256]{1,0:T(8,128)}, f32[512,256]{1,0:T(8,128)S(1)}, u32[]{:S(2)}, u32[]{:S(2)}) collective-permute-start(f32[512,256]{1,0:T(8,128)} %get-tuple-element.187), channel_id=1, source_target_pairs={{0,4},{4,8},{8,12},{12,16},{16,20},{20,24},{24,28},{1,5},{5,9},{9,... | collective-permute-start | bytes 1572872 | tf_op jit(solution)/shard_map/while/body/eval_jaxpr/ppermute | solution.py:10
  148.6 7.8 %collective-permute-done = f32[512,256]{1,0:T(8,128)S(1)} collective-permute-done((f32[512,256]{1,0:T(8,128)}, f32[512,256]{1,0:T(8,128)S(1)}, u32[]{:S(2)}, u32[]{:S(2)}) %collective-permute-start) | collective-permute-done | bytes 524320 | tf_op jit(solution)/shard_map/while/body/eval_jaxpr/ppermute | solution.py:10
  157.3 5.2 %collective-permute-start = (f32[512,256]{1,0:T(8,128)}, f32[512,256]{1,0:T(8,128)S(1)}, u32[]{:S(2)}, u32[]{:S(2)}) collective-permute-start(f32[512,256]{1,0:T(8,128)} %get-tuple-element.187), channel_id=1, source_target_pairs={{0,4},{4,8},{8,12},{12,16},{16,20},{20,24},{24,28},{1,5},{5,9},{9,... | collective-permute-start | bytes 1572872 | tf_op jit(solution)/shard_map/while/body/eval_jaxpr/ppermute | solution.py:10
  162.6 7.0 %collective-permute-done = f32[512,256]{1,0:T(8,128)S(1)} collective-permute-done((f32[512,256]{1,0:T(8,128)}, f32[512,256]{1,0:T(8,128)S(1)}, u32[]{:S(2)}, u32[]{:S(2)}) %collective-permute-start) | collective-permute-done | bytes 524320 | tf_op jit(solution)/shard_map/while/body/eval_jaxpr/ppermute | solution.py:10
  170.5 5.2 %collective-permute-start = (f32[512,256]{1,0:T(8,128)}, f32[512,256]{1,0:T(8,128)S(1)}, u32[]{:S(2)}, u32[]{:S(2)}) collective-permute-start(f32[512,256]{1,0:T(8,128)} %get-tuple-element.187), channel_id=1, source_target_pairs={{0,4},{4,8},{8,12},{12,16},{16,20},{20,24},{24,28},{1,5},{5,9},{9,... | collective-permute-start | bytes 1572872 | tf_op jit(solution)/shard_map/while/body/eval_jaxpr/ppermute | solution.py:10
  175.7 7.0 %collective-permute-done = f32[512,256]{1,0:T(8,128)S(1)} collective-permute-done((f32[512,256]{1,0:T(8,128)}, f32[512,256]{1,0:T(8,128)S(1)}, u32[]{:S(2)}, u32[]{:S(2)}) %collective-permute-start) | collective-permute-done | bytes 524320 | tf_op jit(solution)/shard_map/while/body/eval_jaxpr/ppermute | solution.py:10
  188.9 115.2 %while.25 = (s32[]{:T(128)}, f32[512,256]{1,0:T(8,128)}, f32[512,256]{1,0:T(8,128)}, f32[512]{0:T(512)S(1)}, f32[512,256]{1,0:T(8,128)S(1)}, /*index=5*/s32[]{:T(128)}) while((s32[]{:T(128)}, f32[512,256]{1,0:T(8,128)}, f32[512,256]{1,0:T(8,128)}, f32[512]{0:T(512)S(1)}, f32[512,256]{1,0:T(8,128)S(1)}, /*index=5*/s32[]{:T(128)}) %tuple.60), condition=%wide.region_4.0_spmd, body=%wide.region_3.0_spmd.sunk | while | flops 262146 | bytes 5769353 | solution.py:72
  190.2 11.9 %collective-permute-done.1 = f32[512,256]{1,0:T(8,128)S(1)} collective-permute-done((f32[512,256]{1,0:T(8,128)}, f32[512,256]{1,0:T(8,128)S(1)}, u32[]{:S(2)}, u32[]{:S(2)}) %collective-permute-start.1) | collective-permute-done | bytes 524320 | tf_op jit(solution)/shard_map/while/body/eval_jaxpr/ppermute | solution.py:10
  204.4 13.9 %collective-permute-done.1 = f32[512,256]{1,0:T(8,128)S(1)} collective-permute-done((f32[512,256]{1,0:T(8,128)}, f32[512,256]{1,0:T(8,128)S(1)}, u32[]{:S(2)}, u32[]{:S(2)}) %collective-permute-start.1) | collective-permute-done | bytes 524320 | tf_op jit(solution)/shard_map/while/body/eval_jaxpr/ppermute | solution.py:10
  220.6 15.1 %collective-permute-done.1 = f32[512,256]{1,0:T(8,128)S(1)} collective-permute-done((f32[512,256]{1,0:T(8,128)}, f32[512,256]{1,0:T(8,128)S(1)}, u32[]{:S(2)}, u32[]{:S(2)}) %collective-permute-start.1) | collective-permute-done | bytes 524320 | tf_op jit(solution)/shard_map/while/body/eval_jaxpr/ppermute | solution.py:10
  238.0 15.7 %collective-permute-done.1 = f32[512,256]{1,0:T(8,128)S(1)} collective-permute-done((f32[512,256]{1,0:T(8,128)}, f32[512,256]{1,0:T(8,128)S(1)}, u32[]{:S(2)}, u32[]{:S(2)}) %collective-permute-start.1) | collective-permute-done | bytes 524320 | tf_op jit(solution)/shard_map/while/body/eval_jaxpr/ppermute | solution.py:10
  256.0 16.8 %collective-permute-done.1 = f32[512,256]{1,0:T(8,128)S(1)} collective-permute-done((f32[512,256]{1,0:T(8,128)}, f32[512,256]{1,0:T(8,128)S(1)}, u32[]{:S(2)}, u32[]{:S(2)}) %collective-permute-start.1) | collective-permute-done | bytes 524320 | tf_op jit(solution)/shard_map/while/body/eval_jaxpr/ppermute | solution.py:10
  275.0 15.2 %collective-permute-done.1 = f32[512,256]{1,0:T(8,128)S(1)} collective-permute-done((f32[512,256]{1,0:T(8,128)}, f32[512,256]{1,0:T(8,128)S(1)}, u32[]{:S(2)}, u32[]{:S(2)}) %collective-permute-start.1) | collective-permute-done | bytes 524320 | tf_op jit(solution)/shard_map/while/body/eval_jaxpr/ppermute | solution.py:10
  292.5 10.6 %collective-permute-done.1 = f32[512,256]{1,0:T(8,128)S(1)} collective-permute-done((f32[512,256]{1,0:T(8,128)}, f32[512,256]{1,0:T(8,128)S(1)}, u32[]{:S(2)}, u32[]{:S(2)}) %collective-permute-start.1) | collective-permute-done | bytes 524320 | tf_op jit(solution)/shard_map/while/body/eval_jaxpr/ppermute | solution.py:10
  304.1 2.0 copy.40
  306.2 2.0 add_bitcast_fusion.1
  309.1 2.1 copy.42
  312.2 2.2 copy.43
  314.4 17.9 %all-gather.2.cloned.1.call-done = bf16[2048,2,256]{0,2,1:T(8,128)(2,1)} async-done(((bf16[512,2,256]{0,2,1:T(8,128)(2,1)}), bf16[2048,2,256]{0,2,1:T(8,128)(2,1)}) %all-gather.2.cloned.1.call-update) | async-done | bytes 2097168 | tf_op jit(solution)/shard_map/all_gather | solution.py:87
  332.3 3.0 fusion.6
  (80 shorter events, 37.9 us)
Async XLA Ops:
  7.2 24.6 %copy-start = (bf16[512,2048]{1,0:T(8,128)(2,1)S(1)}, bf16[512,2048]{1,0:T(8,128)(2,1)}, u32[]{:S(2)}) copy-start(bf16[512,2048]{1,0:T(8,128)(2,1)} %param.10) | copy-start | bytes 6291460
  7.2 71.6 %reduce-scatter.2.cloned.1.call-start = ((), (), s32[]{:S(2)}) async-start(), calls=%async_computation.2 | async-start | bytes 5242880 | tf_op jit(solution)/shard_map/reduce_scatter | solution.py:20
  35.1 297.3 %all-gather.2.cloned.1.call-start = ((), (), s32[]{:S(2)}) async-start(), calls=%async_computation.3 | async-start | bytes 2621440 | tf_op jit(solution)/shard_map/all_gather | solution.py:87
  81.9 14.9 %collective-permute-start = (f32[512,256]{1,0:T(8,128)}, f32[512,256]{1,0:T(8,128)S(1)}, u32[]{:S(2)}, u32[]{:S(2)}) collective-permute-start(f32[512,256]{1,0:T(8,128)} %get-tuple-element.187), channel_id=1, source_target_pairs={{0,4},{4,8},{8,12},{12,16},{16,20},{20,24},{24,28},{1,5},{5,9},{9,... | collective-permute-start | bytes 1572872 | tf_op jit(solution)/shard_map/while/body/eval_jaxpr/ppermute | solution.py:10
  96.7 1.0 copy-start.2
  97.7 14.9 %collective-permute-start = (f32[512,256]{1,0:T(8,128)}, f32[512,256]{1,0:T(8,128)S(1)}, u32[]{:S(2)}, u32[]{:S(2)}) collective-permute-start(f32[512,256]{1,0:T(8,128)} %get-tuple-element.187), channel_id=1, source_target_pairs={{0,4},{4,8},{8,12},{12,16},{16,20},{20,24},{24,28},{1,5},{5,9},{9,... | collective-permute-start | bytes 1572872 | tf_op jit(solution)/shard_map/while/body/eval_jaxpr/ppermute | solution.py:10
  112.6 1.0 copy-start.2
  113.6 14.0 %collective-permute-start = (f32[512,256]{1,0:T(8,128)}, f32[512,256]{1,0:T(8,128)S(1)}, u32[]{:S(2)}, u32[]{:S(2)}) collective-permute-start(f32[512,256]{1,0:T(8,128)} %get-tuple-element.187), channel_id=1, source_target_pairs={{0,4},{4,8},{8,12},{12,16},{16,20},{20,24},{24,28},{1,5},{5,9},{9,... | collective-permute-start | bytes 1572872 | tf_op jit(solution)/shard_map/while/body/eval_jaxpr/ppermute | solution.py:10
  127.5 1.0 copy-start.2
  128.5 13.9 %collective-permute-start = (f32[512,256]{1,0:T(8,128)}, f32[512,256]{1,0:T(8,128)S(1)}, u32[]{:S(2)}, u32[]{:S(2)}) collective-permute-start(f32[512,256]{1,0:T(8,128)} %get-tuple-element.187), channel_id=1, source_target_pairs={{0,4},{4,8},{8,12},{12,16},{16,20},{20,24},{24,28},{1,5},{5,9},{9,... | collective-permute-start | bytes 1572872 | tf_op jit(solution)/shard_map/while/body/eval_jaxpr/ppermute | solution.py:10
  142.4 1.0 copy-start.2
  143.4 13.0 %collective-permute-start = (f32[512,256]{1,0:T(8,128)}, f32[512,256]{1,0:T(8,128)S(1)}, u32[]{:S(2)}, u32[]{:S(2)}) collective-permute-start(f32[512,256]{1,0:T(8,128)} %get-tuple-element.187), channel_id=1, source_target_pairs={{0,4},{4,8},{8,12},{12,16},{16,20},{20,24},{24,28},{1,5},{5,9},{9,... | collective-permute-start | bytes 1572872 | tf_op jit(solution)/shard_map/while/body/eval_jaxpr/ppermute | solution.py:10
  156.4 1.0 copy-start.2
  157.3 12.2 %collective-permute-start = (f32[512,256]{1,0:T(8,128)}, f32[512,256]{1,0:T(8,128)S(1)}, u32[]{:S(2)}, u32[]{:S(2)}) collective-permute-start(f32[512,256]{1,0:T(8,128)} %get-tuple-element.187), channel_id=1, source_target_pairs={{0,4},{4,8},{8,12},{12,16},{16,20},{20,24},{24,28},{1,5},{5,9},{9,... | collective-permute-start | bytes 1572872 | tf_op jit(solution)/shard_map/while/body/eval_jaxpr/ppermute | solution.py:10
  169.5 1.0 copy-start.2
  170.5 12.2 %collective-permute-start = (f32[512,256]{1,0:T(8,128)}, f32[512,256]{1,0:T(8,128)S(1)}, u32[]{:S(2)}, u32[]{:S(2)}) collective-permute-start(f32[512,256]{1,0:T(8,128)} %get-tuple-element.187), channel_id=1, source_target_pairs={{0,4},{4,8},{8,12},{12,16},{16,20},{20,24},{24,28},{1,5},{5,9},{9,... | collective-permute-start | bytes 1572872 | tf_op jit(solution)/shard_map/while/body/eval_jaxpr/ppermute | solution.py:10
  182.7 1.0 copy-start.2
  187.1 1.9 copy-start.4
  188.9 13.1 %collective-permute-start.1 = (f32[512,256]{1,0:T(8,128)}, f32[512,256]{1,0:T(8,128)S(1)}, u32[]{:S(2)}, u32[]{:S(2)}) collective-permute-start(f32[512,256]{1,0:T(8,128)} %get-tuple-element.205), channel_id=1, source_target_pairs={{4,0},{8,4},{12,8},{16,12},{20,16},{24,20},{28,24},{5,1},{9,5},{13... | collective-permute-start | bytes 1572872 | tf_op jit(solution)/shard_map/while/body/eval_jaxpr/ppermute | solution.py:10
  202.1 1.0 copy-start.1
  203.1 15.2 %collective-permute-start.1 = (f32[512,256]{1,0:T(8,128)}, f32[512,256]{1,0:T(8,128)S(1)}, u32[]{:S(2)}, u32[]{:S(2)}) collective-permute-start(f32[512,256]{1,0:T(8,128)} %get-tuple-element.205), channel_id=1, source_target_pairs={{4,0},{8,4},{12,8},{16,12},{20,16},{24,20},{28,24},{5,1},{9,5},{13... | collective-permute-start | bytes 1572872 | tf_op jit(solution)/shard_map/while/body/eval_jaxpr/ppermute | solution.py:10
  218.3 1.0 copy-start.1
  219.3 16.4 %collective-permute-start.1 = (f32[512,256]{1,0:T(8,128)}, f32[512,256]{1,0:T(8,128)S(1)}, u32[]{:S(2)}, u32[]{:S(2)}) collective-permute-start(f32[512,256]{1,0:T(8,128)} %get-tuple-element.205), channel_id=1, source_target_pairs={{4,0},{8,4},{12,8},{16,12},{20,16},{24,20},{28,24},{5,1},{9,5},{13... | collective-permute-start | bytes 1572872 | tf_op jit(solution)/shard_map/while/body/eval_jaxpr/ppermute | solution.py:10
  235.7 1.0 copy-start.1
  236.7 17.0 %collective-permute-start.1 = (f32[512,256]{1,0:T(8,128)}, f32[512,256]{1,0:T(8,128)S(1)}, u32[]{:S(2)}, u32[]{:S(2)}) collective-permute-start(f32[512,256]{1,0:T(8,128)} %get-tuple-element.205), channel_id=1, source_target_pairs={{4,0},{8,4},{12,8},{16,12},{20,16},{24,20},{28,24},{5,1},{9,5},{13... | collective-permute-start | bytes 1572872 | tf_op jit(solution)/shard_map/while/body/eval_jaxpr/ppermute | solution.py:10
  253.7 1.0 copy-start.1
  254.7 18.1 %collective-permute-start.1 = (f32[512,256]{1,0:T(8,128)}, f32[512,256]{1,0:T(8,128)S(1)}, u32[]{:S(2)}, u32[]{:S(2)}) collective-permute-start(f32[512,256]{1,0:T(8,128)} %get-tuple-element.205), channel_id=1, source_target_pairs={{4,0},{8,4},{12,8},{16,12},{20,16},{24,20},{28,24},{5,1},{9,5},{13... | collective-permute-start | bytes 1572872 | tf_op jit(solution)/shard_map/while/body/eval_jaxpr/ppermute | solution.py:10
  272.8 1.0 copy-start.1
  273.7 16.5 %collective-permute-start.1 = (f32[512,256]{1,0:T(8,128)}, f32[512,256]{1,0:T(8,128)S(1)}, u32[]{:S(2)}, u32[]{:S(2)}) collective-permute-start(f32[512,256]{1,0:T(8,128)} %get-tuple-element.205), channel_id=1, source_target_pairs={{4,0},{8,4},{12,8},{16,12},{20,16},{24,20},{28,24},{5,1},{9,5},{13... | collective-permute-start | bytes 1572872 | tf_op jit(solution)/shard_map/while/body/eval_jaxpr/ppermute | solution.py:10
  290.2 1.0 copy-start.1
  291.2 11.9 %collective-permute-start.1 = (f32[512,256]{1,0:T(8,128)}, f32[512,256]{1,0:T(8,128)S(1)}, u32[]{:S(2)}, u32[]{:S(2)}) collective-permute-start(f32[512,256]{1,0:T(8,128)} %get-tuple-element.205), channel_id=1, source_target_pairs={{4,0},{8,4},{12,8},{16,12},{20,16},{24,20},{28,24},{5,1},{9,5},{13... | collective-permute-start | bytes 1572872 | tf_op jit(solution)/shard_map/while/body/eval_jaxpr/ppermute | solution.py:10
  303.1 1.0 copy-start.1
  (3 other events, 2.3 us)
Sparse Core Ops, SparseCore 0:
  35.2 43.5 reduce-scatter.1
  309.2 23.0 all-gather.1
where the time goes:
time: 344 us; the launch traced here: 343 us
  waiting for transfers between devices  222 us (65%)
  starting transfers between devices  41.8 us (12%)
  other arithmetic  22.3 us (6%)
  blocking collectives  21.6 us (6%)
  local copies, waits for them, and re-layouts  14.9 us (4%)
  between operations  14.1 us (4%)
  matrix products  6.19 us (2%)
    ppermute x14, waiting for transfers between devices, from_behind(): return lax.ppermute(x, axis, pairs)  161 us
    reduce_scatter x1, waiting for transfers between devices, local(): lax.psum_scatter(jnp.einsum('xd,xme->dme', loading_matrix_block, arrival_...  43 us
    ppermute x14, starting transfers between devices, from_behind(): return lax.ppermute(x, axis, pairs)  41.7 us
    all_to_all x1, blocking collectives, local(): lax.all_to_all(masked, 'tm', split_axis=1, concat_axis=0, tiled=True)  21.6 us
    all_gather x1, waiting for transfers between devices, local(): lax.all_gather(rounded, 'state', axis=0, tiled=True)  17.9 us
    unnamed x14, local copies, waits for them, and re-layouts  7.39 us
  transfers between devices with their start and end apart: 16, of which 16 were waited for; matrix products, arithmetic and copies ran while one was open for 2% of the time, Pallas kernels for 0%

commit v1 on v0

v1 whole, which is shorter than its diff:
```python
import jax
import jax.numpy as jnp
from jax import lax
from jax.sharding import PartitionSpec as P


def local(obs, mask, loadings, decay):
    tm_count = lax.axis_size("tm")
    _, hours, members = obs.shape
    members_here = members // tm_count
    masked = obs * mask[:, :, None].astype(obs.dtype)
    by_member = lax.all_to_all(masked, "tm", split_axis=2, concat_axis=0, tiled=True)
    by_hour = lax.all_to_all(masked, "tm", split_axis=1, concat_axis=0, tiled=True)
    stations_here = by_member.shape[0]
    partial = jnp.dot(
        loadings.T,
        by_member.reshape(stations_here, hours * members_here),
        preferred_element_type=jnp.float32,
    )
    information = lax.psum_scatter(partial, "state", scatter_dimension=0, tiled=True)
    comps = information.shape[0]
    information = information.reshape(comps, hours, members_here)
    decay_all = lax.all_gather(decay, "tm", axis=0, tiled=True)
    state = jnp.zeros((comps, members_here), jnp.float32)
    filtered = []
    for hour in range(hours):
        state = decay_all[hour][:, None] * state + information[:, hour, :]
        filtered.append(state)
    state = jnp.zeros((comps, members_here), jnp.float32)
    smoothed_rows = [None] * hours
    for hour in reversed(range(hours)):
        rate = decay_all[hour]
        state = rate[:, None] * state + (1.0 - rate * rate)[:, None] * filtered[hour]
        smoothed_rows[hour] = state
    smoothed_here = jnp.stack(smoothed_rows, axis=1)
    smoothed = lax.all_to_all(smoothed_here, "tm", split_axis=1, concat_axis=2, tiled=True)
    rounded = smoothed.astype(jnp.bfloat16)
    fitted = jnp.einsum(
        "so,ogy->sgy",
        loadings,
        lax.all_gather(rounded, "state", axis=0, tiled=True),
        preferred_element_type=jnp.float32,
    )
    residual = by_hour.astype(jnp.float32) - fitted
    return (smoothed, residual)


def solution(mesh):
    return jax.shard_map(
        local,
        mesh=mesh,
        in_specs=(
            P(("state", "tm"), None, None),
            P(("state", "tm"), None),
            P("state", None),
            P("tm", "state"),
        ),
        out_specs=(P("state", "tm", None), P("state", "tm", None)),
        check_vma=False,
    )
```

time: 344 us -> 160 us (0.47)
  waiting for transfers between devices: 222 us -> 12.5 us
  blocking collectives: 21.6 us -> 101 us
  starting transfers between devices: 41.8 us -> 0.08 us
  other arithmetic: 22.3 us -> 5.56 us
  local copies, waits for them, and re-layouts: 14.9 us -> 19.2 us
    ppermute x14 -> x0, waiting for transfers between devices: 161 us -> none  [from_behind(): return lax.ppermute(x, axis, pairs)]
    all_to_all x0 -> x2, blocking collectives: none -> 52.8 us  [the longest x1 31.1 us: local(): lax.all_to_all(smoothed_here, 'tm', split_axis=1, concat_axis=2, tiled=True)]
    ppermute x14 -> x0, starting transfers between devices: 41.7 us -> none  [from_behind(): return lax.ppermute(x, axis, pairs)]
    reduce_scatter x1, waiting for transfers between devices: 43 us -> 12.4 us  [local(): lax.psum_scatter(partial, 'state', scatter_dimension=0, tiled=True)]
    all_gather x0 -> x1, blocking collectives: none -> 30.4 us  [local(): decay_all = lax.all_gather(decay, 'tm', axis=0, tiled=True)]
    all_gather x1, waiting for transfers between devices: 17.9 us -> 0.01 us  [local(): lax.all_gather(rounded, 'state', axis=0, tiled=True)]
    add x16 -> x0, other arithmetic: 16.3 us -> none  [the longest x7 6.84 us: backward_turn(): return (incoming, carried_span[:, None] * incoming + back_state)]
    all_to_all x1, blocking collectives: 21.6 us -> 17.5 us  [local(): lax.all_to_all(masked, 'tm', split_axis=1, concat_axis=0, tiled=True)]
  transfers between devices with their start and end apart: 16 -> 2, of which waited for: 16 -> 1; matrix products, arithmetic and copies ran while one was open for 2% -> 4% of each run, Pallas kernels for 0% -> 0%
where the time goes in v1:
time: 160 us
  blocking collectives  101 us (63%)
  local copies, waits for them, and re-layouts  19.2 us (12%)
  between operations  14.3 us (9%)
  waiting for transfers between devices  12.5 us (8%)
  matrix products  7.4 us (5%)
  other arithmetic  5.56 us (3%)
    all_to_all x1, blocking collectives, local(): lax.all_to_all(smoothed_here, 'tm', split_axis=1, concat_axis=2, tiled=True)  31.1 us
    all_gather x1, blocking collectives, local(): decay_all = lax.all_gather(decay, 'tm', axis=0, tiled=True)  30.4 us
    all_to_all x1, blocking collectives, local(): lax.all_to_all(masked, 'tm', split_axis=2, concat_axis=0, tiled=True)  21.7 us
    all_to_all x1, blocking collectives, local(): lax.all_to_all(masked, 'tm', split_axis=1, concat_axis=0, tiled=True)  17.5 us
    reduce_scatter x1, waiting for transfers between devices, local(): lax.psum_scatter(partial, 'state', scatter_dimension=0, tiled=True)  12.4 us
    unnamed x18, local copies, waits for them, and re-layouts  8.67 us
    dot_general x1, matrix products, local(): jnp.dot(loadings.T, by_member.reshape(stations_here, hours * members_here...  4.27 us
    convert_element_type x2, local copies, waits for them, and re-layouts, local(): residual = by_hour.astype(jnp.float32) - fitted  3.59 us
  transfers between devices with their start and end apart: 2, of which 1 were waited for; matrix products, arithmetic and copies ran while one was open for 4% of the time, Pallas kernels for 0%

profile of v1, /device:TPU:0, one launch (start us, length us, event | category | flops | bytes accessed | tf_op | source)
XLA Modules:
  0.0 159.7 jit_solution(3750152631335707092)
XLA Ops:
  7.2 0.0 copy-start
  7.2 0.0 reduce-scatter.2.cloned.1.call-start
  7.2 0.8 convert_element_type.19
  8.1 0.1 copy.35
  8.2 1.2 broadcast_multiply_fusion
  9.4 0.0 copy-start.1
  9.4 2.2 %copy.36 = bf16[64,16,256]{0,1,2:T(8,128)(2,1)} copy(bf16[64,16,256]{2,1,0:T(8,128)(2,1)S(1)} %broadcast_multiply_fusion) | data formatting | bytes 1048576 | tf_op jit(solution)/shard_map/mul | solution.py:11
  11.6 2.3 %reshape.3600 = bf16[8,2,16384]{2,1,0:T(2,128)(2,1)S(1)} reshape(bf16[256,16,64]{2,1,0:T(8,128)(2,1)} %bitcast.54) | data formatting | bytes 1048576
  14.0 21.7 %all_to_all.42 = bf16[8,2,16384]{2,1,0:T(2,128)(2,1)} all-to-all(bf16[8,2,16384]{2,1,0:T(2,128)(2,1)S(1)} %reshape.3600), channel_id=1, replica_groups=mesh['tm'=8,'state'=4] {'tm'}, dimensions={0} | all-to-all | bytes 1048576 | tf_op jit(solution)/shard_map/all_to_all | solution.py:12
  35.7 3.0 %reshape.3601 = bf16[256,16,64]{2,1,0:T(8,128)(2,1)} reshape(bf16[8,2,16384]{2,1,0:T(2,128)(2,1)} %all_to_all.42) | data formatting | bytes 1048576
  38.7 1.9 %copy.38 = bf16[8,64,16,32]{1,0,3,2:T(8,128)(2,1)S(1)} copy(bf16[8,64,16,32]{1,2,3,0:T(8,128)(2,1)} %bitcast.55) | data formatting | bytes 1048576 | tf_op jit(solution)/shard_map/all_to_all | solution.py:12
  40.6 1.4 reshape.3593
  42.0 4.3 %convolution_bitcast_fusion = f32[2048,512]{0,1:T(8,128)} fusion(bf16[512,512]{0,1:T(8,128)(2,1)} %reshape.3593, bf16[512,2048]{1,0:T(8,128)(2,1)S(1)} %copy-done), kind=kOutput, calls=%fused_computation | convolution fusion | flops 1073741824 | bytes 6815744 | tf_op jit(solution)/shard_map/dot_general | solution.py:15
  46.3 0.0 reduce-scatter.2.cloned.1.call-update
  46.3 0.0 all-gather.3.cloned.1.call-start
  46.4 0.6 copy-done.2
  47.0 30.4 %all-gather = f32[8,2,512]{2,1,0:T(2,128)S(1)} all-gather(f32[1,2,512]{2,1,0:T(2,128)S(1)} %bitcast.102), channel_id=1, replica_groups=mesh['tm'=8,'state'=4] {'tm'}, dimensions={0}, use_global_device_ids=true | all-gather | bytes 36864 | tf_op jit(solution)/shard_map/all_gather | solution.py:23
  77.5 12.4 %reduce-scatter.2.cloned.1.call-done = f32[512,512]{0,1:T(8,128)} async-done(((f32[2048,512]{0,1:T(8,128)}), f32[512,512]{0,1:T(8,128)}) %reduce-scatter.2.cloned.1.call-update) | async-done | bytes 1048592 | tf_op jit(solution)/shard_map/reduce_scatter | solution.py:20
  90.0 1.5 add_dynamic-update-slice_fusion
  91.7 0.9 fusion.10
  92.6 31.1 %all_to_all.43 = f32[512,16,32]{0,2,1:T(8,128)S(1)} all-to-all(f32[512,16,32]{0,2,1:T(8,128)S(1)} %fusion.10), channel_id=1, replica_groups=mesh['tm'=8,'state'=4] {'tm'}, dimensions={1} | all-to-all | bytes 2097152 | tf_op jit(solution)/shard_map/all_to_all | solution.py:36
  123.7 0.1 copy.39
  123.8 0.8 bitcast_convert_fusion
  124.6 0.0 all-gather.3.cloned.1.call-update
  124.7 1.2 copy.40
  125.9 17.5 %all_to_all.44 = bf16[64,16,256]{2,0,1:T(8,128)(2,1)S(1)} all-to-all(bf16[64,16,256]{2,0,1:T(8,128)(2,1)S(1)} %copy.40), channel_id=1, replica_groups=mesh['tm'=8,'state'=4] {'tm'}, dimensions={1} | all-to-all | bytes 1048576 | tf_op jit(solution)/shard_map/all_to_all | solution.py:13
  143.4 0.1 convert_bitcast_fusion
  143.5 1.1 copy.41
  144.6 2.5 %copy.42 = f32[512,2,256]{0,2,1:T(8,128)} copy(f32[512,2,256]{2,0,1:T(8,128)} %bitcast.57) | data formatting | bytes 2097152 | tf_op jit(solution)/shard_map/convert_element_type | solution.py:44
  147.1 1.3 copy.43
  148.4 3.1 %fusion.5 = f32[512,2,256]{0,2,1:T(8,128)S(1)} fusion(f32[512,2,256]{0,2,1:T(8,128)} %copy.42, bf16[2048,2,256]{0,2,1:T(8,128)(2,1)} %all-gather.3.cloned.1.call-done, bf16[512,2048]{1,0:T(8,128)(2,1)S(1)} %copy-done), kind=kOutput, calls=%fused_computation.4 | convolution fusion | flops 1074003968 | bytes 6291456 | tf_op jit(solution)/shard_map/so,ogy->sgy/dot_general | solution.py:38
  151.5 1.3 copy.44
  (28 shorter events, 0.3 us)
Async XLA Ops:
  7.2 34.8 %copy-start = (bf16[512,2048]{1,0:T(8,128)(2,1)S(1)}, bf16[512,2048]{1,0:T(8,128)(2,1)}, u32[]{:S(2)}) copy-start(bf16[512,2048]{1,0:T(8,128)(2,1)} %param.6) | copy-start | bytes 6291460
  7.2 82.8 %reduce-scatter.2.cloned.1.call-start = ((), (), s32[]{:S(2)}) async-start(), calls=%async_computation.4 | async-start | bytes 5242880 | tf_op jit(solution)/shard_map/reduce_scatter | solution.py:20
  9.4 26.2 %copy-start.1 = (bf16[64,16,256]{2,1,0:T(8,128)(2,1)}, bf16[64,16,256]{2,1,0:T(8,128)(2,1)S(1)}, u32[]{:S(2)}) copy-start(bf16[64,16,256]{2,1,0:T(8,128)(2,1)S(1)} %broadcast_multiply_fusion) | copy-start | bytes 1572868
  46.3 0.7 copy-start.2
  46.3 102.1 %all-gather.3.cloned.1.call-start = ((), (), s32[]{:S(2)}) async-start(), calls=%async_computation.5 | async-start | bytes 2621440 | tf_op jit(solution)/shard_map/all_gather | solution.py:41
Sparse Core Ops, SparseCore 0:
  46.4 43.5 reduce-scatter.1
  124.8 20.6 all-gather.2

commit v2 on v1

v2 whole, which is shorter than its diff:
```python
import jax
import jax.numpy as jnp
from jax import lax
from jax.sharding import PartitionSpec as P

CHUNKS = 2


def smooth_chunk(information, decay_all):
    comps, hours, width = information.shape
    state = jnp.zeros((comps, width), jnp.float32)
    filtered = []
    for hour in range(hours):
        state = decay_all[hour][:, None] * state + information[:, hour, :]
        filtered.append(state)
    state = jnp.zeros((comps, width), jnp.float32)
    rows = [None] * hours
    for hour in reversed(range(hours)):
        rate = decay_all[hour]
        state = rate[:, None] * state + (1.0 - rate * rate)[:, None] * filtered[hour]
        rows[hour] = state
    return jnp.stack(rows, axis=1)


def local(obs, mask, loadings, decay):
    tm_count = lax.axis_size("tm")
    tm_index = lax.axis_index("tm")
    _, hours, members = obs.shape
    chunk_members = members // CHUNKS
    masked = obs * mask[:, :, None].astype(obs.dtype)
    by_hour = lax.all_to_all(masked, "tm", split_axis=1, concat_axis=0, tiled=True)
    slab_hours, comps = decay.shape
    padded = jnp.zeros((tm_count, slab_hours, comps), jnp.float32)
    padded = lax.dynamic_update_slice(padded, decay[None], (tm_index, 0, 0))
    decay_all = lax.psum(padded, "tm").reshape(tm_count * slab_hours, comps)
    smoothed_parts = []
    residual_parts = []
    for chunk in range(CHUNKS):
        low = chunk * chunk_members
        piece = masked[:, :, low:low + chunk_members]
        by_member = lax.all_to_all(piece, "tm", split_axis=2, concat_axis=0, tiled=True)
        stations_here, _, width = by_member.shape
        partial = jnp.dot(
            loadings.T,
            by_member.reshape(stations_here, hours * width),
            preferred_element_type=jnp.float32,
        )
        information = lax.psum_scatter(partial, "state", scatter_dimension=0, tiled=True)
        information = information.reshape(information.shape[0], hours, width)
        smoothed_here = smooth_chunk(information, decay_all)
        smoothed = lax.all_to_all(smoothed_here, "tm", split_axis=1, concat_axis=2, tiled=True)
        rounded = smoothed.astype(jnp.bfloat16)
        fitted = jnp.einsum(
            "so,ogy->sgy",
            loadings,
            lax.all_gather(rounded, "state", axis=0, tiled=True),
            preferred_element_type=jnp.float32,
        )
        residual = by_hour[:, :, low:low + chunk_members].astype(jnp.float32) - fitted
        smoothed_parts.append(smoothed)
        residual_parts.append(residual)
    return (
        jnp.concatenate(smoothed_parts, axis=2),
        jnp.concatenate(residual_parts, axis=2),
    )


def solution(mesh):
    return jax.shard_map(
        local,
        mesh=mesh,
        in_specs=(
            P(("state", "tm"), None, None),
            P(("state", "tm"), None),
            P("state", None),
            P("tm", "state"),
        ),
        out_specs=(P("state", "tm", None), P("state", "tm", None)),
        check_vma=False,
    )
```

time: 160 us -> 198 us (1.24)
  blocking collectives: 101 us -> 83.4 us
  local copies, waits for them, and re-layouts: 19.2 us -> 35.7 us
  other arithmetic: 5.56 us -> 21.4 us
  waiting for transfers between devices: 12.5 us -> 24.1 us
  starting transfers between devices: 0.08 us -> 8.46 us
    psum x0 -> x1, blocking collectives: none -> 35.2 us  [local(): decay_all = lax.psum(padded, 'tm').reshape(tm_count * slab_hours, comps)]
    all_gather x1 -> x0, blocking collectives: 30.4 us -> none  [local(): decay_all = lax.all_gather(decay, 'tm', axis=0, tiled=True)]
    all_to_all x0 -> x2, waiting for transfers between devices: none -> 23.5 us  [the longest x1 12.1 us: local(): lax.all_to_all(smoothed_here, 'tm', split_axis=1, concat_axis=2, tiled=True)]
    unnamed x18 -> x73, local copies, waits for them, and re-layouts: 8.67 us -> 22.7 us
    reduce_scatter x1 -> x2, waiting for transfers between devices: 12.4 us -> 0.49 us  [local(): lax.psum_scatter(partial, 'state', scatter_dimension=0, tiled=True)]
    all_to_all x2, blocking collectives: 39.2 us -> 28.1 us  [local(): lax.all_to_all(piece, 'tm', split_axis=2, concat_axis=0, tiled=True)]
    all_to_all x1, blocking collectives: 31.1 us -> 20.1 us  [local(): lax.all_to_all(smoothed_here, 'tm', split_axis=1, concat_axis=2, tiled=True)]
    unnamed x8 -> x9, other arithmetic: 1.59 us -> 10.5 us
  transfers between devices with their start and end apart: 2 -> 6, of which waited for: 1 -> 3; matrix products, arithmetic and copies ran while one was open for 4% -> 15% of each run, Pallas kernels for 0% -> 0%
where the time goes in v2:
time: 198 us; the launch traced here: 196 us
  blocking collectives  83.4 us (42%)
  local copies, waits for them, and re-layouts  35.7 us (18%)
  waiting for transfers between devices  24.1 us (12%)
  other arithmetic  21.4 us (11%)
  between operations  14.1 us (7%)
  matrix products  8.94 us (5%)
  starting transfers between devices  8.46 us (4%)
    psum x1, blocking collectives, local(): decay_all = lax.psum(padded, 'tm').reshape(tm_count * slab_hours, comps)  35.2 us
    all_to_all x2, blocking collectives, local(): lax.all_to_all(piece, 'tm', split_axis=2, concat_axis=0, tiled=True)  28.1 us
    unnamed x73, local copies, waits for them, and re-layouts  22.7 us
    all_to_all x1, blocking collectives, local(): lax.all_to_all(smoothed_here, 'tm', split_axis=1, concat_axis=2, tiled=True)  20.1 us
    all_to_all x1, waiting for transfers between devices, local(): lax.all_to_all(smoothed_here, 'tm', split_axis=1, concat_axis=2, tiled=True)  12.1 us
    all_to_all x1, waiting for transfers between devices, local(): lax.all_to_all(masked, 'tm', split_axis=1, concat_axis=0, tiled=True)  11.4 us
    unnamed x9, other arithmetic  10.5 us
    dot_general x2, matrix products, local(): jnp.einsum('so,ogy->sgy', loadings, lax.all_gather(rounded, 'state', axis...  4.83 us
  transfers between devices with their start and end apart: 6, of which 3 were waited for; matrix products, arithmetic and copies ran while one was open for 15% of the time, Pallas kernels for 0%

profile of v2, /device:TPU:0, one launch (start us, length us, event | category | flops | bytes accessed | tf_op | source)
XLA Modules:
  0.0 196.1 jit_solution(5214605081453235125)
XLA Ops:
  8.1 3.5 %copy.34 = bf16[64,16,256]{0,1,2:T(8,128)(2,1)} copy(bf16[64,16,256]{2,1,0:T(8,128)(2,1)} %param.4) | data formatting | bytes 1048576 | tf_op args[0]
  14.0 1.4 reshape.7069
  15.5 16.1 %all_to_all.84 = bf16[8,2,8192]{2,1,0:T(2,128)(2,1)} all-to-all(bf16[8,2,8192]{2,1,0:T(2,128)(2,1)S(1)} %reshape.7069), channel_id=1, replica_groups=mesh['tm'=8,'state'=4] {'tm'}, dimensions={0} | all-to-all | bytes 524288 | tf_op jit(solution)/shard_map/all_to_all | solution.py:41
  31.6 2.1 %reshape.7070 = bf16[128,16,64]{2,1,0:T(8,128)(2,1)} reshape(bf16[8,2,8192]{2,1,0:T(2,128)(2,1)} %all_to_all.84) | data formatting | bytes 524288
  33.7 2.2 %copy.39 = bf16[8,64,16,16]{1,0,3,2:T(8,128)(2,1)} copy(bf16[8,64,16,16]{1,2,3,0:T(8,128)(2,1)} %bitcast.86) | data formatting | bytes 524288 | tf_op jit(solution)/shard_map/all_to_all | solution.py:41
  35.9 1.4 reshape.7066
  37.2 2.0 %convolution_bitcast_fusion = f32[2048,256]{0,1:T(8,128)} fusion(bf16[512,256]{0,1:T(8,128)(2,1)S(1)} %reshape.7066, bf16[512,2048]{1,0:T(8,128)(2,1)S(1)} %copy-done), kind=kOutput, calls=%fused_computation | convolution fusion | flops 536870912 | bytes 4456448 | tf_op jit(solution)/shard_map/dot_general | solution.py:43
  39.4 1.4 reshape.7071
  40.8 12.1 %all_to_all.85 = bf16[8,2,8192]{2,1,0:T(2,128)(2,1)} all-to-all(bf16[8,2,8192]{2,1,0:T(2,128)(2,1)S(1)} %reshape.7071), channel_id=1, replica_groups=mesh['tm'=8,'state'=4] {'tm'}, dimensions={0} | all-to-all | bytes 524288 | tf_op jit(solution)/shard_map/all_to_all | solution.py:41
  52.8 2.1 %reshape.7072 = bf16[128,16,64]{2,1,0:T(8,128)(2,1)} reshape(bf16[8,2,8192]{2,1,0:T(2,128)(2,1)} %all_to_all.85) | data formatting | bytes 524288
  55.0 2.3 %copy.36 = bf16[8,64,16,16]{1,0,3,2:T(8,128)(2,1)} copy(bf16[8,64,16,16]{1,2,3,0:T(8,128)(2,1)} %bitcast.87) | data formatting | bytes 524288 | tf_op jit(solution)/shard_map/all_to_all | solution.py:41
  57.3 1.4 reshape.7064
  58.6 2.1 %convolution_bitcast_fusion.1 = f32[2048,256]{0,1:T(8,128)} fusion(bf16[512,256]{0,1:T(8,128)(2,1)S(1)} %reshape.7064, bf16[512,2048]{1,0:T(8,128)(2,1)S(1)} %copy-done), kind=kOutput, calls=%fused_computation.1 | convolution fusion | flops 536870912 | bytes 4456448 | tf_op jit(solution)/shard_map/dot_general | solution.py:43
  61.4 35.2 %psum.7 = f32[16,512]{1,0:T(8,128)S(1)} all-reduce(f32[16,512]{1,0:T(8,128)S(1)} %reshape.7063), channel_id=1, replica_groups=mesh['tm'=8,'state'=4] {'tm'}, use_global_device_ids=true, to_apply=%region_0.0 | all-reduce | flops 8192 | bytes 65536 | tf_op jit(solution)/shard_map/psum | solution.py:35
  101.6 1.9 constant_dynamic-update-slice_fusion.31
  104.0 1.3 constant_dynamic-update-slice_fusion.15
  105.4 1.4 constant_dynamic-update-slice_fusion.14
  107.4 1.4 constant_dynamic-update-slice_fusion.12
  109.4 1.3 constant_dynamic-update-slice_fusion.10
  115.1 1.3 constant_dynamic-update-slice_fusion.2
  117.0 1.5 constant_dynamic-update-slice_fusion
  118.5 20.1 %all_to_all.86 = f32[512,16,16]{0,2,1:T(8,128)S(1)} all-to-all(f32[512,16,16]{0,2,1:T(8,128)} %get-tuple-element.61), channel_id=1, replica_groups=mesh['tm'=8,'state'=4] {'tm'}, dimensions={1} | all-to-all | bytes 1048576 | tf_op jit(solution)/shard_map/all_to_all | solution.py:51
  140.2 4.2 %all-to-all-start.1 = ((f32[512,16,16]{0,2,1:T(8,128)}), f32[512,16,16]{0,2,1:T(8,128)}, u32[]{:S(2)}, u32[]{:S(2)}) async-start(f32[512,16,16]{0,2,1:T(8,128)} %copy-done.3), calls=%async_computation.2 | async-start | bytes 1048576 | tf_op jit(solution)/shard_map/all_to_all | solution.py:51
  144.3 1.6 copy.41
  146.0 12.1 %all-to-all-done.1 = f32[512,16,16]{0,2,1:T(8,128)} async-done(((f32[512,16,16]{0,2,1:T(8,128)}), f32[512,16,16]{0,2,1:T(8,128)}, u32[]{:S(2)}, u32[]{:S(2)}) %all-to-all-start.1) | async-done | bytes 524320 | tf_op jit(solution)/shard_map/all_to_all | solution.py:51
  158.0 4.1 %all-to-all-start.4 = ((bf16[64,16,256]{2,0,1:T(8,128)(2,1)}), bf16[64,16,256]{2,0,1:T(8,128)(2,1)}, u32[]{:S(2)}, u32[]{:S(2)}) async-start(bf16[64,16,256]{2,0,1:T(8,128)(2,1)} %copy.41), calls=%async_computation.6 | async-start | bytes 1048576 | tf_op jit(solution)/shard_map/all_to_all | solution.py:31
  164.1 11.4 %all-to-all-done.4 = bf16[64,16,256]{2,0,1:T(8,128)(2,1)} async-done(((bf16[64,16,256]{2,0,1:T(8,128)(2,1)}), bf16[64,16,256]{2,0,1:T(8,128)(2,1)}, u32[]{:S(2)}, u32[]{:S(2)}) %all-to-all-start.4) | async-done | bytes 524320 | tf_op jit(solution)/shard_map/all_to_all | solution.py:31
  177.4 1.8 copy.49
  181.1 2.2 %copy.45 = f32[512,2,256]{2,1,0:T(2,128)} copy(f32[512,2,256]{0,2,1:T(8,128)} %pad_maximum_fusion) | data formatting | bytes 2097152
  183.4 2.8 %fusion.13 = f32[512,2,128]{0,2,1:T(8,128)} fusion(bf16[2048,2,128]{0,2,1:T(8,128)(2,1)} %all-gather.5.cloned.1.call-done, bf16[512,2048]{1,0:T(8,128)(2,1)S(1)} %copy-done, bf16[512,2,128]{0,2,1:T(8,128)(2,1)S(1)} %copy-done.6), kind=kOutput, calls=%fused_computation.9 | convolution fusion | flops 537133056 | bytes 3932160 | tf_op jit(solution)/shard_map/so,ogy->sgy/dot_general | solution.py:53
  186.2 2.0 %fusion.7 = f32[512,2,128]{0,2,1:T(8,128)S(1)} fusion(bf16[2048,2,128]{0,2,1:T(8,128)(2,1)} %all-gather.3.cloned.1.call-done, bf16[512,2048]{1,0:T(8,128)(2,1)S(1)} %copy-done, bf16[512,2,128]{0,2,1:T(8,128)(2,1)S(1)} %copy-done.5), kind=kOutput, calls=%fused_computation.7 | convolution fusion | flops 537133056 | bytes 3932160 | tf_op jit(solution)/shard_map/so,ogy->sgy/dot_general | solution.py:53
  188.3 1.3 copy.46
  (103 shorter events, 22.9 us)
Async XLA Ops:
  7.2 30.1 %copy-start = (bf16[512,2048]{1,0:T(8,128)(2,1)S(1)}, bf16[512,2048]{1,0:T(8,128)(2,1)}, u32[]{:S(2)}) copy-start(bf16[512,2048]{1,0:T(8,128)(2,1)} %param.6) | copy-start | bytes 6291460
  7.2 94.3 %reduce-scatter.5.cloned.1.call-start = ((), (), s32[]{:S(2)}) async-start(), calls=%async_computation.8 | async-start | bytes 2621440 | tf_op jit(solution)/shard_map/reduce_scatter | solution.py:48
  39.3 64.7 %reduce-scatter.3.cloned.1.call-start = ((), (), s32[]{:S(2)}) async-start(), calls=%async_computation.7 | async-start | bytes 2621440 | tf_op jit(solution)/shard_map/reduce_scatter | solution.py:48
  60.7 0.7 copy-start.24
  60.7 122.6 %all-gather.5.cloned.1.call-start = ((), (), s32[]{:S(2)}) async-start(), calls=%async_computation.10 | async-start | bytes 1310720 | tf_op jit(solution)/shard_map/all_gather | solution.py:56
  96.6 4.9 %copy-start.7 = (f32[1,512]{1,0:T(1,128)}, f32[1,512]{1,0:T(1,128)S(1)}, u32[]{:S(2)}) copy-start(f32[1,512]{1,0:T(1,128)S(1)} %get-tuple-element.50) | copy-start | bytes 6148
  96.6 4.9 %copy-start.9 = (f32[1,512]{1,0:T(1,128)}, f32[1,512]{1,0:T(1,128)S(1)}, u32[]{:S(2)}) copy-start(f32[1,512]{1,0:T(1,128)S(1)} %get-tuple-element.52) | copy-start | bytes 6148
  96.6 4.9 %copy-start.11 = (f32[1,512]{1,0:T(1,128)}, f32[1,512]{1,0:T(1,128)S(1)}, u32[]{:S(2)}) copy-start(f32[1,512]{1,0:T(1,128)S(1)} %get-tuple-element.54) | copy-start | bytes 6148
  96.7 4.9 %copy-start.12 = (f32[1,512]{1,0:T(1,128)}, f32[1,512]{1,0:T(1,128)S(1)}, u32[]{:S(2)}) copy-start(f32[1,512]{1,0:T(1,128)S(1)} %get-tuple-element.56) | copy-start | bytes 6148
  96.7 4.9 %copy-start.13 = (f32[1,512]{1,0:T(1,128)}, f32[1,512]{1,0:T(1,128)S(1)}, u32[]{:S(2)}) copy-start(f32[1,512]{1,0:T(1,128)S(1)} %get-tuple-element.58) | copy-start | bytes 6148
  96.7 4.9 %copy-start.17 = (f32[1,512]{1,0:T(1,128)}, f32[1,512]{1,0:T(1,128)S(1)}, u32[]{:S(2)}) copy-start(f32[1,512]{1,0:T(1,128)S(1)} %get-tuple-element.47) | copy-start | bytes 6148
  96.7 4.9 %copy-start.18 = (f32[1,512]{1,0:T(1,128)}, f32[1,512]{1,0:T(1,128)S(1)}, u32[]{:S(2)}) copy-start(f32[1,512]{1,0:T(1,128)S(1)} %get-tuple-element.49) | copy-start | bytes 6148
  96.7 4.9 %copy-start.19 = (f32[1,512]{1,0:T(1,128)}, f32[1,512]{1,0:T(1,128)S(1)}, u32[]{:S(2)}) copy-start(f32[1,512]{1,0:T(1,128)S(1)} %get-tuple-element.51) | copy-start | bytes 6148
  96.7 4.9 %copy-start.20 = (f32[1,512]{1,0:T(1,128)}, f32[1,512]{1,0:T(1,128)S(1)}, u32[]{:S(2)}) copy-start(f32[1,512]{1,0:T(1,128)S(1)} %get-tuple-element.53) | copy-start | bytes 6148
  96.7 4.9 %copy-start.21 = (f32[1,512]{1,0:T(1,128)}, f32[1,512]{1,0:T(1,128)S(1)}, u32[]{:S(2)}) copy-start(f32[1,512]{1,0:T(1,128)S(1)} %get-tuple-element.55) | copy-start | bytes 6148
  96.7 4.9 %copy-start.22 = (f32[1,512]{1,0:T(1,128)}, f32[1,512]{1,0:T(1,128)S(1)}, u32[]{:S(2)}) copy-start(f32[1,512]{1,0:T(1,128)S(1)} %get-tuple-element.57) | copy-start | bytes 6148
  96.7 4.9 %copy-start.23 = (f32[1,512]{1,0:T(1,128)}, f32[1,512]{1,0:T(1,128)S(1)}, u32[]{:S(2)}) copy-start(f32[1,512]{1,0:T(1,128)S(1)} %get-tuple-element.59) | copy-start | bytes 6148
  104.0 7.3 %copy-start.10 = (f32[1,512]{1,0:T(1,128)S(1)}, f32[1,512]{1,0:T(1,128)}, u32[]{:S(2)}) copy-start(f32[1,512]{1,0:T(1,128)} %copy-done.9) | copy-start | bytes 6148
  104.0 7.3 %copy-start.16 = (f32[512]{0:T(512)S(1)}, f32[512]{0:T(512)}, u32[]{:S(2)}) copy-start(f32[512]{0:T(512)} %get-tuple-element.86) | copy-start | bytes 6148
  104.0 8.6 %copy-start.8 = (f32[1,512]{1,0:T(1,128)S(1)}, f32[1,512]{1,0:T(1,128)}, u32[]{:S(2)}) copy-start(f32[1,512]{1,0:T(1,128)} %copy-done.7) | copy-start | bytes 6148
  104.0 8.6 %copy-start.15 = (f32[512]{0:T(512)S(1)}, f32[512]{0:T(512)}, u32[]{:S(2)}) copy-start(f32[512]{0:T(512)} %get-tuple-element.88) | copy-start | bytes 6148
  104.0 9.8 %copy-start.14 = (f32[512]{0:T(512)S(1)}, f32[512]{0:T(512)}, u32[]{:S(2)}) copy-start(f32[512]{0:T(512)} %get-tuple-element.90) | copy-start | bytes 6148
  118.5 20.1 %copy-start.3 = (f32[512,16,16]{0,2,1:T(8,128)}, f32[512,16,16]{0,2,1:T(8,128)S(1)}, u32[]{:S(2)}) copy-start(f32[512,16,16]{0,2,1:T(8,128)S(1)} %get-tuple-element.60) | copy-start | bytes 1572868
  138.6 0.8 copy-start.1
  140.2 17.9 %all-to-all-start.1 = ((f32[512,16,16]{0,2,1:T(8,128)}), f32[512,16,16]{0,2,1:T(8,128)}, u32[]{:S(2)}, u32[]{:S(2)}) async-start(f32[512,16,16]{0,2,1:T(8,128)} %copy-done.3), calls=%async_computation.2 | async-start | bytes 1048576 | tf_op jit(solution)/shard_map/all_to_all | solution.py:51
  158.0 17.5 %all-to-all-start.4 = ((bf16[64,16,256]{2,0,1:T(8,128)(2,1)}), bf16[64,16,256]{2,0,1:T(8,128)(2,1)}, u32[]{:S(2)}, u32[]{:S(2)}) async-start(bf16[64,16,256]{2,0,1:T(8,128)(2,1)} %copy.41), calls=%async_computation.6 | async-start | bytes 1048576 | tf_op jit(solution)/shard_map/all_to_all | solution.py:31
  162.2 24.0 %all-gather.3.cloned.1.call-start = ((), (), s32[]{:S(2)}) async-start(), calls=%async_computation.9 | async-start | bytes 1310720 | tf_op jit(solution)/shard_map/all_gather | solution.py:56
  163.3 16.7 %copy-start.2 = (f32[512,8,2,16]{0,3,1,2:T(8,128)S(1)}, f32[512,8,2,16]{0,3,1,2:T(8,128)}, u32[]{:S(2)}) copy-start(f32[512,8,2,16]{0,3,1,2:T(8,128)} %copy-done.1) | copy-start | bytes 1572868
  180.1 3.3 %copy-start.6 = (bf16[512,2,128]{0,2,1:T(8,128)(2,1)S(1)}, bf16[512,2,128]{0,2,1:T(8,128)(2,1)}, u32[]{:S(2)}) copy-start(bf16[512,2,128]{0,2,1:T(8,128)(2,1)} %copy.50) | copy-start | bytes 786436
  183.3 2.8 %copy-start.5 = (bf16[512,2,128]{0,2,1:T(8,128)(2,1)S(1)}, bf16[512,2,128]{0,2,1:T(8,128)(2,1)}, u32[]{:S(2)}) copy-start(bf16[512,2,128]{0,2,1:T(8,128)(2,1)} %copy.49) | copy-start | bytes 786436
  186.2 2.0 %copy-start.4 = (f32[512,2,128]{0,2,1:T(8,128)S(1)}, f32[512,2,128]{0,2,1:T(8,128)}, u32[]{:S(2)}) copy-start(f32[512,2,128]{0,2,1:T(8,128)} %fusion.13) | copy-start | bytes 1572868
Sparse Core Ops, SparseCore 0:
  39.4 30.4 reduce-scatter.4
  72.6 31.3 reduce-scatter.2
  140.3 14.7 all-gather.4
  164.3 17.0 all-gather.2

commit v3 on v2

--- a/solution.py
+++ b/solution.py
@@ -1,38 +1,57 @@
 import jax
 import jax.numpy as jnp
 from jax import lax
+from jax.experimental import pallas as pl
+from jax.experimental.pallas import tpu as pltpu
 from jax.sharding import PartitionSpec as P
 
 CHUNKS = 2
+LANES = 128
+
+
+def recurrence_kernel(rate_ref, info_ref, out_ref):
+    hours = info_ref.shape[0]
+    state = jnp.zeros(info_ref.shape[1:], jnp.float32)
+    for hour in range(hours):
+        state = rate_ref[hour] * state + info_ref[hour]
+        out_ref[hour] = state
+    state = jnp.zeros(info_ref.shape[1:], jnp.float32)
+    for hour in reversed(range(hours)):
+        rate = rate_ref[hour]
+        state = rate * state + (1.0 - rate * rate) * out_ref[hour]
+        out_ref[hour] = state
+
+
+def run_recurrence(rates, information):
+    return pl.pallas_call(
+        recurrence_kernel,
+        out_shape=jax.ShapeDtypeStruct(information.shape, jnp.float32),
+        in_specs=[pl.BlockSpec(memory_space=pltpu.VMEM)] * 2,
+        out_specs=pl.BlockSpec(memory_space=pltpu.VMEM),
+    )(rates, information)
 
 
 def smooth_chunk(information, decay_all):
     comps, hours, width = information.shape
-    state = jnp.zeros((comps, width), jnp.float32)
-    filtered = []
-    for hour in range(hours):
-        state = decay_all[hour][:, None] * state + information[:, hour, :]
-        filtered.append(state)
-    state = jnp.zeros((comps, width), jnp.float32)
-    rows = [None] * hours
-    for hour in reversed(range(hours)):
-        rate = decay_all[hour]
-        state = rate[:, None] * state + (1.0 - rate * rate)[:, None] * filtered[hour]
-        rows[hour] = state
-    return jnp.stack(rows, axis=1)
+    hours_first = jnp.transpose(information, (1, 0, 2))
+    rates = jnp.broadcast_to(decay_all[:, :, None], (hours, comps, width))
+    if (comps * width) % LANES == 0:
+        dense = (hours, comps * width // LANES, LANES)
+        out = run_recurrence(rates.reshape(dense), hours_first.reshape(dense))
+    else:
+        out = run_recurrence(rates, hours_first)
+    return jnp.transpose(out.reshape(hours, comps, width), (1, 0, 2))
 
 
 def local(obs, mask, loadings, decay):
     tm_count = lax.axis_size("tm")
-    tm_index = lax.axis_index("tm")
     _, hours, members = obs.shape
     chunk_members = members // CHUNKS
     masked = obs * mask[:, :, None].astype(obs.dtype)
+    copies = jnp.broadcast_to(decay[None], (tm_count,) + decay.shape)
+    decay_all = lax.all_to_all(copies, "tm", split_axis=0, concat_axis=0, tiled=True)
+    decay_all = decay_all.reshape(hours, decay.shape[1])
     by_hour = lax.all_to_all(masked, "tm", split_axis=1, concat_axis=0, tiled=True)
-    slab_hours, comps = decay.shape
-    padded = jnp.zeros((tm_count, slab_hours, comps), jnp.float32)
-    padded = lax.dynamic_update_slice(padded, decay[None], (tm_index, 0, 0))
-    decay_all = lax.psum(padded, "tm").reshape(tm_count * slab_hours, comps)
     smoothed_parts = []
     residual_parts = []
     for chunk in range(CHUNKS):

time: 198 us -> 187 us (0.944)
  local copies, waits for them, and re-layouts: 35.7 us -> 67.4 us
  blocking collectives: 83.4 us -> 54.8 us
  other arithmetic: 21.4 us -> 4.75 us
  Pallas kernels: 0 us -> 4.28 us
    psum x1 -> x0, blocking collectives: 35.2 us -> none  [local(): decay_all = lax.psum(padded, 'tm').reshape(tm_count * slab_hours, comps)]
    reshape x1 -> x7, local copies, waits for them, and re-layouts: 0.02 us -> 26.4 us  [the longest x3 11.9 us: smooth_chunk(): out = run_recurrence(rates.reshape(dense), hours_first.reshape(dense))]
    unnamed x9 -> x0, other arithmetic: 10.5 us -> none
    all_to_all x0 -> x1, blocking collectives: none -> 10.1 us  [local(): lax.all_to_all(copies, 'tm', split_axis=0, concat_axis=0, tiled=True)]
    transpose x0 -> x2, local copies, waits for them, and re-layouts: none -> 7.02 us  [smooth_chunk(): return jnp.transpose(out.reshape(hours, comps, width), (1, 0, 2))]
    unnamed x73 -> x23, local copies, waits for them, and re-layouts: 22.7 us -> 18.3 us
    pallas_call x0 -> x2, Pallas kernels: none -> 4.28 us  [run_recurrence(): pl.pallas_call(recurrence_kernel, out_shape=jax.ShapeDtypeStruct(informat...]
    sub x7 -> x0, other arithmetic: 4.14 us -> none  [smooth_chunk(): 1.0 - rate * rate]
  transfers between devices with their start and end apart: 6 -> 6, of which waited for: 3 -> 2; matrix products, arithmetic and copies ran while one was open for 15% -> 32% of each run, Pallas kernels for 0% -> 2%
where the time goes in v3:
time: 187 us; the launch traced here: 186 us
  local copies, waits for them, and re-layouts  67.4 us (36%)
  blocking collectives  54.8 us (29%)
  waiting for transfers between devices  23.5 us (13%)
  between operations  13.9 us (7%)
  matrix products  8.99 us (5%)
  starting transfers between devices  8.46 us (5%)
  other arithmetic  4.75 us (3%)
  Pallas kernels  4.28 us (2%)
    all_to_all x2, blocking collectives, local(): lax.all_to_all(piece, 'tm', split_axis=2, concat_axis=0, tiled=True)  28.1 us
    unnamed x23, local copies, waits for them, and re-layouts  18.3 us
    all_to_all x1, blocking collectives, local(): lax.all_to_all(smoothed_here, 'tm', split_axis=1, concat_axis=2, tiled=True)  16.6 us
    all_to_all x1, waiting for transfers between devices, local(): lax.all_to_all(smoothed_here, 'tm', split_axis=1, concat_axis=2, tiled=True)  11.9 us
    reshape x3, local copies, waits for them, and re-layouts, smooth_chunk(): out = run_recurrence(rates.reshape(dense), hours_first.reshape(dense))  11.9 us
    all_to_all x1, waiting for transfers between devices, local(): lax.all_to_all(masked, 'tm', split_axis=1, concat_axis=0, tiled=True)  11.5 us
    all_to_all x1, blocking collectives, local(): lax.all_to_all(copies, 'tm', split_axis=0, concat_axis=0, tiled=True)  10.1 us
    reshape x2, local copies, waits for them, and re-layouts, smooth_chunk(): return jnp.transpose(out.reshape(hours, comps, width), (1, 0, 2))  7.43 us
  transfers between devices with their start and end apart: 6, of which 2 were waited for; matrix products, arithmetic and copies ran while one was open for 32% of the time, Pallas kernels for 2%

profile of v3, /device:TPU:0, one launch (start us, length us, event | category | flops | bytes accessed | tf_op | source)
XLA Modules:
  0.0 186.0 jit_solution(13874485534348682524)
XLA Ops:
  8.1 3.5 %copy.42 = bf16[64,16,256]{0,1,2:T(8,128)(2,1)} copy(bf16[64,16,256]{2,1,0:T(8,128)(2,1)} %param.4) | data formatting | bytes 1048576 | tf_op args[0]
  15.5 16.1 %all_to_all.89 = bf16[8,2,8192]{2,1,0:T(2,128)(2,1)} all-to-all(bf16[8,2,8192]{2,1,0:T(2,128)(2,1)S(1)} %reshape.50), channel_id=1, replica_groups=mesh['tm'=8,'state'=4] {'tm'}, dimensions={0} | all-to-all | bytes 524288 | tf_op jit(solution)/shard_map/all_to_all | solution.py:60
  31.6 2.1 %reshape.51 = bf16[128,16,64]{2,1,0:T(8,128)(2,1)} reshape(bf16[8,2,8192]{2,1,0:T(2,128)(2,1)} %all_to_all.89) | data formatting | bytes 524288
  33.7 2.2 %copy.44 = bf16[8,64,16,16]{1,0,3,2:T(8,128)(2,1)} copy(bf16[8,64,16,16]{1,2,3,0:T(8,128)(2,1)} %bitcast.76) | data formatting | bytes 524288 | tf_op jit(solution)/shard_map/all_to_all | solution.py:60
  37.3 2.1 %convolution_bitcast_fusion.1 = f32[2048,256]{0,1:T(8,128)} fusion(bf16[512,256]{0,1:T(8,128)(2,1)S(1)} %reshape.39, bf16[512,2048]{1,0:T(8,128)(2,1)S(1)} %copy-done), kind=kOutput, calls=%fused_computation.1 | convolution fusion | flops 536870912 | bytes 4456448 | tf_op jit(solution)/shard_map/dot_general | solution.py:62
  40.8 12.1 %all_to_all.90 = bf16[8,2,8192]{2,1,0:T(2,128)(2,1)} all-to-all(bf16[8,2,8192]{2,1,0:T(2,128)(2,1)S(1)} %reshape.48), channel_id=1, replica_groups=mesh['tm'=8,'state'=4] {'tm'}, dimensions={0} | all-to-all | bytes 524288 | tf_op jit(solution)/shard_map/all_to_all | solution.py:60
  52.9 2.1 %reshape.49 = bf16[128,16,64]{2,1,0:T(8,128)(2,1)} reshape(bf16[8,2,8192]{2,1,0:T(2,128)(2,1)} %all_to_all.90) | data formatting | bytes 524288
  55.0 2.3 %copy.49 = bf16[8,64,16,16]{1,0,3,2:T(8,128)(2,1)} copy(bf16[8,64,16,16]{1,2,3,0:T(8,128)(2,1)} %bitcast.77) | data formatting | bytes 524288 | tf_op jit(solution)/shard_map/all_to_all | solution.py:60
  58.7 2.1 %convolution_bitcast_fusion = f32[2048,256]{0,1:T(8,128)} fusion(bf16[512,256]{0,1:T(8,128)(2,1)S(1)} %reshape.43, bf16[512,2048]{1,0:T(8,128)(2,1)S(1)} %copy-done), kind=kOutput, calls=%fused_computation | convolution fusion | flops 536870912 | bytes 4456448 | tf_op jit(solution)/shard_map/dot_general | solution.py:62
  61.5 10.1 %all_to_all.91 = f32[8,2,512]{2,1,0:T(2,128)S(1)} all-to-all(f32[8,2,512]{2,1,0:T(2,128)S(1)} %broadcast_in_dim.6), channel_id=1, replica_groups=mesh['tm'=8,'state'=4] {'tm'}, dimensions={0} | all-to-all | bytes 65536 | tf_op jit(solution)/shard_map/all_to_all | solution.py:52
  71.6 2.6 %broadcast_in_dim.8 = f32[16,512,16]{2,1,0:T(8,128)} broadcast(f32[16,512]{1,0:T(8,128)S(1)} %broadcast_in_dim.7), dimensions={0,1} | broadcast | bytes 557056 | tf_op jit(solution)/shard_map/broadcast_in_dim | solution.py:37
  74.1 3.9 %reshape.38.rate_ref = f32[16,64,128]{2,1,0:T(8,128)} reshape(f32[16,512,16]{2,1,0:T(8,128)} %broadcast_in_dim.8) | data formatting | bytes 1048576 | tf_op jit(solution)/shard_map/reshape | solution.py:40
  78.1 3.6 %copy.45 = f32[512,16,16]{2,0,1:T(8,128)} copy(f32[512,16,16]{0,2,1:T(8,128)} %bitcast.82) | data formatting | bytes 1048576 | tf_op jit(solution)/shard_map/reshape | solution.py:68
  81.6 4.0 %reshape.41.info_ref = f32[16,64,128]{2,1,0:T(8,128)} reshape(f32[16,512,16]{2,1,0:T(8,128)} %bitcast.69) | data formatting | bytes 1048576 | tf_op jit(solution)/shard_map/reshape | solution.py:40
  85.6 2.1 %shard_map.59 = f32[16,64,128]{2,1,0:T(8,128)} custom-call(f32[16,64,128]{2,1,0:T(8,128)} %reshape.38.rate_ref, f32[16,64,128]{2,1,0:T(8,128)} %reshape.41.info_ref), custom_call_target="tpu_custom_call" | custom-call | tf_op jit(solution)/shard_map/pallas_call | solution.py:26
  87.8 3.7 %reshape.42 = f32[16,512,16]{2,1,0:T(8,128)} reshape(f32[16,64,128]{2,1,0:T(8,128)} %shard_map.59) | data formatting | bytes 1048576 | tf_op jit(solution)/shard_map/reshape | solution.py:43
  91.5 3.5 %copy.46 = f32[512,16,16]{0,2,1:T(8,128)} copy(f32[512,16,16]{2,0,1:T(8,128)} %bitcast.70) | data formatting | bytes 1048576 | tf_op jit(solution)/shard_map/transpose | solution.py:43
  95.0 16.6 %all_to_all.92 = f32[512,16,16]{0,2,1:T(8,128)S(1)} all-to-all(f32[512,16,16]{0,2,1:T(8,128)} %copy.46), channel_id=1, replica_groups=mesh['tm'=8,'state'=4] {'tm'}, dimensions={1} | all-to-all | bytes 1048576 | tf_op jit(solution)/shard_map/all_to_all | solution.py:70
  113.2 3.5 %copy.50 = f32[512,16,16]{2,0,1:T(8,128)} copy(f32[512,16,16]{0,2,1:T(8,128)} %bitcast.81) | data formatting | bytes 1048576 | tf_op jit(solution)/shard_map/reshape | solution.py:68
  116.8 4.0 %reshape.45.info_ref = f32[16,64,128]{2,1,0:T(8,128)} reshape(f32[16,512,16]{2,1,0:T(8,128)} %bitcast.71) | data formatting | bytes 1048576 | tf_op jit(solution)/shard_map/reshape | solution.py:40
  120.7 2.1 %shard_map.60 = f32[16,64,128]{2,1,0:T(8,128)} custom-call(f32[16,64,128]{2,1,0:T(8,128)} %reshape.38.rate_ref, f32[16,64,128]{2,1,0:T(8,128)} %reshape.45.info_ref), custom_call_target="tpu_custom_call" | custom-call | tf_op jit(solution)/shard_map/pallas_call | solution.py:26
  122.9 3.7 %reshape.46 = f32[16,512,16]{2,1,0:T(8,128)} reshape(f32[16,64,128]{2,1,0:T(8,128)} %shard_map.60) | data formatting | bytes 1048576 | tf_op jit(solution)/shard_map/reshape | solution.py:43
  126.6 3.5 %copy.51 = f32[512,16,16]{0,2,1:T(8,128)} copy(f32[512,16,16]{2,0,1:T(8,128)} %bitcast.72) | data formatting | bytes 1048576 | tf_op jit(solution)/shard_map/transpose | solution.py:43
  130.1 4.2 %all-to-all-start.4 = ((f32[512,16,16]{0,2,1:T(8,128)}), f32[512,16,16]{0,2,1:T(8,128)}, u32[]{:S(2)}, u32[]{:S(2)}) async-start(f32[512,16,16]{0,2,1:T(8,128)} %copy.51), calls=%async_computation.6 | async-start | bytes 1048576 | tf_op jit(solution)/shard_map/all_to_all | solution.py:70
  134.3 1.6 copy.53
  135.9 11.9 %all-to-all-done.4 = f32[512,16,16]{0,2,1:T(8,128)} async-done(((f32[512,16,16]{0,2,1:T(8,128)}), f32[512,16,16]{0,2,1:T(8,128)}, u32[]{:S(2)}, u32[]{:S(2)}) %all-to-all-start.4) | async-done | bytes 524320 | tf_op jit(solution)/shard_map/all_to_all | solution.py:70
  147.8 4.1 %all-to-all-start.5 = ((bf16[64,16,256]{2,0,1:T(8,128)(2,1)}), bf16[64,16,256]{2,0,1:T(8,128)(2,1)}, u32[]{:S(2)}, u32[]{:S(2)}) async-start(bf16[64,16,256]{2,0,1:T(8,128)(2,1)} %copy.53), calls=%async_computation.7 | async-start | bytes 1048576 | tf_op jit(solution)/shard_map/all_to_all | solution.py:54
  153.9 11.5 %all-to-all-done.5 = bf16[64,16,256]{2,0,1:T(8,128)(2,1)} async-done(((bf16[64,16,256]{2,0,1:T(8,128)(2,1)}), bf16[64,16,256]{2,0,1:T(8,128)(2,1)}, u32[]{:S(2)}, u32[]{:S(2)}) %all-to-all-start.5) | async-done | bytes 524320 | tf_op jit(solution)/shard_map/all_to_all | solution.py:54
  167.2 1.8 copy.61
  171.0 2.2 %copy.57 = f32[512,2,256]{2,1,0:T(2,128)} copy(f32[512,2,256]{0,2,1:T(8,128)} %pad_maximum_fusion) | data formatting | bytes 2097152
  173.2 2.8 %fusion.7 = f32[512,2,128]{0,2,1:T(8,128)} fusion(bf16[2048,2,128]{0,2,1:T(8,128)(2,1)} %all-gather.3.cloned.1.call-done, bf16[512,2048]{1,0:T(8,128)(2,1)S(1)} %copy-done, bf16[512,2,128]{0,2,1:T(8,128)(2,1)S(1)} %copy-done.5), kind=kOutput, calls=%fused_computation.7 | convolution fusion | flops 537133056 | bytes 3932160 | tf_op jit(solution)/shard_map/so,ogy->sgy/dot_general | solution.py:72
  176.0 2.0 %fusion.13 = f32[512,2,128]{0,2,1:T(8,128)S(1)} fusion(bf16[2048,2,128]{0,2,1:T(8,128)(2,1)} %all-gather.5.cloned.1.call-done, bf16[512,2048]{1,0:T(8,128)(2,1)S(1)} %copy-done, bf16[512,2,128]{0,2,1:T(8,128)(2,1)S(1)} %copy-done.4), kind=kOutput, calls=%fused_computation.9 | convolution fusion | flops 537133056 | bytes 3932160 | tf_op jit(solution)/shard_map/so,ogy->sgy/dot_general | solution.py:72
  (45 shorter events, 18.4 us)
Async XLA Ops:
  7.2 30.1 %copy-start = (bf16[512,2048]{1,0:T(8,128)(2,1)S(1)}, bf16[512,2048]{1,0:T(8,128)(2,1)}, u32[]{:S(2)}) copy-start(bf16[512,2048]{1,0:T(8,128)(2,1)} %param.6) | copy-start | bytes 6291460
  7.2 70.9 %reduce-scatter.3.cloned.1.call-start = ((), (), s32[]{:S(2)}) async-start(), calls=%async_computation.8 | async-start | bytes 2621440 | tf_op jit(solution)/shard_map/reduce_scatter | solution.py:67
  39.4 73.9 %reduce-scatter.5.cloned.1.call-start = ((), (), s32[]{:S(2)}) async-start(), calls=%async_computation.9 | async-start | bytes 2621440 | tf_op jit(solution)/shard_map/reduce_scatter | solution.py:67
  60.8 0.7 copy-start.6
  60.8 112.4 %all-gather.3.cloned.1.call-start = ((), (), s32[]{:S(2)}) async-start(), calls=%async_computation.10 | async-start | bytes 1310720 | tf_op jit(solution)/shard_map/all_gather | solution.py:75
  111.6 0.8 copy-start.1
  130.1 17.7 %all-to-all-start.4 = ((f32[512,16,16]{0,2,1:T(8,128)}), f32[512,16,16]{0,2,1:T(8,128)}, u32[]{:S(2)}, u32[]{:S(2)}) async-start(f32[512,16,16]{0,2,1:T(8,128)} %copy.51), calls=%async_computation.6 | async-start | bytes 1048576 | tf_op jit(solution)/shard_map/all_to_all | solution.py:70
  147.8 17.5 %all-to-all-start.5 = ((bf16[64,16,256]{2,0,1:T(8,128)(2,1)}), bf16[64,16,256]{2,0,1:T(8,128)(2,1)}, u32[]{:S(2)}, u32[]{:S(2)}) async-start(bf16[64,16,256]{2,0,1:T(8,128)(2,1)} %copy.53), calls=%async_computation.7 | async-start | bytes 1048576 | tf_op jit(solution)/shard_map/all_to_all | solution.py:54
  152.0 24.0 %all-gather.5.cloned.1.call-start = ((), (), s32[]{:S(2)}) async-start(), calls=%async_computation.11 | async-start | bytes 1310720 | tf_op jit(solution)/shard_map/all_gather | solution.py:75
  153.1 16.8 %copy-start.2 = (f32[512,8,2,16]{0,3,1,2:T(8,128)S(1)}, f32[512,8,2,16]{0,3,1,2:T(8,128)}, u32[]{:S(2)}) copy-start(f32[512,8,2,16]{0,3,1,2:T(8,128)} %copy-done.1) | copy-start | bytes 1572868
  169.9 3.3 %copy-start.5 = (bf16[512,2,128]{0,2,1:T(8,128)(2,1)S(1)}, bf16[512,2,128]{0,2,1:T(8,128)(2,1)}, u32[]{:S(2)}) copy-start(bf16[512,2,128]{0,2,1:T(8,128)(2,1)} %copy.61) | copy-start | bytes 786436
  173.2 2.8 %copy-start.4 = (bf16[512,2,128]{0,2,1:T(8,128)(2,1)S(1)}, bf16[512,2,128]{0,2,1:T(8,128)(2,1)}, u32[]{:S(2)}) copy-start(bf16[512,2,128]{0,2,1:T(8,128)(2,1)} %copy.62) | copy-start | bytes 786436
  176.0 2.0 %copy-start.3 = (f32[512,2,128]{0,2,1:T(8,128)S(1)}, f32[512,2,128]{0,2,1:T(8,128)}, u32[]{:S(2)}) copy-start(f32[512,2,128]{0,2,1:T(8,128)} %fusion.7) | copy-start | bytes 1572868
Sparse Core Ops, SparseCore 0:
  39.5 30.4 reduce-scatter.2
  72.6 31.3 reduce-scatter.4
  113.3 15.8 all-gather.2
  154.1 18.1 all-gather.4

commit v4 on v1

--- a/solution.py
+++ b/solution.py
@@ -6,21 +6,28 @@
 
 def local(obs, mask, loadings, decay):
     tm_count = lax.axis_size("tm")
-    _, hours, members = obs.shape
+    stations_local, hours, members = obs.shape
     members_here = members // tm_count
+    hours_here = hours // tm_count
     masked = obs * mask[:, :, None].astype(obs.dtype)
-    by_member = lax.all_to_all(masked, "tm", split_axis=2, concat_axis=0, tiled=True)
-    by_hour = lax.all_to_all(masked, "tm", split_axis=1, concat_axis=0, tiled=True)
-    stations_here = by_member.shape[0]
-    partial = jnp.dot(
-        loadings.T,
-        by_member.reshape(stations_here, hours * members_here),
-        preferred_element_type=jnp.float32,
+    outgoing = jnp.transpose(
+        masked.reshape(stations_local, hours, tm_count, members_here), (2, 0, 1, 3)
     )
+    by_member = lax.all_to_all(outgoing, "tm", split_axis=0, concat_axis=0, tiled=True)
+    stations_here = tm_count * stations_local
+    by_member = by_member.reshape(stations_here, hours * members_here)
+    outgoing = jnp.transpose(
+        masked.reshape(stations_local, tm_count, hours_here, members), (1, 0, 2, 3)
+    )
+    by_hour = lax.all_to_all(outgoing, "tm", split_axis=0, concat_axis=0, tiled=True)
+    by_hour = by_hour.reshape(stations_here, hours_here, members)
+    copies = jnp.broadcast_to(decay[None], (tm_count,) + decay.shape)
+    decay_all = lax.all_to_all(copies, "tm", split_axis=0, concat_axis=0, tiled=True)
+    decay_all = decay_all.reshape(hours, decay.shape[1])
+    partial = jnp.dot(loadings.T, by_member, preferred_element_type=jnp.float32)
     information = lax.psum_scatter(partial, "state", scatter_dimension=0, tiled=True)
     comps = information.shape[0]
     information = information.reshape(comps, hours, members_here)
-    decay_all = lax.all_gather(decay, "tm", axis=0, tiled=True)
     state = jnp.zeros((comps, members_here), jnp.float32)
     filtered = []
     for hour in range(hours):

time: 160 us -> 166 us (1.038)
  waiting for transfers between devices: 12.5 us -> 32.8 us
  blocking collectives: 101 us -> 80.8 us
  local copies, waits for them, and re-layouts: 19.2 us -> 23.3 us
    all_gather x1 -> x0, blocking collectives: 30.4 us -> none  [local(): decay_all = lax.all_gather(decay, 'tm', axis=0, tiled=True)]
    reduce_scatter x1, waiting for transfers between devices: 12.4 us -> 32.8 us  [local(): lax.psum_scatter(partial, 'state', scatter_dimension=0, tiled=True)]
    all_to_all x2 -> x3, blocking collectives: 39.2 us -> 49.7 us  [the longest x2 39.6 us: local(): lax.all_to_all(outgoing, 'tm', split_axis=0, concat_axis=0, tiled=True)]
    unnamed x18 -> x20, local copies, waits for them, and re-layouts: 8.67 us -> 13 us
    mul x2 -> x0, local copies, waits for them, and re-layouts: 3.39 us -> none  [local(): masked = obs * mask[:, :, None].astype(obs.dtype)]
    reshape x1 -> x3, local copies, waits for them, and re-layouts: 1.41 us -> 3.7 us  [the longest x1 2.55 us: local(): by_member = by_member.reshape(stations_here, hours * members_here)]
    convert_element_type x2 -> x1, local copies, waits for them, and re-layouts: 3.59 us -> 2.52 us  [local(): residual = by_hour.astype(jnp.float32) - fitted]
where the time goes in v4:
time: 166 us; the launch traced here: 165 us
  blocking collectives  80.8 us (49%)
  waiting for transfers between devices  32.8 us (20%)
  local copies, waits for them, and re-layouts  23.3 us (14%)
  between operations  14.3 us (9%)
  matrix products  7.39 us (4%)
  other arithmetic  6.45 us (4%)
    all_to_all x2, blocking collectives, local(): lax.all_to_all(outgoing, 'tm', split_axis=0, concat_axis=0, tiled=True)  39.6 us
    reduce_scatter x1, waiting for transfers between devices, local(): lax.psum_scatter(partial, 'state', scatter_dimension=0, tiled=True)  32.8 us
    all_to_all x1, blocking collectives, local(): lax.all_to_all(smoothed_here, 'tm', split_axis=1, concat_axis=2, tiled=True)  31.1 us
    unnamed x20, local copies, waits for them, and re-layouts  13 us
    all_to_all x1, blocking collectives, local(): lax.all_to_all(copies, 'tm', split_axis=0, concat_axis=0, tiled=True)  10.1 us
    dot_general x1, matrix products, local(): partial = jnp.dot(loadings.T, by_member, preferred_element_type=jnp.float32)  4.26 us
  transfers between devices with their start and end apart: 2, of which 1 were waited for; matrix products, arithmetic and copies ran while one was open for 4% of the time, Pallas kernels for 0%

profile of v4, /device:TPU:0, one launch (start us, length us, event | category | flops | bytes accessed | tf_op | source)
XLA Modules:
  0.0 165.1 jit_solution(15938785075299070081)
XLA Ops:
  7.2 0.0 copy-start
  7.2 0.0 reduce-scatter.2.cloned.1.call-start
  7.2 2.7 %copy.18 = bf16[64,16,256]{0,2,1:T(8,128)(2,1)} copy(bf16[64,16,256]{2,1,0:T(8,128)(2,1)} %param.4) | data formatting | bytes 1048576 | tf_op args[0]
  9.9 0.7 convert_element_type.13
  10.6 1.3 broadcast_multiply_fusion
  11.9 1.1 copy.28
  13.0 3.0 %reshape.3608 = bf16[8,2,16384]{2,1,0:T(2,128)(2,1)} reshape(bf16[8,16,32,64]{3,2,1,0:T(8,128)(2,1)} %bitcast.59) | data formatting | bytes 1048576
  16.0 21.9 %all_to_all.33 = bf16[8,2,16384]{2,1,0:T(2,128)(2,1)} all-to-all(bf16[8,2,16384]{2,1,0:T(2,128)(2,1)} %reshape.3608), channel_id=1, replica_groups=mesh['tm'=8,'state'=4] {'tm'}, dimensions={0} | all-to-all | bytes 1048576 | tf_op jit(solution)/shard_map/all_to_all | solution.py:16
  37.9 3.0 %reshape.3609 = bf16[8,16,32,64]{3,2,1,0:T(8,128)(2,1)} reshape(bf16[8,2,16384]{2,1,0:T(2,128)(2,1)} %all_to_all.33) | data formatting | bytes 1048576
  40.9 2.9 %copy.20 = bf16[8,64,16,32]{1,0,3,2:T(8,128)(2,1)} copy(bf16[8,64,16,32]{1,3,2,0:T(8,128)(2,1)} %bitcast.57) | data formatting | bytes 1048576 | tf_op jit(solution)/shard_map/all_to_all | solution.py:16
  43.8 2.6 %reshape.3603 = bf16[512,512]{0,1:T(8,128)(2,1)} reshape(bf16[8,64,16,32]{1,0,3,2:T(8,128)(2,1)} %copy.20) | data formatting | bytes 1048576 | tf_op jit(solution)/shard_map/reshape | solution.py:18
  46.4 4.3 %convolution_bitcast_fusion = f32[2048,512]{0,1:T(8,128)} fusion(bf16[512,512]{0,1:T(8,128)(2,1)} %reshape.3603, bf16[512,2048]{1,0:T(8,128)(2,1)S(1)} %copy-done), kind=kOutput, calls=%fused_computation | convolution fusion | flops 1073741824 | bytes 6815744 | tf_op jit(solution)/shard_map/dot_general | solution.py:27
  50.6 0.0 reduce-scatter.2.cloned.1.call-update
  50.6 0.0 all-gather.2.cloned.1.call-start
  50.7 0.6 copy-done.3
  51.3 10.1 %all_to_all.34 = f32[8,2,512]{2,1,0:T(2,128)S(1)} all-to-all(f32[8,2,512]{2,1,0:T(2,128)S(1)} %broadcast_in_dim.2), channel_id=1, replica_groups=mesh['tm'=8,'state'=4] {'tm'}, dimensions={0} | all-to-all | bytes 65536 | tf_op jit(solution)/shard_map/all_to_all | solution.py:25
  61.6 32.8 %reduce-scatter.2.cloned.1.call-done = f32[512,512]{0,1:T(8,128)} async-done(((f32[2048,512]{0,1:T(8,128)}), f32[512,512]{0,1:T(8,128)}) %reduce-scatter.2.cloned.1.call-update) | async-done | bytes 1048592 | tf_op jit(solution)/shard_map/reduce_scatter | solution.py:28
  94.3 1.5 add_dynamic-update-slice_fusion
  96.1 0.9 fusion.10
  97.0 31.1 %all_to_all.35 = f32[512,16,32]{0,2,1:T(8,128)S(1)} all-to-all(f32[512,16,32]{0,2,1:T(8,128)S(1)} %fusion.10), channel_id=1, replica_groups=mesh['tm'=8,'state'=4] {'tm'}, dimensions={1} | all-to-all | bytes 2097152 | tf_op jit(solution)/shard_map/all_to_all | solution.py:43
  128.0 0.1 copy.21
  128.1 0.0 copy-start.1
  128.1 1.0 copy-done.1
  129.1 0.8 bitcast_convert_fusion.1
  130.0 0.0 all-gather.2.cloned.1.call-update
  130.0 1.1 copy.22
  131.1 17.7 %all_to_all.36 = bf16[8,64,2,256]{3,1,2,0:T(8,128)(2,1)S(1)} all-to-all(bf16[8,64,2,256]{3,1,2,0:T(8,128)(2,1)} %bitcast.60), channel_id=1, replica_groups=mesh['tm'=8,'state'=4] {'tm'}, dimensions={0} | all-to-all | bytes 1048576 | tf_op jit(solution)/shard_map/all_to_all | solution.py:22
  148.9 1.1 bitcast_convert_fusion
  150.0 2.5 %copy.24 = f32[512,2,256]{0,2,1:T(8,128)} copy(f32[512,2,256]{2,0,1:T(8,128)} %bitcast_convert_fusion) | data formatting | bytes 2097152 | tf_op jit(solution)/shard_map/convert_element_type | solution.py:51
  152.5 1.3 copy.25
  153.8 3.1 %fusion.5 = f32[512,2,256]{0,2,1:T(8,128)S(1)} fusion(f32[512,2,256]{0,2,1:T(8,128)} %copy.24, bf16[2048,2,256]{0,2,1:T(8,128)(2,1)} %all-gather.2.cloned.1.call-done, bf16[512,2048]{1,0:T(8,128)(2,1)S(1)} %copy-done), kind=kOutput, calls=%fused_computation.4 | convolution fusion | flops 1074003968 | bytes 6291456 | tf_op jit(solution)/shard_map/so,ogy->sgy/dot_general | solution.py:45
  156.9 1.3 copy.26
  (31 shorter events, 0.3 us)
Async XLA Ops:
  7.2 39.2 %copy-start = (bf16[512,2048]{1,0:T(8,128)(2,1)S(1)}, bf16[512,2048]{1,0:T(8,128)(2,1)}, u32[]{:S(2)}) copy-start(bf16[512,2048]{1,0:T(8,128)(2,1)} %param.6) | copy-start | bytes 6291460
  7.2 87.1 %reduce-scatter.2.cloned.1.call-start = ((), (), s32[]{:S(2)}) async-start(), calls=%async_computation.5 | async-start | bytes 5242880 | tf_op jit(solution)/shard_map/reduce_scatter | solution.py:28
  50.6 0.7 copy-start.3
  50.6 103.1 %all-gather.2.cloned.1.call-start = ((), (), s32[]{:S(2)}) async-start(), calls=%async_computation.6 | async-start | bytes 2621440 | tf_op jit(solution)/shard_map/all_gather | solution.py:48
  128.1 1.0 copy-start.1
  148.9 3.6 %copy-start.2 = (f32[512,8,2,32]{0,3,1,2:T(8,128)S(1)}, f32[512,8,2,32]{0,3,1,2:T(8,128)}, u32[]{:S(2)}) copy-start(f32[512,8,2,32]{0,3,1,2:T(8,128)} %copy-done.1) | copy-start | bytes 3145732
Sparse Core Ops, SparseCore 0:
  50.8 43.5 reduce-scatter.1
  130.1 20.6 all-gather.1

commit v5 on v4

v5 whole, which is shorter than its diff:
```python
import jax
import jax.numpy as jnp
from jax import lax
from jax.experimental import pallas as pl
from jax.experimental.pallas import tpu as pltpu
from jax.sharding import PartitionSpec as P


def information_kernel(x_ref, l_ref, out_ref):
    out_ref[...] = lax.dot_general(
        x_ref[...], l_ref[...], (((0,), (0,)), ((), ())),
        preferred_element_type=jnp.float32,
    )


def recurrence_kernel(rate_ref, info_ref, out_ref):
    hours = info_ref.shape[0]
    state = jnp.zeros(info_ref.shape[1:], jnp.float32)
    for hour in range(hours):
        state = rate_ref[pl.ds(hour, 1), :] * state + info_ref[hour]
        out_ref[hour] = state
    state = jnp.zeros(info_ref.shape[1:], jnp.float32)
    for hour in reversed(range(hours)):
        rate = rate_ref[pl.ds(hour, 1), :]
        state = rate * state + (1.0 - rate * rate) * out_ref[hour]
        out_ref[hour] = state


def vmem_call(kernel, out_shape, count, cost):
    return pl.pallas_call(
        kernel,
        out_shape=out_shape,
        in_specs=[pl.BlockSpec(memory_space=pltpu.VMEM)] * count,
        out_specs=pl.BlockSpec(memory_space=pltpu.VMEM),
        cost_estimate=cost,
    )


def local(obs, mask, loadings, decay):
    tm_count = lax.axis_size("tm")
    stations_local, hours, members = obs.shape
    members_here = members // tm_count
    masked = obs * mask[:, :, None].astype(obs.dtype)
    outgoing = jnp.transpose(
        masked.reshape(stations_local, hours, tm_count, members_here), (2, 0, 1, 3)
    ).reshape(tm_count, stations_local, hours * members_here)
    by_member = lax.all_to_all(outgoing, "tm", split_axis=0, concat_axis=0, tiled=True)
    stations_here = tm_count * stations_local
    by_member = by_member.reshape(stations_here, hours * members_here)
    by_hour = lax.all_to_all(masked, "tm", split_axis=1, concat_axis=0, tiled=True)
    copies = jnp.broadcast_to(decay[None], (tm_count,) + decay.shape)
    decay_all = lax.all_to_all(copies, "tm", split_axis=0, concat_axis=0, tiled=True)
    decay_all = decay_all.reshape(hours, decay.shape[1])
    all_comps = loadings.shape[1]
    columns = hours * members_here
    partial = vmem_call(
        information_kernel,
        jax.ShapeDtypeStruct((columns, all_comps), jnp.float32),
        2,
        pl.CostEstimate(
            flops=2 * stations_here * columns * all_comps,
            bytes_accessed=2 * stations_here * (columns + all_comps) + 4 * columns * all_comps,
            transcendentals=0,
        ),
    )(by_member, loadings)
    information = lax.psum_scatter(partial, "state", scatter_dimension=1, tiled=True)
    comps = information.shape[1]
    information = information.reshape(hours, members_here, comps)
    smoothed_here = vmem_call(
        recurrence_kernel,
        jax.ShapeDtypeStruct(information.shape, jnp.float32),
        2,
        pl.CostEstimate(
            flops=5 * hours * members_here * comps,
            bytes_accessed=8 * hours * members_here * comps,
            transcendentals=0,
        ),
    )(decay_all, information)
    gathered = lax.all_to_all(smoothed_here, "tm", split_axis=0, concat_axis=1, tiled=True)
    rounded = gathered.astype(jnp.bfloat16)
    full = lax.all_gather(rounded, "state", axis=2, tiled=True)
    fitted = jnp.einsum("so,gyo->sgy", loadings, full, preferred_element_type=jnp.float32)
    residual = by_hour.astype(jnp.float32) - fitted
    smoothed = jnp.transpose(gathered, (2, 0, 1))
    return (smoothed, residual)


def solution(mesh):
    return jax.shard_map(
        local,
        mesh=mesh,
        in_specs=(
            P(("state", "tm"), None, None),
            P(("state", "tm"), None),
            P("state", None),
            P("tm", "state"),
        ),
        out_specs=(P("state", "tm", None), P("state", "tm", None)),
        check_vma=False,
    )
```

time: 166 us -> 148 us (0.89)
  local copies, waits for them, and re-layouts: 23.3 us -> 6.82 us
  Pallas kernels: 0 us -> 7.41 us
  other arithmetic: 6.45 us -> 1.73 us
  matrix products: 7.39 us -> 3.5 us
    all_to_all x2 -> x1, blocking collectives: 39.6 us -> 21.7 us  [local(): lax.all_to_all(outgoing, 'tm', split_axis=0, concat_axis=0, tiled=True)]
    all_to_all x1 -> x2, blocking collectives: 31.1 us -> 48.8 us  [the longest x1 31.3 us: local(): lax.all_to_all(smoothed_here, 'tm', split_axis=0, concat_axis=1, tiled=True)]
    unnamed x20 -> x5, local copies, waits for them, and re-layouts: 13 us -> 4.9 us
    pallas_call x0 -> x2, Pallas kernels: none -> 7.41 us  [the longest x1 4.99 us: local(): vmem_call(information_kernel, jax.ShapeDtypeStruct((columns, all_comps),...]
    dot_general x2 -> x1, matrix products: 7.39 us -> 3.5 us  [local(): jnp.einsum('so,gyo->sgy', loadings, full, preferred_element_type=jnp.floa...]
    reshape x2 -> x1, local copies, waits for them, and re-layouts: 3.68 us -> 0.33 us  [local(): outgoing = jnp.transpose(masked.reshape(stations_local, hours, tm_count,...]
    all_to_all x3 -> x1, local copies, waits for them, and re-layouts: 2.99 us -> 0.09 us  [local(): lax.all_to_all(smoothed_here, 'tm', split_axis=0, concat_axis=1, tiled=True)]
    convert_element_type x1 -> x2, local copies, waits for them, and re-layouts: 2.52 us -> 0.43 us  [local(): residual = by_hour.astype(jnp.float32) - fitted]
  transfers between devices with their start and end apart: 2 -> 2, of which waited for: 1 -> 2; matrix products, arithmetic and copies ran while one was open for 4% -> 2% of each run, Pallas kernels for 0% -> 0%
where the time goes in v5:
time: 148 us
  blocking collectives  80.6 us (54%)
  waiting for transfers between devices  33.4 us (23%)
  between operations  14.1 us (10%)
  Pallas kernels  7.41 us (5%)
  local copies, waits for them, and re-layouts  6.82 us (5%)
  matrix products  3.5 us (2%)
  other arithmetic  1.73 us (1%)
    reduce_scatter x1, waiting for transfers between devices, local(): lax.psum_scatter(partial, 'state', scatter_dimension=1, tiled=True)  32.3 us
    all_to_all x1, blocking collectives, local(): lax.all_to_all(smoothed_here, 'tm', split_axis=0, concat_axis=1, tiled=True)  31.3 us
    all_to_all x1, blocking collectives, local(): lax.all_to_all(outgoing, 'tm', split_axis=0, concat_axis=0, tiled=True)  21.7 us
    all_to_all x1, blocking collectives, local(): lax.all_to_all(masked, 'tm', split_axis=1, concat_axis=0, tiled=True)  17.6 us
    all_to_all x1, blocking collectives, local(): lax.all_to_all(copies, 'tm', split_axis=0, concat_axis=0, tiled=True)  10.1 us
    pallas_call x1, Pallas kernels, local(): vmem_call(information_kernel, jax.ShapeDtypeStruct((columns, all_comps),...  4.99 us
    unnamed x5, local copies, waits for them, and re-layouts  4.9 us
    dot_general x1, matrix products, local(): jnp.einsum('so,gyo->sgy', loadings, full, preferred_element_type=jnp.floa...  3.5 us
  transfers between devices with their start and end apart: 2, of which 2 were waited for; matrix products, arithmetic and copies ran while one was open for 2% of the time, Pallas kernels for 0%

profile of v5, /device:TPU:0, one launch (start us, length us, event | category | flops | bytes accessed | tf_op | source)
XLA Modules:
  0.0 147.6 jit_solution(12122961019929289788)
XLA Ops:
  7.2 0.0 reduce-scatter.2.cloned.1.call-start
  7.2 1.7 %copy.28 = bf16[64,16,256]{0,2,1:T(8,128)(2,1)S(1)} copy(bf16[64,16,256]{2,1,0:T(8,128)(2,1)} %param.4) | data formatting | bytes 1048576 | tf_op args[0]
  8.9 0.7 convert_element_type.19
  9.6 0.1 broadcast_multiply_fusion
  9.7 0.1 copy.29
  9.8 0.3 copy.30
  10.1 21.7 %all_to_all.37 = bf16[8,64,512]{2,1,0:T(8,128)(2,1)} all-to-all(bf16[8,64,512]{2,1,0:T(8,128)(2,1)S(1)} %copy.30), channel_id=1, replica_groups=mesh['tm'=8,'state'=4] {'tm'}, dimensions={0} | all-to-all | bytes 1048576 | tf_op jit(solution)/shard_map/all_to_all | solution.py:47
  31.8 5.0 %shard_map.59 = f32[512,2048]{1,0:T(8,128)} custom-call(bf16[512,512]{1,0:T(8,128)(2,1)} %bitcast.36, bf16[512,2048]{1,0:T(8,128)(2,1)} %l_ref.1), custom_call_target="tpu_custom_call" | custom-call | flops 1073741824 | bytes 6815744 | tf_op jit(solution)/shard_map/pallas_call | solution.py:56
  36.8 0.0 copy-start
  36.8 0.0 reduce-scatter.2.cloned.1.call-update
  36.8 0.0 all-gather.2.cloned.1.call-start
  36.9 0.6 copy-done
  37.5 10.1 %all_to_all.38 = f32[8,2,512]{2,1,0:T(2,128)S(1)} all-to-all(f32[8,2,512]{2,1,0:T(2,128)S(1)} %broadcast_in_dim.2), channel_id=1, replica_groups=mesh['tm'=8,'state'=4] {'tm'}, dimensions={0} | all-to-all | bytes 65536 | tf_op jit(solution)/shard_map/all_to_all | solution.py:52
  47.6 0.6 reshape.26.rate_ref
  48.2 32.3 %reduce-scatter.2.cloned.1.call-done = f32[512,512]{1,0:T(8,128)} async-done(((f32[512,2048]{1,0:T(8,128)}), f32[512,512]{1,0:T(8,128)}) %reduce-scatter.2.cloned.1.call-update) | async-done | bytes 1048592 | tf_op jit(solution)/shard_map/reduce_scatter | solution.py:66
  80.5 2.4 %shard_map.60 = f32[16,32,512]{2,1,0:T(8,128)} custom-call(f32[16,512]{1,0:T(8,128)} %reshape.26.rate_ref, f32[16,32,512]{2,1,0:T(8,128)} %bitcast.37), custom_call_target="tpu_custom_call" | custom-call | flops 1310720 | bytes 2097152 | tf_op jit(solution)/shard_map/pallas_call | solution.py:69
  82.9 31.3 %all_to_all.39 = f32[16,32,512]{2,1,0:T(8,128)S(1)} all-to-all(f32[16,32,512]{2,1,0:T(8,128)} %shard_map.60), channel_id=1, replica_groups=mesh['tm'=8,'state'=4] {'tm'}, dimensions={0} | all-to-all | bytes 2097152 | tf_op jit(solution)/shard_map/all_to_all | solution.py:79
  114.2 0.1 copy.31
  114.3 0.8 bitcast_convert_fusion
  115.1 0.0 all-gather.2.cloned.1.call-update
  115.2 0.3 copy.32
  115.5 17.6 %all_to_all.40 = bf16[64,16,256]{2,0,1:T(8,128)(2,1)S(1)} all-to-all(bf16[64,16,256]{2,0,1:T(8,128)(2,1)S(1)} %copy.32), channel_id=1, replica_groups=mesh['tm'=8,'state'=4] {'tm'}, dimensions={1} | all-to-all | bytes 1048576 | tf_op jit(solution)/shard_map/all_to_all | solution.py:50
  133.1 0.1 convert_bitcast_fusion
  133.2 0.1 copy.33
  133.3 0.3 copy.34
  133.6 1.3 copy.35
  134.9 1.1 all-gather.2.cloned.1.call-done
  136.0 3.5 %fusion.5 = f32[512,2,256]{0,2,1:T(8,128)S(1)} fusion(f32[512,2,256]{0,2,1:T(8,128)S(1)} %copy.34, bf16[2,256,2048]{2,1,0:T(8,128)(2,1)} %all-gather.2.cloned.1.call-done, bf16[512,2048]{1,0:T(8,128)(2,1)} %l_ref.1), kind=kOutput, calls=%fused_computation.3 | convolution fusion | flops 1074003968 | bytes 6291456 | tf_op jit(solution)/shard_map/so,gyo->sgy/dot_general | solution.py:82
  139.5 1.3 copy.36
  (1 shorter events, 0.0 us)
Async XLA Ops:
  7.2 73.3 %reduce-scatter.2.cloned.1.call-start = ((), (), s32[]{:S(2)}) async-start(), calls=%async_computation.5 | async-start | bytes 5242880 | tf_op jit(solution)/shard_map/reduce_scatter | solution.py:66
  36.8 0.7 copy-start
  36.8 99.2 %all-gather.2.cloned.1.call-start = ((), (), s32[]{:S(2)}) async-start(), calls=%async_computation.6 | async-start | bytes 2621440 | tf_op jit(solution)/shard_map/all_gather | solution.py:81
Sparse Core Ops, SparseCore 0:
  37.0 43.5 reduce-scatter.1
  115.3 20.6 all-gather.1

commit v6 on v5

--- a/solution.py
+++ b/solution.py
@@ -7,10 +7,29 @@
 
 
 def information_kernel(x_ref, l_ref, out_ref):
-    out_ref[...] = lax.dot_general(
+    total = lax.dot_general(
         x_ref[...], l_ref[...], (((0,), (0,)), ((), ())),
         preferred_element_type=jnp.float32,
     )
+    levels = out_ref.ndim - 2
+    width = out_ref.shape[-1]
+    for block in range(2 ** levels):
+        bits = tuple((block >> level) & 1 for level in range(levels))
+        out_ref[bits] = total[:, block * width:(block + 1) * width]
+
+
+def halving_reduce(blocks, axis):
+    count = lax.axis_size(axis)
+    me = lax.axis_index(axis)
+    level = 0
+    while blocks.ndim > 2:
+        bit = (me >> level) & 1
+        keep = jnp.where(bit == 0, blocks[0], blocks[1])
+        send = jnp.where(bit == 0, blocks[1], blocks[0])
+        pairs = [(i, i ^ (1 << level)) for i in range(count)]
+        blocks = keep + lax.ppermute(send, axis, pairs)
+        level += 1
+    return blocks
 
 
 def recurrence_kernel(rate_ref, info_ref, out_ref):
@@ -53,9 +72,13 @@
     decay_all = decay_all.reshape(hours, decay.shape[1])
     all_comps = loadings.shape[1]
     columns = hours * members_here
+    state_count = lax.axis_size("state")
+    levels = state_count.bit_length() - 1
     partial = vmem_call(
         information_kernel,
-        jax.ShapeDtypeStruct((columns, all_comps), jnp.float32),
+        jax.ShapeDtypeStruct(
+            (2,) * levels + (columns, all_comps // state_count), jnp.float32
+        ),
         2,
         pl.CostEstimate(
             flops=2 * stations_here * columns * all_comps,
@@ -63,7 +86,7 @@
             transcendentals=0,
         ),
     )(by_member, loadings)
-    information = lax.psum_scatter(partial, "state", scatter_dimension=1, tiled=True)
+    information = halving_reduce(partial, "state")
     comps = information.shape[1]
     information = information.reshape(hours, members_here, comps)
     smoothed_here = vmem_call(

time: 148 us -> 145 us (0.980)
  blocking collectives: 80.6 us -> 56.5 us
  other arithmetic: 1.73 us -> 11.8 us
  starting transfers between devices: 0.08 us -> 8.88 us
    reduce_scatter x1 -> x0, waiting for transfers between devices: 32.3 us -> none  [local(): lax.psum_scatter(partial, 'state', scatter_dimension=1, tiled=True)]
    all_to_all x1 -> x0, blocking collectives: 21.7 us -> none  [local(): lax.all_to_all(outgoing, 'tm', split_axis=0, concat_axis=0, tiled=True)]
    ppermute x0 -> x2, waiting for transfers between devices: none -> 17.5 us  [halving_reduce(): blocks = keep + lax.ppermute(send, axis, pairs)]
    all_to_all x0 -> x1, waiting for transfers between devices: none -> 14.4 us  [local(): lax.all_to_all(outgoing, 'tm', split_axis=0, concat_axis=0, tiled=True)]
    all_to_all x0 -> x1, starting transfers between devices: none -> 7.25 us  [local(): lax.all_to_all(outgoing, 'tm', split_axis=0, concat_axis=0, tiled=True)]
    add x0 -> x2, other arithmetic: none -> 6.15 us  [halving_reduce(): blocks = keep + lax.ppermute(send, axis, pairs)]
    select_n x0 -> x2, other arithmetic: none -> 3.88 us  [halving_reduce(): send = jnp.where(bit == 0, blocks[1], blocks[0])]
    all_to_all x1, blocking collectives: 31.3 us -> 29 us  [local(): lax.all_to_all(smoothed_here, 'tm', split_axis=0, concat_axis=1, tiled=True)]
  transfers between devices with their start and end apart: 2 -> 4, of which waited for: 2 -> 4; matrix products, arithmetic and copies ran while one was open for 2% -> 2% of each run, Pallas kernels for 0% -> 0%
where the time goes in v6:
time: 145 us; the launch traced here: 144 us
  blocking collectives  56.5 us (39%)
  waiting for transfers between devices  34.2 us (24%)
  between operations  14.1 us (10%)
  other arithmetic  11.8 us (8%)
  starting transfers between devices  8.88 us (6%)
  local copies, waits for them, and re-layouts  7.79 us (5%)
  Pallas kernels  7.4 us (5%)
  matrix products  3.5 us (2%)
    all_to_all x1, blocking collectives, local(): lax.all_to_all(smoothed_here, 'tm', split_axis=0, concat_axis=1, tiled=True)  29 us
    ppermute x2, waiting for transfers between devices, halving_reduce(): blocks = keep + lax.ppermute(send, axis, pairs)  17.5 us
    all_to_all x1, blocking collectives, local(): lax.all_to_all(masked, 'tm', split_axis=1, concat_axis=0, tiled=True)  17.3 us
    all_to_all x1, waiting for transfers between devices, local(): lax.all_to_all(outgoing, 'tm', split_axis=0, concat_axis=0, tiled=True)  14.4 us
    all_to_all x1, blocking collectives, local(): lax.all_to_all(copies, 'tm', split_axis=0, concat_axis=0, tiled=True)  10.1 us
    all_to_all x1, starting transfers between devices, local(): lax.all_to_all(outgoing, 'tm', split_axis=0, concat_axis=0, tiled=True)  7.25 us
    add x2, other arithmetic, halving_reduce(): blocks = keep + lax.ppermute(send, axis, pairs)  6.15 us
    unnamed x7, local copies, waits for them, and re-layouts  5.09 us
  transfers between devices with their start and end apart: 4, of which 4 were waited for; matrix products, arithmetic and copies ran while one was open for 2% of the time, Pallas kernels for 0%

profile of v6, /device:TPU:0, one launch (start us, length us, event | category | flops | bytes accessed | tf_op | source)
XLA Modules:
  0.0 144.1 jit_solution(10668583995117313261)
XLA Ops:
  7.2 1.7 %copy.28 = bf16[64,16,256]{0,2,1:T(8,128)(2,1)S(1)} copy(bf16[64,16,256]{2,1,0:T(8,128)(2,1)} %param.4) | data formatting | bytes 1048576 | tf_op args[0]
  8.9 0.7 convert_element_type.19
  9.6 0.1 broadcast_multiply_fusion
  9.6 0.1 copy.29
  9.7 1.1 copy.30
  10.9 7.3 %all-to-all-start.1 = ((bf16[8,64,512]{2,1,0:T(8,128)(2,1)}), bf16[8,64,512]{2,1,0:T(8,128)(2,1)S(1)}, u32[]{:S(2)}, u32[]{:S(2)}) async-start(bf16[8,64,512]{2,1,0:T(8,128)(2,1)} %copy.30), calls=%async_computation.1 | async-start | bytes 1048576 | tf_op jit(solution)/shard_map/all_to_all | solution.py:66
  18.2 14.4 %all-to-all-done.1 = bf16[8,64,512]{2,1,0:T(8,128)(2,1)S(1)} async-done(((bf16[8,64,512]{2,1,0:T(8,128)(2,1)}), bf16[8,64,512]{2,1,0:T(8,128)(2,1)S(1)}, u32[]{:S(2)}, u32[]{:S(2)}) %all-to-all-start.1) | async-done | bytes 524320 | tf_op jit(solution)/shard_map/all_to_all | solution.py:66
  32.6 0.8 copy-done
  33.4 5.0 %shard_map.59 = f32[2,2,512,512]{3,2,1,0:T(8,128)} custom-call(bf16[512,512]{1,0:T(8,128)(2,1)} %bitcast.45, bf16[512,2048]{1,0:T(8,128)(2,1)} %l_ref.1), custom_call_target="tpu_custom_call" | custom-call | flops 1073741824 | bytes 6815744 | tf_op jit(solution)/shard_map/pallas_call | solution.py:77
  38.4 2.7 %select_bitcast_fusion = f32[2,512,512]{2,1,0:T(8,128)S(1)} fusion(f32[2,2,512,512]{3,2,1,0:T(8,128)} %shard_map.59, pred[]{:T(512)S(6)} %eq.9), kind=kLoop, calls=%fused_computation.3 | loop fusion | flops 524288 | bytes 6291457 | tf_op jit(solution)/shard_map/jit(_where)/select_n | solution.py:28
  41.1 0.1 collective-permute-start
  41.2 4.3 %collective-permute-done = f32[2,512,512]{2,1,0:T(8,128)} collective-permute-done((f32[2,512,512]{2,1,0:T(8,128)S(1)}, f32[2,512,512]{2,1,0:T(8,128)}, u32[]{:S(2)}, u32[]{:S(2)}) %collective-permute-start) | collective-permute-done | bytes 2097184 | tf_op jit(solution)/shard_map/ppermute | solution.py:30
  45.4 3.6 %bitcast_add_fusion = f32[2,512,512]{2,1,0:T(8,128)S(1)} fusion(f32[2,512,512]{2,1,0:T(8,128)} %collective-permute-done, f32[2,2,512,512]{3,2,1,0:T(8,128)} %shard_map.59, pred[]{:T(512)S(6)} %eq.9), kind=kLoop, calls=%fused_computation.2 | loop fusion | flops 1048576 | bytes 8388609 | tf_op jit(solution)/shard_map/add | solution.py:30
  49.1 1.2 select_bitcast_fusion.1
  50.3 1.5 %collective-permute-start.1 = (f32[512,512]{1,0:T(8,128)}, f32[512,512]{1,0:T(8,128)}, u32[]{:S(2)}, u32[]{:S(2)}) collective-permute-start(f32[512,512]{1,0:T(8,128)} %select_bitcast_fusion.1), channel_id=1, source_target_pairs={{0,2},{1,3},{2,0},{3,1},{4,6},{5,7},{6,4},{7,5},{8,10},{9,11},{10,... | collective-permute-start | bytes 3145736 | tf_op jit(solution)/shard_map/ppermute | solution.py:30
  51.8 10.1 %all_to_all.37 = f32[8,2,512]{2,1,0:T(2,128)S(1)} all-to-all(f32[8,2,512]{2,1,0:T(2,128)S(1)} %broadcast_in_dim.2), channel_id=1, replica_groups=mesh['tm'=8,'state'=4] {'tm'}, dimensions={0} | all-to-all | bytes 65536 | tf_op jit(solution)/shard_map/all_to_all | solution.py:71
  61.9 0.6 reshape.34.rate_ref
  62.5 13.2 %collective-permute-done.1 = f32[512,512]{1,0:T(8,128)} collective-permute-done((f32[512,512]{1,0:T(8,128)}, f32[512,512]{1,0:T(8,128)}, u32[]{:S(2)}, u32[]{:S(2)}) %collective-permute-start.1) | collective-permute-done | bytes 1048608 | tf_op jit(solution)/shard_map/ppermute | solution.py:30
  75.8 2.5 %bitcast_add_fusion.1 = f32[512,512]{1,0:T(8,128)} fusion(f32[512,512]{1,0:T(8,128)} %collective-permute-done.1, f32[2,512,512]{2,1,0:T(8,128)S(1)} %bitcast_add_fusion, pred[]{:T(512)S(6)} %eq.8), kind=kLoop, calls=%fused_computation.8 | loop fusion | flops 524288 | bytes 4194305 | tf_op jit(solution)/shard_map/add | solution.py:30
  78.3 2.4 %shard_map.60 = f32[16,32,512]{2,1,0:T(8,128)} custom-call(f32[16,512]{1,0:T(8,128)} %reshape.34.rate_ref, f32[16,32,512]{2,1,0:T(8,128)} %bitcast.40), custom_call_target="tpu_custom_call" | custom-call | flops 1310720 | bytes 2097152 | tf_op jit(solution)/shard_map/pallas_call | solution.py:92
  80.7 29.0 %all_to_all.38 = f32[16,32,512]{2,1,0:T(8,128)S(1)} all-to-all(f32[16,32,512]{2,1,0:T(8,128)} %shard_map.60), channel_id=1, replica_groups=mesh['tm'=8,'state'=4] {'tm'}, dimensions={0} | all-to-all | bytes 2097152 | tf_op jit(solution)/shard_map/all_to_all | solution.py:102
  109.8 0.1 copy.31
  109.9 0.8 bitcast_convert_fusion
  110.7 0.3 copy.32
  111.1 17.3 %all_to_all.39 = bf16[64,16,256]{2,0,1:T(8,128)(2,1)S(1)} all-to-all(bf16[64,16,256]{2,0,1:T(8,128)(2,1)S(1)} %copy.32), channel_id=1, replica_groups=mesh['tm'=8,'state'=4] {'tm'}, dimensions={1} | all-to-all | bytes 1048576 | tf_op jit(solution)/shard_map/all_to_all | solution.py:69
  128.4 0.1 convert_bitcast_fusion
  128.5 0.1 copy.33
  128.6 0.3 copy.34
  128.9 1.3 copy.35
  130.2 2.2 %all-gather.2.cloned.1.call-done = bf16[2,256,2048]{2,1,0:T(8,128)(2,1)} async-done(((bf16[2,256,512]{2,1,0:T(8,128)(2,1)}), bf16[2,256,2048]{2,1,0:T(8,128)(2,1)}) %all-gather.2.cloned.1.call-update) | async-done | bytes 2097168 | tf_op jit(solution)/shard_map/all_gather | solution.py:104
  132.5 3.5 %fusion.5 = f32[512,2,256]{0,2,1:T(8,128)S(1)} fusion(f32[512,2,256]{0,2,1:T(8,128)S(1)} %copy.34, bf16[2,256,2048]{2,1,0:T(8,128)(2,1)} %all-gather.2.cloned.1.call-done, bf16[512,2048]{1,0:T(8,128)(2,1)} %l_ref.1), kind=kOutput, calls=%fused_computation.5 | convolution fusion | flops 1074003968 | bytes 6291456 | tf_op jit(solution)/shard_map/so,gyo->sgy/dot_general | solution.py:105
  136.0 1.3 copy.36
  (6 shorter events, 0.1 us)
Async XLA Ops:
  10.9 21.7 %all-to-all-start.1 = ((bf16[8,64,512]{2,1,0:T(8,128)(2,1)}), bf16[8,64,512]{2,1,0:T(8,128)(2,1)S(1)}, u32[]{:S(2)}, u32[]{:S(2)}) async-start(bf16[8,64,512]{2,1,0:T(8,128)(2,1)} %copy.30), calls=%async_computation.1 | async-start | bytes 1048576 | tf_op jit(solution)/shard_map/all_to_all | solution.py:66
  18.1 114.3 %all-gather.2.cloned.1.call-start = ((), (), s32[]{:S(2)}) async-start(), calls=%async_computation.4 | async-start | bytes 2621440 | tf_op jit(solution)/shard_map/all_gather | solution.py:104
  32.6 0.8 copy-start
  41.1 4.4 %collective-permute-start = (f32[2,512,512]{2,1,0:T(8,128)S(1)}, f32[2,512,512]{2,1,0:T(8,128)}, u32[]{:S(2)}, u32[]{:S(2)}) collective-permute-start(f32[2,512,512]{2,1,0:T(8,128)S(1)} %select_bitcast_fusion), channel_id=1, source_target_pairs={{0,1},{1,0},{2,3},{3,2},{4,5},{5,4},{6,7},{7,6},{8,9},{9,8},{10,11... | collective-permute-start | bytes 6291464 | tf_op jit(solution)/shard_map/ppermute | solution.py:30
  49.1 2.7 %copy-start.1 = (f32[2,512]{1,0:T(2,128)S(1)}, f32[2,512]{1,0:T(2,128)}, u32[]{:S(2)}) copy-start(f32[2,512]{1,0:T(2,128)} %param.7) | copy-start | bytes 12292
  50.3 25.5 %collective-permute-start.1 = (f32[512,512]{1,0:T(8,128)}, f32[512,512]{1,0:T(8,128)}, u32[]{:S(2)}, u32[]{:S(2)}) collective-permute-start(f32[512,512]{1,0:T(8,128)} %select_bitcast_fusion.1), channel_id=1, source_target_pairs={{0,2},{1,3},{2,0},{3,1},{4,6},{5,7},{6,4},{7,5},{8,10},{9,11},{10,... | collective-permute-start | bytes 3145736 | tf_op jit(solution)/shard_map/ppermute | solution.py:30
Sparse Core Ops, SparseCore 0:
  110.8 21.5 all-gather.1

commit v7 on v5

--- a/solution.py
+++ b/solution.py
@@ -6,32 +6,56 @@
 from jax.sharding import PartitionSpec as P
 
 
-def information_kernel(x_ref, l_ref, out_ref):
-    out_ref[...] = lax.dot_general(
-        x_ref[...], l_ref[...], (((0,), (0,)), ((), ())),
-        preferred_element_type=jnp.float32,
-    )
+def information_kernel(me_ref, x_ref, l_ref, send_ref, keep_ref):
+    me = me_ref[0]
+    levels = send_ref.ndim - 1
+    width = send_ref.shape[-1]
+    flipped = x_ref[...].T
+    for slot in range(2 ** levels):
+        relative = tuple((slot >> level) & 1 for level in range(levels))
+        block = 0
+        for level in range(levels):
+            block = block + ((relative[level] ^ ((me >> level) & 1) ^ 1) << level)
+        columns = l_ref[:, pl.ds(pl.multiple_of(block * width, width), width)]
+        target = keep_ref if relative[0] else send_ref
+        target[relative[1:]] = jnp.dot(flipped, columns, preferred_element_type=jnp.float32)
 
 
-def recurrence_kernel(rate_ref, info_ref, out_ref):
-    hours = info_ref.shape[0]
-    state = jnp.zeros(info_ref.shape[1:], jnp.float32)
+def halving_reduce(blocks, axis):
+    count = lax.axis_size(axis)
+    level = 0
+    outgoing, keep = blocks
+    received = lax.ppermute(outgoing, axis, [(i, i ^ 1) for i in range(count)])
+    while keep.ndim > 2:
+        level += 1
+        outgoing = keep[0] + received[0]
+        pairs = [(i, i ^ (1 << level)) for i in range(count)]
+        arriving = lax.ppermute(outgoing, axis, pairs)
+        keep = keep[1] + received[1]
+        received = arriving
+    return keep, received
+
+
+def recurrence_kernel(rate_ref, keep_ref, received_ref, out_ref):
+    hours = out_ref.shape[0]
+    state = jnp.zeros(out_ref.shape[1:], jnp.float32)
     for hour in range(hours):
-        state = rate_ref[pl.ds(hour, 1), :] * state + info_ref[hour]
+        state = rate_ref[pl.ds(hour, 1), :] * state + (keep_ref[hour] + received_ref[hour])
         out_ref[hour] = state
-    state = jnp.zeros(info_ref.shape[1:], jnp.float32)
+    state = jnp.zeros(out_ref.shape[1:], jnp.float32)
     for hour in reversed(range(hours)):
         rate = rate_ref[pl.ds(hour, 1), :]
         state = rate * state + (1.0 - rate * rate) * out_ref[hour]
         out_ref[hour] = state
 
 
-def vmem_call(kernel, out_shape, count, cost):
+def vmem_call(kernel, out_shape, count, cost, scalars=0):
     return pl.pallas_call(
         kernel,
         out_shape=out_shape,
-        in_specs=[pl.BlockSpec(memory_space=pltpu.VMEM)] * count,
-        out_specs=pl.BlockSpec(memory_space=pltpu.VMEM),
+        in_specs=[pl.BlockSpec(memory_space=pltpu.SMEM)] * scalars
+        + [pl.BlockSpec(memory_space=pltpu.VMEM)] * count,
+        out_specs=jax.tree.map(lambda _: pl.BlockSpec(memory_space=pltpu.VMEM), out_shape),
         cost_estimate=cost,
     )
 
@@ -53,29 +77,35 @@
     decay_all = decay_all.reshape(hours, decay.shape[1])
     all_comps = loadings.shape[1]
     columns = hours * members_here
+    state_count = lax.axis_size("state")
+    levels = state_count.bit_length() - 1
     partial = vmem_call(
         information_kernel,
-        jax.ShapeDtypeStruct((columns, all_comps), jnp.float32),
+        (jax.ShapeDtypeStruct(
+            (2,) * (levels - 1) + (columns, all_comps // state_count), jnp.float32
+        ),) * 2,
         2,
         pl.CostEstimate(
             flops=2 * stations_here * columns * all_comps,
             bytes_accessed=2 * stations_here * (columns + all_comps) + 4 * columns * all_comps,
             transcendentals=0,
         ),
-    )(by_member, loadings)
-    information = lax.psum_scatter(partial, "state", scatter_dimension=1, tiled=True)
-    comps = information.shape[1]
-    information = information.reshape(hours, members_here, comps)
+        scalars=1,
+    )(lax.axis_index("state").reshape(1).astype(jnp.int32), by_member, loadings)
+    keep, received = halving_reduce(partial, "state")
+    comps = keep.shape[1]
+    keep = keep.reshape(hours, members_here, comps)
+    received = received.reshape(hours, members_here, comps)
     smoothed_here = vmem_call(
         recurrence_kernel,
-        jax.ShapeDtypeStruct(information.shape, jnp.float32),
-        2,
+        jax.ShapeDtypeStruct(keep.shape, jnp.float32),
+        3,
         pl.CostEstimate(
             flops=5 * hours * members_here * comps,
-            bytes_accessed=8 * hours * members_here * comps,
+            bytes_accessed=12 * hours * members_here * comps,
             transcendentals=0,
         ),
-    )(decay_all, information)
+    )(decay_all, keep, received)
     gathered = lax.all_to_all(smoothed_here, "tm", split_axis=0, concat_axis=1, tiled=True)
     rounded = gathered.astype(jnp.bfloat16)
     full = lax.all_gather(rounded, "state", axis=2, tiled=True)

time: 148 us -> 138 us (0.932)
  blocking collectives: 80.6 us -> 56.5 us
  starting transfers between devices: 0.08 us -> 8.82 us
  other arithmetic: 1.73 us -> 4.73 us
  local copies, waits for them, and re-layouts: 6.82 us -> 8.75 us
    reduce_scatter x1 -> x0, waiting for transfers between devices: 32.3 us -> none  [local(): lax.psum_scatter(partial, 'state', scatter_dimension=1, tiled=True)]
    all_to_all x1 -> x0, blocking collectives: 21.7 us -> none  [local(): lax.all_to_all(outgoing, 'tm', split_axis=0, concat_axis=0, tiled=True)]
    ppermute x0 -> x2, waiting for transfers between devices: none -> 17.3 us  [the longest x1 12.9 us: halving_reduce(): arriving = lax.ppermute(outgoing, axis, pairs)]
    all_to_all x0 -> x1, waiting for transfers between devices: none -> 14.4 us  [local(): lax.all_to_all(outgoing, 'tm', split_axis=0, concat_axis=0, tiled=True)]
    all_to_all x0 -> x1, starting transfers between devices: none -> 7.25 us  [local(): lax.all_to_all(outgoing, 'tm', split_axis=0, concat_axis=0, tiled=True)]
    add x0 -> x1, other arithmetic: none -> 3 us  [halving_reduce(): outgoing = keep[0] + received[0]]
    all_to_all x1, blocking collectives: 31.3 us -> 29 us  [local(): lax.all_to_all(smoothed_here, 'tm', split_axis=0, concat_axis=1, tiled=True)]
    ppermute x0 -> x2, starting transfers between devices: none -> 1.53 us  [the longest x1 1.52 us: halving_reduce(): arriving = lax.ppermute(outgoing, axis, pairs)]
  transfers between devices with their start and end apart: 2 -> 4, of which waited for: 2 -> 4; matrix products, arithmetic and copies ran while one was open for 2% -> 2% of each run, Pallas kernels for 0% -> 0%
where the time goes in v7:
time: 138 us
  blocking collectives  56.5 us (41%)
  waiting for transfers between devices  33.9 us (25%)
  between operations  14.1 us (10%)
  starting transfers between devices  8.82 us (6%)
  local copies, waits for them, and re-layouts  8.75 us (6%)
  Pallas kernels  7.5 us (5%)
  other arithmetic  4.73 us (3%)
  matrix products  3.5 us (3%)
    all_to_all x1, blocking collectives, local(): lax.all_to_all(smoothed_here, 'tm', split_axis=0, concat_axis=1, tiled=True)  29 us
    all_to_all x1, blocking collectives, local(): lax.all_to_all(masked, 'tm', split_axis=1, concat_axis=0, tiled=True)  17.3 us
    all_to_all x1, waiting for transfers between devices, local(): lax.all_to_all(outgoing, 'tm', split_axis=0, concat_axis=0, tiled=True)  14.4 us
    ppermute x1, waiting for transfers between devices, halving_reduce(): arriving = lax.ppermute(outgoing, axis, pairs)  12.9 us
    all_to_all x1, blocking collectives, local(): lax.all_to_all(copies, 'tm', split_axis=0, concat_axis=0, tiled=True)  10.1 us
    all_to_all x1, starting transfers between devices, local(): lax.all_to_all(outgoing, 'tm', split_axis=0, concat_axis=0, tiled=True)  7.25 us
    unnamed x9, local copies, waits for them, and re-layouts  6.06 us
    pallas_call x1, Pallas kernels, local(): vmem_call(information_kernel, (jax.ShapeDtypeStruct((2,) * (levels - 1) +...  4.73 us
  transfers between devices with their start and end apart: 4, of which 4 were waited for; matrix products, arithmetic and copies ran while one was open for 2% of the time, Pallas kernels for 0%

profile of v7, /device:TPU:0, one launch (start us, length us, event | category | flops | bytes accessed | tf_op | source)
XLA Modules:
  0.0 137.8 jit_solution(4511209585311487948)
XLA Ops:
  7.2 1.7 %copy.28 = bf16[64,16,256]{0,2,1:T(8,128)(2,1)S(1)} copy(bf16[64,16,256]{2,1,0:T(8,128)(2,1)} %param.4) | data formatting | bytes 1048576 | tf_op args[0]
  8.9 0.7 convert_element_type.19
  9.6 0.1 broadcast_multiply_fusion
  9.6 0.1 copy.29
  9.7 1.1 copy.30
  10.9 7.3 %all-to-all-start.1 = ((bf16[8,64,512]{2,1,0:T(8,128)(2,1)}), bf16[8,64,512]{2,1,0:T(8,128)(2,1)S(1)}, u32[]{:S(2)}, u32[]{:S(2)}) async-start(bf16[8,64,512]{2,1,0:T(8,128)(2,1)} %copy.30), calls=%async_computation.1 | async-start | bytes 1048576 | tf_op jit(solution)/shard_map/all_to_all | solution.py:71
  18.1 0.0 all-gather.2.cloned.1.call-start
  18.2 14.4 %all-to-all-done.1 = bf16[8,64,512]{2,1,0:T(8,128)(2,1)S(1)} async-done(((bf16[8,64,512]{2,1,0:T(8,128)(2,1)}), bf16[8,64,512]{2,1,0:T(8,128)(2,1)S(1)}, u32[]{:S(2)}, u32[]{:S(2)}) %all-to-all-start.1) | async-done | bytes 524320 | tf_op jit(solution)/shard_map/all_to_all | solution.py:71
  32.6 0.8 copy-done.1
  33.4 4.7 %shard_map.59 = (f32[2,512,512]{2,1,0:T(8,128)}, f32[2,512,512]{2,1,0:T(8,128)}) custom-call(s32[1]{0:T(128)} %bitcast.me_ref, bf16[512,512]{1,0:T(8,128)(2,1)} %bitcast.42, bf16[512,2048]{1,0:T(8,128)(2,1)} %l_ref.1), custom_call_target="tpu_custom_call" | custom-call | flops 1073741824 | bytes 6815744 | tf_op jit(solution)/shard_map/pallas_call | solution.py:82
  38.1 0.0 collective-permute-start
  38.1 4.4 %collective-permute-done = f32[2,512,512]{2,1,0:T(8,128)S(1)} collective-permute-done((f32[2,512,512]{2,1,0:T(8,128)}, f32[2,512,512]{2,1,0:T(8,128)S(1)}, u32[]{:S(2)}, u32[]{:S(2)}) %collective-permute-start) | collective-permute-done | bytes 2097184 | tf_op jit(solution)/shard_map/ppermute | solution.py:28
  42.5 3.0 %fusion.8 = (f32[512,512]{1,0:T(8,128)S(1)}, f32[1,512,512]{2,1,0:T(8,128)}) fusion(f32[2,512,512]{2,1,0:T(8,128)S(1)} %collective-permute-done, f32[2,512,512]{2,1,0:T(8,128)} %get-tuple-element.4), kind=kLoop, calls=%fused_computation.5 | loop fusion | flops 524288 | bytes 6291456 | tf_op jit(solution)/shard_map/add | solution.py:31
  45.5 1.5 %collective-permute-start.1 = (f32[512,512]{1,0:T(8,128)S(1)}, f32[512,512]{1,0:T(8,128)S(1)}, u32[]{:S(2)}, u32[]{:S(2)}) collective-permute-start(f32[512,512]{1,0:T(8,128)S(1)} %get-tuple-element.14), channel_id=1, source_target_pairs={{0,2},{1,3},{2,0},{3,1},{4,6},{5,7},{6,4},{7,5},{8,10},{9,11},{10,... | collective-permute-start | bytes 3145736 | tf_op jit(solution)/shard_map/ppermute | solution.py:33
  47.0 10.1 %all_to_all.37 = f32[8,2,512]{2,1,0:T(2,128)S(1)} all-to-all(f32[8,2,512]{2,1,0:T(2,128)S(1)} %broadcast_in_dim.2), channel_id=1, replica_groups=mesh['tm'=8,'state'=4] {'tm'}, dimensions={0} | all-to-all | bytes 65536 | tf_op jit(solution)/shard_map/all_to_all | solution.py:76
  57.2 0.6 reshape.34.rate_ref
  57.8 12.9 %collective-permute-done.1 = f32[512,512]{1,0:T(8,128)S(1)} collective-permute-done((f32[512,512]{1,0:T(8,128)S(1)}, f32[512,512]{1,0:T(8,128)S(1)}, u32[]{:S(2)}, u32[]{:S(2)}) %collective-permute-start.1) | collective-permute-done | bytes 1048608 | tf_op jit(solution)/shard_map/ppermute | solution.py:33
  70.7 1.0 copy-done
  71.7 2.8 %shard_map.60 = f32[16,32,512]{2,1,0:T(8,128)} custom-call(f32[16,512]{1,0:T(8,128)} %reshape.34.rate_ref, f32[16,32,512]{2,1,0:T(8,128)} %bitcast.36, f32[16,32,512]{2,1,0:T(8,128)} %bitcast.41), custom_call_target="tpu_custom_call" | custom-call | flops 1310720 | bytes 3145728 | tf_op jit(solution)/shard_map/pallas_call | solution.py:99
  74.4 29.0 %all_to_all.38 = f32[16,32,512]{2,1,0:T(8,128)S(1)} all-to-all(f32[16,32,512]{2,1,0:T(8,128)} %shard_map.60), channel_id=1, replica_groups=mesh['tm'=8,'state'=4] {'tm'}, dimensions={0} | all-to-all | bytes 2097152 | tf_op jit(solution)/shard_map/all_to_all | solution.py:109
  103.5 0.1 copy.31
  103.6 0.8 bitcast_convert_fusion
  104.4 0.0 all-gather.2.cloned.1.call-update
  104.4 0.3 copy.32
  104.8 17.3 %all_to_all.39 = bf16[64,16,256]{2,0,1:T(8,128)(2,1)S(1)} all-to-all(bf16[64,16,256]{2,0,1:T(8,128)(2,1)S(1)} %copy.32), channel_id=1, replica_groups=mesh['tm'=8,'state'=4] {'tm'}, dimensions={1} | all-to-all | bytes 1048576 | tf_op jit(solution)/shard_map/all_to_all | solution.py:74
  122.1 0.1 convert_bitcast_fusion
  122.2 0.1 copy.33
  122.3 0.3 copy.34
  122.7 1.3 copy.35
  124.0 2.2 %all-gather.2.cloned.1.call-done = bf16[2,256,2048]{2,1,0:T(8,128)(2,1)} async-done(((bf16[2,256,512]{2,1,0:T(8,128)(2,1)}), bf16[2,256,2048]{2,1,0:T(8,128)(2,1)}) %all-gather.2.cloned.1.call-update) | async-done | bytes 2097168 | tf_op jit(solution)/shard_map/all_gather | solution.py:111
  126.2 3.5 %fusion.5 = f32[512,2,256]{0,2,1:T(8,128)S(1)} fusion(f32[512,2,256]{0,2,1:T(8,128)S(1)} %copy.34, bf16[2,256,2048]{2,1,0:T(8,128)(2,1)} %all-gather.2.cloned.1.call-done, bf16[512,2048]{1,0:T(8,128)(2,1)} %l_ref.1), kind=kOutput, calls=%fused_computation.3 | convolution fusion | flops 1074003968 | bytes 6291456 | tf_op jit(solution)/shard_map/so,gyo->sgy/dot_general | solution.py:112
  129.7 1.3 copy.36
  (5 shorter events, 0.0 us)
Async XLA Ops:
  10.9 21.7 %all-to-all-start.1 = ((bf16[8,64,512]{2,1,0:T(8,128)(2,1)}), bf16[8,64,512]{2,1,0:T(8,128)(2,1)S(1)}, u32[]{:S(2)}, u32[]{:S(2)}) async-start(bf16[8,64,512]{2,1,0:T(8,128)(2,1)} %copy.30), calls=%async_computation.1 | async-start | bytes 1048576 | tf_op jit(solution)/shard_map/all_to_all | solution.py:71
  18.1 108.1 %all-gather.2.cloned.1.call-start = ((), (), s32[]{:S(2)}) async-start(), calls=%async_computation.4 | async-start | bytes 2621440 | tf_op jit(solution)/shard_map/all_gather | solution.py:111
  32.6 0.8 copy-start.1
  38.1 4.4 %collective-permute-start = (f32[2,512,512]{2,1,0:T(8,128)}, f32[2,512,512]{2,1,0:T(8,128)S(1)}, u32[]{:S(2)}, u32[]{:S(2)}) collective-permute-start(f32[2,512,512]{2,1,0:T(8,128)} %get-tuple-element.5), channel_id=1, source_target_pairs={{0,1},{1,0},{2,3},{3,2},{4,5},{5,4},{6,7},{7,6},{8,9},{9,8},{10,11... | collective-permute-start | bytes 6291464 | tf_op jit(solution)/shard_map/ppermute | solution.py:28
  42.5 4.5 %copy-start.2 = (f32[2,512]{1,0:T(2,128)S(1)}, f32[2,512]{1,0:T(2,128)}, u32[]{:S(2)}) copy-start(f32[2,512]{1,0:T(2,128)} %param.7) | copy-start | bytes 12292
  45.5 25.2 %collective-permute-start.1 = (f32[512,512]{1,0:T(8,128)S(1)}, f32[512,512]{1,0:T(8,128)S(1)}, u32[]{:S(2)}, u32[]{:S(2)}) collective-permute-start(f32[512,512]{1,0:T(8,128)S(1)} %get-tuple-element.14), channel_id=1, source_target_pairs={{0,2},{1,3},{2,0},{3,1},{4,6},{5,7},{6,4},{7,5},{8,10},{9,11},{10,... | collective-permute-start | bytes 3145736 | tf_op jit(solution)/shard_map/ppermute | solution.py:33
  70.7 1.0 copy-start
Sparse Core Ops, SparseCore 0:
  104.6 21.5 all-gather.1

commit v8 on v7

v8 whole, which is shorter than its diff:
```python
import functools

import jax
import jax.numpy as jnp
from jax import lax
from jax.experimental import pallas as pl
from jax.experimental.pallas import tpu as pltpu
from jax.sharding import PartitionSpec as P

CHUNKS = 2


def information_kernel(hours, me_ref, x_ref, l_ref, send_ref, keep_ref):
    me = me_ref[0]
    chunks = send_ref.shape[0]
    levels = send_ref.ndim - 2
    rows, width = send_ref.shape[-2:]
    flipped = x_ref[...].T
    for slot in range(2 ** levels):
        relative = tuple((slot >> level) & 1 for level in range(levels))
        block = 0
        for level in range(levels):
            block = block + ((relative[level] ^ ((me >> level) & 1) ^ 1) << level)
        columns = l_ref[:, pl.ds(pl.multiple_of(block * width, width), width)]
        total = jnp.dot(flipped, columns, preferred_element_type=jnp.float32)
        total = total.reshape(hours, chunks, rows // hours, width)
        target = keep_ref if relative[0] else send_ref
        for chunk in range(chunks):
            target[(chunk,) + relative[1:]] = total[:, chunk].reshape(rows, width)


def halving_reduce(outgoing, keep, axis):
    count = lax.axis_size(axis)
    level = 0
    received = lax.ppermute(outgoing, axis, [(i, i ^ 1) for i in range(count)])
    while keep.ndim > 2:
        level += 1
        outgoing = keep[0] + received[0]
        pairs = [(i, i ^ (1 << level)) for i in range(count)]
        arriving = lax.ppermute(outgoing, axis, pairs)
        keep = keep[1] + received[1]
        received = arriving
    return keep, received


def recurrence_kernel(rate_ref, keep_ref, received_ref, out_ref):
    hours = out_ref.shape[0]
    state = jnp.zeros(out_ref.shape[1:], jnp.float32)
    for hour in range(hours):
        state = rate_ref[pl.ds(hour, 1), :] * state + (keep_ref[hour] + received_ref[hour])
        out_ref[hour] = state
    state = jnp.zeros(out_ref.shape[1:], jnp.float32)
    for hour in reversed(range(hours)):
        rate = rate_ref[pl.ds(hour, 1), :]
        state = rate * state + (1.0 - rate * rate) * out_ref[hour]
        out_ref[hour] = state


def vmem_call(kernel, out_shape, count, cost, scalars=0):
    return pl.pallas_call(
        kernel,
        out_shape=out_shape,
        in_specs=[pl.BlockSpec(memory_space=pltpu.SMEM)] * scalars
        + [pl.BlockSpec(memory_space=pltpu.VMEM)] * count,
        out_specs=jax.tree.map(lambda _: pl.BlockSpec(memory_space=pltpu.VMEM), out_shape),
        cost_estimate=cost,
    )


def local(obs, mask, loadings, decay):
    tm_count = lax.axis_size("tm")
    state_count = lax.axis_size("state")
    levels = state_count.bit_length() - 1
    stations_local, hours, members = obs.shape
    members_here = members // tm_count
    chunk_members = members_here // CHUNKS
    masked = obs * mask[:, :, None].astype(obs.dtype)
    outgoing = jnp.transpose(
        masked.reshape(stations_local, hours, CHUNKS, tm_count, chunk_members),
        (3, 0, 1, 2, 4),
    ).reshape(tm_count, stations_local, hours * members_here)
    by_member = lax.all_to_all(outgoing, "tm", split_axis=0, concat_axis=0, tiled=True)
    stations_here = tm_count * stations_local
    by_member = by_member.reshape(stations_here, hours * members_here)
    by_hour = lax.all_to_all(masked, "tm", split_axis=1, concat_axis=0, tiled=True)
    copies = jnp.broadcast_to(decay[None], (tm_count,) + decay.shape)
    decay_all = lax.all_to_all(copies, "tm", split_axis=0, concat_axis=0, tiled=True)
    decay_all = decay_all.reshape(hours, decay.shape[1])
    all_comps = loadings.shape[1]
    comps = all_comps // state_count
    rows = hours * chunk_members
    half = jax.ShapeDtypeStruct((CHUNKS,) + (2,) * (levels - 1) + (rows, comps), jnp.float32)
    outgoing, keep = vmem_call(
        functools.partial(information_kernel, hours),
        (half, half),
        2,
        pl.CostEstimate(
            flops=2 * stations_here * hours * members_here * all_comps,
            bytes_accessed=2 * stations_here * (hours * members_here + all_comps)
            + 4 * hours * members_here * all_comps,
            transcendentals=0,
        ),
        scalars=1,
    )(lax.axis_index("state").reshape(1).astype(jnp.int32), by_member, loadings)
    smoothed_parts = []
    residual_parts = []
    for chunk in range(CHUNKS):
        kept, received = halving_reduce(outgoing[chunk], keep[chunk], "state")
        kept = kept.reshape(hours, chunk_members, comps)
        received = received.reshape(hours, chunk_members, comps)
        smoothed_here = vmem_call(
            recurrence_kernel,
            jax.ShapeDtypeStruct(kept.shape, jnp.float32),
            3,
            pl.CostEstimate(
                flops=6 * hours * chunk_members * comps,
                bytes_accessed=12 * hours * chunk_members * comps,
                transcendentals=0,
            ),
        )(decay_all, kept, received)
        gathered = lax.all_to_all(smoothed_here, "tm", split_axis=0, concat_axis=1, tiled=True)
        rounded = gathered.astype(jnp.bfloat16)
        full = lax.all_gather(rounded, "state", axis=2, tiled=True)
        fitted = jnp.einsum("so,gyo->sgy", loadings, full, preferred_element_type=jnp.float32)
        low = chunk * members // CHUNKS
        picked = by_hour[:, :, low:low + members // CHUNKS]
        residual_parts.append(picked.astype(jnp.float32) - fitted)
        smoothed_parts.append(jnp.transpose(gathered, (2, 0, 1)))
    return (
        jnp.concatenate(smoothed_parts, axis=2),
        jnp.concatenate(residual_parts, axis=2),
    )


def solution(mesh):
    return jax.shard_map(
        local,
        mesh=mesh,
        in_specs=(
            P(("state", "tm"), None, None),
            P(("state", "tm"), None),
            P("state", None),
            P("tm", "state"),
        ),
        out_specs=(P("state", "tm", None), P("state", "tm", None)),
        check_vma=False,
    )
```

time: 138 us -> 138 us (level)
  blocking collectives: 56.5 us -> 10.1 us
  waiting for transfers between devices: 33.9 us -> 59 us
  starting transfers between devices: 8.82 us -> 21.9 us
  local copies, waits for them, and re-layouts: 8.75 us -> 12.8 us
  matrix products: 3.5 us -> 5.33 us
  Pallas kernels: 7.5 us -> 9.03 us
    all_to_all x2 -> x0, blocking collectives: 46.4 us -> none  [the longest x1 29 us: local(): lax.all_to_all(smoothed_here, 'tm', split_axis=0, concat_axis=1, tiled=True)]
    all_to_all x0 -> x3, waiting for transfers between devices: none -> 39.2 us  [the longest x2 25.6 us: local(): lax.all_to_all(smoothed_here, 'tm', split_axis=0, concat_axis=1, tiled=True)]
    ppermute x1 -> x2, waiting for transfers between devices: 12.9 us -> 0.01 us  [halving_reduce(): arriving = lax.ppermute(outgoing, axis, pairs)]
    all_to_all x0 -> x3, starting transfers between devices: none -> 10.9 us  [the longest x2 7.28 us: local(): lax.all_to_all(smoothed_here, 'tm', split_axis=0, concat_axis=1, tiled=True)]
    squeeze x0 -> x1, local copies, waits for them, and re-layouts: none -> 1.9 us  [local(): kept, received = halving_reduce(outgoing[chunk], keep[chunk], 'state')]
    dot_general x1 -> x2, matrix products: 3.5 us -> 5.33 us  [local(): jnp.einsum('so,gyo->sgy', loadings, full, preferred_element_type=jnp.floa...]
    add x1, other arithmetic: 3 us -> 1.2 us  [halving_reduce(): outgoing = keep[0] + received[0]]
    add x0 -> x2, other arithmetic: none -> 1.76 us  [halving_reduce(): keep = keep[1] + received[1]]
  transfers between devices with their start and end apart: 4 -> 10, of which waited for: 4 -> 7; matrix products, arithmetic and copies ran while one was open for 2% -> 8% of each run, Pallas kernels for 0% -> 2%
where the time goes in v8:
time: 138 us
  waiting for transfers between devices  59 us (43%)
  starting transfers between devices  21.9 us (16%)
  between operations  14.2 us (10%)
  local copies, waits for them, and re-layouts  12.8 us (9%)
  blocking collectives  10.1 us (7%)
  Pallas kernels  9.03 us (7%)
  other arithmetic  5.36 us (4%)
  matrix products  5.33 us (4%)
    all_to_all x2, waiting for transfers between devices, local(): lax.all_to_all(smoothed_here, 'tm', split_axis=0, concat_axis=1, tiled=True)  25.6 us
    all_to_all x1, waiting for transfers between devices, local(): lax.all_to_all(outgoing, 'tm', split_axis=0, concat_axis=0, tiled=True)  14.5 us
    all_to_all x1, waiting for transfers between devices, local(): lax.all_to_all(masked, 'tm', split_axis=1, concat_axis=0, tiled=True)  13.6 us
    all_to_all x1, blocking collectives, local(): lax.all_to_all(copies, 'tm', split_axis=0, concat_axis=0, tiled=True)  10.1 us
    all_to_all x2, starting transfers between devices, local(): lax.all_to_all(smoothed_here, 'tm', split_axis=0, concat_axis=1, tiled=True)  7.28 us
    all_to_all x1, starting transfers between devices, local(): lax.all_to_all(outgoing, 'tm', split_axis=0, concat_axis=0, tiled=True)  7.25 us
    unnamed x17, local copies, waits for them, and re-layouts  6.36 us
    dot_general x2, matrix products, local(): jnp.einsum('so,gyo->sgy', loadings, full, preferred_element_type=jnp.floa...  5.33 us
  transfers between devices with their start and end apart: 10, of which 7 were waited for; matrix products, arithmetic and copies ran while one was open for 8% of the time, Pallas kernels for 2%

profile of v8, /device:TPU:0, one launch (start us, length us, event | category | flops | bytes accessed | tf_op | source)
XLA Modules:
  0.0 137.7 jit_solution(13928352100557411026)
XLA Ops:
  7.9 1.7 %copy.33 = bf16[64,16,256]{0,2,1:T(8,128)(2,1)S(1)} copy(bf16[64,16,256]{2,1,0:T(8,128)(2,1)} %param.4) | data formatting | bytes 1048576 | tf_op args[0]
  9.8 1.1 copy.35
  11.0 7.3 %all-to-all-start.1 = ((bf16[8,64,512]{2,1,0:T(8,128)(2,1)}), bf16[8,64,512]{2,1,0:T(8,128)(2,1)S(1)}, u32[]{:S(2)}, u32[]{:S(2)}) async-start(bf16[8,64,512]{2,1,0:T(8,128)(2,1)} %copy.35), calls=%async_computation.1 | async-start | bytes 1048576 | tf_op jit(solution)/shard_map/all_to_all | solution.py:82
  18.2 14.5 %all-to-all-done.1 = bf16[8,64,512]{2,1,0:T(8,128)(2,1)S(1)} async-done(((bf16[8,64,512]{2,1,0:T(8,128)(2,1)}), bf16[8,64,512]{2,1,0:T(8,128)(2,1)S(1)}, u32[]{:S(2)}, u32[]{:S(2)}) %all-to-all-start.1) | async-done | bytes 524320 | tf_op jit(solution)/shard_map/all_to_all | solution.py:82
  32.7 0.8 copy-done.4
  33.5 4.7 %shard_map.59 = (f32[2,2,256,512]{3,2,1,0:T(8,128)}, f32[2,2,256,512]{3,2,1,0:T(8,128)}) custom-call(s32[1]{0:T(128)} %bitcast.me_ref, bf16[512,512]{1,0:T(8,128)(2,1)} %bitcast.81, bf16[512,2048]{1,0:T(8,128)(2,1)} %l_ref.1), custom_call_target="tpu_custom_call" | custom-call | flops 1073741824 | bytes 6815744 | tf_op jit(solution)/shard_map/pallas_call | solution.py:93
  38.3 1.9 %slice_bitcast_fusion.1 = (f32[2,256,512]{2,1,0:T(8,128)S(1)}, f32[2,256,512]{2,1,0:T(8,128)S(1)}) fusion(f32[2,2,256,512]{3,2,1,0:T(8,128)} %get-tuple-element.5), kind=kLoop, calls=%fused_computation.11 | loop fusion | bytes 4194304 | tf_op jit(solution)/shard_map/squeeze | solution.py:108
  40.8 2.1 %collective-permute-done = f32[2,256,512]{2,1,0:T(8,128)S(1)} collective-permute-done((f32[2,256,512]{2,1,0:T(8,128)S(1)}, f32[2,256,512]{2,1,0:T(8,128)S(1)}, u32[]{:S(2)}, u32[]{:S(2)}) %collective-permute-start) | collective-permute-done | bytes 1048608 | tf_op jit(solution)/shard_map/ppermute | solution.py:35
  42.9 1.5 %collective-permute-done.2 = f32[2,256,512]{2,1,0:T(8,128)S(1)} collective-permute-done((f32[2,256,512]{2,1,0:T(8,128)S(1)}, f32[2,256,512]{2,1,0:T(8,128)S(1)}, u32[]{:S(2)}, u32[]{:S(2)}) %collective-permute-start.2) | collective-permute-done | bytes 1048608 | tf_op jit(solution)/shard_map/ppermute | solution.py:35
  44.4 1.0 copy-done.1
  45.4 1.2 fusion.17
  46.6 1.5 %collective-permute-start.1 = (f32[256,512]{1,0:T(8,128)}, f32[256,512]{1,0:T(8,128)}, u32[]{:S(2)}, u32[]{:S(2)}) collective-permute-start(f32[256,512]{1,0:T(8,128)} %get-tuple-element.14), channel_id=1, source_target_pairs={{0,2},{1,3},{2,0},{3,1},{4,6},{5,7},{6,4},{7,5},{8,10},{9,11},{10,... | collective-permute-start | bytes 1572872 | tf_op jit(solution)/shard_map/ppermute | solution.py:40
  48.1 10.1 %all_to_all.64 = f32[8,2,512]{2,1,0:T(2,128)S(1)} all-to-all(f32[8,2,512]{2,1,0:T(2,128)S(1)} %broadcast_in_dim.2), channel_id=1, replica_groups=mesh['tm'=8,'state'=4] {'tm'}, dimensions={0} | all-to-all | bytes 65536 | tf_op jit(solution)/shard_map/all_to_all | solution.py:87
  58.9 0.9 fusion.18
  60.1 0.9 add.14.keep_ref
  61.0 2.2 %shard_map.60 = f32[16,16,512]{2,1,0:T(8,128)} custom-call(f32[16,512]{1,0:T(8,128)} %reshape.42.rate_ref, f32[16,16,512]{2,1,0:T(8,128)} %add.14.keep_ref, f32[16,16,512]{2,1,0:T(8,128)} %bitcast.10.received_ref), custom_call_target="tpu_custom_call" | custom-call | flops 786432 | bytes 1572864 | tf_op jit(solution)/shard_map/pallas_call | solution.py:111
  63.1 3.7 %all-to-all-start.2 = ((f32[16,16,512]{2,1,0:T(8,128)}), f32[16,16,512]{2,1,0:T(8,128)S(1)}, u32[]{:S(2)}, u32[]{:S(2)}) async-start(f32[16,16,512]{2,1,0:T(8,128)} %shard_map.60), calls=%async_computation.2 | async-start | bytes 1048576 | tf_op jit(solution)/shard_map/all_to_all | solution.py:121
  66.8 1.6 %collective-permute-start.3 = (f32[256,512]{1,0:T(8,128)}, f32[256,512]{1,0:T(8,128)}, u32[]{:S(2)}, u32[]{:S(2)}) collective-permute-start(f32[256,512]{1,0:T(8,128)} %get-tuple-element.15), channel_id=1, source_target_pairs={{0,2},{1,3},{2,0},{3,1},{4,6},{5,7},{6,4},{7,5},{8,10},{9,11},{10,... | collective-permute-start | bytes 1572872 | tf_op jit(solution)/shard_map/ppermute | solution.py:40
  68.4 12.4 %all-to-all-done.2 = f32[16,16,512]{2,1,0:T(8,128)S(1)} async-done(((f32[16,16,512]{2,1,0:T(8,128)}), f32[16,16,512]{2,1,0:T(8,128)S(1)}, u32[]{:S(2)}, u32[]{:S(2)}) %all-to-all-start.2) | async-done | bytes 524320 | tf_op jit(solution)/shard_map/all_to_all | solution.py:121
  80.9 0.7 bitcast_convert_fusion.1
  81.7 0.9 add.16.keep_ref
  82.6 2.1 %shard_map.61 = f32[16,16,512]{2,1,0:T(8,128)} custom-call(f32[16,512]{1,0:T(8,128)} %reshape.42.rate_ref, f32[16,16,512]{2,1,0:T(8,128)} %add.16.keep_ref, f32[16,16,512]{2,1,0:T(8,128)} %bitcast.20.received_ref), custom_call_target="tpu_custom_call" | custom-call | flops 786432 | bytes 1572864 | tf_op jit(solution)/shard_map/pallas_call | solution.py:111
  84.7 3.6 %all-to-all-start.3 = ((f32[16,16,512]{2,1,0:T(8,128)}), f32[16,16,512]{2,1,0:T(8,128)S(1)}, u32[]{:S(2)}, u32[]{:S(2)}) async-start(f32[16,16,512]{2,1,0:T(8,128)} %shard_map.61), calls=%async_computation.3 | async-start | bytes 1048576 | tf_op jit(solution)/shard_map/all_to_all | solution.py:121
  88.3 1.1 copy.38
  89.5 13.2 %all-to-all-done.3 = f32[16,16,512]{2,1,0:T(8,128)S(1)} async-done(((f32[16,16,512]{2,1,0:T(8,128)}), f32[16,16,512]{2,1,0:T(8,128)S(1)}, u32[]{:S(2)}, u32[]{:S(2)}) %all-to-all-start.3) | async-done | bytes 524320 | tf_op jit(solution)/shard_map/all_to_all | solution.py:121
  102.6 3.6 %all-to-all-start.4 = ((bf16[64,16,256]{2,0,1:T(8,128)(2,1)}), bf16[64,16,256]{2,0,1:T(8,128)(2,1)S(1)}, u32[]{:S(2)}, u32[]{:S(2)}) async-start(bf16[64,16,256]{2,0,1:T(8,128)(2,1)} %copy.38), calls=%async_computation.4 | async-start | bytes 1048576 | tf_op jit(solution)/shard_map/all_to_all | solution.py:85
  107.1 13.6 %all-to-all-done.4 = bf16[64,16,256]{2,0,1:T(8,128)(2,1)S(1)} async-done(((bf16[64,16,256]{2,0,1:T(8,128)(2,1)}), bf16[64,16,256]{2,0,1:T(8,128)(2,1)S(1)}, u32[]{:S(2)}, u32[]{:S(2)}) %all-to-all-start.4) | async-done | bytes 524320 | tf_op jit(solution)/shard_map/all_to_all | solution.py:85
  121.2 1.3 copy.42
  122.6 2.7 %fusion.7 = f32[512,2,128]{0,2,1:T(8,128)S(1)} fusion(bf16[2,128,2048]{2,1,0:T(8,128)(2,1)} %all-gather.3.cloned.1.call-done, bf16[512,2048]{1,0:T(8,128)(2,1)} %l_ref.1, bf16[512,2,128]{0,2,1:T(8,128)(2,1)S(1)} %copy.44), kind=kOutput, calls=%fused_computation.5 | convolution fusion | flops 537133056 | bytes 3932160 | tf_op jit(solution)/shard_map/so,gyo->sgy/dot_general | solution.py:124
  125.2 1.6 %all-gather.5.cloned.1.call-done = bf16[2,128,2048]{2,1,0:T(8,128)(2,1)} async-done(((bf16[2,128,512]{2,1,0:T(8,128)(2,1)}), bf16[2,128,2048]{2,1,0:T(8,128)(2,1)}) %all-gather.5.cloned.1.call-update) | async-done | bytes 1048592 | tf_op jit(solution)/shard_map/all_gather | solution.py:123
  126.8 2.7 %fusion.13 = f32[512,2,128]{0,2,1:T(8,128)S(1)} fusion(bf16[2,128,2048]{2,1,0:T(8,128)(2,1)} %all-gather.5.cloned.1.call-done, bf16[512,2048]{1,0:T(8,128)(2,1)} %l_ref.1, bf16[512,2,128]{0,2,1:T(8,128)(2,1)S(1)} %copy.45), kind=kOutput, calls=%fused_computation.7 | convolution fusion | flops 537133056 | bytes 3932160 | tf_op jit(solution)/shard_map/so,gyo->sgy/dot_general | solution.py:124
  129.6 1.3 copy.43
  (37 shorter events, 4.0 us)
Async XLA Ops:
  11.0 21.7 %all-to-all-start.1 = ((bf16[8,64,512]{2,1,0:T(8,128)(2,1)}), bf16[8,64,512]{2,1,0:T(8,128)(2,1)S(1)}, u32[]{:S(2)}, u32[]{:S(2)}) async-start(bf16[8,64,512]{2,1,0:T(8,128)(2,1)} %copy.35), calls=%async_computation.1 | async-start | bytes 1048576 | tf_op jit(solution)/shard_map/all_to_all | solution.py:82
  32.7 0.8 copy-start.4
  38.2 7.1 %copy-start = (f32[2,2,256,512]{3,2,1,0:T(8,128)S(1)}, f32[2,2,256,512]{3,2,1,0:T(8,128)}, u32[]{:S(2)}) copy-start(f32[2,2,256,512]{3,2,1,0:T(8,128)} %get-tuple-element.4) | copy-start | bytes 6291460
  40.2 7.9 %copy-start.5 = (f32[2,512]{1,0:T(2,128)S(1)}, f32[2,512]{1,0:T(2,128)}, u32[]{:S(2)}) copy-start(f32[2,512]{1,0:T(2,128)} %param.7) | copy-start | bytes 12292
  40.2 2.7 %collective-permute-start = (f32[2,256,512]{2,1,0:T(8,128)S(1)}, f32[2,256,512]{2,1,0:T(8,128)S(1)}, u32[]{:S(2)}, u32[]{:S(2)}) collective-permute-start(f32[2,256,512]{2,1,0:T(8,128)S(1)} %get-tuple-element.16), channel_id=1, source_target_pairs={{0,1},{1,0},{2,3},{3,2},{4,5},{5,4},{6,7},{7,6},{8,9},{9,8},{10,11... | collective-permute-start | bytes 3145736 | tf_op jit(solution)/shard_map/ppermute | solution.py:35
  40.3 4.1 %collective-permute-start.2 = (f32[2,256,512]{2,1,0:T(8,128)S(1)}, f32[2,256,512]{2,1,0:T(8,128)S(1)}, u32[]{:S(2)}, u32[]{:S(2)}) collective-permute-start(f32[2,256,512]{2,1,0:T(8,128)S(1)} %get-tuple-element.17), channel_id=1, source_target_pairs={{0,1},{1,0},{2,3},{3,2},{4,5},{5,4},{6,7},{7,6},{8,9},{9,8},{10,11... | collective-permute-start | bytes 3145736 | tf_op jit(solution)/shard_map/ppermute | solution.py:35
  42.9 3.7 %copy-start.2 = (f32[2,256,512]{2,1,0:T(8,128)}, f32[2,256,512]{2,1,0:T(8,128)S(1)}, u32[]{:S(2)}) copy-start(f32[2,256,512]{2,1,0:T(8,128)S(1)} %collective-permute-done) | copy-start | bytes 3145732
  44.4 1.0 copy-start.1
  46.6 14.4 %collective-permute-start.1 = (f32[256,512]{1,0:T(8,128)}, f32[256,512]{1,0:T(8,128)}, u32[]{:S(2)}, u32[]{:S(2)}) collective-permute-start(f32[256,512]{1,0:T(8,128)} %get-tuple-element.14), channel_id=1, source_target_pairs={{0,2},{1,3},{2,0},{3,1},{4,6},{5,7},{6,4},{7,5},{8,10},{9,11},{10,... | collective-permute-start | bytes 1572872 | tf_op jit(solution)/shard_map/ppermute | solution.py:40
  58.9 1.2 slice-start.1
  63.1 18.6 %slice-start = ((f32[2,256,512]{2,1,0:T(8,128)}), f32[1,256,512]{2,1,0:T(8,128)S(1)}, s32[]{:S(2)}) async-start(f32[2,256,512]{2,1,0:T(8,128)} %copy-done.1), calls=%async_computation.7 | async-start | bytes 1048576 | tf_op jit(solution)/shard_map/slice | solution.py:41
  63.1 18.6 %copy-start.3 = (f32[1,1,256,512]{3,2,1,0:T(8,128)S(1)}, f32[1,1,256,512]{3,2,1,0:T(8,128)}, u32[]{:S(2)}) copy-start(f32[1,1,256,512]{3,2,1,0:T(8,128)} %get-tuple-element.19) | copy-start | bytes 1572868
  63.1 17.7 %all-to-all-start.2 = ((f32[16,16,512]{2,1,0:T(8,128)}), f32[16,16,512]{2,1,0:T(8,128)S(1)}, u32[]{:S(2)}, u32[]{:S(2)}) async-start(f32[16,16,512]{2,1,0:T(8,128)} %shard_map.60), calls=%async_computation.2 | async-start | bytes 1048576 | tf_op jit(solution)/shard_map/all_to_all | solution.py:121
  66.8 55.8 %all-gather.3.cloned.1.call-start = ((), (), s32[]{:S(2)}) async-start(), calls=%async_computation.5 | async-start | bytes 1310720 | tf_op jit(solution)/shard_map/all_gather | solution.py:123
  66.8 15.7 %collective-permute-start.3 = (f32[256,512]{1,0:T(8,128)}, f32[256,512]{1,0:T(8,128)}, u32[]{:S(2)}, u32[]{:S(2)}) collective-permute-start(f32[256,512]{1,0:T(8,128)} %get-tuple-element.15), channel_id=1, source_target_pairs={{0,2},{1,3},{2,0},{3,1},{4,6},{5,7},{6,4},{7,5},{8,10},{9,11},{10,... | collective-permute-start | bytes 1572872 | tf_op jit(solution)/shard_map/ppermute | solution.py:40
  84.7 17.9 %all-to-all-start.3 = ((f32[16,16,512]{2,1,0:T(8,128)}), f32[16,16,512]{2,1,0:T(8,128)S(1)}, u32[]{:S(2)}, u32[]{:S(2)}) async-start(f32[16,16,512]{2,1,0:T(8,128)} %shard_map.61), calls=%async_computation.3 | async-start | bytes 1048576 | tf_op jit(solution)/shard_map/all_to_all | solution.py:121
  102.6 18.1 %all-to-all-start.4 = ((bf16[64,16,256]{2,0,1:T(8,128)(2,1)}), bf16[64,16,256]{2,0,1:T(8,128)(2,1)S(1)}, u32[]{:S(2)}, u32[]{:S(2)}) async-start(bf16[64,16,256]{2,0,1:T(8,128)(2,1)} %copy.38), calls=%async_computation.4 | async-start | bytes 1048576 | tf_op jit(solution)/shard_map/all_to_all | solution.py:85
  106.2 20.6 %all-gather.5.cloned.1.call-start = ((), (), s32[]{:S(2)}) async-start(), calls=%async_computation.6 | async-start | bytes 1310720 | tf_op jit(solution)/shard_map/all_gather | solution.py:123
Sparse Core Ops, SparseCore 0:
  81.8 15.7 all-gather.2
  108.6 18.1 all-gather.4

commit v9 on v8

--- a/solution.py
+++ b/solution.py
@@ -10,11 +10,11 @@
 CHUNKS = 2
 
 
-def information_kernel(hours, me_ref, x_ref, l_ref, send_ref, keep_ref):
+def information_kernel(hours, me_ref, x_ref, l_ref, *out_refs):
     me = me_ref[0]
-    chunks = send_ref.shape[0]
-    levels = send_ref.ndim - 2
-    rows, width = send_ref.shape[-2:]
+    chunks = len(out_refs) // 2
+    levels = out_refs[0].ndim - 1
+    rows, width = out_refs[0].shape[-2:]
     flipped = x_ref[...].T
     for slot in range(2 ** levels):
         relative = tuple((slot >> level) & 1 for level in range(levels))
@@ -24,9 +24,9 @@
         columns = l_ref[:, pl.ds(pl.multiple_of(block * width, width), width)]
         total = jnp.dot(flipped, columns, preferred_element_type=jnp.float32)
         total = total.reshape(hours, chunks, rows // hours, width)
-        target = keep_ref if relative[0] else send_ref
         for chunk in range(chunks):
-            target[(chunk,) + relative[1:]] = total[:, chunk].reshape(rows, width)
+            target = out_refs[2 * chunk + relative[0]]
+            target[relative[1:]] = total[:, chunk].reshape(rows, width)
 
 
 def halving_reduce(outgoing, keep, axis):
@@ -89,10 +89,10 @@
     all_comps = loadings.shape[1]
     comps = all_comps // state_count
     rows = hours * chunk_members
-    half = jax.ShapeDtypeStruct((CHUNKS,) + (2,) * (levels - 1) + (rows, comps), jnp.float32)
-    outgoing, keep = vmem_call(
+    half = jax.ShapeDtypeStruct((2,) * (levels - 1) + (rows, comps), jnp.float32)
+    halves = vmem_call(
         functools.partial(information_kernel, hours),
-        (half, half),
+        (half,) * (2 * CHUNKS),
         2,
         pl.CostEstimate(
             flops=2 * stations_here * hours * members_here * all_comps,
@@ -105,7 +105,7 @@
     smoothed_parts = []
     residual_parts = []
     for chunk in range(CHUNKS):
-        kept, received = halving_reduce(outgoing[chunk], keep[chunk], "state")
+        kept, received = halving_reduce(halves[2 * chunk], halves[2 * chunk + 1], "state")
         kept = kept.reshape(hours, chunk_members, comps)
         received = received.reshape(hours, chunk_members, comps)
         smoothed_here = vmem_call(

time: 138 us -> 136 us (0.986)
  local copies, waits for them, and re-layouts: 12.8 us -> 10.3 us
  waiting for transfers between devices: 59 us -> 56.5 us
  other arithmetic: 5.36 us -> 6.94 us
  starting transfers between devices: 21.9 us -> 23.3 us
    all_to_all x2, waiting for transfers between devices: 25.6 us -> 21.6 us  [local(): lax.all_to_all(smoothed_here, 'tm', split_axis=0, concat_axis=1, tiled=True)]
    add x1 -> x2, other arithmetic: 1.2 us -> 4.57 us  [halving_reduce(): outgoing = keep[0] + received[0]]
    ppermute x2, waiting for transfers between devices: 0.01 us -> 2.48 us  [halving_reduce(): arriving = lax.ppermute(outgoing, axis, pairs)]
    all_to_all x2, starting transfers between devices: 7.28 us -> 9.24 us  [local(): lax.all_to_all(smoothed_here, 'tm', split_axis=0, concat_axis=1, tiled=True)]
    squeeze x1 -> x0, local copies, waits for them, and re-layouts: 1.9 us -> none  [local(): kept, received = halving_reduce(outgoing[chunk], keep[chunk], 'state')]
    add x2 -> x0, other arithmetic: 1.76 us -> none  [halving_reduce(): keep = keep[1] + received[1]]
  transfers between devices with their start and end apart: 10 -> 10, of which waited for: 7 -> 8; matrix products, arithmetic and copies ran while one was open for 8% -> 8% of each run, Pallas kernels for 2% -> 3%
where the time goes in v9:
time: 136 us; the launch traced here: 135 us
  waiting for transfers between devices  56.5 us (42%)
  starting transfers between devices  23.3 us (17%)
  between operations  14.2 us (10%)
  local copies, waits for them, and re-layouts  10.3 us (8%)
  blocking collectives  10.1 us (7%)
  Pallas kernels  9.05 us (7%)
  other arithmetic  6.94 us (5%)
  matrix products  4.79 us (4%)
    all_to_all x2, waiting for transfers between devices, local(): lax.all_to_all(smoothed_here, 'tm', split_axis=0, concat_axis=1, tiled=True)  21.6 us
    all_to_all x1, waiting for transfers between devices, local(): lax.all_to_all(outgoing, 'tm', split_axis=0, concat_axis=0, tiled=True)  14.5 us
    all_to_all x1, waiting for transfers between devices, local(): lax.all_to_all(masked, 'tm', split_axis=1, concat_axis=0, tiled=True)  12.7 us
    all_to_all x1, blocking collectives, local(): lax.all_to_all(copies, 'tm', split_axis=0, concat_axis=0, tiled=True)  10.1 us
    all_to_all x2, starting transfers between devices, local(): lax.all_to_all(smoothed_here, 'tm', split_axis=0, concat_axis=1, tiled=True)  9.24 us
    all_to_all x1, starting transfers between devices, local(): lax.all_to_all(outgoing, 'tm', split_axis=0, concat_axis=0, tiled=True)  7.25 us
    unnamed x17, local copies, waits for them, and re-layouts  6.98 us
    dot_general x2, matrix products, local(): jnp.einsum('so,gyo->sgy', loadings, full, preferred_element_type=jnp.floa...  4.79 us
  transfers between devices with their start and end apart: 10, of which 8 were waited for; matrix products, arithmetic and copies ran while one was open for 8% of the time, Pallas kernels for 3%

profile of v9, /device:TPU:0, one launch (start us, length us, event | category | flops | bytes accessed | tf_op | source)
XLA Modules:
  0.0 135.1 jit_solution(1010987926767458401)
XLA Ops:
  7.9 1.7 %copy.33 = bf16[64,16,256]{0,2,1:T(8,128)(2,1)S(1)} copy(bf16[64,16,256]{2,1,0:T(8,128)(2,1)} %param.4) | data formatting | bytes 1048576 | tf_op args[0]
  9.9 1.1 copy.35
  11.0 7.3 %all-to-all-start.1 = ((bf16[8,64,512]{2,1,0:T(8,128)(2,1)}), bf16[8,64,512]{2,1,0:T(8,128)(2,1)S(1)}, u32[]{:S(2)}, u32[]{:S(2)}) async-start(bf16[8,64,512]{2,1,0:T(8,128)(2,1)} %copy.35), calls=%async_computation.1 | async-start | bytes 1048576 | tf_op jit(solution)/shard_map/all_to_all | solution.py:82
  18.2 14.5 %all-to-all-done.1 = bf16[8,64,512]{2,1,0:T(8,128)(2,1)S(1)} async-done(((bf16[8,64,512]{2,1,0:T(8,128)(2,1)}), bf16[8,64,512]{2,1,0:T(8,128)(2,1)S(1)}, u32[]{:S(2)}, u32[]{:S(2)}) %all-to-all-start.1) | async-done | bytes 524320 | tf_op jit(solution)/shard_map/all_to_all | solution.py:82
  32.7 0.8 copy-done.3
  33.5 4.8 %shard_map.59 = (f32[2,256,512]{2,1,0:T(8,128)}, f32[2,256,512]{2,1,0:T(8,128)}, f32[2,256,512]{2,1,0:T(8,128)}, f32[2,256,512]{2,1,0:T(8,128)}) custom-call(s32[1]{0:T(128)} %bitcast.me_ref, bf16[512,512]{1,0:T(8,128)(2,1)} %bitcast.67, bf16[512,2048]{1,0:T(8,128)(2,1)} %l_ref.1), custom_call_target="tpu_custom_call" | custom-call | flops 1073741824 | bytes 6815744 | tf_op jit(solution)/shard_map/pallas_call | solution.py:93
  38.3 2.9 %collective-permute-done = f32[2,256,512]{2,1,0:T(8,128)S(1)} collective-permute-done((f32[2,256,512]{2,1,0:T(8,128)}, f32[2,256,512]{2,1,0:T(8,128)S(1)}, u32[]{:S(2)}, u32[]{:S(2)}) %collective-permute-start) | collective-permute-done | bytes 1048608 | tf_op jit(solution)/shard_map/ppermute | solution.py:35
  41.2 2.2 %fusion.17 = (f32[256,512]{1,0:T(8,128)S(1)}, f32[1,256,512]{2,1,0:T(8,128)}) fusion(f32[2,256,512]{2,1,0:T(8,128)S(1)} %collective-permute-done, f32[2,256,512]{2,1,0:T(8,128)} %get-tuple-element.6), kind=kLoop, calls=%fused_computation.14 | loop fusion | flops 262144 | bytes 3145728 | tf_op jit(solution)/shard_map/add | solution.py:38
  43.4 1.5 %collective-permute-start.1 = (f32[256,512]{1,0:T(8,128)S(1)}, f32[256,512]{1,0:T(8,128)S(1)}, u32[]{:S(2)}, u32[]{:S(2)}) collective-permute-start(f32[256,512]{1,0:T(8,128)S(1)} %get-tuple-element.18), channel_id=1, source_target_pairs={{0,2},{1,3},{2,0},{3,1},{4,6},{5,7},{6,4},{7,5},{8,10},{9,11},{10,... | collective-permute-start | bytes 1572872 | tf_op jit(solution)/shard_map/ppermute | solution.py:40
  44.9 10.1 %all_to_all.64 = f32[8,2,512]{2,1,0:T(2,128)S(1)} all-to-all(f32[8,2,512]{2,1,0:T(2,128)S(1)} %broadcast_in_dim.2), channel_id=1, replica_groups=mesh['tm'=8,'state'=4] {'tm'}, dimensions={0} | all-to-all | bytes 65536 | tf_op jit(solution)/shard_map/all_to_all | solution.py:87
  55.6 1.7 %collective-permute-done.1 = f32[256,512]{1,0:T(8,128)S(1)} collective-permute-done((f32[256,512]{1,0:T(8,128)S(1)}, f32[256,512]{1,0:T(8,128)S(1)}, u32[]{:S(2)}, u32[]{:S(2)}) %collective-permute-start.1) | collective-permute-done | bytes 524320 | tf_op jit(solution)/shard_map/ppermute | solution.py:40
  57.3 0.8 copy-done.2
  58.1 2.1 %shard_map.60 = f32[16,16,512]{2,1,0:T(8,128)} custom-call(f32[16,512]{1,0:T(8,128)} %reshape.38.rate_ref, f32[16,16,512]{2,1,0:T(8,128)} %bitcast.62, f32[16,16,512]{2,1,0:T(8,128)} %bitcast.66), custom_call_target="tpu_custom_call" | custom-call | flops 786432 | bytes 1572864 | tf_op jit(solution)/shard_map/pallas_call | solution.py:111
  60.3 3.6 %all-to-all-start.2 = ((f32[16,16,512]{2,1,0:T(8,128)}), f32[16,16,512]{2,1,0:T(8,128)S(1)}, u32[]{:S(2)}, u32[]{:S(2)}) async-start(f32[16,16,512]{2,1,0:T(8,128)} %shard_map.60), calls=%async_computation.2 | async-start | bytes 1048576 | tf_op jit(solution)/shard_map/all_to_all | solution.py:121
  64.0 2.4 %fusion.16 = (f32[256,512]{1,0:T(8,128)}, f32[1,256,512]{2,1,0:T(8,128)}) fusion(f32[2,256,512]{2,1,0:T(8,128)} %collective-permute-done.2, f32[2,256,512]{2,1,0:T(8,128)S(1)} %copy-done), kind=kLoop, calls=%fused_computation.11 | loop fusion | flops 262144 | bytes 3145728 | tf_op jit(solution)/shard_map/add | solution.py:38
  66.3 1.5 %collective-permute-start.3 = (f32[256,512]{1,0:T(8,128)}, f32[256,512]{1,0:T(8,128)S(1)}, u32[]{:S(2)}, u32[]{:S(2)}) collective-permute-start(f32[256,512]{1,0:T(8,128)} %get-tuple-element.20), channel_id=1, source_target_pairs={{0,2},{1,3},{2,0},{3,1},{4,6},{5,7},{6,4},{7,5},{8,10},{9,11},{10,... | collective-permute-start | bytes 1572872 | tf_op jit(solution)/shard_map/ppermute | solution.py:40
  67.9 10.1 %all-to-all-done.2 = f32[16,16,512]{2,1,0:T(8,128)S(1)} async-done(((f32[16,16,512]{2,1,0:T(8,128)}), f32[16,16,512]{2,1,0:T(8,128)S(1)}, u32[]{:S(2)}, u32[]{:S(2)}) %all-to-all-start.2) | async-done | bytes 524320 | tf_op jit(solution)/shard_map/all_to_all | solution.py:121
  78.0 0.7 bitcast_convert_fusion.1
  78.8 0.8 collective-permute-done.3
  79.6 0.8 copy-done.1
  80.3 2.1 %shard_map.61 = f32[16,16,512]{2,1,0:T(8,128)} custom-call(f32[16,512]{1,0:T(8,128)} %reshape.38.rate_ref, f32[16,16,512]{2,1,0:T(8,128)} %bitcast.59, f32[16,16,512]{2,1,0:T(8,128)} %bitcast.65), custom_call_target="tpu_custom_call" | custom-call | flops 786432 | bytes 1572864 | tf_op jit(solution)/shard_map/pallas_call | solution.py:111
  82.5 5.6 %all-to-all-start.3 = ((f32[16,16,512]{2,1,0:T(8,128)}), f32[16,16,512]{2,1,0:T(8,128)S(1)}, u32[]{:S(2)}, u32[]{:S(2)}) async-start(f32[16,16,512]{2,1,0:T(8,128)} %shard_map.61), calls=%async_computation.3 | async-start | bytes 1048576 | tf_op jit(solution)/shard_map/all_to_all | solution.py:121
  88.1 1.1 copy.38
  89.2 11.5 %all-to-all-done.3 = f32[16,16,512]{2,1,0:T(8,128)S(1)} async-done(((f32[16,16,512]{2,1,0:T(8,128)}), f32[16,16,512]{2,1,0:T(8,128)S(1)}, u32[]{:S(2)}, u32[]{:S(2)}) %all-to-all-start.3) | async-done | bytes 524320 | tf_op jit(solution)/shard_map/all_to_all | solution.py:121
  100.7 3.6 %all-to-all-start.4 = ((bf16[64,16,256]{2,0,1:T(8,128)(2,1)}), bf16[64,16,256]{2,0,1:T(8,128)(2,1)S(1)}, u32[]{:S(2)}, u32[]{:S(2)}) async-start(bf16[64,16,256]{2,0,1:T(8,128)(2,1)} %copy.38), calls=%async_computation.4 | async-start | bytes 1048576 | tf_op jit(solution)/shard_map/all_to_all | solution.py:85
  104.4 0.7 bitcast_convert_fusion
  105.2 12.7 %all-to-all-done.4 = bf16[64,16,256]{2,0,1:T(8,128)(2,1)S(1)} async-done(((bf16[64,16,256]{2,0,1:T(8,128)(2,1)}), bf16[64,16,256]{2,0,1:T(8,128)(2,1)S(1)}, u32[]{:S(2)}, u32[]{:S(2)}) %all-to-all-start.4) | async-done | bytes 524320 | tf_op jit(solution)/shard_map/all_to_all | solution.py:85
  118.4 1.3 copy.42
  119.7 2.8 %fusion.7 = f32[512,2,128]{0,2,1:T(8,128)S(1)} fusion(bf16[2,128,2048]{2,1,0:T(8,128)(2,1)} %all-gather.3.cloned.1.call-done, bf16[512,2048]{1,0:T(8,128)(2,1)} %l_ref.1, bf16[512,2,128]{0,2,1:T(8,128)(2,1)S(1)} %copy.44), kind=kOutput, calls=%fused_computation.5 | convolution fusion | flops 537133056 | bytes 3932160 | tf_op jit(solution)/shard_map/so,gyo->sgy/dot_general | solution.py:124
  122.5 2.4 %all-gather.5.cloned.1.call-done = bf16[2,128,2048]{2,1,0:T(8,128)(2,1)} async-done(((bf16[2,128,512]{2,1,0:T(8,128)(2,1)}), bf16[2,128,2048]{2,1,0:T(8,128)(2,1)}) %all-gather.5.cloned.1.call-update) | async-done | bytes 1048592 | tf_op jit(solution)/shard_map/all_gather | solution.py:123
  124.9 2.0 %fusion.13 = f32[512,2,128]{0,2,1:T(8,128)S(1)} fusion(bf16[2,128,2048]{2,1,0:T(8,128)(2,1)} %all-gather.5.cloned.1.call-done, bf16[512,2048]{1,0:T(8,128)(2,1)S(1)} %copy-done.5, bf16[512,2,128]{0,2,1:T(8,128)(2,1)S(1)} %copy.45), kind=kOutput, calls=%fused_computation.7 | convolution fusion | flops 537133056 | bytes 3932160 | tf_op jit(solution)/shard_map/so,gyo->sgy/dot_general | solution.py:124
  127.0 1.3 copy.43
  (30 shorter events, 2.4 us)
Async XLA Ops:
  11.0 21.7 %all-to-all-start.1 = ((bf16[8,64,512]{2,1,0:T(8,128)(2,1)}), bf16[8,64,512]{2,1,0:T(8,128)(2,1)S(1)}, u32[]{:S(2)}, u32[]{:S(2)}) async-start(bf16[8,64,512]{2,1,0:T(8,128)(2,1)} %copy.35), calls=%async_computation.1 | async-start | bytes 1048576 | tf_op jit(solution)/shard_map/all_to_all | solution.py:82
  32.7 0.8 copy-start.3
  38.3 6.6 %copy-start.4 = (f32[2,512]{1,0:T(2,128)S(1)}, f32[2,512]{1,0:T(2,128)}, u32[]{:S(2)}) copy-start(f32[2,512]{1,0:T(2,128)} %param.7) | copy-start | bytes 12292
  38.3 2.9 %collective-permute-start = (f32[2,256,512]{2,1,0:T(8,128)}, f32[2,256,512]{2,1,0:T(8,128)S(1)}, u32[]{:S(2)}, u32[]{:S(2)}) collective-permute-start(f32[2,256,512]{2,1,0:T(8,128)} %get-tuple-element.7), channel_id=1, source_target_pairs={{0,1},{1,0},{2,3},{3,2},{4,5},{5,4},{6,7},{7,6},{8,9},{9,8},{10,11... | collective-permute-start | bytes 3145736 | tf_op jit(solution)/shard_map/ppermute | solution.py:35
  43.4 20.6 %copy-start = (f32[2,256,512]{2,1,0:T(8,128)S(1)}, f32[2,256,512]{2,1,0:T(8,128)}, u32[]{:S(2)}) copy-start(f32[2,256,512]{2,1,0:T(8,128)} %get-tuple-element.8) | copy-start | bytes 3145732
  43.4 14.0 %collective-permute-start.1 = (f32[256,512]{1,0:T(8,128)S(1)}, f32[256,512]{1,0:T(8,128)S(1)}, u32[]{:S(2)}, u32[]{:S(2)}) collective-permute-start(f32[256,512]{1,0:T(8,128)S(1)} %get-tuple-element.18), channel_id=1, source_target_pairs={{0,2},{1,3},{2,0},{3,1},{4,6},{5,7},{6,4},{7,5},{8,10},{9,11},{10,... | collective-permute-start | bytes 1572872 | tf_op jit(solution)/shard_map/ppermute | solution.py:40
  44.9 19.1 %collective-permute-start.2 = (f32[2,256,512]{2,1,0:T(8,128)}, f32[2,256,512]{2,1,0:T(8,128)}, u32[]{:S(2)}, u32[]{:S(2)}) collective-permute-start(f32[2,256,512]{2,1,0:T(8,128)} %get-tuple-element.9), channel_id=1, source_target_pairs={{0,1},{1,0},{2,3},{3,2},{4,5},{5,4},{6,7},{7,6},{8,9},{9,8},{10,11... | collective-permute-start | bytes 3145736 | tf_op jit(solution)/shard_map/ppermute | solution.py:35
  57.3 0.8 copy-start.2
  60.3 17.7 %all-to-all-start.2 = ((f32[16,16,512]{2,1,0:T(8,128)}), f32[16,16,512]{2,1,0:T(8,128)S(1)}, u32[]{:S(2)}, u32[]{:S(2)}) async-start(f32[16,16,512]{2,1,0:T(8,128)} %shard_map.60), calls=%async_computation.2 | async-start | bytes 1048576 | tf_op jit(solution)/shard_map/all_to_all | solution.py:121
  63.9 55.8 %all-gather.3.cloned.1.call-start = ((), (), s32[]{:S(2)}) async-start(), calls=%async_computation.5 | async-start | bytes 1310720 | tf_op jit(solution)/shard_map/all_gather | solution.py:123
  66.3 13.2 %collective-permute-start.3 = (f32[256,512]{1,0:T(8,128)}, f32[256,512]{1,0:T(8,128)S(1)}, u32[]{:S(2)}, u32[]{:S(2)}) collective-permute-start(f32[256,512]{1,0:T(8,128)} %get-tuple-element.20), channel_id=1, source_target_pairs={{0,2},{1,3},{2,0},{3,1},{4,6},{5,7},{6,4},{7,5},{8,10},{9,11},{10,... | collective-permute-start | bytes 1572872 | tf_op jit(solution)/shard_map/ppermute | solution.py:40
  79.6 0.8 copy-start.1
  82.5 18.2 %all-to-all-start.3 = ((f32[16,16,512]{2,1,0:T(8,128)}), f32[16,16,512]{2,1,0:T(8,128)S(1)}, u32[]{:S(2)}, u32[]{:S(2)}) async-start(f32[16,16,512]{2,1,0:T(8,128)} %shard_map.61), calls=%async_computation.3 | async-start | bytes 1048576 | tf_op jit(solution)/shard_map/all_to_all | solution.py:121
  100.7 17.1 %all-to-all-start.4 = ((bf16[64,16,256]{2,0,1:T(8,128)(2,1)}), bf16[64,16,256]{2,0,1:T(8,128)(2,1)S(1)}, u32[]{:S(2)}, u32[]{:S(2)}) async-start(bf16[64,16,256]{2,0,1:T(8,128)(2,1)} %copy.38), calls=%async_computation.4 | async-start | bytes 1048576 | tf_op jit(solution)/shard_map/all_to_all | solution.py:85
  104.3 20.6 %all-gather.5.cloned.1.call-start = ((), (), s32[]{:S(2)}) async-start(), calls=%async_computation.6 | async-start | bytes 1310720 | tf_op jit(solution)/shard_map/all_gather | solution.py:123
  119.7 5.3 %copy-start.5 = (bf16[512,2048]{1,0:T(8,128)(2,1)S(1)}, bf16[512,2048]{1,0:T(8,128)(2,1)}, u32[]{:S(2)}) copy-start(bf16[512,2048]{1,0:T(8,128)(2,1)} %l_ref.1) | copy-start | bytes 6291460
Sparse Core Ops, SparseCore 0:
  78.9 15.7 all-gather.2
  106.7 18.1 all-gather.4

commit v10 on v9

--- a/solution.py
+++ b/solution.py
@@ -10,12 +10,13 @@
 CHUNKS = 2
 
 
-def information_kernel(hours, me_ref, x_ref, l_ref, *out_refs):
+def information_kernel(hours, stations, me_ref, x_ref, l_ref, *out_refs):
     me = me_ref[0]
     chunks = len(out_refs) // 2
     levels = out_refs[0].ndim - 1
     rows, width = out_refs[0].shape[-2:]
-    flipped = x_ref[...].T
+    senders = x_ref.shape[0]
+    flipped = x_ref[:, :stations, :].reshape(senders * stations, x_ref.shape[2]).T
     for slot in range(2 ** levels):
         relative = tuple((slot >> level) & 1 for level in range(levels))
         block = 0
@@ -79,19 +80,28 @@
         masked.reshape(stations_local, hours, CHUNKS, tm_count, chunk_members),
         (3, 0, 1, 2, 4),
     ).reshape(tm_count, stations_local, hours * members_here)
+    high = lax.reduce_precision(decay, exponent_bits=8, mantissa_bits=7)
+    middle = lax.reduce_precision(decay - high, exponent_bits=8, mantissa_bits=7)
+    low = decay - high - middle
+    pieces = jnp.stack([high, middle, low]).astype(obs.dtype).reshape(-1, hours * members_here)
+    spare = (-(stations_local + pieces.shape[0])) % 16
+    pieces = jnp.pad(pieces, ((0, spare), (0, 0)))
+    pieces = jnp.broadcast_to(pieces[None], (tm_count,) + pieces.shape)
+    outgoing = jnp.concatenate([outgoing, pieces], axis=1)
     by_member = lax.all_to_all(outgoing, "tm", split_axis=0, concat_axis=0, tiled=True)
     stations_here = tm_count * stations_local
-    by_member = by_member.reshape(stations_here, hours * members_here)
-    by_hour = lax.all_to_all(masked, "tm", split_axis=1, concat_axis=0, tiled=True)
-    copies = jnp.broadcast_to(decay[None], (tm_count,) + decay.shape)
-    decay_all = lax.all_to_all(copies, "tm", split_axis=0, concat_axis=0, tiled=True)
-    decay_all = decay_all.reshape(hours, decay.shape[1])
+    slab_hours, comps_here = decay.shape
+    arrived = by_member[:, stations_local:stations_local + 3 * slab_hours * comps_here // (hours * members_here)]
+    arrived = arrived.reshape(tm_count, 3, slab_hours, comps_here).astype(jnp.float32)
+    decay_all = (arrived[:, 0] + arrived[:, 1] + arrived[:, 2]).reshape(hours, comps_here)
+    masked_later, by_member = lax.optimization_barrier((masked, by_member))
+    by_hour = lax.all_to_all(masked_later, "tm", split_axis=1, concat_axis=0, tiled=True)
     all_comps = loadings.shape[1]
     comps = all_comps // state_count
     rows = hours * chunk_members
     half = jax.ShapeDtypeStruct((2,) * (levels - 1) + (rows, comps), jnp.float32)
     halves = vmem_call(
-        functools.partial(information_kernel, hours),
+        functools.partial(information_kernel, hours, stations_local),
         (half,) * (2 * CHUNKS),
         2,
         pl.CostEstimate(
@@ -106,6 +116,8 @@
     residual_parts = []
     for chunk in range(CHUNKS):
         kept, received = halving_reduce(halves[2 * chunk], halves[2 * chunk + 1], "state")
+        if chunk == 0:
+            by_hour, kept, received = lax.optimization_barrier((by_hour, kept, received))
         kept = kept.reshape(hours, chunk_members, comps)
         received = received.reshape(hours, chunk_members, comps)
         smoothed_here = vmem_call(

time: 136 us -> 135 us (level)
  blocking collectives: 10.1 us -> 18 us
  waiting for transfers between devices: 56.5 us -> 50.5 us
  starting transfers between devices: 23.3 us -> 19.7 us
    all_to_all x2 -> x1, waiting for transfers between devices: 21.6 us -> 10.1 us  [local(): lax.all_to_all(smoothed_here, 'tm', split_axis=0, concat_axis=1, tiled=True)]
    all_gather x2, waiting for transfers between devices: 2.43 us -> 11.7 us  [local(): full = lax.all_gather(rounded, 'state', axis=2, tiled=True)]
    all_to_all x1, blocking collectives: 10.1 us -> 18 us  [local(): lax.all_to_all(smoothed_here, 'tm', split_axis=0, concat_axis=1, tiled=True)]
    all_to_all x2 -> x1, starting transfers between devices: 9.24 us -> 5.64 us  [local(): lax.all_to_all(smoothed_here, 'tm', split_axis=0, concat_axis=1, tiled=True)]
    ppermute x2, waiting for transfers between devices: 2.87 us -> 0.01 us  [halving_reduce(): received = lax.ppermute(outgoing, axis, [(i, i ^ 1) for i in range(count)])]
    all_to_all x1, waiting for transfers between devices: 14.5 us -> 17.3 us  [local(): lax.all_to_all(outgoing, 'tm', split_axis=0, concat_axis=0, tiled=True)]
    ppermute x2, waiting for transfers between devices: 2.48 us -> 0.6 us  [halving_reduce(): arriving = lax.ppermute(outgoing, axis, pairs)]
    all_to_all x1, waiting for transfers between devices: 12.7 us -> 10.8 us  [local(): lax.all_to_all(masked_later, 'tm', split_axis=1, concat_axis=0, tiled=True)]
  transfers between devices with their start and end apart: 10 -> 9, of which waited for: 8 -> 6; matrix products, arithmetic and copies ran while one was open for 8% -> 9% of each run, Pallas kernels for 3% -> 3%
where the time goes in v10:
time: 135 us
  waiting for transfers between devices  50.5 us (37%)
  starting transfers between devices  19.7 us (15%)
  blocking collectives  18 us (13%)
  between operations  14.2 us (11%)
  local copies, waits for them, and re-layouts  9.48 us (7%)
  Pallas kernels  9.1 us (7%)
  other arithmetic  8.21 us (6%)
  matrix products  5.33 us (4%)
    all_to_all x1, blocking collectives, local(): lax.all_to_all(smoothed_here, 'tm', split_axis=0, concat_axis=1, tiled=True)  18 us
    all_to_all x1, waiting for transfers between devices, local(): lax.all_to_all(outgoing, 'tm', split_axis=0, concat_axis=0, tiled=True)  17.3 us
    all_gather x2, waiting for transfers between devices, local(): full = lax.all_gather(rounded, 'state', axis=2, tiled=True)  11.7 us
    all_to_all x1, waiting for transfers between devices, local(): lax.all_to_all(masked_later, 'tm', split_axis=1, concat_axis=0, tiled=True)  10.8 us
    all_to_all x1, waiting for transfers between devices, local(): lax.all_to_all(smoothed_here, 'tm', split_axis=0, concat_axis=1, tiled=True)  10.1 us
    all_to_all x1, starting transfers between devices, local(): lax.all_to_all(outgoing, 'tm', split_axis=0, concat_axis=0, tiled=True)  7.25 us
    unnamed x13, local copies, waits for them, and re-layouts  6.73 us
    all_to_all x1, starting transfers between devices, local(): lax.all_to_all(smoothed_here, 'tm', split_axis=0, concat_axis=1, tiled=True)  5.64 us
  transfers between devices with their start and end apart: 9, of which 6 were waited for; matrix products, arithmetic and copies ran while one was open for 9% of the time, Pallas kernels for 3%

profile of v10, /device:TPU:0, one launch (start us, length us, event | category | flops | bytes accessed | tf_op | source)
XLA Modules:
  0.0 134.6 jit_solution(12622534938558184457)
XLA Ops:
  7.2 0.7 convert_element_type.29
  7.9 0.7 fusion.20
  8.6 1.7 %copy.53 = bf16[64,16,256]{0,2,1:T(8,128)(2,1)S(1)} copy(bf16[64,16,256]{2,1,0:T(8,128)(2,1)} %param.4) | data formatting | bytes 1048576 | tf_op args[0]
  10.9 0.9 pad_maximum_fusion.2
  11.8 7.3 %all-to-all-start = ((bf16[8,80,512]{2,1,0:T(8,128)(2,1)}), bf16[8,80,512]{2,1,0:T(8,128)(2,1)S(1)}, u32[]{:S(2)}, u32[]{:S(2)}) async-start(bf16[8,80,512]{2,1,0:T(8,128)(2,1)} %pad_maximum_fusion.2), calls=%async_computation | async-start | bytes 1310720 | tf_op jit(solution)/shard_map/all_to_all | solution.py:91
  19.1 17.3 %all-to-all-done.x_ref = bf16[8,80,512]{2,1,0:T(8,128)(2,1)S(1)} async-done(((bf16[8,80,512]{2,1,0:T(8,128)(2,1)}), bf16[8,80,512]{2,1,0:T(8,128)(2,1)S(1)}, u32[]{:S(2)}, u32[]{:S(2)}) %all-to-all-start) | async-done | bytes 655392 | tf_op jit(solution)/shard_map/all_to_all | solution.py:91
  36.4 0.8 copy-done.2
  37.2 4.8 %shard_map.59 = (f32[2,256,512]{2,1,0:T(8,128)}, f32[2,256,512]{2,1,0:T(8,128)}, f32[2,256,512]{2,1,0:T(8,128)}, f32[2,256,512]{2,1,0:T(8,128)}) custom-call(s32[1]{0:T(128)} %bitcast.10.me_ref, bf16[8,80,512]{2,1,0:T(8,128)(2,1)} %copy-done.2, bf16[512,2048]{1,0:T(8,128)(2,1)} %l_ref.1), custom_call_target="tpu_custom_call" | custom-call | flops 1073741824 | bytes 6815744 | tf_op jit(solution)/shard_map/pallas_call | solution.py:103
  42.1 1.1 copy.58
  43.2 3.7 %all-to-all-start.1 = ((bf16[64,16,256]{2,0,1:T(8,128)(2,1)}), bf16[64,16,256]{2,0,1:T(8,128)(2,1)S(1)}, u32[]{:S(2)}, u32[]{:S(2)}) async-start(bf16[64,16,256]{2,0,1:T(8,128)(2,1)} %copy.58), calls=%async_computation.1 | async-start | bytes 1048576 | tf_op jit(solution)/shard_map/all_to_all | solution.py:98
  46.9 1.2 fusion.17
  48.0 1.5 %collective-permute-start.1 = (f32[256,512]{1,0:T(8,128)}, f32[256,512]{1,0:T(8,128)S(1)}, u32[]{:S(2)}, u32[]{:S(2)}) collective-permute-start(f32[256,512]{1,0:T(8,128)} %get-tuple-element.30), channel_id=1, source_target_pairs={{0,2},{1,3},{2,0},{3,1},{4,6},{5,7},{6,4},{7,5},{8,10},{9,11},{10,... | collective-permute-start | bytes 1572872 | tf_op jit(solution)/shard_map/ppermute | solution.py:41
  49.6 0.8 slice_convert_fusion
  50.6 0.6 add.41.rate_ref
  51.2 10.8 %all-to-all-done.1 = bf16[64,16,256]{2,0,1:T(8,128)(2,1)S(1)} async-done(((bf16[64,16,256]{2,0,1:T(8,128)(2,1)}), bf16[64,16,256]{2,0,1:T(8,128)(2,1)S(1)}, u32[]{:S(2)}, u32[]{:S(2)}) %all-to-all-start.1) | async-done | bytes 524320 | tf_op jit(solution)/shard_map/all_to_all | solution.py:98
  62.1 0.3 collective-permute-done.1
  62.4 0.8 copy-done.3
  63.2 2.1 %shard_map.60 = f32[16,16,512]{2,1,0:T(8,128)} custom-call(f32[16,512]{1,0:T(8,128)} %add.41.rate_ref, f32[16,16,512]{2,1,0:T(8,128)} %bitcast.71, f32[16,16,512]{2,1,0:T(8,128)} %bitcast.75), custom_call_target="tpu_custom_call" | custom-call | flops 786432 | bytes 1572864 | tf_op jit(solution)/shard_map/pallas_call | solution.py:123
  65.4 5.6 %all-to-all-start.2 = ((f32[16,16,512]{2,1,0:T(8,128)}), f32[16,16,512]{2,1,0:T(8,128)S(1)}, u32[]{:S(2)}, u32[]{:S(2)}) async-start(f32[16,16,512]{2,1,0:T(8,128)} %shard_map.60), calls=%async_computation.2 | async-start | bytes 1048576 | tf_op jit(solution)/shard_map/all_to_all | solution.py:133
  71.1 2.2 %fusion.16 = (f32[256,512]{1,0:T(8,128)S(1)}, f32[1,256,512]{2,1,0:T(8,128)}) fusion(f32[2,256,512]{2,1,0:T(8,128)} %collective-permute-done.2, f32[2,256,512]{2,1,0:T(8,128)S(1)} %copy-done), kind=kLoop, calls=%fused_computation.12 | loop fusion | flops 262144 | bytes 3145728 | tf_op jit(solution)/shard_map/add | solution.py:39
  73.3 1.5 %collective-permute-start.3 = (f32[256,512]{1,0:T(8,128)S(1)}, f32[256,512]{1,0:T(8,128)S(1)}, u32[]{:S(2)}, u32[]{:S(2)}) collective-permute-start(f32[256,512]{1,0:T(8,128)S(1)} %get-tuple-element.32), channel_id=1, source_target_pairs={{0,2},{1,3},{2,0},{3,1},{4,6},{5,7},{6,4},{7,5},{8,10},{9,11},{10,... | collective-permute-start | bytes 1572872 | tf_op jit(solution)/shard_map/ppermute | solution.py:41
  74.8 10.1 %all-to-all-done.2 = f32[16,16,512]{2,1,0:T(8,128)S(1)} async-done(((f32[16,16,512]{2,1,0:T(8,128)}), f32[16,16,512]{2,1,0:T(8,128)S(1)}, u32[]{:S(2)}, u32[]{:S(2)}) %all-to-all-start.2) | async-done | bytes 524320 | tf_op jit(solution)/shard_map/all_to_all | solution.py:133
  84.9 0.7 bitcast_convert_fusion.1
  86.0 0.8 copy-done.4
  86.8 2.1 %shard_map.61 = f32[16,16,512]{2,1,0:T(8,128)} custom-call(f32[16,512]{1,0:T(8,128)} %add.41.rate_ref, f32[16,16,512]{2,1,0:T(8,128)} %bitcast.72, f32[16,16,512]{2,1,0:T(8,128)} %bitcast.76), custom_call_target="tpu_custom_call" | custom-call | flops 786432 | bytes 1572864 | tf_op jit(solution)/shard_map/pallas_call | solution.py:123
  88.9 18.0 %all_to_all.59 = f32[16,16,512]{2,1,0:T(8,128)S(1)} all-to-all(f32[16,16,512]{2,1,0:T(8,128)} %shard_map.61), channel_id=1, replica_groups=mesh['tm'=8,'state'=4] {'tm'}, dimensions={0} | all-to-all | bytes 1048576 | tf_op jit(solution)/shard_map/all_to_all | solution.py:133
  106.9 0.7 bitcast_convert_fusion
  108.0 1.3 copy.64
  109.3 2.7 %fusion.7 = f32[512,2,128]{0,2,1:T(8,128)S(1)} fusion(bf16[2,128,2048]{2,1,0:T(8,128)(2,1)} %all-gather.3.cloned.1.call-done, bf16[512,2048]{1,0:T(8,128)(2,1)} %l_ref.1, bf16[512,2,256]{0,2,1:T(8,128)(2,1)S(1)} %copy.62), kind=kOutput, calls=%fused_computation.5 | convolution fusion | flops 537133056 | bytes 3932160 | tf_op jit(solution)/shard_map/so,gyo->sgy/dot_general | solution.py:136
  112.0 11.7 %all-gather.5.cloned.1.call-done = bf16[2,128,2048]{2,1,0:T(8,128)(2,1)} async-done(((bf16[2,128,512]{2,1,0:T(8,128)(2,1)}), bf16[2,128,2048]{2,1,0:T(8,128)(2,1)}) %all-gather.5.cloned.1.call-update) | async-done | bytes 1048592 | tf_op jit(solution)/shard_map/all_gather | solution.py:135
  123.7 2.7 %fusion.13 = f32[512,2,128]{0,2,1:T(8,128)S(1)} fusion(bf16[2,128,2048]{2,1,0:T(8,128)(2,1)} %all-gather.5.cloned.1.call-done, bf16[512,2048]{1,0:T(8,128)(2,1)} %l_ref.1, bf16[512,2,256]{0,2,1:T(8,128)(2,1)S(1)} %copy.62), kind=kOutput, calls=%fused_computation.7 | convolution fusion | flops 537133056 | bytes 3932160 | tf_op jit(solution)/shard_map/so,gyo->sgy/dot_general | solution.py:136
  126.4 1.3 copy.65
  (33 shorter events, 1.7 us)
Async XLA Ops:
  11.8 24.5 %all-to-all-start = ((bf16[8,80,512]{2,1,0:T(8,128)(2,1)}), bf16[8,80,512]{2,1,0:T(8,128)(2,1)S(1)}, u32[]{:S(2)}, u32[]{:S(2)}) async-start(bf16[8,80,512]{2,1,0:T(8,128)(2,1)} %pad_maximum_fusion.2), calls=%async_computation | async-start | bytes 1310720 | tf_op jit(solution)/shard_map/all_to_all | solution.py:91
  36.4 0.8 copy-start.2
  42.1 4.8 %copy-start.1 = (f32[2,256,512]{2,1,0:T(8,128)S(1)}, f32[2,256,512]{2,1,0:T(8,128)}, u32[]{:S(2)}) copy-start(f32[2,256,512]{2,1,0:T(8,128)} %get-tuple-element.13) | copy-start | bytes 3145732
  42.1 4.8 %collective-permute-start = (f32[2,256,512]{2,1,0:T(8,128)}, f32[2,256,512]{2,1,0:T(8,128)S(1)}, u32[]{:S(2)}, u32[]{:S(2)}) collective-permute-start(f32[2,256,512]{2,1,0:T(8,128)} %get-tuple-element.14), channel_id=1, source_target_pairs={{0,1},{1,0},{2,3},{3,2},{4,5},{5,4},{6,7},{7,6},{8,9},{9,8},{10,11... | collective-permute-start | bytes 3145736 | tf_op jit(solution)/shard_map/ppermute | solution.py:36
  43.2 18.9 %all-to-all-start.1 = ((bf16[64,16,256]{2,0,1:T(8,128)(2,1)}), bf16[64,16,256]{2,0,1:T(8,128)(2,1)S(1)}, u32[]{:S(2)}, u32[]{:S(2)}) async-start(bf16[64,16,256]{2,0,1:T(8,128)(2,1)} %copy.58), calls=%async_computation.1 | async-start | bytes 1048576 | tf_op jit(solution)/shard_map/all_to_all | solution.py:98
  48.0 14.4 %collective-permute-start.1 = (f32[256,512]{1,0:T(8,128)}, f32[256,512]{1,0:T(8,128)S(1)}, u32[]{:S(2)}, u32[]{:S(2)}) collective-permute-start(f32[256,512]{1,0:T(8,128)} %get-tuple-element.30), channel_id=1, source_target_pairs={{0,2},{1,3},{2,0},{3,1},{4,6},{5,7},{6,4},{7,5},{8,10},{9,11},{10,... | collective-permute-start | bytes 1572872 | tf_op jit(solution)/shard_map/ppermute | solution.py:41
  49.6 21.5 %collective-permute-start.2 = (f32[2,256,512]{2,1,0:T(8,128)}, f32[2,256,512]{2,1,0:T(8,128)}, u32[]{:S(2)}, u32[]{:S(2)}) collective-permute-start(f32[2,256,512]{2,1,0:T(8,128)} %get-tuple-element.18), channel_id=1, source_target_pairs={{0,1},{1,0},{2,3},{3,2},{4,5},{5,4},{6,7},{7,6},{8,9},{9,8},{10,11... | collective-permute-start | bytes 3145736 | tf_op jit(solution)/shard_map/ppermute | solution.py:36
  50.5 20.6 %copy-start = (f32[2,256,512]{2,1,0:T(8,128)S(1)}, f32[2,256,512]{2,1,0:T(8,128)}, u32[]{:S(2)}) copy-start(f32[2,256,512]{2,1,0:T(8,128)} %get-tuple-element.17) | copy-start | bytes 3145732
  62.4 0.8 copy-start.3
  65.4 19.5 %all-to-all-start.2 = ((f32[16,16,512]{2,1,0:T(8,128)}), f32[16,16,512]{2,1,0:T(8,128)S(1)}, u32[]{:S(2)}, u32[]{:S(2)}) async-start(f32[16,16,512]{2,1,0:T(8,128)} %shard_map.60), calls=%async_computation.2 | async-start | bytes 1048576 | tf_op jit(solution)/shard_map/all_to_all | solution.py:133
  71.0 38.3 %all-gather.3.cloned.1.call-start = ((), (), s32[]{:S(2)}) async-start(), calls=%async_computation.4 | async-start | bytes 1310720 | tf_op jit(solution)/shard_map/all_gather | solution.py:135
  73.3 12.7 %collective-permute-start.3 = (f32[256,512]{1,0:T(8,128)S(1)}, f32[256,512]{1,0:T(8,128)S(1)}, u32[]{:S(2)}, u32[]{:S(2)}) collective-permute-start(f32[256,512]{1,0:T(8,128)S(1)} %get-tuple-element.32), channel_id=1, source_target_pairs={{0,2},{1,3},{2,0},{3,1},{4,6},{5,7},{6,4},{7,5},{8,10},{9,11},{10,... | collective-permute-start | bytes 1572872 | tf_op jit(solution)/shard_map/ppermute | solution.py:41
  85.7 38.0 %all-gather.5.cloned.1.call-start = ((), (), s32[]{:S(2)}) async-start(), calls=%async_computation.5 | async-start | bytes 1310720 | tf_op jit(solution)/shard_map/all_gather | solution.py:135
  86.0 0.8 copy-start.4
Sparse Core Ops, SparseCore 0:
  85.8 15.7 all-gather.2
  107.8 15.7 all-gather.4

commit v11 on v10

--- a/solution.py
+++ b/solution.py
@@ -42,6 +42,21 @@
         keep = keep[1] + received[1]
         received = arriving
     return keep, received
+
+
+def doubling_gather(block, axis):
+    count = lax.axis_size(axis)
+    me = lax.axis_index(axis)
+    levels = count.bit_length() - 1
+    held = block[None]
+    for level in reversed(range(levels)):
+        pairs = [(i, i ^ (1 << level)) for i in range(count)]
+        held = jnp.concatenate([held, lax.ppermute(held, axis, pairs)], axis=0)
+    order = jnp.arange(count) ^ me
+    flipped = jnp.zeros_like(order)
+    for level in range(levels):
+        flipped = flipped | (((order >> level) & 1) << (levels - 1 - level))
+    return jnp.take(held, flipped, axis=0)
 
 
 def recurrence_kernel(rate_ref, keep_ref, received_ref, out_ref):
@@ -132,7 +147,13 @@
         )(decay_all, kept, received)
         gathered = lax.all_to_all(smoothed_here, "tm", split_axis=0, concat_axis=1, tiled=True)
         rounded = gathered.astype(jnp.bfloat16)
-        full = lax.all_gather(rounded, "state", axis=2, tiled=True)
+        if chunk == CHUNKS - 1:
+            every = doubling_gather(rounded, "state")
+            full = jnp.transpose(every, (1, 2, 0, 3)).reshape(
+                rounded.shape[:2] + (every.shape[0] * rounded.shape[2],)
+            )
+        else:
+            full = lax.all_gather(rounded, "state", axis=2, tiled=True)
         fitted = jnp.einsum("so,gyo->sgy", loadings, full, preferred_element_type=jnp.float32)
         low = chunk * members // CHUNKS
         picked = by_hour[:, :, low:low + members // CHUNKS]

time: 135 us -> 135 us (level)
  blocking collectives: 18 us -> 0 us
  starting transfers between devices: 19.7 us -> 27.4 us
  waiting for transfers between devices: 50.5 us -> 57.9 us
  other arithmetic: 8.21 us -> 9.66 us
    all_to_all x1 -> x0, blocking collectives: 18 us -> none  [local(): lax.all_to_all(smoothed_here, 'tm', split_axis=0, concat_axis=1, tiled=True)]
    ppermute x2, waiting for transfers between devices: 0.6 us -> 11 us  [halving_reduce(): arriving = lax.ppermute(outgoing, axis, pairs)]
    all_gather x2 -> x1, waiting for transfers between devices: 11.7 us -> 2.88 us  [local(): full = lax.all_gather(rounded, 'state', axis=2, tiled=True)]
    all_to_all x1 -> x2, starting transfers between devices: 5.64 us -> 11.4 us  [local(): lax.all_to_all(smoothed_here, 'tm', split_axis=0, concat_axis=1, tiled=True)]
    ppermute x0 -> x2, waiting for transfers between devices: none -> 4.67 us  [doubling_gather(): held = jnp.concatenate([held, lax.ppermute(held, axis, pairs)], axis=0)]
    concatenate x0 -> x2, other arithmetic: none -> 1.99 us  [doubling_gather(): held = jnp.concatenate([held, lax.ppermute(held, axis, pairs)], axis=0)]
    all_to_all x1 -> x2, waiting for transfers between devices: 10.1 us -> 11.7 us  [local(): lax.all_to_all(smoothed_here, 'tm', split_axis=0, concat_axis=1, tiled=True)]
    ppermute x0 -> x2, starting transfers between devices: none -> 1.59 us  [doubling_gather(): held = jnp.concatenate([held, lax.ppermute(held, axis, pairs)], axis=0)]
  transfers between devices with their start and end apart: 9 -> 11, of which waited for: 6 -> 8; matrix products, arithmetic and copies ran while one was open for 9% -> 11% of each run, Pallas kernels for 3% -> 3%
where the time goes in v11:
time: 135 us; the launch traced here: 134 us
  waiting for transfers between devices  57.9 us (43%)
  starting transfers between devices  27.4 us (20%)
  between operations  14.3 us (11%)
  local copies, waits for them, and re-layouts  10.8 us (8%)
  other arithmetic  9.66 us (7%)
  Pallas kernels  9.1 us (7%)
  matrix products  5.02 us (4%)
    all_to_all x1, waiting for transfers between devices, local(): lax.all_to_all(outgoing, 'tm', split_axis=0, concat_axis=0, tiled=True)  17.3 us
    all_to_all x2, waiting for transfers between devices, local(): lax.all_to_all(smoothed_here, 'tm', split_axis=0, concat_axis=1, tiled=True)  11.7 us
    all_to_all x2, starting transfers between devices, local(): lax.all_to_all(smoothed_here, 'tm', split_axis=0, concat_axis=1, tiled=True)  11.4 us
    ppermute x2, waiting for transfers between devices, halving_reduce(): arriving = lax.ppermute(outgoing, axis, pairs)  11 us
    all_to_all x1, waiting for transfers between devices, local(): lax.all_to_all(masked_later, 'tm', split_axis=1, concat_axis=0, tiled=True)  10.4 us
    all_to_all x1, starting transfers between devices, local(): lax.all_to_all(outgoing, 'tm', split_axis=0, concat_axis=0, tiled=True)  7.25 us
    unnamed x13, local copies, waits for them, and re-layouts  6.73 us
    dot_general x2, matrix products, local(): jnp.einsum('so,gyo->sgy', loadings, full, preferred_element_type=jnp.floa...  5.02 us
  transfers between devices with their start and end apart: 11, of which 8 were waited for; matrix products, arithmetic and copies ran while one was open for 11% of the time, Pallas kernels for 3%

profile of v11, /device:TPU:0, one launch (start us, length us, event | category | flops | bytes accessed | tf_op | source)
XLA Modules:
  0.0 134.1 jit_solution(10049959190797682901)
XLA Ops:
  8.6 1.7 %copy.71 = bf16[64,16,256]{0,2,1:T(8,128)(2,1)S(1)} copy(bf16[64,16,256]{2,1,0:T(8,128)(2,1)} %param.4) | data formatting | bytes 1048576 | tf_op args[0]
  10.9 0.9 pad_maximum_fusion.3
  11.8 7.3 %all-to-all-start = ((bf16[8,80,512]{2,1,0:T(8,128)(2,1)}), bf16[8,80,512]{2,1,0:T(8,128)(2,1)S(1)}, u32[]{:S(2)}, u32[]{:S(2)}) async-start(bf16[8,80,512]{2,1,0:T(8,128)(2,1)} %pad_maximum_fusion.3), calls=%async_computation | async-start | bytes 1310720 | tf_op jit(solution)/shard_map/all_to_all | solution.py:106
  19.1 17.3 %all-to-all-done.x_ref = bf16[8,80,512]{2,1,0:T(8,128)(2,1)S(1)} async-done(((bf16[8,80,512]{2,1,0:T(8,128)(2,1)}), bf16[8,80,512]{2,1,0:T(8,128)(2,1)S(1)}, u32[]{:S(2)}, u32[]{:S(2)}) %all-to-all-start) | async-done | bytes 655392 | tf_op jit(solution)/shard_map/all_to_all | solution.py:106
  36.4 0.8 copy-done.2
  37.2 4.8 %shard_map.59 = (f32[2,256,512]{2,1,0:T(8,128)}, f32[2,256,512]{2,1,0:T(8,128)}, f32[2,256,512]{2,1,0:T(8,128)}, f32[2,256,512]{2,1,0:T(8,128)}) custom-call(s32[1]{0:T(128)} %bitcast.10.me_ref, bf16[8,80,512]{2,1,0:T(8,128)(2,1)} %copy-done.2, bf16[512,2048]{1,0:T(8,128)(2,1)} %l_ref.1), custom_call_target="tpu_custom_call" | custom-call | flops 1073741824 | bytes 6815744 | tf_op jit(solution)/shard_map/pallas_call | solution.py:118
  42.6 1.1 copy.76
  43.7 3.6 %all-to-all-start.1 = ((bf16[64,16,256]{2,0,1:T(8,128)(2,1)}), bf16[64,16,256]{2,0,1:T(8,128)(2,1)S(1)}, u32[]{:S(2)}, u32[]{:S(2)}) async-start(bf16[64,16,256]{2,0,1:T(8,128)(2,1)} %copy.76), calls=%async_computation.1 | async-start | bytes 1048576 | tf_op jit(solution)/shard_map/all_to_all | solution.py:113
  47.3 1.2 fusion.17
  48.5 1.5 %collective-permute-start.1 = (f32[256,512]{1,0:T(8,128)}, f32[256,512]{1,0:T(8,128)S(1)}, u32[]{:S(2)}, u32[]{:S(2)}) collective-permute-start(f32[256,512]{1,0:T(8,128)} %get-tuple-element.32), channel_id=1, source_target_pairs={{0,2},{1,3},{2,0},{3,1},{4,6},{5,7},{6,4},{7,5},{8,10},{9,11},{10,... | collective-permute-start | bytes 1572872 | tf_op jit(solution)/shard_map/ppermute | solution.py:41
  50.0 0.8 slice_convert_fusion
  51.6 10.4 %all-to-all-done.1 = bf16[64,16,256]{2,0,1:T(8,128)(2,1)S(1)} async-done(((bf16[64,16,256]{2,0,1:T(8,128)(2,1)}), bf16[64,16,256]{2,0,1:T(8,128)(2,1)S(1)}, u32[]{:S(2)}, u32[]{:S(2)}) %all-to-all-start.1) | async-done | bytes 524320 | tf_op jit(solution)/shard_map/all_to_all | solution.py:113
  62.4 0.8 copy-done.3
  63.2 2.1 %shard_map.60 = f32[16,16,512]{2,1,0:T(8,128)} custom-call(f32[16,512]{1,0:T(8,128)} %add.56.rate_ref, f32[16,16,512]{2,1,0:T(8,128)} %bitcast.83, f32[16,16,512]{2,1,0:T(8,128)} %bitcast.87), custom_call_target="tpu_custom_call" | custom-call | flops 786432 | bytes 1572864 | tf_op jit(solution)/shard_map/pallas_call | solution.py:138
  65.4 5.6 %all-to-all-start.2 = ((f32[16,16,512]{2,1,0:T(8,128)}), f32[16,16,512]{2,1,0:T(8,128)S(1)}, u32[]{:S(2)}, u32[]{:S(2)}) async-start(f32[16,16,512]{2,1,0:T(8,128)} %shard_map.60), calls=%async_computation.2 | async-start | bytes 1048576 | tf_op jit(solution)/shard_map/all_to_all | solution.py:148
  71.0 2.2 %fusion.16 = (f32[256,512]{1,0:T(8,128)S(1)}, f32[1,256,512]{2,1,0:T(8,128)}) fusion(f32[2,256,512]{2,1,0:T(8,128)} %collective-permute-done.2, f32[2,256,512]{2,1,0:T(8,128)S(1)} %copy-done), kind=kLoop, calls=%fused_computation.15 | loop fusion | flops 262144 | bytes 3145728 | tf_op jit(solution)/shard_map/add | solution.py:39
  73.2 1.5 %collective-permute-start.3 = (f32[256,512]{1,0:T(8,128)S(1)}, f32[256,512]{1,0:T(8,128)S(1)}, u32[]{:S(2)}, u32[]{:S(2)}) collective-permute-start(f32[256,512]{1,0:T(8,128)S(1)} %get-tuple-element.34), channel_id=1, source_target_pairs={{0,2},{1,3},{2,0},{3,1},{4,6},{5,7},{6,4},{7,5},{8,10},{9,11},{10,... | collective-permute-start | bytes 1572872 | tf_op jit(solution)/shard_map/ppermute | solution.py:41
  74.7 10.6 %collective-permute-done.3 = f32[256,512]{1,0:T(8,128)S(1)} collective-permute-done((f32[256,512]{1,0:T(8,128)S(1)}, f32[256,512]{1,0:T(8,128)S(1)}, u32[]{:S(2)}, u32[]{:S(2)}) %collective-permute-start.3) | collective-permute-done | bytes 524320 | tf_op jit(solution)/shard_map/ppermute | solution.py:41
  85.4 0.8 copy-done.4
  86.2 2.1 %shard_map.61 = f32[16,16,512]{2,1,0:T(8,128)} custom-call(f32[16,512]{1,0:T(8,128)} %add.56.rate_ref, f32[16,16,512]{2,1,0:T(8,128)} %bitcast.84, f32[16,16,512]{2,1,0:T(8,128)} %bitcast.88), custom_call_target="tpu_custom_call" | custom-call | flops 786432 | bytes 1572864 | tf_op jit(solution)/shard_map/pallas_call | solution.py:138
  88.3 5.7 %all-to-all-start.3 = ((f32[16,16,512]{2,1,0:T(8,128)}), f32[16,16,512]{2,1,0:T(8,128)S(1)}, u32[]{:S(2)}, u32[]{:S(2)}) async-start(f32[16,16,512]{2,1,0:T(8,128)} %shard_map.61), calls=%async_computation.3 | async-start | bytes 1048576 | tf_op jit(solution)/shard_map/all_to_all | solution.py:148
  94.1 11.7 %all-to-all-done.3 = f32[16,16,512]{2,1,0:T(8,128)S(1)} async-done(((f32[16,16,512]{2,1,0:T(8,128)}), f32[16,16,512]{2,1,0:T(8,128)S(1)}, u32[]{:S(2)}, u32[]{:S(2)}) %all-to-all-start.3) | async-done | bytes 524320 | tf_op jit(solution)/shard_map/all_to_all | solution.py:148
  105.8 1.6 %collective-permute-start.4 = (bf16[1,2,128,512]{3,2,1,0:T(8,128)(2,1)S(1)}, bf16[1,2,128,512]{3,2,1,0:T(8,128)(2,1)S(1)}, u32[]{:S(2)}, u32[]{:S(2)}) collective-permute-start(bf16[1,2,128,512]{3,2,1,0:T(8,128)(2,1)S(1)} %bitcast.77), channel_id=1, source_target_pairs={{0,2},{1,3},{2,0},{3,1},{4,6},{5,7},{6,4},{7,5},{8,10},{9,11},{10,... | collective-permute-start | bytes 786440 | tf_op jit(solution)/shard_map/ppermute | solution.py:54
  107.4 0.7 bitcast_convert_fusion.1
  108.2 4.1 %collective-permute-done.4 = bf16[1,2,128,512]{3,2,1,0:T(8,128)(2,1)S(1)} collective-permute-done((bf16[1,2,128,512]{3,2,1,0:T(8,128)(2,1)S(1)}, bf16[1,2,128,512]{3,2,1,0:T(8,128)(2,1)S(1)}, u32[]{:S(2)}, u32[]{:S(2)}) %collective-permute-start.4) | collective-permute-done | bytes 262176 | tf_op jit(solution)/shard_map/ppermute | solution.py:54
  112.3 0.8 pad_maximum_fusion.4
  113.5 1.3 copy.84
  115.4 1.1 pad_maximum_fusion.1
  118.0 2.4 %fusion.13 = f32[512,2,128]{0,2,1:T(8,128)S(1)} fusion(bf16[2,128,2048]{1,2,0:T(8,128)(2,1)S(1)} %bitcast.86, bf16[512,2048]{1,0:T(8,128)(2,1)} %l_ref.1, bf16[512,2,256]{0,2,1:T(8,128)(2,1)S(1)} %copy.80), kind=kOutput, calls=%fused_computation.8 | convolution fusion | flops 537133056 | bytes 3932160 | tf_op jit(solution)/shard_map/so,gyo->sgy/dot_general | solution.py:157
  120.4 2.9 %all-gather.2.cloned.1.call-done = bf16[2,128,2048]{2,1,0:T(8,128)(2,1)} async-done(((bf16[2,128,512]{2,1,0:T(8,128)(2,1)}), bf16[2,128,2048]{2,1,0:T(8,128)(2,1)}) %all-gather.2.cloned.1.call-update) | async-done | bytes 1048592 | tf_op jit(solution)/shard_map/all_gather | solution.py:156
  123.2 2.7 %fusion.7 = f32[512,2,128]{0,2,1:T(8,128)S(1)} fusion(bf16[2,128,2048]{2,1,0:T(8,128)(2,1)} %all-gather.2.cloned.1.call-done, bf16[512,2048]{1,0:T(8,128)(2,1)} %l_ref.1, bf16[512,2,256]{0,2,1:T(8,128)(2,1)S(1)} %copy.80), kind=kOutput, calls=%fused_computation.6 | convolution fusion | flops 537133056 | bytes 3932160 | tf_op jit(solution)/shard_map/so,gyo->sgy/dot_general | solution.py:157
  126.0 1.3 copy.85
  (43 shorter events, 6.2 us)
Async XLA Ops:
  11.8 24.5 %all-to-all-start = ((bf16[8,80,512]{2,1,0:T(8,128)(2,1)}), bf16[8,80,512]{2,1,0:T(8,128)(2,1)S(1)}, u32[]{:S(2)}, u32[]{:S(2)}) async-start(bf16[8,80,512]{2,1,0:T(8,128)(2,1)} %pad_maximum_fusion.3), calls=%async_computation | async-start | bytes 1310720 | tf_op jit(solution)/shard_map/all_to_all | solution.py:106
  36.4 0.8 copy-start.2
  42.0 5.3 %copy-start.1 = (f32[2,256,512]{2,1,0:T(8,128)S(1)}, f32[2,256,512]{2,1,0:T(8,128)}, u32[]{:S(2)}) copy-start(f32[2,256,512]{2,1,0:T(8,128)} %get-tuple-element.13) | copy-start | bytes 3145732
  42.0 5.3 %collective-permute-start = (f32[2,256,512]{2,1,0:T(8,128)}, f32[2,256,512]{2,1,0:T(8,128)S(1)}, u32[]{:S(2)}, u32[]{:S(2)}) collective-permute-start(f32[2,256,512]{2,1,0:T(8,128)} %get-tuple-element.14), channel_id=1, source_target_pairs={{0,1},{1,0},{2,3},{3,2},{4,5},{5,4},{6,7},{7,6},{8,9},{9,8},{10,11... | collective-permute-start | bytes 3145736 | tf_op jit(solution)/shard_map/ppermute | solution.py:36
  42.1 28.9 %collective-permute-start.2 = (f32[2,256,512]{2,1,0:T(8,128)}, f32[2,256,512]{2,1,0:T(8,128)}, u32[]{:S(2)}, u32[]{:S(2)}) collective-permute-start(f32[2,256,512]{2,1,0:T(8,128)} %get-tuple-element.18), channel_id=1, source_target_pairs={{0,1},{1,0},{2,3},{3,2},{4,5},{5,4},{6,7},{7,6},{8,9},{9,8},{10,11... | collective-permute-start | bytes 3145736 | tf_op jit(solution)/shard_map/ppermute | solution.py:36
  43.7 18.4 %all-to-all-start.1 = ((bf16[64,16,256]{2,0,1:T(8,128)(2,1)}), bf16[64,16,256]{2,0,1:T(8,128)(2,1)S(1)}, u32[]{:S(2)}, u32[]{:S(2)}) async-start(bf16[64,16,256]{2,0,1:T(8,128)(2,1)} %copy.76), calls=%async_computation.1 | async-start | bytes 1048576 | tf_op jit(solution)/shard_map/all_to_all | solution.py:113
  48.5 13.9 %collective-permute-start.1 = (f32[256,512]{1,0:T(8,128)}, f32[256,512]{1,0:T(8,128)S(1)}, u32[]{:S(2)}, u32[]{:S(2)}) collective-permute-start(f32[256,512]{1,0:T(8,128)} %get-tuple-element.32), channel_id=1, source_target_pairs={{0,2},{1,3},{2,0},{3,1},{4,6},{5,7},{6,4},{7,5},{8,10},{9,11},{10,... | collective-permute-start | bytes 1572872 | tf_op jit(solution)/shard_map/ppermute | solution.py:41
  50.9 20.1 %copy-start = (f32[2,256,512]{2,1,0:T(8,128)S(1)}, f32[2,256,512]{2,1,0:T(8,128)}, u32[]{:S(2)}) copy-start(f32[2,256,512]{2,1,0:T(8,128)} %get-tuple-element.17) | copy-start | bytes 3145732
  62.4 0.8 copy-start.3
  65.4 23.0 %all-to-all-start.2 = ((f32[16,16,512]{2,1,0:T(8,128)}), f32[16,16,512]{2,1,0:T(8,128)S(1)}, u32[]{:S(2)}, u32[]{:S(2)}) async-start(f32[16,16,512]{2,1,0:T(8,128)} %shard_map.60), calls=%async_computation.2 | async-start | bytes 1048576 | tf_op jit(solution)/shard_map/all_to_all | solution.py:148
  73.2 12.2 %collective-permute-start.3 = (f32[256,512]{1,0:T(8,128)S(1)}, f32[256,512]{1,0:T(8,128)S(1)}, u32[]{:S(2)}, u32[]{:S(2)}) collective-permute-start(f32[256,512]{1,0:T(8,128)S(1)} %get-tuple-element.34), channel_id=1, source_target_pairs={{0,2},{1,3},{2,0},{3,1},{4,6},{5,7},{6,4},{7,5},{8,10},{9,11},{10,... | collective-permute-start | bytes 1572872 | tf_op jit(solution)/shard_map/ppermute | solution.py:41
  85.4 0.8 copy-start.4
  88.3 17.5 %all-to-all-start.3 = ((f32[16,16,512]{2,1,0:T(8,128)}), f32[16,16,512]{2,1,0:T(8,128)S(1)}, u32[]{:S(2)}, u32[]{:S(2)}) async-start(f32[16,16,512]{2,1,0:T(8,128)} %shard_map.61), calls=%async_computation.3 | async-start | bytes 1048576 | tf_op jit(solution)/shard_map/all_to_all | solution.py:148
  94.0 29.2 %all-gather.2.cloned.1.call-start = ((), (), s32[]{:S(2)}) async-start(), calls=%async_computation.4 | async-start | bytes 1310720 | tf_op jit(solution)/shard_map/all_gather | solution.py:156
  105.8 6.4 %collective-permute-start.4 = (bf16[1,2,128,512]{3,2,1,0:T(8,128)(2,1)S(1)}, bf16[1,2,128,512]{3,2,1,0:T(8,128)(2,1)S(1)}, u32[]{:S(2)}, u32[]{:S(2)}) collective-permute-start(bf16[1,2,128,512]{3,2,1,0:T(8,128)(2,1)S(1)} %bitcast.77), channel_id=1, source_target_pairs={{0,2},{1,3},{2,0},{3,1},{4,6},{5,7},{6,4},{7,5},{8,10},{9,11},{10,... | collective-permute-start | bytes 786440 | tf_op jit(solution)/shard_map/ppermute | solution.py:54
  113.1 2.3 %collective-permute-start.5 = (bf16[2,2,128,512]{3,2,1,0:T(8,128)(2,1)}, bf16[2,2,128,512]{3,2,1,0:T(8,128)(2,1)}, u32[]{:S(2)}, u32[]{:S(2)}) collective-permute-start(bf16[2,2,128,512]{3,2,1,0:T(8,128)(2,1)} %pad_maximum_fusion.4), channel_id=1, source_target_pairs={{0,1},{1,0},{2,3},{3,2},{4,5},{5,4},{6,7},{7,6},{8,9},{9,8},{10,11... | collective-permute-start | bytes 1572872 | tf_op jit(solution)/shard_map/ppermute | solution.py:54
Sparse Core Ops, SparseCore 0:
  108.3 14.8 all-gather.1

commit v12 on v11

--- a/solution.py
+++ b/solution.py
@@ -30,18 +30,17 @@
             target[relative[1:]] = total[:, chunk].reshape(rows, width)
 
 
-def halving_reduce(outgoing, keep, axis):
+def halving_stages(outgoing, keep, axis):
     count = lax.axis_size(axis)
     level = 0
-    received = lax.ppermute(outgoing, axis, [(i, i ^ 1) for i in range(count)])
+    pairs = [(i, i ^ 1) for i in range(count)]
     while keep.ndim > 2:
+        received = lax.ppermute(outgoing, axis, pairs)
         level += 1
         outgoing = keep[0] + received[0]
+        keep = keep[1] + received[1]
         pairs = [(i, i ^ (1 << level)) for i in range(count)]
-        arriving = lax.ppermute(outgoing, axis, pairs)
-        keep = keep[1] + received[1]
-        received = arriving
-    return keep, received
+    return keep, outgoing, pairs
 
 
 def doubling_gather(block, axis):
@@ -129,10 +128,16 @@
     )(lax.axis_index("state").reshape(1).astype(jnp.int32), by_member, loadings)
     smoothed_parts = []
     residual_parts = []
+    last = [halving_stages(halves[2 * c], halves[2 * c + 1], "state") for c in range(CHUNKS)]
+    kept, outgoing, pairs = last[0]
+    received = lax.ppermute(outgoing, "state", pairs)
+    later = [(k, o) for k, o, _ in last[1:]]
+    by_hour, kept, received, later = lax.optimization_barrier((by_hour, kept, received, later))
+    addends = [(kept, received)] + [
+        (k, lax.ppermute(o, "state", last[c + 1][2])) for c, (k, o) in enumerate(later)
+    ]
     for chunk in range(CHUNKS):
-        kept, received = halving_reduce(halves[2 * chunk], halves[2 * chunk + 1], "state")
-        if chunk == 0:
-            by_hour, kept, received = lax.optimization_barrier((by_hour, kept, received))
+        kept, received = addends[chunk]
         kept = kept.reshape(hours, chunk_members, comps)
         received = received.reshape(hours, chunk_members, comps)
         smoothed_here = vmem_call(

time: 135 us -> 134 us (level)
  waiting for transfers between devices: 57.9 us -> 55.3 us
    unnamed x13 -> x15, local copies, waits for them, and re-layouts: 6.73 us -> 6.95 us
  transfers between devices with their start and end apart: 11 -> 11, of which waited for: 8 -> 6; matrix products, arithmetic and copies ran while one was open for 11% -> 12% of each run, Pallas kernels for 3% -> 2%
where the time goes in v12:
time: 134 us; the launch traced here: 133 us
  waiting for transfers between devices  55.3 us (41%)
  starting transfers between devices  26.9 us (20%)
  between operations  14.3 us (11%)
  local copies, waits for them, and re-layouts  11.8 us (9%)
  other arithmetic  11 us (8%)
  Pallas kernels  9.11 us (7%)
  matrix products  5.02 us (4%)
    all_to_all x1, waiting for transfers between devices, local(): lax.all_to_all(outgoing, 'tm', split_axis=0, concat_axis=0, tiled=True)  17.3 us
    all_to_all x2, waiting for transfers between devices, local(): lax.all_to_all(smoothed_here, 'tm', split_axis=0, concat_axis=1, tiled=True)  11.7 us
    all_to_all x2, starting transfers between devices, local(): lax.all_to_all(smoothed_here, 'tm', split_axis=0, concat_axis=1, tiled=True)  10.8 us
    ppermute x1, waiting for transfers between devices, local(): lax.ppermute(o, 'state', last[c + 1][2])  10.6 us
    all_to_all x1, waiting for transfers between devices, local(): lax.all_to_all(masked_later, 'tm', split_axis=1, concat_axis=0, tiled=True)  9.08 us
    all_to_all x1, starting transfers between devices, local(): lax.all_to_all(outgoing, 'tm', split_axis=0, concat_axis=0, tiled=True)  7.25 us
    unnamed x15, local copies, waits for them, and re-layouts  6.95 us
    dot_general x2, matrix products, local(): jnp.einsum('so,gyo->sgy', loadings, full, preferred_element_type=jnp.floa...  5.02 us
  transfers between devices with their start and end apart: 11, of which 6 were waited for; matrix products, arithmetic and copies ran while one was open for 12% of the time, Pallas kernels for 2%

profile of v12, /device:TPU:0, one launch (start us, length us, event | category | flops | bytes accessed | tf_op | source)
XLA Modules:
  0.0 133.3 jit_solution(4604188457666545916)
XLA Ops:
  7.9 1.7 %copy.71 = bf16[64,16,256]{0,2,1:T(8,128)(2,1)S(1)} copy(bf16[64,16,256]{2,1,0:T(8,128)(2,1)} %param.4) | data formatting | bytes 1048576 | tf_op args[0]
  10.9 0.9 pad_maximum_fusion.3
  11.8 7.3 %all-to-all-start = ((bf16[8,80,512]{2,1,0:T(8,128)(2,1)}), bf16[8,80,512]{2,1,0:T(8,128)(2,1)S(1)}, u32[]{:S(2)}, u32[]{:S(2)}) async-start(bf16[8,80,512]{2,1,0:T(8,128)(2,1)} %pad_maximum_fusion.3), calls=%async_computation | async-start | bytes 1310720 | tf_op jit(solution)/shard_map/all_to_all | solution.py:105
  19.1 17.3 %all-to-all-done.x_ref = bf16[8,80,512]{2,1,0:T(8,128)(2,1)S(1)} async-done(((bf16[8,80,512]{2,1,0:T(8,128)(2,1)}), bf16[8,80,512]{2,1,0:T(8,128)(2,1)S(1)}, u32[]{:S(2)}, u32[]{:S(2)}) %all-to-all-start) | async-done | bytes 655392 | tf_op jit(solution)/shard_map/all_to_all | solution.py:105
  36.4 0.9 copy-done.2
  37.3 4.8 %shard_map.59 = (f32[2,256,512]{2,1,0:T(8,128)}, f32[2,256,512]{2,1,0:T(8,128)}, f32[2,256,512]{2,1,0:T(8,128)}, f32[2,256,512]{2,1,0:T(8,128)}) custom-call(s32[1]{0:T(128)} %bitcast.10.me_ref, bf16[8,80,512]{2,1,0:T(8,128)(2,1)} %copy-done.2, bf16[512,2048]{1,0:T(8,128)(2,1)} %l_ref.1), custom_call_target="tpu_custom_call" | custom-call | flops 1073741824 | bytes 6815744 | tf_op jit(solution)/shard_map/pallas_call | solution.py:117
  42.6 1.1 copy.76
  43.7 3.6 %all-to-all-start.1 = ((bf16[64,16,256]{2,0,1:T(8,128)(2,1)}), bf16[64,16,256]{2,0,1:T(8,128)(2,1)S(1)}, u32[]{:S(2)}, u32[]{:S(2)}) async-start(bf16[64,16,256]{2,0,1:T(8,128)(2,1)} %copy.76), calls=%async_computation.1 | async-start | bytes 1048576 | tf_op jit(solution)/shard_map/all_to_all | solution.py:112
  47.4 2.5 %fusion.18 = (f32[256,512]{1,0:T(8,128)}, f32[256,512]{1,0:T(8,128)}) fusion(f32[2,256,512]{2,1,0:T(8,128)} %collective-permute-done, f32[2,256,512]{2,1,0:T(8,128)S(1)} %copy-done.1), kind=kLoop, calls=%fused_computation.19 | loop fusion | flops 262144 | bytes 3145728 | tf_op jit(solution)/shard_map/add | solution.py:40
  49.9 1.5 %collective-permute-start.1 = (f32[256,512]{1,0:T(8,128)}, f32[256,512]{1,0:T(8,128)S(1)}, u32[]{:S(2)}, u32[]{:S(2)}) collective-permute-start(f32[256,512]{1,0:T(8,128)} %get-tuple-element.38), channel_id=1, source_target_pairs={{0,2},{1,3},{2,0},{3,1},{4,6},{5,7},{6,4},{7,5},{8,10},{9,11},{10,... | collective-permute-start | bytes 1572872 | tf_op jit(solution)/shard_map/ppermute | solution.py:133
  51.4 0.8 slice_convert_fusion
  53.0 9.1 %all-to-all-done.1 = bf16[64,16,256]{2,0,1:T(8,128)(2,1)S(1)} async-done(((bf16[64,16,256]{2,0,1:T(8,128)(2,1)}), bf16[64,16,256]{2,0,1:T(8,128)(2,1)S(1)}, u32[]{:S(2)}, u32[]{:S(2)}) %all-to-all-start.1) | async-done | bytes 524320 | tf_op jit(solution)/shard_map/all_to_all | solution.py:112
  62.1 2.2 %fusion.16 = (f32[256,512]{1,0:T(8,128)S(1)}, f32[256,512]{1,0:T(8,128)}) fusion(f32[2,256,512]{2,1,0:T(8,128)} %collective-permute-done.2, f32[2,256,512]{2,1,0:T(8,128)S(1)} %copy-done), kind=kLoop, calls=%fused_computation.15 | loop fusion | flops 262144 | bytes 3145728 | tf_op jit(solution)/shard_map/add | solution.py:40
  64.3 0.8 copy-done.3
  65.1 2.1 %shard_map.60 = f32[16,16,512]{2,1,0:T(8,128)} custom-call(f32[16,512]{1,0:T(8,128)} %add.55.rate_ref, f32[16,16,512]{2,1,0:T(8,128)} %bitcast.83, f32[16,16,512]{2,1,0:T(8,128)} %bitcast.89), custom_call_target="tpu_custom_call" | custom-call | flops 786432 | bytes 1572864 | tf_op jit(solution)/shard_map/pallas_call | solution.py:143
  67.3 5.1 %all-to-all-start.2 = ((f32[16,16,512]{2,1,0:T(8,128)}), f32[16,16,512]{2,1,0:T(8,128)S(1)}, u32[]{:S(2)}, u32[]{:S(2)}) async-start(f32[16,16,512]{2,1,0:T(8,128)} %shard_map.60), calls=%async_computation.2 | async-start | bytes 1048576 | tf_op jit(solution)/shard_map/all_to_all | solution.py:153
  72.4 1.5 %collective-permute-start.3 = (f32[256,512]{1,0:T(8,128)S(1)}, f32[256,512]{1,0:T(8,128)S(1)}, u32[]{:S(2)}, u32[]{:S(2)}) collective-permute-start(f32[256,512]{1,0:T(8,128)S(1)} %get-tuple-element.22), channel_id=1, source_target_pairs={{0,2},{1,3},{2,0},{3,1},{4,6},{5,7},{6,4},{7,5},{8,10},{9,11},{10,... | collective-permute-start | bytes 1572872 | tf_op jit(solution)/shard_map/ppermute | solution.py:137
  73.9 10.6 %collective-permute-done.3 = f32[256,512]{1,0:T(8,128)S(1)} collective-permute-done((f32[256,512]{1,0:T(8,128)S(1)}, f32[256,512]{1,0:T(8,128)S(1)}, u32[]{:S(2)}, u32[]{:S(2)}) %collective-permute-start.3) | collective-permute-done | bytes 524320 | tf_op jit(solution)/shard_map/ppermute | solution.py:137
  84.5 0.8 copy-done.4
  85.3 2.1 %shard_map.61 = f32[16,16,512]{2,1,0:T(8,128)} custom-call(f32[16,512]{1,0:T(8,128)} %add.55.rate_ref, f32[16,16,512]{2,1,0:T(8,128)} %bitcast.86, f32[16,16,512]{2,1,0:T(8,128)} %bitcast.90), custom_call_target="tpu_custom_call" | custom-call | flops 786432 | bytes 1572864 | tf_op jit(solution)/shard_map/pallas_call | solution.py:143
  87.5 5.7 %all-to-all-start.3 = ((f32[16,16,512]{2,1,0:T(8,128)}), f32[16,16,512]{2,1,0:T(8,128)S(1)}, u32[]{:S(2)}, u32[]{:S(2)}) async-start(f32[16,16,512]{2,1,0:T(8,128)} %shard_map.61), calls=%async_computation.3 | async-start | bytes 1048576 | tf_op jit(solution)/shard_map/all_to_all | solution.py:153
  93.3 11.7 %all-to-all-done.3 = f32[16,16,512]{2,1,0:T(8,128)S(1)} async-done(((f32[16,16,512]{2,1,0:T(8,128)}), f32[16,16,512]{2,1,0:T(8,128)S(1)}, u32[]{:S(2)}, u32[]{:S(2)}) %all-to-all-start.3) | async-done | bytes 524320 | tf_op jit(solution)/shard_map/all_to_all | solution.py:153
  105.0 1.6 %collective-permute-start.4 = (bf16[1,2,128,512]{3,2,1,0:T(8,128)(2,1)S(1)}, bf16[1,2,128,512]{3,2,1,0:T(8,128)(2,1)S(1)}, u32[]{:S(2)}, u32[]{:S(2)}) collective-permute-start(bf16[1,2,128,512]{3,2,1,0:T(8,128)(2,1)S(1)} %bitcast.79), channel_id=1, source_target_pairs={{0,2},{1,3},{2,0},{3,1},{4,6},{5,7},{6,4},{7,5},{8,10},{9,11},{10,... | collective-permute-start | bytes 786440 | tf_op jit(solution)/shard_map/ppermute | solution.py:53
  107.3 4.1 %collective-permute-done.4 = bf16[1,2,128,512]{3,2,1,0:T(8,128)(2,1)S(1)} collective-permute-done((bf16[1,2,128,512]{3,2,1,0:T(8,128)(2,1)S(1)}, bf16[1,2,128,512]{3,2,1,0:T(8,128)(2,1)S(1)}, u32[]{:S(2)}, u32[]{:S(2)}) %collective-permute-start.4) | collective-permute-done | bytes 262176 | tf_op jit(solution)/shard_map/ppermute | solution.py:53
  111.4 0.8 pad_maximum_fusion.4
  112.3 1.0 copy.80
  113.4 1.3 copy.84
  114.7 1.1 pad_maximum_fusion.1
  117.6 2.4 %fusion.13 = f32[512,2,128]{0,2,1:T(8,128)S(1)} fusion(bf16[2,128,2048]{1,2,0:T(8,128)(2,1)S(1)} %bitcast.88, bf16[512,2048]{1,0:T(8,128)(2,1)} %l_ref.1, bf16[512,2,256]{0,2,1:T(8,128)(2,1)S(1)} %copy-done.5), kind=kOutput, calls=%fused_computation.8 | convolution fusion | flops 537133056 | bytes 3932160 | tf_op jit(solution)/shard_map/so,gyo->sgy/dot_general | solution.py:162
  119.9 2.5 %all-gather.2.cloned.1.call-done = bf16[2,128,2048]{2,1,0:T(8,128)(2,1)} async-done(((bf16[2,128,512]{2,1,0:T(8,128)(2,1)}), bf16[2,128,2048]{2,1,0:T(8,128)(2,1)}) %all-gather.2.cloned.1.call-update) | async-done | bytes 1048592 | tf_op jit(solution)/shard_map/all_gather | solution.py:161
  122.4 2.7 %fusion.7 = f32[512,2,128]{0,2,1:T(8,128)S(1)} fusion(bf16[2,128,2048]{2,1,0:T(8,128)(2,1)} %all-gather.2.cloned.1.call-done, bf16[512,2048]{1,0:T(8,128)(2,1)} %l_ref.1, bf16[512,2,256]{0,2,1:T(8,128)(2,1)S(1)} %copy-done.5), kind=kOutput, calls=%fused_computation.6 | convolution fusion | flops 537133056 | bytes 3932160 | tf_op jit(solution)/shard_map/so,gyo->sgy/dot_general | solution.py:162
  125.2 1.3 copy.85
  (45 shorter events, 6.1 us)
Async XLA Ops:
  11.8 24.5 %all-to-all-start = ((bf16[8,80,512]{2,1,0:T(8,128)(2,1)}), bf16[8,80,512]{2,1,0:T(8,128)(2,1)S(1)}, u32[]{:S(2)}, u32[]{:S(2)}) async-start(bf16[8,80,512]{2,1,0:T(8,128)(2,1)} %pad_maximum_fusion.3), calls=%async_computation | async-start | bytes 1310720 | tf_op jit(solution)/shard_map/all_to_all | solution.py:105
  36.4 0.9 copy-start.2
  42.1 5.3 %copy-start.1 = (f32[2,256,512]{2,1,0:T(8,128)S(1)}, f32[2,256,512]{2,1,0:T(8,128)}, u32[]{:S(2)}) copy-start(f32[2,256,512]{2,1,0:T(8,128)} %get-tuple-element.15) | copy-start | bytes 3145732
  42.1 5.3 %collective-permute-start = (f32[2,256,512]{2,1,0:T(8,128)}, f32[2,256,512]{2,1,0:T(8,128)}, u32[]{:S(2)}, u32[]{:S(2)}) collective-permute-start(f32[2,256,512]{2,1,0:T(8,128)} %get-tuple-element.16), channel_id=1, source_target_pairs={{0,1},{1,0},{2,3},{3,2},{4,5},{5,4},{6,7},{7,6},{8,9},{9,8},{10,11... | collective-permute-start | bytes 3145736 | tf_op jit(solution)/shard_map/ppermute | solution.py:38
  42.1 20.0 %collective-permute-start.2 = (f32[2,256,512]{2,1,0:T(8,128)}, f32[2,256,512]{2,1,0:T(8,128)}, u32[]{:S(2)}, u32[]{:S(2)}) collective-permute-start(f32[2,256,512]{2,1,0:T(8,128)} %get-tuple-element.18), channel_id=1, source_target_pairs={{0,1},{1,0},{2,3},{3,2},{4,5},{5,4},{6,7},{7,6},{8,9},{9,8},{10,11... | collective-permute-start | bytes 3145736 | tf_op jit(solution)/shard_map/ppermute | solution.py:38
  43.7 18.4 %all-to-all-start.1 = ((bf16[64,16,256]{2,0,1:T(8,128)(2,1)}), bf16[64,16,256]{2,0,1:T(8,128)(2,1)S(1)}, u32[]{:S(2)}, u32[]{:S(2)}) async-start(bf16[64,16,256]{2,0,1:T(8,128)(2,1)} %copy.76), calls=%async_computation.1 | async-start | bytes 1048576 | tf_op jit(solution)/shard_map/all_to_all | solution.py:112
  47.4 14.8 %copy-start = (f32[2,256,512]{2,1,0:T(8,128)S(1)}, f32[2,256,512]{2,1,0:T(8,128)}, u32[]{:S(2)}) copy-start(f32[2,256,512]{2,1,0:T(8,128)} %get-tuple-element.17) | copy-start | bytes 3145732
  49.9 14.5 %collective-permute-start.1 = (f32[256,512]{1,0:T(8,128)}, f32[256,512]{1,0:T(8,128)S(1)}, u32[]{:S(2)}, u32[]{:S(2)}) collective-permute-start(f32[256,512]{1,0:T(8,128)} %get-tuple-element.38), channel_id=1, source_target_pairs={{0,2},{1,3},{2,0},{3,1},{4,6},{5,7},{6,4},{7,5},{8,10},{9,11},{10,... | collective-permute-start | bytes 1572872 | tf_op jit(solution)/shard_map/ppermute | solution.py:133
  64.3 0.8 copy-start.3
  67.3 20.2 %all-to-all-start.2 = ((f32[16,16,512]{2,1,0:T(8,128)}), f32[16,16,512]{2,1,0:T(8,128)S(1)}, u32[]{:S(2)}, u32[]{:S(2)}) async-start(f32[16,16,512]{2,1,0:T(8,128)} %shard_map.60), calls=%async_computation.2 | async-start | bytes 1048576 | tf_op jit(solution)/shard_map/all_to_all | solution.py:153
  72.4 12.2 %collective-permute-start.3 = (f32[256,512]{1,0:T(8,128)S(1)}, f32[256,512]{1,0:T(8,128)S(1)}, u32[]{:S(2)}, u32[]{:S(2)}) collective-permute-start(f32[256,512]{1,0:T(8,128)S(1)} %get-tuple-element.22), channel_id=1, source_target_pairs={{0,2},{1,3},{2,0},{3,1},{4,6},{5,7},{6,4},{7,5},{8,10},{9,11},{10,... | collective-permute-start | bytes 1572872 | tf_op jit(solution)/shard_map/ppermute | solution.py:137
  84.5 0.8 copy-start.4
  87.5 17.5 %all-to-all-start.3 = ((f32[16,16,512]{2,1,0:T(8,128)}), f32[16,16,512]{2,1,0:T(8,128)S(1)}, u32[]{:S(2)}, u32[]{:S(2)}) async-start(f32[16,16,512]{2,1,0:T(8,128)} %shard_map.61), calls=%async_computation.3 | async-start | bytes 1048576 | tf_op jit(solution)/shard_map/all_to_all | solution.py:153
  93.2 29.2 %all-gather.2.cloned.1.call-start = ((), (), s32[]{:S(2)}) async-start(), calls=%async_computation.4 | async-start | bytes 1310720 | tf_op jit(solution)/shard_map/all_gather | solution.py:161
  105.0 6.4 %collective-permute-start.4 = (bf16[1,2,128,512]{3,2,1,0:T(8,128)(2,1)S(1)}, bf16[1,2,128,512]{3,2,1,0:T(8,128)(2,1)S(1)}, u32[]{:S(2)}, u32[]{:S(2)}) collective-permute-start(bf16[1,2,128,512]{3,2,1,0:T(8,128)(2,1)S(1)} %bitcast.79), channel_id=1, source_target_pairs={{0,2},{1,3},{2,0},{3,1},{4,6},{5,7},{6,4},{7,5},{8,10},{9,11},{10,... | collective-permute-start | bytes 786440 | tf_op jit(solution)/shard_map/ppermute | solution.py:53
  112.3 2.5 %collective-permute-start.5 = (bf16[2,2,128,512]{3,2,1,0:T(8,128)(2,1)}, bf16[2,2,128,512]{3,2,1,0:T(8,128)(2,1)}, u32[]{:S(2)}, u32[]{:S(2)}) collective-permute-start(bf16[2,2,128,512]{3,2,1,0:T(8,128)(2,1)} %pad_maximum_fusion.4), channel_id=1, source_target_pairs={{0,1},{1,0},{2,3},{3,2},{4,5},{5,4},{6,7},{7,6},{8,9},{9,8},{10,11... | collective-permute-start | bytes 1572872 | tf_op jit(solution)/shard_map/ppermute | solution.py:53
  116.5 1.1 copy-start.5
Sparse Core Ops, SparseCore 0:
  107.5 14.8 all-gather.1

commit v13 on v12

--- a/solution.py
+++ b/solution.py
@@ -45,17 +45,33 @@
 
 def doubling_gather(block, axis):
     count = lax.axis_size(axis)
-    me = lax.axis_index(axis)
     levels = count.bit_length() - 1
-    held = block[None]
+    pieces = [block]
     for level in reversed(range(levels)):
         pairs = [(i, i ^ (1 << level)) for i in range(count)]
-        held = jnp.concatenate([held, lax.ppermute(held, axis, pairs)], axis=0)
-    order = jnp.arange(count) ^ me
-    flipped = jnp.zeros_like(order)
-    for level in range(levels):
-        flipped = flipped | (((order >> level) & 1) << (levels - 1 - level))
-    return jnp.take(held, flipped, axis=0)
+        pieces = pieces + [lax.ppermute(piece, axis, pairs) for piece in pieces]
+    return pieces
+
+
+def fitted_kernel(me_ref, l_ref, *refs):
+    *piece_refs, out_ref = refs
+    me = me_ref[0]
+    levels = len(piece_refs).bit_length() - 1
+    width = piece_refs[0].shape[-1]
+    for hour in range(out_ref.shape[0]):
+        total = None
+        for position, piece_ref in enumerate(piece_refs):
+            flipped = 0
+            for level in range(levels):
+                flipped |= ((position >> level) & 1) << (levels - 1 - level)
+            block = me ^ flipped
+            columns = l_ref[:, pl.ds(pl.multiple_of(block * width, width), width)]
+            part = lax.dot_general(
+                columns, piece_ref[hour], (((1,), (1,)), ((), ())),
+                preferred_element_type=jnp.float32,
+            )
+            total = part if total is None else total + part
+        out_ref[hour] = total
 
 
 def recurrence_kernel(rate_ref, keep_ref, received_ref, out_ref):
@@ -153,13 +169,27 @@
         gathered = lax.all_to_all(smoothed_here, "tm", split_axis=0, concat_axis=1, tiled=True)
         rounded = gathered.astype(jnp.bfloat16)
         if chunk == CHUNKS - 1:
-            every = doubling_gather(rounded, "state")
-            full = jnp.transpose(every, (1, 2, 0, 3)).reshape(
-                rounded.shape[:2] + (every.shape[0] * rounded.shape[2],)
-            )
+            pieces = doubling_gather(rounded, "state")
+            slab_hours, width, _ = rounded.shape
+            fitted = vmem_call(
+                fitted_kernel,
+                jax.ShapeDtypeStruct((slab_hours, stations_here, width), jnp.float32),
+                1 + len(pieces),
+                pl.CostEstimate(
+                    flops=2 * stations_here * slab_hours * width * all_comps,
+                    bytes_accessed=2 * stations_here * all_comps
+                    + 2 * slab_hours * width * all_comps
+                    + 4 * slab_hours * stations_here * width,
+                    transcendentals=0,
+                ),
+                scalars=1,
+            )(lax.axis_index("state").reshape(1).astype(jnp.int32), loadings, *pieces)
+            fitted = jnp.transpose(fitted, (1, 0, 2))
         else:
             full = lax.all_gather(rounded, "state", axis=2, tiled=True)
-        fitted = jnp.einsum("so,gyo->sgy", loadings, full, preferred_element_type=jnp.float32)
+            fitted = jnp.einsum(
+                "so,gyo->sgy", loadings, full, preferred_element_type=jnp.float32
+            )
         low = chunk * members // CHUNKS
         picked = by_hour[:, :, low:low + members // CHUNKS]
         residual_parts.append(picked.astype(jnp.float32) - fitted)

time: 134 us -> 133 us (level)
  Pallas kernels: 9.11 us -> 13 us
  matrix products: 5.02 us -> 2.02 us
  other arithmetic: 11 us -> 8.22 us
  waiting for transfers between devices: 55.3 us -> 57.2 us
  local copies, waits for them, and re-layouts: 11.8 us -> 10.4 us
    ppermute x2 -> x3, waiting for transfers between devices: 4.1 us -> 8.72 us  [doubling_gather(): pieces = pieces + [lax.ppermute(piece, axis, pairs) for piece in pieces]]
    pallas_call x0 -> x1, Pallas kernels: none -> 3.85 us  [local(): vmem_call(fitted_kernel, jax.ShapeDtypeStruct((slab_hours, stations_here,...]
    dot_general x2 -> x1, matrix products: 5.02 us -> 2.02 us  [local(): jnp.einsum('so,gyo->sgy', loadings, full, preferred_element_type=jnp.floa...]
    all_gather x1, waiting for transfers between devices: 2.46 us -> 0.01 us  [local(): full = lax.all_gather(rounded, 'state', axis=2, tiled=True)]
    concatenate x2 -> x0, other arithmetic: 1.99 us -> none  [doubling_gather(): held = jnp.concatenate([held, lax.ppermute(held, axis, pairs)], axis=0)]
    ppermute x1, waiting for transfers between devices: 0.01 us -> 1.82 us  [local(): received = lax.ppermute(outgoing, 'state', pairs)]
    unnamed x15 -> x23, local copies, waits for them, and re-layouts: 6.95 us -> 7.83 us
  transfers between devices with their start and end apart: 11 -> 12, of which waited for: 6 -> 7; matrix products, arithmetic and copies ran while one was open for 12% -> 7% of each run, Pallas kernels for 2% -> 5%
where the time goes in v13:
time: 133 us; the launch traced here: 132 us
  waiting for transfers between devices  57.2 us (43%)
  starting transfers between devices  27.4 us (21%)
  between operations  14.2 us (11%)
  Pallas kernels  13 us (10%)
  local copies, waits for them, and re-layouts  10.4 us (8%)
  other arithmetic  8.22 us (6%)
  matrix products  2.02 us (2%)
    all_to_all x1, waiting for transfers between devices, local(): lax.all_to_all(outgoing, 'tm', split_axis=0, concat_axis=0, tiled=True)  17.3 us
    all_to_all x2, starting transfers between devices, local(): lax.all_to_all(smoothed_here, 'tm', split_axis=0, concat_axis=1, tiled=True)  11.3 us
    all_to_all x2, waiting for transfers between devices, local(): lax.all_to_all(smoothed_here, 'tm', split_axis=0, concat_axis=1, tiled=True)  10.9 us
    ppermute x1, waiting for transfers between devices, local(): lax.ppermute(o, 'state', last[c + 1][2])  10.6 us
    ppermute x3, waiting for transfers between devices, doubling_gather(): pieces = pieces + [lax.ppermute(piece, axis, pairs) for piece in pieces]  8.72 us
    unnamed x23, local copies, waits for them, and re-layouts  7.83 us
    all_to_all x1, waiting for transfers between devices, local(): lax.all_to_all(masked_later, 'tm', split_axis=1, concat_axis=0, tiled=True)  7.82 us
    all_to_all x1, starting transfers between devices, local(): lax.all_to_all(outgoing, 'tm', split_axis=0, concat_axis=0, tiled=True)  7.25 us
  transfers between devices with their start and end apart: 12, of which 7 were waited for; matrix products, arithmetic and copies ran while one was open for 7% of the time, Pallas kernels for 5%

profile of v13, /device:TPU:0, one launch (start us, length us, event | category | flops | bytes accessed | tf_op | source)
XLA Modules:
  0.0 132.5 jit_solution(1101365066357014398)
XLA Ops:
  7.2 0.7 convert_element_type.29
  7.9 0.7 fusion.10
  8.6 1.7 %copy.40 = bf16[64,16,256]{0,2,1:T(8,128)(2,1)S(1)} copy(bf16[64,16,256]{2,1,0:T(8,128)(2,1)} %param.4) | data formatting | bytes 1048576 | tf_op args[0]
  10.9 0.9 pad_maximum_fusion.2
  11.8 7.3 %all-to-all-start = ((bf16[8,80,512]{2,1,0:T(8,128)(2,1)}), bf16[8,80,512]{2,1,0:T(8,128)(2,1)S(1)}, u32[]{:S(2)}, u32[]{:S(2)}) async-start(bf16[8,80,512]{2,1,0:T(8,128)(2,1)} %pad_maximum_fusion.2), calls=%async_computation | async-start | bytes 1310720 | tf_op jit(solution)/shard_map/all_to_all | solution.py:121
  19.1 17.3 %all-to-all-done.x_ref = bf16[8,80,512]{2,1,0:T(8,128)(2,1)S(1)} async-done(((bf16[8,80,512]{2,1,0:T(8,128)(2,1)}), bf16[8,80,512]{2,1,0:T(8,128)(2,1)S(1)}, u32[]{:S(2)}, u32[]{:S(2)}) %all-to-all-start) | async-done | bytes 655392 | tf_op jit(solution)/shard_map/all_to_all | solution.py:121
  36.4 0.8 copy-done.5
  37.2 4.8 %shard_map.59 = (f32[2,256,512]{2,1,0:T(8,128)}, f32[2,256,512]{2,1,0:T(8,128)}, f32[2,256,512]{2,1,0:T(8,128)}, f32[2,256,512]{2,1,0:T(8,128)}) custom-call(s32[1]{0:T(128)} %bitcast.10.me_ref, bf16[8,80,512]{2,1,0:T(8,128)(2,1)} %copy-done.5, bf16[512,2048]{1,0:T(8,128)(2,1)} %l_ref.3), custom_call_target="tpu_custom_call" | custom-call | flops 1073741824 | bytes 6815744 | tf_op jit(solution)/shard_map/pallas_call | solution.py:133
  42.6 1.1 copy.45
  43.7 3.6 %all-to-all-start.1 = ((bf16[64,16,256]{2,0,1:T(8,128)(2,1)}), bf16[64,16,256]{2,0,1:T(8,128)(2,1)S(1)}, u32[]{:S(2)}, u32[]{:S(2)}) async-start(bf16[64,16,256]{2,0,1:T(8,128)(2,1)} %copy.45), calls=%async_computation.1 | async-start | bytes 1048576 | tf_op jit(solution)/shard_map/all_to_all | solution.py:128
  47.3 1.0 copy-done.3
  48.3 2.8 %fusion.7 = (f32[256,512]{1,0:T(8,128)}, f32[256,512]{1,0:T(8,128)}) fusion(f32[2,256,512]{2,1,0:T(8,128)} %copy-done.3, f32[2,256,512]{2,1,0:T(8,128)} %get-tuple-element.15), kind=kLoop, calls=%fused_computation.11 | loop fusion | flops 262144 | bytes 3145728 | tf_op jit(solution)/shard_map/add | solution.py:40
  51.1 1.5 %collective-permute-start.1 = (f32[256,512]{1,0:T(8,128)}, f32[256,512]{1,0:T(8,128)}, u32[]{:S(2)}, u32[]{:S(2)}) collective-permute-start(f32[256,512]{1,0:T(8,128)} %get-tuple-element.34), channel_id=1, source_target_pairs={{0,2},{1,3},{2,0},{3,1},{4,6},{5,7},{6,4},{7,5},{8,10},{9,11},{10,... | collective-permute-start | bytes 1572872 | tf_op jit(solution)/shard_map/ppermute | solution.py:149
  52.6 0.8 slice_convert_fusion
  54.2 7.8 %all-to-all-done.1 = bf16[64,16,256]{2,0,1:T(8,128)(2,1)S(1)} async-done(((bf16[64,16,256]{2,0,1:T(8,128)(2,1)}), bf16[64,16,256]{2,0,1:T(8,128)(2,1)S(1)}, u32[]{:S(2)}, u32[]{:S(2)}) %all-to-all-start.1) | async-done | bytes 524320 | tf_op jit(solution)/shard_map/all_to_all | solution.py:128
  62.1 1.2 fusion.5
  63.3 1.8 %collective-permute-done.1 = f32[256,512]{1,0:T(8,128)} collective-permute-done((f32[256,512]{1,0:T(8,128)}, f32[256,512]{1,0:T(8,128)}, u32[]{:S(2)}, u32[]{:S(2)}) %collective-permute-start.1) | collective-permute-done | bytes 524320 | tf_op jit(solution)/shard_map/ppermute | solution.py:149
  65.1 2.2 %shard_map.60 = f32[16,16,512]{2,1,0:T(8,128)} custom-call(f32[16,512]{1,0:T(8,128)} %add.40.rate_ref, f32[16,16,512]{2,1,0:T(8,128)} %bitcast.59, f32[16,16,512]{2,1,0:T(8,128)} %bitcast.16.received_ref), custom_call_target="tpu_custom_call" | custom-call | flops 786432 | bytes 1572864 | tf_op jit(solution)/shard_map/pallas_call | solution.py:159
  67.3 5.6 %all-to-all-start.2 = ((f32[16,16,512]{2,1,0:T(8,128)}), f32[16,16,512]{2,1,0:T(8,128)S(1)}, u32[]{:S(2)}, u32[]{:S(2)}) async-start(f32[16,16,512]{2,1,0:T(8,128)} %shard_map.60), calls=%async_computation.2 | async-start | bytes 1048576 | tf_op jit(solution)/shard_map/all_to_all | solution.py:169
  72.9 1.6 %collective-permute-start.3 = (f32[256,512]{1,0:T(8,128)S(1)}, f32[256,512]{1,0:T(8,128)S(1)}, u32[]{:S(2)}, u32[]{:S(2)}) collective-permute-start(f32[256,512]{1,0:T(8,128)S(1)} %copy-done.7), channel_id=1, source_target_pairs={{0,2},{1,3},{2,0},{3,1},{4,6},{5,7},{6,4},{7,5},{8,10},{9,11},{10,... | collective-permute-start | bytes 1572872 | tf_op jit(solution)/shard_map/ppermute | solution.py:153
  74.5 10.6 %collective-permute-done.3 = f32[256,512]{1,0:T(8,128)S(1)} collective-permute-done((f32[256,512]{1,0:T(8,128)S(1)}, f32[256,512]{1,0:T(8,128)S(1)}, u32[]{:S(2)}, u32[]{:S(2)}) %collective-permute-start.3) | collective-permute-done | bytes 524320 | tf_op jit(solution)/shard_map/ppermute | solution.py:153
  85.1 0.8 copy-done.6
  85.9 2.2 %shard_map.61 = f32[16,16,512]{2,1,0:T(8,128)} custom-call(f32[16,512]{1,0:T(8,128)} %add.40.rate_ref, f32[16,16,512]{2,1,0:T(8,128)} %bitcast.62, f32[16,16,512]{2,1,0:T(8,128)} %bitcast.64), custom_call_target="tpu_custom_call" | custom-call | flops 786432 | bytes 1572864 | tf_op jit(solution)/shard_map/pallas_call | solution.py:159
  88.1 5.7 %all-to-all-start.3 = ((f32[16,16,512]{2,1,0:T(8,128)}), f32[16,16,512]{2,1,0:T(8,128)S(1)}, u32[]{:S(2)}, u32[]{:S(2)}) async-start(f32[16,16,512]{2,1,0:T(8,128)} %shard_map.61), calls=%async_computation.3 | async-start | bytes 1048576 | tf_op jit(solution)/shard_map/all_to_all | solution.py:169
  93.8 0.8 bitcast_convert_fusion.1
  94.6 10.9 %all-to-all-done.3 = f32[16,16,512]{2,1,0:T(8,128)S(1)} async-done(((f32[16,16,512]{2,1,0:T(8,128)}), f32[16,16,512]{2,1,0:T(8,128)S(1)}, u32[]{:S(2)}, u32[]{:S(2)}) %all-to-all-start.3) | async-done | bytes 524320 | tf_op jit(solution)/shard_map/all_to_all | solution.py:169
  105.6 1.6 %collective-permute-start.4 = (bf16[2,128,512]{2,1,0:T(8,128)(2,1)S(1)}, bf16[2,128,512]{2,1,0:T(8,128)(2,1)S(1)}, u32[]{:S(2)}, u32[]{:S(2)}) collective-permute-start(bf16[2,128,512]{2,1,0:T(8,128)(2,1)S(1)} %bitcast_convert_fusion.refs_0_), channel_id=1, source_target_pairs={{0,2},{1,3},{2,0},{3,1},{4,6},{5,7},{6,4},{7,5},{8,10},{9,11},{10,... | collective-permute-start | bytes 786440 | tf_op jit(solution)/shard_map/ppermute | solution.py:52
  107.2 8.5 %collective-permute-done.4.refs_1_ = bf16[2,128,512]{2,1,0:T(8,128)(2,1)S(1)} collective-permute-done((bf16[2,128,512]{2,1,0:T(8,128)(2,1)S(1)}, bf16[2,128,512]{2,1,0:T(8,128)(2,1)S(1)}, u32[]{:S(2)}, u32[]{:S(2)}) %collective-permute-start.4) | collective-permute-done | bytes 262176 | tf_op jit(solution)/shard_map/ppermute | solution.py:52
  115.7 1.3 copy.50
  117.8 3.9 %shard_map.62 = f32[2,512,128]{2,1,0:T(8,128)} custom-call(s32[1]{0:T(128)} %bitcast.10.me_ref, bf16[512,2048]{1,0:T(8,128)(2,1)} %l_ref.3, bf16[2,128,512]{2,1,0:T(8,128)(2,1)} %copy-done.4, bf16[2,128,512]{2,1,0:T(8,128)(2,1)} %copy-done.8, bf16[2,128,512]{2,1,0:T(8,128)(2,1)} %copy-done.9, bf16[2,128,512]{2,1,0:T(8,128)(2,1)} %collective-permute-done.6.refs_3_), custom_call_target="tpu_custom_call" | custom-call | flops 536870912 | bytes 3670016 | tf_op jit(solution)/shard_map/pallas_call | solution.py:174
  121.6 2.0 %fusion.2 = f32[512,2,128]{2,0,1:T(8,128)S(1)} fusion(bf16[2,128,2048]{2,1,0:T(8,128)(2,1)} %all-gather.2.cloned.1.call-done, bf16[512,2048]{1,0:T(8,128)(2,1)S(1)} %copy-done), kind=kOutput, calls=%fused_computation.2 | convolution fusion | flops 536870912 | bytes 3670016 | tf_op jit(solution)/shard_map/so,gyo->sgy/dot_general | solution.py:190
  123.8 1.8 %copy.51 = f32[512,2,256]{2,1,0:T(2,128)} copy(f32[512,2,256]{2,0,1:T(8,128)S(1)} %pad_maximum_fusion.1) | data formatting | bytes 2097152
  (47 shorter events, 3.1 us)
Async XLA Ops:
  11.8 24.5 %all-to-all-start = ((bf16[8,80,512]{2,1,0:T(8,128)(2,1)}), bf16[8,80,512]{2,1,0:T(8,128)(2,1)S(1)}, u32[]{:S(2)}, u32[]{:S(2)}) async-start(bf16[8,80,512]{2,1,0:T(8,128)(2,1)} %pad_maximum_fusion.2), calls=%async_computation | async-start | bytes 1310720 | tf_op jit(solution)/shard_map/all_to_all | solution.py:121
  36.4 0.8 copy-start.5
  42.1 5.3 %collective-permute-start = (f32[2,256,512]{2,1,0:T(8,128)}, f32[2,256,512]{2,1,0:T(8,128)S(1)}, u32[]{:S(2)}, u32[]{:S(2)}) collective-permute-start(f32[2,256,512]{2,1,0:T(8,128)} %get-tuple-element.16), channel_id=1, source_target_pairs={{0,1},{1,0},{2,3},{3,2},{4,5},{5,4},{6,7},{7,6},{8,9},{9,8},{10,11... | collective-permute-start | bytes 3145736 | tf_op jit(solution)/shard_map/ppermute | solution.py:38
  42.1 20.0 %collective-permute-start.2 = (f32[2,256,512]{2,1,0:T(8,128)}, f32[2,256,512]{2,1,0:T(8,128)S(1)}, u32[]{:S(2)}, u32[]{:S(2)}) collective-permute-start(f32[2,256,512]{2,1,0:T(8,128)} %get-tuple-element.18), channel_id=1, source_target_pairs={{0,1},{1,0},{2,3},{3,2},{4,5},{5,4},{6,7},{7,6},{8,9},{9,8},{10,11... | collective-permute-start | bytes 3145736 | tf_op jit(solution)/shard_map/ppermute | solution.py:38
  43.7 18.4 %all-to-all-start.1 = ((bf16[64,16,256]{2,0,1:T(8,128)(2,1)}), bf16[64,16,256]{2,0,1:T(8,128)(2,1)S(1)}, u32[]{:S(2)}, u32[]{:S(2)}) async-start(bf16[64,16,256]{2,0,1:T(8,128)(2,1)} %copy.45), calls=%async_computation.1 | async-start | bytes 1048576 | tf_op jit(solution)/shard_map/all_to_all | solution.py:128
  47.3 1.0 copy-start.3
  48.3 13.8 %copy-start.2 = (f32[2,256,512]{2,1,0:T(8,128)S(1)}, f32[2,256,512]{2,1,0:T(8,128)}, u32[]{:S(2)}) copy-start(f32[2,256,512]{2,1,0:T(8,128)} %get-tuple-element.17) | copy-start | bytes 3145732
  51.1 14.0 %collective-permute-start.1 = (f32[256,512]{1,0:T(8,128)}, f32[256,512]{1,0:T(8,128)}, u32[]{:S(2)}, u32[]{:S(2)}) collective-permute-start(f32[256,512]{1,0:T(8,128)} %get-tuple-element.34), channel_id=1, source_target_pairs={{0,2},{1,3},{2,0},{3,1},{4,6},{5,7},{6,4},{7,5},{8,10},{9,11},{10,... | collective-permute-start | bytes 1572872 | tf_op jit(solution)/shard_map/ppermute | solution.py:149
  63.3 9.6 %copy-start.7 = (f32[256,512]{1,0:T(8,128)S(1)}, f32[256,512]{1,0:T(8,128)}, u32[]{:S(2)}) copy-start(f32[256,512]{1,0:T(8,128)} %get-tuple-element.22) | copy-start | bytes 1572868
  67.3 20.8 %all-to-all-start.2 = ((f32[16,16,512]{2,1,0:T(8,128)}), f32[16,16,512]{2,1,0:T(8,128)S(1)}, u32[]{:S(2)}, u32[]{:S(2)}) async-start(f32[16,16,512]{2,1,0:T(8,128)} %shard_map.60), calls=%async_computation.2 | async-start | bytes 1048576 | tf_op jit(solution)/shard_map/all_to_all | solution.py:169
  72.9 12.2 %collective-permute-start.3 = (f32[256,512]{1,0:T(8,128)S(1)}, f32[256,512]{1,0:T(8,128)S(1)}, u32[]{:S(2)}, u32[]{:S(2)}) collective-permute-start(f32[256,512]{1,0:T(8,128)S(1)} %copy-done.7), channel_id=1, source_target_pairs={{0,2},{1,3},{2,0},{3,1},{4,6},{5,7},{6,4},{7,5},{8,10},{9,11},{10,... | collective-permute-start | bytes 1572872 | tf_op jit(solution)/shard_map/ppermute | solution.py:153
  85.1 0.8 copy-start.6
  88.1 17.4 %all-to-all-start.3 = ((f32[16,16,512]{2,1,0:T(8,128)}), f32[16,16,512]{2,1,0:T(8,128)S(1)}, u32[]{:S(2)}, u32[]{:S(2)}) async-start(f32[16,16,512]{2,1,0:T(8,128)} %shard_map.61), calls=%async_computation.3 | async-start | bytes 1048576 | tf_op jit(solution)/shard_map/all_to_all | solution.py:169
  93.7 27.9 %all-gather.2.cloned.1.call-start = ((), (), s32[]{:S(2)}) async-start(), calls=%async_computation.4 | async-start | bytes 1310720 | tf_op jit(solution)/shard_map/all_gather | solution.py:189
  105.6 11.4 %copy-start.4 = (bf16[2,128,512]{2,1,0:T(8,128)(2,1)}, bf16[2,128,512]{2,1,0:T(8,128)(2,1)S(1)}, u32[]{:S(2)}) copy-start(bf16[2,128,512]{2,1,0:T(8,128)(2,1)S(1)} %bitcast_convert_fusion.refs_0_) | copy-start | bytes 786436
  105.6 10.0 %collective-permute-start.4 = (bf16[2,128,512]{2,1,0:T(8,128)(2,1)S(1)}, bf16[2,128,512]{2,1,0:T(8,128)(2,1)S(1)}, u32[]{:S(2)}, u32[]{:S(2)}) collective-permute-start(bf16[2,128,512]{2,1,0:T(8,128)(2,1)S(1)} %bitcast_convert_fusion.refs_0_), channel_id=1, source_target_pairs={{0,2},{1,3},{2,0},{3,1},{4,6},{5,7},{6,4},{7,5},{8,10},{9,11},{10,... | collective-permute-start | bytes 786440 | tf_op jit(solution)/shard_map/ppermute | solution.py:52
  107.2 9.8 %collective-permute-start.5 = (bf16[2,128,512]{2,1,0:T(8,128)(2,1)S(1)}, bf16[2,128,512]{2,1,0:T(8,128)(2,1)S(1)}, u32[]{:S(2)}, u32[]{:S(2)}) collective-permute-start(bf16[2,128,512]{2,1,0:T(8,128)(2,1)S(1)} %bitcast_convert_fusion.refs_0_), channel_id=1, source_target_pairs={{0,1},{1,0},{2,3},{3,2},{4,5},{5,4},{6,7},{7,6},{8,9},{9,8},{10,11... | collective-permute-start | bytes 786440 | tf_op jit(solution)/shard_map/ppermute | solution.py:52
  115.7 1.4 %copy-start.8 = (bf16[2,128,512]{2,1,0:T(8,128)(2,1)}, bf16[2,128,512]{2,1,0:T(8,128)(2,1)S(1)}, u32[]{:S(2)}) copy-start(bf16[2,128,512]{2,1,0:T(8,128)(2,1)S(1)} %collective-permute-done.4.refs_1_) | copy-start | bytes 786436
  115.7 1.7 %collective-permute-start.6 = (bf16[2,128,512]{2,1,0:T(8,128)(2,1)S(1)}, bf16[2,128,512]{2,1,0:T(8,128)(2,1)}, u32[]{:S(2)}, u32[]{:S(2)}) collective-permute-start(bf16[2,128,512]{2,1,0:T(8,128)(2,1)S(1)} %collective-permute-done.4.refs_1_), channel_id=1, source_target_pairs={{0,1},{1,0},{2,3},{3,2},{4,5},{5,4},{6,7},{7,6},{8,9},{9,8},{10,11... | collective-permute-start | bytes 786440 | tf_op jit(solution)/shard_map/ppermute | solution.py:52
  117.0 4.6 %copy-start = (bf16[512,2048]{1,0:T(8,128)(2,1)S(1)}, bf16[512,2048]{1,0:T(8,128)(2,1)}, u32[]{:S(2)}) copy-start(bf16[512,2048]{1,0:T(8,128)(2,1)} %l_ref.3) | copy-start | bytes 6291460
  117.0 0.7 copy-start.9
  121.6 2.0 %copy-start.1 = (f32[2,512,128]{2,1,0:T(8,128)S(1)}, f32[2,512,128]{2,1,0:T(8,128)}, u32[]{:S(2)}) copy-start(f32[2,512,128]{2,1,0:T(8,128)} %shard_map.62) | copy-start | bytes 1572868
Sparse Core Ops, SparseCore 0:
  96.1 20.0 all-gather.1

commit v14 on v13

--- a/solution.py
+++ b/solution.py
@@ -58,20 +58,22 @@
     me = me_ref[0]
     levels = len(piece_refs).bit_length() - 1
     width = piece_refs[0].shape[-1]
-    for hour in range(out_ref.shape[0]):
-        total = None
-        for position, piece_ref in enumerate(piece_refs):
-            flipped = 0
-            for level in range(levels):
-                flipped |= ((position >> level) & 1) << (levels - 1 - level)
-            block = me ^ flipped
-            columns = l_ref[:, pl.ds(pl.multiple_of(block * width, width), width)]
-            part = lax.dot_general(
-                columns, piece_ref[hour], (((1,), (1,)), ((), ())),
-                preferred_element_type=jnp.float32,
-            )
-            total = part if total is None else total + part
-        out_ref[hour] = total
+    hours, members, _ = piece_refs[0].shape
+    total = None
+    for position, piece_ref in enumerate(piece_refs):
+        flipped = 0
+        for level in range(levels):
+            flipped |= ((position >> level) & 1) << (levels - 1 - level)
+        block = me ^ flipped
+        columns = l_ref[:, pl.ds(pl.multiple_of(block * width, width), width)]
+        piece = piece_ref[...].reshape(hours * members, width)
+        part = lax.dot_general(
+            columns, piece, (((1,), (1,)), ((), ())),
+            preferred_element_type=jnp.float32,
+        )
+        total = part if total is None else total + part
+    for hour in range(hours):
+        out_ref[hour] = total[:, hour * members:(hour + 1) * members]
 
 
 def recurrence_kernel(rate_ref, keep_ref, received_ref, out_ref):
@@ -170,6 +172,9 @@
         rounded = gathered.astype(jnp.bfloat16)
         if chunk == CHUNKS - 1:
             pieces = doubling_gather(rounded, "state")
+            smoothed_parts.append(jnp.transpose(gathered, (2, 0, 1)))
+            smoothed = jnp.concatenate(smoothed_parts, axis=2)
+            smoothed, pieces = lax.optimization_barrier((smoothed, pieces))
             slab_hours, width, _ = rounded.shape
             fitted = vmem_call(
                 fitted_kernel,
@@ -193,11 +198,9 @@
         low = chunk * members // CHUNKS
         picked = by_hour[:, :, low:low + members // CHUNKS]
         residual_parts.append(picked.astype(jnp.float32) - fitted)
-        smoothed_parts.append(jnp.transpose(gathered, (2, 0, 1)))
-    return (
-        jnp.concatenate(smoothed_parts, axis=2),
-        jnp.concatenate(residual_parts, axis=2),
-    )
+        if chunk < CHUNKS - 1:
+            smoothed_parts.append(jnp.transpose(gathered, (2, 0, 1)))
+    return (smoothed, jnp.concatenate(residual_parts, axis=2))
 
 
 def solution(mesh):

time: 133 us -> 134 us (level)
    unnamed x23 -> x25, local copies, waits for them, and re-layouts: 7.83 us -> 8.1 us
  transfers between devices with their start and end apart: 12 -> 12, of which waited for: 7 -> 7; matrix products, arithmetic and copies ran while one was open for 7% -> 7% of each run, Pallas kernels for 5% -> 4%
where the time goes in v14:
time: 134 us
  waiting for transfers between devices  58.4 us (44%)
  starting transfers between devices  27.4 us (20%)
  between operations  14.3 us (11%)
  Pallas kernels  12.6 us (9%)
  local copies, waits for them, and re-layouts  10.6 us (8%)
  other arithmetic  8.21 us (6%)
  matrix products  2.02 us (2%)
    all_to_all x1, waiting for transfers between devices, local(): lax.all_to_all(outgoing, 'tm', split_axis=0, concat_axis=0, tiled=True)  17.3 us
    all_to_all x2, starting transfers between devices, local(): lax.all_to_all(smoothed_here, 'tm', split_axis=0, concat_axis=1, tiled=True)  11.3 us
    all_to_all x2, waiting for transfers between devices, local(): lax.all_to_all(smoothed_here, 'tm', split_axis=0, concat_axis=1, tiled=True)  10.9 us
    ppermute x1, waiting for transfers between devices, local(): lax.ppermute(o, 'state', last[c + 1][2])  10.6 us
    ppermute x3, waiting for transfers between devices, doubling_gather(): pieces = pieces + [lax.ppermute(piece, axis, pairs) for piece in pieces]  9.89 us
    unnamed x25, local copies, waits for them, and re-layouts  8.1 us
    all_to_all x1, waiting for transfers between devices, local(): lax.all_to_all(masked_later, 'tm', split_axis=1, concat_axis=0, tiled=True)  7.83 us
    all_to_all x1, starting transfers between devices, local(): lax.all_to_all(outgoing, 'tm', split_axis=0, concat_axis=0, tiled=True)  7.25 us
  transfers between devices with their start and end apart: 12, of which 7 were waited for; matrix products, arithmetic and copies ran while one was open for 7% of the time, Pallas kernels for 4%

profile of v14, /device:TPU:0, one launch (start us, length us, event | category | flops | bytes accessed | tf_op | source)
XLA Modules:
  0.0 133.5 jit_solution(6280987456825603550)
XLA Ops:
  8.6 1.7 %copy.40 = bf16[64,16,256]{0,2,1:T(8,128)(2,1)S(1)} copy(bf16[64,16,256]{2,1,0:T(8,128)(2,1)} %param.4) | data formatting | bytes 1048576 | tf_op args[0]
  10.9 0.9 pad_maximum_fusion.2
  11.8 7.3 %all-to-all-start = ((bf16[8,80,512]{2,1,0:T(8,128)(2,1)}), bf16[8,80,512]{2,1,0:T(8,128)(2,1)S(1)}, u32[]{:S(2)}, u32[]{:S(2)}) async-start(bf16[8,80,512]{2,1,0:T(8,128)(2,1)} %pad_maximum_fusion.2), calls=%async_computation | async-start | bytes 1310720 | tf_op jit(solution)/shard_map/all_to_all | solution.py:123
  19.1 17.3 %all-to-all-done.x_ref = bf16[8,80,512]{2,1,0:T(8,128)(2,1)S(1)} async-done(((bf16[8,80,512]{2,1,0:T(8,128)(2,1)}), bf16[8,80,512]{2,1,0:T(8,128)(2,1)S(1)}, u32[]{:S(2)}, u32[]{:S(2)}) %all-to-all-start) | async-done | bytes 655392 | tf_op jit(solution)/shard_map/all_to_all | solution.py:123
  36.4 0.8 copy-done.5
  37.2 4.8 %shard_map.59 = (f32[2,256,512]{2,1,0:T(8,128)}, f32[2,256,512]{2,1,0:T(8,128)}, f32[2,256,512]{2,1,0:T(8,128)}, f32[2,256,512]{2,1,0:T(8,128)}) custom-call(s32[1]{0:T(128)} %bitcast.10.me_ref, bf16[8,80,512]{2,1,0:T(8,128)(2,1)} %copy-done.5, bf16[512,2048]{1,0:T(8,128)(2,1)} %l_ref.3), custom_call_target="tpu_custom_call" | custom-call | flops 1073741824 | bytes 6815744 | tf_op jit(solution)/shard_map/pallas_call | solution.py:135
  42.6 1.1 copy.45
  43.7 3.6 %all-to-all-start.1 = ((bf16[64,16,256]{2,0,1:T(8,128)(2,1)}), bf16[64,16,256]{2,0,1:T(8,128)(2,1)S(1)}, u32[]{:S(2)}, u32[]{:S(2)}) async-start(bf16[64,16,256]{2,0,1:T(8,128)(2,1)} %copy.45), calls=%async_computation.1 | async-start | bytes 1048576 | tf_op jit(solution)/shard_map/all_to_all | solution.py:130
  47.3 1.0 copy-done.3
  48.3 2.8 %fusion.7 = (f32[256,512]{1,0:T(8,128)}, f32[256,512]{1,0:T(8,128)}) fusion(f32[2,256,512]{2,1,0:T(8,128)} %copy-done.3, f32[2,256,512]{2,1,0:T(8,128)} %get-tuple-element.20), kind=kLoop, calls=%fused_computation.11 | loop fusion | flops 262144 | bytes 3145728 | tf_op jit(solution)/shard_map/add | solution.py:40
  51.1 1.5 %collective-permute-start.1 = (f32[256,512]{1,0:T(8,128)}, f32[256,512]{1,0:T(8,128)}, u32[]{:S(2)}, u32[]{:S(2)}) collective-permute-start(f32[256,512]{1,0:T(8,128)} %get-tuple-element.44), channel_id=1, source_target_pairs={{0,2},{1,3},{2,0},{3,1},{4,6},{5,7},{6,4},{7,5},{8,10},{9,11},{10,... | collective-permute-start | bytes 1572872 | tf_op jit(solution)/shard_map/ppermute | solution.py:151
  52.6 0.8 slice_convert_fusion
  54.2 7.8 %all-to-all-done.1 = bf16[64,16,256]{2,0,1:T(8,128)(2,1)S(1)} async-done(((bf16[64,16,256]{2,0,1:T(8,128)(2,1)}), bf16[64,16,256]{2,0,1:T(8,128)(2,1)S(1)}, u32[]{:S(2)}, u32[]{:S(2)}) %all-to-all-start.1) | async-done | bytes 524320 | tf_op jit(solution)/shard_map/all_to_all | solution.py:130
  62.1 1.2 fusion.5
  63.3 1.8 %collective-permute-done.1 = f32[256,512]{1,0:T(8,128)} collective-permute-done((f32[256,512]{1,0:T(8,128)}, f32[256,512]{1,0:T(8,128)}, u32[]{:S(2)}, u32[]{:S(2)}) %collective-permute-start.1) | collective-permute-done | bytes 524320 | tf_op jit(solution)/shard_map/ppermute | solution.py:151
  65.1 2.1 %shard_map.60 = f32[16,16,512]{2,1,0:T(8,128)} custom-call(f32[16,512]{1,0:T(8,128)} %add.40.rate_ref, f32[16,16,512]{2,1,0:T(8,128)} %bitcast.59, f32[16,16,512]{2,1,0:T(8,128)} %bitcast.16.received_ref), custom_call_target="tpu_custom_call" | custom-call | flops 786432 | bytes 1572864 | tf_op jit(solution)/shard_map/pallas_call | solution.py:161
  67.2 5.6 %all-to-all-start.2 = ((f32[16,16,512]{2,1,0:T(8,128)}), f32[16,16,512]{2,1,0:T(8,128)S(1)}, u32[]{:S(2)}, u32[]{:S(2)}) async-start(f32[16,16,512]{2,1,0:T(8,128)} %shard_map.60), calls=%async_computation.2 | async-start | bytes 1048576 | tf_op jit(solution)/shard_map/all_to_all | solution.py:171
  72.9 1.6 %collective-permute-start.3 = (f32[256,512]{1,0:T(8,128)S(1)}, f32[256,512]{1,0:T(8,128)S(1)}, u32[]{:S(2)}, u32[]{:S(2)}) collective-permute-start(f32[256,512]{1,0:T(8,128)S(1)} %copy-done.7), channel_id=1, source_target_pairs={{0,2},{1,3},{2,0},{3,1},{4,6},{5,7},{6,4},{7,5},{8,10},{9,11},{10,... | collective-permute-start | bytes 1572872 | tf_op jit(solution)/shard_map/ppermute | solution.py:155
  74.5 10.6 %collective-permute-done.3 = f32[256,512]{1,0:T(8,128)S(1)} collective-permute-done((f32[256,512]{1,0:T(8,128)S(1)}, f32[256,512]{1,0:T(8,128)S(1)}, u32[]{:S(2)}, u32[]{:S(2)}) %collective-permute-start.3) | collective-permute-done | bytes 524320 | tf_op jit(solution)/shard_map/ppermute | solution.py:155
  85.1 0.8 copy-done.6
  85.9 2.1 %shard_map.61 = f32[16,16,512]{2,1,0:T(8,128)} custom-call(f32[16,512]{1,0:T(8,128)} %add.40.rate_ref, f32[16,16,512]{2,1,0:T(8,128)} %bitcast.62, f32[16,16,512]{2,1,0:T(8,128)} %bitcast.64), custom_call_target="tpu_custom_call" | custom-call | flops 786432 | bytes 1572864 | tf_op jit(solution)/shard_map/pallas_call | solution.py:161
  88.0 5.7 %all-to-all-start.3 = ((f32[16,16,512]{2,1,0:T(8,128)}), f32[16,16,512]{2,1,0:T(8,128)S(1)}, u32[]{:S(2)}, u32[]{:S(2)}) async-start(f32[16,16,512]{2,1,0:T(8,128)} %shard_map.61), calls=%async_computation.3 | async-start | bytes 1048576 | tf_op jit(solution)/shard_map/all_to_all | solution.py:171
  93.8 0.8 bitcast_convert_fusion
  94.6 10.9 %all-to-all-done.3 = f32[16,16,512]{2,1,0:T(8,128)S(1)} async-done(((f32[16,16,512]{2,1,0:T(8,128)}), f32[16,16,512]{2,1,0:T(8,128)S(1)}, u32[]{:S(2)}, u32[]{:S(2)}) %all-to-all-start.3) | async-done | bytes 524320 | tf_op jit(solution)/shard_map/all_to_all | solution.py:171
  105.6 1.6 %collective-permute-start.4 = (bf16[2,128,512]{2,1,0:T(8,128)(2,1)S(1)}, bf16[2,128,512]{2,1,0:T(8,128)(2,1)S(1)}, u32[]{:S(2)}, u32[]{:S(2)}) collective-permute-start(bf16[2,128,512]{2,1,0:T(8,128)(2,1)S(1)} %bitcast_convert_fusion.1.refs_0_), channel_id=1, source_target_pairs={{0,2},{1,3},{2,0},{3,1},{4,6},{5,7},{6,4},{7,5},{8,10},{9,11},{10,... | collective-permute-start | bytes 786440 | tf_op jit(solution)/shard_map/ppermute | solution.py:52
  107.2 8.5 %collective-permute-done.4.refs_1_ = bf16[2,128,512]{2,1,0:T(8,128)(2,1)S(1)} collective-permute-done((bf16[2,128,512]{2,1,0:T(8,128)(2,1)S(1)}, bf16[2,128,512]{2,1,0:T(8,128)(2,1)S(1)}, u32[]{:S(2)}, u32[]{:S(2)}) %collective-permute-start.4) | collective-permute-done | bytes 262176 | tf_op jit(solution)/shard_map/ppermute | solution.py:52
  115.7 1.4 %collective-permute-done.6.refs_3_ = bf16[2,128,512]{2,1,0:T(8,128)(2,1)S(1)} collective-permute-done((bf16[2,128,512]{2,1,0:T(8,128)(2,1)S(1)}, bf16[2,128,512]{2,1,0:T(8,128)(2,1)S(1)}, u32[]{:S(2)}, u32[]{:S(2)}) %collective-permute-start.6) | collective-permute-done | bytes 262176 | tf_op jit(solution)/shard_map/ppermute | solution.py:52
  117.2 0.7 copy-done.10
  117.9 1.3 copy.50
  119.2 3.5 %shard_map.62 = f32[2,512,128]{2,1,0:T(8,128)} custom-call(s32[1]{0:T(128)} %bitcast.10.me_ref, bf16[512,2048]{1,0:T(8,128)(2,1)} %l_ref.3, bf16[2,128,512]{2,1,0:T(8,128)(2,1)} %copy-done.4, bf16[2,128,512]{2,1,0:T(8,128)(2,1)} %copy-done.8, bf16[2,128,512]{2,1,0:T(8,128)(2,1)} %copy-done.9, bf16[2,128,512]{2,1,0:T(8,128)(2,1)} %copy-done.10), custom_call_target="tpu_custom_call" | custom-call | flops 536870912 | bytes 3670016 | tf_op jit(solution)/shard_map/pallas_call | solution.py:179
  122.7 2.0 %fusion.2 = f32[512,2,128]{2,0,1:T(8,128)S(1)} fusion(bf16[2,128,2048]{2,1,0:T(8,128)(2,1)} %all-gather.2.cloned.1.call-done, bf16[512,2048]{1,0:T(8,128)(2,1)S(1)} %copy-done), kind=kOutput, calls=%fused_computation.2 | convolution fusion | flops 536870912 | bytes 3670016 | tf_op jit(solution)/shard_map/so,gyo->sgy/dot_general | solution.py:195
  124.9 1.8 %copy.51 = f32[512,2,256]{2,1,0:T(2,128)} copy(f32[512,2,256]{2,0,1:T(8,128)S(1)} %pad_maximum_fusion.1) | data formatting | bytes 2097152
  (49 shorter events, 3.8 us)
Async XLA Ops:
  11.8 24.5 %all-to-all-start = ((bf16[8,80,512]{2,1,0:T(8,128)(2,1)}), bf16[8,80,512]{2,1,0:T(8,128)(2,1)S(1)}, u32[]{:S(2)}, u32[]{:S(2)}) async-start(bf16[8,80,512]{2,1,0:T(8,128)(2,1)} %pad_maximum_fusion.2), calls=%async_computation | async-start | bytes 1310720 | tf_op jit(solution)/shard_map/all_to_all | solution.py:123
  36.4 0.8 copy-start.5
  42.0 5.3 %collective-permute-start = (f32[2,256,512]{2,1,0:T(8,128)}, f32[2,256,512]{2,1,0:T(8,128)S(1)}, u32[]{:S(2)}, u32[]{:S(2)}) collective-permute-start(f32[2,256,512]{2,1,0:T(8,128)} %get-tuple-element.21), channel_id=1, source_target_pairs={{0,1},{1,0},{2,3},{3,2},{4,5},{5,4},{6,7},{7,6},{8,9},{9,8},{10,11... | collective-permute-start | bytes 3145736 | tf_op jit(solution)/shard_map/ppermute | solution.py:38
  42.0 20.0 %collective-permute-start.2 = (f32[2,256,512]{2,1,0:T(8,128)}, f32[2,256,512]{2,1,0:T(8,128)S(1)}, u32[]{:S(2)}, u32[]{:S(2)}) collective-permute-start(f32[2,256,512]{2,1,0:T(8,128)} %get-tuple-element.23), channel_id=1, source_target_pairs={{0,1},{1,0},{2,3},{3,2},{4,5},{5,4},{6,7},{7,6},{8,9},{9,8},{10,11... | collective-permute-start | bytes 3145736 | tf_op jit(solution)/shard_map/ppermute | solution.py:38
  43.7 18.4 %all-to-all-start.1 = ((bf16[64,16,256]{2,0,1:T(8,128)(2,1)}), bf16[64,16,256]{2,0,1:T(8,128)(2,1)S(1)}, u32[]{:S(2)}, u32[]{:S(2)}) async-start(bf16[64,16,256]{2,0,1:T(8,128)(2,1)} %copy.45), calls=%async_computation.1 | async-start | bytes 1048576 | tf_op jit(solution)/shard_map/all_to_all | solution.py:130
  47.3 1.0 copy-start.3
  48.3 13.8 %copy-start.2 = (f32[2,256,512]{2,1,0:T(8,128)S(1)}, f32[2,256,512]{2,1,0:T(8,128)}, u32[]{:S(2)}) copy-start(f32[2,256,512]{2,1,0:T(8,128)} %get-tuple-element.22) | copy-start | bytes 3145732
  51.1 14.0 %collective-permute-start.1 = (f32[256,512]{1,0:T(8,128)}, f32[256,512]{1,0:T(8,128)}, u32[]{:S(2)}, u32[]{:S(2)}) collective-permute-start(f32[256,512]{1,0:T(8,128)} %get-tuple-element.44), channel_id=1, source_target_pairs={{0,2},{1,3},{2,0},{3,1},{4,6},{5,7},{6,4},{7,5},{8,10},{9,11},{10,... | collective-permute-start | bytes 1572872 | tf_op jit(solution)/shard_map/ppermute | solution.py:151
  63.3 9.6 %copy-start.7 = (f32[256,512]{1,0:T(8,128)S(1)}, f32[256,512]{1,0:T(8,128)}, u32[]{:S(2)}) copy-start(f32[256,512]{1,0:T(8,128)} %get-tuple-element.27) | copy-start | bytes 1572868
  67.2 20.8 %all-to-all-start.2 = ((f32[16,16,512]{2,1,0:T(8,128)}), f32[16,16,512]{2,1,0:T(8,128)S(1)}, u32[]{:S(2)}, u32[]{:S(2)}) async-start(f32[16,16,512]{2,1,0:T(8,128)} %shard_map.60), calls=%async_computation.2 | async-start | bytes 1048576 | tf_op jit(solution)/shard_map/all_to_all | solution.py:171
  72.9 12.2 %collective-permute-start.3 = (f32[256,512]{1,0:T(8,128)S(1)}, f32[256,512]{1,0:T(8,128)S(1)}, u32[]{:S(2)}, u32[]{:S(2)}) collective-permute-start(f32[256,512]{1,0:T(8,128)S(1)} %copy-done.7), channel_id=1, source_target_pairs={{0,2},{1,3},{2,0},{3,1},{4,6},{5,7},{6,4},{7,5},{8,10},{9,11},{10,... | collective-permute-start | bytes 1572872 | tf_op jit(solution)/shard_map/ppermute | solution.py:155
  85.1 0.8 copy-start.6
  88.0 17.4 %all-to-all-start.3 = ((f32[16,16,512]{2,1,0:T(8,128)}), f32[16,16,512]{2,1,0:T(8,128)S(1)}, u32[]{:S(2)}, u32[]{:S(2)}) async-start(f32[16,16,512]{2,1,0:T(8,128)} %shard_map.61), calls=%async_computation.3 | async-start | bytes 1048576 | tf_op jit(solution)/shard_map/all_to_all | solution.py:171
  93.7 29.0 %all-gather.2.cloned.1.call-start = ((), (), s32[]{:S(2)}) async-start(), calls=%async_computation.4 | async-start | bytes 1310720 | tf_op jit(solution)/shard_map/all_gather | solution.py:194
  105.6 13.6 %copy-start.4 = (bf16[2,128,512]{2,1,0:T(8,128)(2,1)}, bf16[2,128,512]{2,1,0:T(8,128)(2,1)S(1)}, u32[]{:S(2)}) copy-start(bf16[2,128,512]{2,1,0:T(8,128)(2,1)S(1)} %bitcast_convert_fusion.1.refs_0_) | copy-start | bytes 786436
  105.6 10.1 %collective-permute-start.4 = (bf16[2,128,512]{2,1,0:T(8,128)(2,1)S(1)}, bf16[2,128,512]{2,1,0:T(8,128)(2,1)S(1)}, u32[]{:S(2)}, u32[]{:S(2)}) collective-permute-start(bf16[2,128,512]{2,1,0:T(8,128)(2,1)S(1)} %bitcast_convert_fusion.1.refs_0_), channel_id=1, source_target_pairs={{0,2},{1,3},{2,0},{3,1},{4,6},{5,7},{6,4},{7,5},{8,10},{9,11},{10,... | collective-permute-start | bytes 786440 | tf_op jit(solution)/shard_map/ppermute | solution.py:52
  107.2 8.5 %collective-permute-start.5 = (bf16[2,128,512]{2,1,0:T(8,128)(2,1)S(1)}, bf16[2,128,512]{2,1,0:T(8,128)(2,1)S(1)}, u32[]{:S(2)}, u32[]{:S(2)}) collective-permute-start(bf16[2,128,512]{2,1,0:T(8,128)(2,1)S(1)} %bitcast_convert_fusion.1.refs_0_), channel_id=1, source_target_pairs={{0,1},{1,0},{2,3},{3,2},{4,5},{5,4},{6,7},{7,6},{8,9},{9,8},{10,11... | collective-permute-start | bytes 786440 | tf_op jit(solution)/shard_map/ppermute | solution.py:52
  115.6 3.5 %copy-start.8 = (bf16[2,128,512]{2,1,0:T(8,128)(2,1)}, bf16[2,128,512]{2,1,0:T(8,128)(2,1)S(1)}, u32[]{:S(2)}) copy-start(bf16[2,128,512]{2,1,0:T(8,128)(2,1)S(1)} %collective-permute-done.4.refs_1_) | copy-start | bytes 786436
  115.6 1.5 %collective-permute-start.6 = (bf16[2,128,512]{2,1,0:T(8,128)(2,1)S(1)}, bf16[2,128,512]{2,1,0:T(8,128)(2,1)S(1)}, u32[]{:S(2)}, u32[]{:S(2)}) collective-permute-start(bf16[2,128,512]{2,1,0:T(8,128)(2,1)S(1)} %collective-permute-done.4.refs_1_), channel_id=1, source_target_pairs={{0,1},{1,0},{2,3},{3,2},{4,5},{5,4},{6,7},{7,6},{8,9},{9,8},{10,11... | collective-permute-start | bytes 786440 | tf_op jit(solution)/shard_map/ppermute | solution.py:52
  115.7 3.5 %copy-start.9 = (bf16[2,128,512]{2,1,0:T(8,128)(2,1)}, bf16[2,128,512]{2,1,0:T(8,128)(2,1)S(1)}, u32[]{:S(2)}) copy-start(bf16[2,128,512]{2,1,0:T(8,128)(2,1)S(1)} %collective-permute-done.5.refs_2_) | copy-start | bytes 786436
  117.2 0.7 copy-start.10
  119.2 3.5 %copy-start = (bf16[512,2048]{1,0:T(8,128)(2,1)S(1)}, bf16[512,2048]{1,0:T(8,128)(2,1)}, u32[]{:S(2)}) copy-start(bf16[512,2048]{1,0:T(8,128)(2,1)} %l_ref.3) | copy-start | bytes 6291460
  122.7 2.0 %copy-start.1 = (f32[2,512,128]{2,1,0:T(8,128)S(1)}, f32[2,512,128]{2,1,0:T(8,128)}, u32[]{:S(2)}) copy-start(f32[2,512,128]{2,1,0:T(8,128)} %shard_map.62) | copy-start | bytes 1572868
Sparse Core Ops, SparseCore 0:
  96.1 20.0 all-gather.1

commit v15 on v13

--- a/solution.py
+++ b/solution.py
@@ -168,28 +168,22 @@
         )(decay_all, kept, received)
         gathered = lax.all_to_all(smoothed_here, "tm", split_axis=0, concat_axis=1, tiled=True)
         rounded = gathered.astype(jnp.bfloat16)
-        if chunk == CHUNKS - 1:
-            pieces = doubling_gather(rounded, "state")
-            slab_hours, width, _ = rounded.shape
-            fitted = vmem_call(
-                fitted_kernel,
-                jax.ShapeDtypeStruct((slab_hours, stations_here, width), jnp.float32),
-                1 + len(pieces),
-                pl.CostEstimate(
-                    flops=2 * stations_here * slab_hours * width * all_comps,
-                    bytes_accessed=2 * stations_here * all_comps
-                    + 2 * slab_hours * width * all_comps
-                    + 4 * slab_hours * stations_here * width,
-                    transcendentals=0,
-                ),
-                scalars=1,
-            )(lax.axis_index("state").reshape(1).astype(jnp.int32), loadings, *pieces)
-            fitted = jnp.transpose(fitted, (1, 0, 2))
-        else:
-            full = lax.all_gather(rounded, "state", axis=2, tiled=True)
-            fitted = jnp.einsum(
-                "so,gyo->sgy", loadings, full, preferred_element_type=jnp.float32
-            )
+        pieces = doubling_gather(rounded, "state")
+        slab_hours, width, _ = rounded.shape
+        fitted = vmem_call(
+            fitted_kernel,
+            jax.ShapeDtypeStruct((slab_hours, stations_here, width), jnp.float32),
+            1 + len(pieces),
+            pl.CostEstimate(
+                flops=2 * stations_here * slab_hours * width * all_comps,
+                bytes_accessed=2 * stations_here * all_comps
+                + 2 * slab_hours * width * all_comps
+                + 4 * slab_hours * stations_here * width,
+                transcendentals=0,
+            ),
+            scalars=1,
+        )(lax.axis_index("state").reshape(1).astype(jnp.int32), loadings, *pieces)
+        fitted = jnp.transpose(fitted, (1, 0, 2))
         low = chunk * members // CHUNKS
         picked = by_hour[:, :, low:low + members // CHUNKS]
         residual_parts.append(picked.astype(jnp.float32) - fitted)

time: 133 us -> 118 us (0.89)
  between operations: 14.2 us -> 0.87 us
  waiting for transfers between devices: 57.2 us -> 51.9 us
  Pallas kernels: 13 us -> 16.8 us
  starting transfers between devices: 27.4 us -> 29.6 us
  matrix products: 2.02 us -> 0 us
    ppermute x3 -> x6, waiting for transfers between devices: 8.72 us -> 4.26 us  [doubling_gather(): pieces = pieces + [lax.ppermute(piece, axis, pairs) for piece in pieces]]
    pallas_call x1 -> x2, Pallas kernels: 3.85 us -> 7.71 us  [local(): vmem_call(fitted_kernel, jax.ShapeDtypeStruct((slab_hours, stations_here,...]
    ppermute x3 -> x6, starting transfers between devices: 1.59 us -> 3.77 us  [doubling_gather(): pieces = pieces + [lax.ppermute(piece, axis, pairs) for piece in pieces]]
    dot_general x1 -> x0, matrix products: 2.02 us -> none  [local(): jnp.einsum('so,gyo->sgy', loadings, full, preferred_element_type=jnp.floa...]
    all_to_all x1, waiting for transfers between devices: 7.82 us -> 9.19 us  [local(): lax.all_to_all(masked_later, 'tm', split_axis=1, concat_axis=0, tiled=True)]
    ppermute x1, waiting for transfers between devices: 1.82 us -> 0.46 us  [local(): received = lax.ppermute(outgoing, 'state', pairs)]
    unnamed x23 -> x25, local copies, waits for them, and re-layouts: 7.83 us -> 7.12 us
  transfers between devices with their start and end apart: 12 -> 14, of which waited for: 7 -> 6; matrix products, arithmetic and copies ran while one was open for 7% -> 7% of each run, Pallas kernels for 5% -> 5%
where the time goes in v15:
time: 118 us; the launch traced here: 117 us
  waiting for transfers between devices  51.9 us (44%)
  starting transfers between devices  29.6 us (25%)
  Pallas kernels  16.8 us (14%)
  local copies, waits for them, and re-layouts  9.69 us (8%)
  other arithmetic  8.11 us (7%)
    all_to_all x1, waiting for transfers between devices, local(): lax.all_to_all(outgoing, 'tm', split_axis=0, concat_axis=0, tiled=True)  17.3 us
    all_to_all x2, starting transfers between devices, local(): lax.all_to_all(smoothed_here, 'tm', split_axis=0, concat_axis=1, tiled=True)  11.3 us
    ppermute x1, waiting for transfers between devices, local(): lax.ppermute(o, 'state', last[c + 1][2])  10.6 us
    all_to_all x2, waiting for transfers between devices, local(): lax.all_to_all(smoothed_here, 'tm', split_axis=0, concat_axis=1, tiled=True)  10.1 us
    all_to_all x1, waiting for transfers between devices, local(): lax.all_to_all(masked_later, 'tm', split_axis=1, concat_axis=0, tiled=True)  9.19 us
    pallas_call x2, Pallas kernels, local(): vmem_call(fitted_kernel, jax.ShapeDtypeStruct((slab_hours, stations_here,...  7.71 us
    all_to_all x1, starting transfers between devices, local(): lax.all_to_all(outgoing, 'tm', split_axis=0, concat_axis=0, tiled=True)  7.25 us
    unnamed x25, local copies, waits for them, and re-layouts  7.12 us
  transfers between devices with their start and end apart: 14, of which 6 were waited for; matrix products, arithmetic and copies ran while one was open for 7% of the time, Pallas kernels for 5%

profile of v15, /device:TPU:0, one launch (start us, length us, event | category | flops | bytes accessed | tf_op | source)
XLA Modules:
  0.0 117.0 jit_solution(8910997702328582593)
XLA Ops:
  0.6 0.7 convert_element_type.29
  1.3 0.7 fusion.5
  2.1 1.7 %copy.37 = bf16[64,16,256]{0,2,1:T(8,128)(2,1)S(1)} copy(bf16[64,16,256]{2,1,0:T(8,128)(2,1)} %param.4) | data formatting | bytes 1048576 | tf_op args[0]
  4.4 0.9 pad_maximum_fusion.2
  5.3 7.3 %all-to-all-start = ((bf16[8,80,512]{2,1,0:T(8,128)(2,1)}), bf16[8,80,512]{2,1,0:T(8,128)(2,1)S(1)}, u32[]{:S(2)}, u32[]{:S(2)}) async-start(bf16[8,80,512]{2,1,0:T(8,128)(2,1)} %pad_maximum_fusion.2), calls=%async_computation | async-start | bytes 1310720 | tf_op jit(solution)/shard_map/all_to_all | solution.py:121
  12.6 17.3 %all-to-all-done.x_ref = bf16[8,80,512]{2,1,0:T(8,128)(2,1)S(1)} async-done(((bf16[8,80,512]{2,1,0:T(8,128)(2,1)}), bf16[8,80,512]{2,1,0:T(8,128)(2,1)S(1)}, u32[]{:S(2)}, u32[]{:S(2)}) %all-to-all-start) | async-done | bytes 655392 | tf_op jit(solution)/shard_map/all_to_all | solution.py:121
  29.9 0.8 copy-done.5
  30.7 4.8 %shard_map.59 = (f32[2,256,512]{2,1,0:T(8,128)}, f32[2,256,512]{2,1,0:T(8,128)}, f32[2,256,512]{2,1,0:T(8,128)}, f32[2,256,512]{2,1,0:T(8,128)}) custom-call(s32[1]{0:T(128)} %bitcast.10.me_ref, bf16[8,80,512]{2,1,0:T(8,128)(2,1)} %copy-done.5, bf16[512,2048]{1,0:T(8,128)(2,1)} %l_ref.5), custom_call_target="tpu_custom_call" | custom-call | flops 1073741824 | bytes 6815744 | tf_op jit(solution)/shard_map/pallas_call | solution.py:133
  36.0 1.2 copy.42
  37.2 3.6 %all-to-all-start.1 = ((bf16[64,16,256]{2,0,1:T(8,128)(2,1)}), bf16[64,16,256]{2,0,1:T(8,128)(2,1)S(1)}, u32[]{:S(2)}, u32[]{:S(2)}) async-start(bf16[64,16,256]{2,0,1:T(8,128)(2,1)} %copy.42), calls=%async_computation.1 | async-start | bytes 1048576 | tf_op jit(solution)/shard_map/all_to_all | solution.py:128
  40.8 2.4 %fusion.2 = (f32[256,512]{1,0:T(8,128)}, f32[256,512]{1,0:T(8,128)}) fusion(f32[2,256,512]{2,1,0:T(8,128)} %collective-permute-done, f32[2,256,512]{2,1,0:T(8,128)S(1)} %copy-done.2), kind=kLoop, calls=%fused_computation.8 | loop fusion | flops 262144 | bytes 3145728 | tf_op jit(solution)/shard_map/add | solution.py:40
  43.2 1.5 %collective-permute-start.1 = (f32[256,512]{1,0:T(8,128)}, f32[256,512]{1,0:T(8,128)}, u32[]{:S(2)}, u32[]{:S(2)}) collective-permute-start(f32[256,512]{1,0:T(8,128)} %get-tuple-element.34), channel_id=1, source_target_pairs={{0,2},{1,3},{2,0},{3,1},{4,6},{5,7},{6,4},{7,5},{8,10},{9,11},{10,... | collective-permute-start | bytes 1572872 | tf_op jit(solution)/shard_map/ppermute | solution.py:149
  44.7 0.8 slice_convert_fusion
  46.3 9.2 %all-to-all-done.1 = bf16[64,16,256]{2,0,1:T(8,128)(2,1)S(1)} async-done(((bf16[64,16,256]{2,0,1:T(8,128)(2,1)}), bf16[64,16,256]{2,0,1:T(8,128)(2,1)S(1)}, u32[]{:S(2)}, u32[]{:S(2)}) %all-to-all-start.1) | async-done | bytes 524320 | tf_op jit(solution)/shard_map/all_to_all | solution.py:128
  55.6 1.2 %fusion = (f32[256,512]{1,0:T(8,128)}, f32[256,512]{1,0:T(8,128)}) fusion(f32[2,256,512]{2,1,0:T(8,128)S(1)} %collective-permute-done.2, f32[2,256,512]{2,1,0:T(8,128)S(1)} %copy-done.1), kind=kLoop, calls=%fused_computation.4 | loop fusion | flops 262144 | bytes 3145728 | tf_op jit(solution)/shard_map/add | solution.py:40
  57.2 2.2 %shard_map.60 = f32[16,16,512]{2,1,0:T(8,128)} custom-call(f32[16,512]{1,0:T(8,128)} %add.40.rate_ref, f32[16,16,512]{2,1,0:T(8,128)} %bitcast.53, f32[16,16,512]{2,1,0:T(8,128)} %bitcast.16.received_ref), custom_call_target="tpu_custom_call" | custom-call | flops 786432 | bytes 1572864 | tf_op jit(solution)/shard_map/pallas_call | solution.py:159
  59.4 5.6 %all-to-all-start.2 = ((f32[16,16,512]{2,1,0:T(8,128)}), f32[16,16,512]{2,1,0:T(8,128)S(1)}, u32[]{:S(2)}, u32[]{:S(2)}) async-start(f32[16,16,512]{2,1,0:T(8,128)} %shard_map.60), calls=%async_computation.2 | async-start | bytes 1048576 | tf_op jit(solution)/shard_map/all_to_all | solution.py:169
  65.1 1.6 %collective-permute-start.3 = (f32[256,512]{1,0:T(8,128)S(1)}, f32[256,512]{1,0:T(8,128)S(1)}, u32[]{:S(2)}, u32[]{:S(2)}) collective-permute-start(f32[256,512]{1,0:T(8,128)S(1)} %copy-done.7), channel_id=1, source_target_pairs={{0,2},{1,3},{2,0},{3,1},{4,6},{5,7},{6,4},{7,5},{8,10},{9,11},{10,... | collective-permute-start | bytes 1572872 | tf_op jit(solution)/shard_map/ppermute | solution.py:153
  66.7 10.6 %collective-permute-done.3 = f32[256,512]{1,0:T(8,128)S(1)} collective-permute-done((f32[256,512]{1,0:T(8,128)S(1)}, f32[256,512]{1,0:T(8,128)S(1)}, u32[]{:S(2)}, u32[]{:S(2)}) %collective-permute-start.3) | collective-permute-done | bytes 524320 | tf_op jit(solution)/shard_map/ppermute | solution.py:153
  77.3 0.8 copy-done.6
  78.1 2.1 %shard_map.61 = f32[16,16,512]{2,1,0:T(8,128)} custom-call(f32[16,512]{1,0:T(8,128)} %add.40.rate_ref, f32[16,16,512]{2,1,0:T(8,128)} %bitcast.56, f32[16,16,512]{2,1,0:T(8,128)} %bitcast.58), custom_call_target="tpu_custom_call" | custom-call | flops 786432 | bytes 1572864 | tf_op jit(solution)/shard_map/pallas_call | solution.py:159
  80.2 5.7 %all-to-all-start.3 = ((f32[16,16,512]{2,1,0:T(8,128)}), f32[16,16,512]{2,1,0:T(8,128)S(1)}, u32[]{:S(2)}, u32[]{:S(2)}) async-start(f32[16,16,512]{2,1,0:T(8,128)} %shard_map.61), calls=%async_computation.3 | async-start | bytes 1048576 | tf_op jit(solution)/shard_map/all_to_all | solution.py:169
  86.0 1.6 %collective-permute-start.4 = (bf16[2,128,512]{2,1,0:T(8,128)(2,1)S(1)}, bf16[2,128,512]{2,1,0:T(8,128)(2,1)S(1)}, u32[]{:S(2)}, u32[]{:S(2)}) collective-permute-start(bf16[2,128,512]{2,1,0:T(8,128)(2,1)S(1)} %bitcast_convert_fusion.1.refs_0_), channel_id=1, source_target_pairs={{0,2},{1,3},{2,0},{3,1},{4,6},{5,7},{6,4},{7,5},{8,10},{9,11},{10,... | collective-permute-start | bytes 786440 | tf_op jit(solution)/shard_map/ppermute | solution.py:52
  87.6 10.1 %all-to-all-done.3 = f32[16,16,512]{2,1,0:T(8,128)S(1)} async-done(((f32[16,16,512]{2,1,0:T(8,128)}), f32[16,16,512]{2,1,0:T(8,128)S(1)}, u32[]{:S(2)}, u32[]{:S(2)}) %all-to-all-start.3) | async-done | bytes 524320 | tf_op jit(solution)/shard_map/all_to_all | solution.py:169
  97.7 1.6 %collective-permute-start.7 = (bf16[2,128,512]{2,1,0:T(8,128)(2,1)S(1)}, bf16[2,128,512]{2,1,0:T(8,128)(2,1)S(1)}, u32[]{:S(2)}, u32[]{:S(2)}) collective-permute-start(bf16[2,128,512]{2,1,0:T(8,128)(2,1)S(1)} %bitcast_convert_fusion.refs_0_), channel_id=1, source_target_pairs={{0,2},{1,3},{2,0},{3,1},{4,6},{5,7},{6,4},{7,5},{8,10},{9,11},{10,... | collective-permute-start | bytes 786440 | tf_op jit(solution)/shard_map/ppermute | solution.py:52
  99.9 4.2 %collective-permute-done.7.refs_1_ = bf16[2,128,512]{2,1,0:T(8,128)(2,1)S(1)} collective-permute-done((bf16[2,128,512]{2,1,0:T(8,128)(2,1)S(1)}, bf16[2,128,512]{2,1,0:T(8,128)(2,1)S(1)}, u32[]{:S(2)}, u32[]{:S(2)}) %collective-permute-start.7) | collective-permute-done | bytes 262176 | tf_op jit(solution)/shard_map/ppermute | solution.py:52
  104.3 1.3 %copy.46 = f32[512,2,256]{2,1,0:T(2,128)} copy(f32[512,2,256]{0,2,1:T(8,128)S(1)} %pad_maximum_fusion) | data formatting | bytes 2097152
  105.6 3.9 %shard_map.62 = f32[2,512,128]{2,1,0:T(8,128)} custom-call(s32[1]{0:T(128)} %bitcast.10.me_ref, bf16[512,2048]{1,0:T(8,128)(2,1)} %l_ref.5, bf16[2,128,512]{2,1,0:T(8,128)(2,1)} %copy-done.3, bf16[2,128,512]{2,1,0:T(8,128)(2,1)} %copy-done.8, bf16[2,128,512]{2,1,0:T(8,128)(2,1)} %collective-permute-done.5.refs_2_, ...), custom_call_target="tpu_custom_call" | custom-call | flops 536870912 | bytes 3670016 | tf_op jit(solution)/shard_map/pallas_call | solution.py:173
  109.5 0.7 copy-done.10
  110.2 3.8 %shard_map.63 = f32[2,512,128]{2,1,0:T(8,128)} custom-call(s32[1]{0:T(128)} %bitcast.10.me_ref, bf16[512,2048]{1,0:T(8,128)(2,1)} %l_ref.5, bf16[2,128,512]{2,1,0:T(8,128)(2,1)} %copy-done.4, bf16[2,128,512]{2,1,0:T(8,128)(2,1)} %copy-done.9, bf16[2,128,512]{2,1,0:T(8,128)(2,1)} %copy-done.10, bf16[2,128,512]{2,1,0:T(8,128)(2,1)} %collective-permute-done.9.refs_3_), custom_call_target="tpu_custom_call" | custom-call | flops 536870912 | bytes 3670016 | tf_op jit(solution)/shard_map/pallas_call | solution.py:173
  114.0 1.1 bitcast_subtract_fusion.1
  115.2 1.8 %copy.47 = f32[512,2,256]{2,1,0:T(2,128)} copy(f32[512,2,256]{2,0,1:T(8,128)S(1)} %pad_maximum_fusion.1) | data formatting | bytes 2097152
  (52 shorter events, 3.3 us)
Async XLA Ops:
  5.3 24.5 %all-to-all-start = ((bf16[8,80,512]{2,1,0:T(8,128)(2,1)}), bf16[8,80,512]{2,1,0:T(8,128)(2,1)S(1)}, u32[]{:S(2)}, u32[]{:S(2)}) async-start(bf16[8,80,512]{2,1,0:T(8,128)(2,1)} %pad_maximum_fusion.2), calls=%async_computation | async-start | bytes 1310720 | tf_op jit(solution)/shard_map/all_to_all | solution.py:121
  29.9 0.8 copy-start.5
  35.5 5.3 %collective-permute-start = (f32[2,256,512]{2,1,0:T(8,128)}, f32[2,256,512]{2,1,0:T(8,128)}, u32[]{:S(2)}, u32[]{:S(2)}) collective-permute-start(f32[2,256,512]{2,1,0:T(8,128)} %get-tuple-element.16), channel_id=1, source_target_pairs={{0,1},{1,0},{2,3},{3,2},{4,5},{5,4},{6,7},{7,6},{8,9},{9,8},{10,11... | collective-permute-start | bytes 3145736 | tf_op jit(solution)/shard_map/ppermute | solution.py:38
  35.5 5.3 %copy-start.2 = (f32[2,256,512]{2,1,0:T(8,128)S(1)}, f32[2,256,512]{2,1,0:T(8,128)}, u32[]{:S(2)}) copy-start(f32[2,256,512]{2,1,0:T(8,128)} %get-tuple-element.15) | copy-start | bytes 3145732
  35.5 20.1 %collective-permute-start.2 = (f32[2,256,512]{2,1,0:T(8,128)}, f32[2,256,512]{2,1,0:T(8,128)S(1)}, u32[]{:S(2)}, u32[]{:S(2)}) collective-permute-start(f32[2,256,512]{2,1,0:T(8,128)} %get-tuple-element.18), channel_id=1, source_target_pairs={{0,1},{1,0},{2,3},{3,2},{4,5},{5,4},{6,7},{7,6},{8,9},{9,8},{10,11... | collective-permute-start | bytes 3145736 | tf_op jit(solution)/shard_map/ppermute | solution.py:38
  37.2 18.4 %all-to-all-start.1 = ((bf16[64,16,256]{2,0,1:T(8,128)(2,1)}), bf16[64,16,256]{2,0,1:T(8,128)(2,1)S(1)}, u32[]{:S(2)}, u32[]{:S(2)}) async-start(bf16[64,16,256]{2,0,1:T(8,128)(2,1)} %copy.42), calls=%async_computation.1 | async-start | bytes 1048576 | tf_op jit(solution)/shard_map/all_to_all | solution.py:128
  43.2 12.4 %copy-start.1 = (f32[2,256,512]{2,1,0:T(8,128)S(1)}, f32[2,256,512]{2,1,0:T(8,128)}, u32[]{:S(2)}) copy-start(f32[2,256,512]{2,1,0:T(8,128)} %get-tuple-element.17) | copy-start | bytes 3145732
  43.2 14.0 %collective-permute-start.1 = (f32[256,512]{1,0:T(8,128)}, f32[256,512]{1,0:T(8,128)}, u32[]{:S(2)}, u32[]{:S(2)}) collective-permute-start(f32[256,512]{1,0:T(8,128)} %get-tuple-element.34), channel_id=1, source_target_pairs={{0,2},{1,3},{2,0},{3,1},{4,6},{5,7},{6,4},{7,5},{8,10},{9,11},{10,... | collective-permute-start | bytes 1572872 | tf_op jit(solution)/shard_map/ppermute | solution.py:149
  57.2 7.8 %copy-start.7 = (f32[256,512]{1,0:T(8,128)S(1)}, f32[256,512]{1,0:T(8,128)}, u32[]{:S(2)}) copy-start(f32[256,512]{1,0:T(8,128)} %get-tuple-element.22) | copy-start | bytes 1572868
  59.4 20.8 %all-to-all-start.2 = ((f32[16,16,512]{2,1,0:T(8,128)}), f32[16,16,512]{2,1,0:T(8,128)S(1)}, u32[]{:S(2)}, u32[]{:S(2)}) async-start(f32[16,16,512]{2,1,0:T(8,128)} %shard_map.60), calls=%async_computation.2 | async-start | bytes 1048576 | tf_op jit(solution)/shard_map/all_to_all | solution.py:169
  65.1 12.2 %collective-permute-start.3 = (f32[256,512]{1,0:T(8,128)S(1)}, f32[256,512]{1,0:T(8,128)S(1)}, u32[]{:S(2)}, u32[]{:S(2)}) collective-permute-start(f32[256,512]{1,0:T(8,128)S(1)} %copy-done.7), channel_id=1, source_target_pairs={{0,2},{1,3},{2,0},{3,1},{4,6},{5,7},{6,4},{7,5},{8,10},{9,11},{10,... | collective-permute-start | bytes 1572872 | tf_op jit(solution)/shard_map/ppermute | solution.py:153
  77.3 0.8 copy-start.6
  80.2 17.4 %all-to-all-start.3 = ((f32[16,16,512]{2,1,0:T(8,128)}), f32[16,16,512]{2,1,0:T(8,128)S(1)}, u32[]{:S(2)}, u32[]{:S(2)}) async-start(f32[16,16,512]{2,1,0:T(8,128)} %shard_map.61), calls=%async_computation.3 | async-start | bytes 1048576 | tf_op jit(solution)/shard_map/all_to_all | solution.py:169
  86.0 18.3 %copy-start.3 = (bf16[2,128,512]{2,1,0:T(8,128)(2,1)}, bf16[2,128,512]{2,1,0:T(8,128)(2,1)S(1)}, u32[]{:S(2)}) copy-start(bf16[2,128,512]{2,1,0:T(8,128)(2,1)S(1)} %bitcast_convert_fusion.1.refs_0_) | copy-start | bytes 786436
  86.0 13.4 %collective-permute-start.4 = (bf16[2,128,512]{2,1,0:T(8,128)(2,1)S(1)}, bf16[2,128,512]{2,1,0:T(8,128)(2,1)S(1)}, u32[]{:S(2)}, u32[]{:S(2)}) collective-permute-start(bf16[2,128,512]{2,1,0:T(8,128)(2,1)S(1)} %bitcast_convert_fusion.1.refs_0_), channel_id=1, source_target_pairs={{0,2},{1,3},{2,0},{3,1},{4,6},{5,7},{6,4},{7,5},{8,10},{9,11},{10,... | collective-permute-start | bytes 786440 | tf_op jit(solution)/shard_map/ppermute | solution.py:52
  97.7 7.8 %copy-start.4 = (bf16[2,128,512]{2,1,0:T(8,128)(2,1)}, bf16[2,128,512]{2,1,0:T(8,128)(2,1)S(1)}, u32[]{:S(2)}) copy-start(bf16[2,128,512]{2,1,0:T(8,128)(2,1)S(1)} %bitcast_convert_fusion.refs_0_) | copy-start | bytes 786436
  97.7 6.4 %collective-permute-start.7 = (bf16[2,128,512]{2,1,0:T(8,128)(2,1)S(1)}, bf16[2,128,512]{2,1,0:T(8,128)(2,1)S(1)}, u32[]{:S(2)}, u32[]{:S(2)}) collective-permute-start(bf16[2,128,512]{2,1,0:T(8,128)(2,1)S(1)} %bitcast_convert_fusion.refs_0_), channel_id=1, source_target_pairs={{0,2},{1,3},{2,0},{3,1},{4,6},{5,7},{6,4},{7,5},{8,10},{9,11},{10,... | collective-permute-start | bytes 786440 | tf_op jit(solution)/shard_map/ppermute | solution.py:52
  99.3 6.2 %collective-permute-start.5 = (bf16[2,128,512]{2,1,0:T(8,128)(2,1)S(1)}, bf16[2,128,512]{2,1,0:T(8,128)(2,1)}, u32[]{:S(2)}, u32[]{:S(2)}) collective-permute-start(bf16[2,128,512]{2,1,0:T(8,128)(2,1)S(1)} %bitcast_convert_fusion.1.refs_0_), channel_id=1, source_target_pairs={{0,1},{1,0},{2,3},{3,2},{4,5},{5,4},{6,7},{7,6},{8,9},{9,8},{10,11... | collective-permute-start | bytes 786440 | tf_op jit(solution)/shard_map/ppermute | solution.py:52
  99.3 6.2 %copy-start.8 = (bf16[2,128,512]{2,1,0:T(8,128)(2,1)}, bf16[2,128,512]{2,1,0:T(8,128)(2,1)S(1)}, u32[]{:S(2)}) copy-start(bf16[2,128,512]{2,1,0:T(8,128)(2,1)S(1)} %collective-permute-done.4.refs_1_) | copy-start | bytes 786436
  99.4 6.2 %collective-permute-start.6 = (bf16[2,128,512]{2,1,0:T(8,128)(2,1)S(1)}, bf16[2,128,512]{2,1,0:T(8,128)(2,1)}, u32[]{:S(2)}, u32[]{:S(2)}) collective-permute-start(bf16[2,128,512]{2,1,0:T(8,128)(2,1)S(1)} %collective-permute-done.4.refs_1_), channel_id=1, source_target_pairs={{0,1},{1,0},{2,3},{3,2},{4,5},{5,4},{6,7},{7,6},{8,9},{9,8},{10,11... | collective-permute-start | bytes 786440 | tf_op jit(solution)/shard_map/ppermute | solution.py:52
  99.9 9.6 %collective-permute-start.8 = (bf16[2,128,512]{2,1,0:T(8,128)(2,1)S(1)}, bf16[2,128,512]{2,1,0:T(8,128)(2,1)S(1)}, u32[]{:S(2)}, u32[]{:S(2)}) collective-permute-start(bf16[2,128,512]{2,1,0:T(8,128)(2,1)S(1)} %bitcast_convert_fusion.refs_0_), channel_id=1, source_target_pairs={{0,1},{1,0},{2,3},{3,2},{4,5},{5,4},{6,7},{7,6},{8,9},{9,8},{10,11... | collective-permute-start | bytes 786440 | tf_op jit(solution)/shard_map/ppermute | solution.py:52
  104.2 1.4 %copy-start.9 = (bf16[2,128,512]{2,1,0:T(8,128)(2,1)}, bf16[2,128,512]{2,1,0:T(8,128)(2,1)S(1)}, u32[]{:S(2)}) copy-start(bf16[2,128,512]{2,1,0:T(8,128)(2,1)S(1)} %collective-permute-done.7.refs_1_) | copy-start | bytes 786436
  104.2 5.3 %collective-permute-start.9 = (bf16[2,128,512]{2,1,0:T(8,128)(2,1)S(1)}, bf16[2,128,512]{2,1,0:T(8,128)(2,1)}, u32[]{:S(2)}, u32[]{:S(2)}) collective-permute-start(bf16[2,128,512]{2,1,0:T(8,128)(2,1)S(1)} %collective-permute-done.7.refs_1_), channel_id=1, source_target_pairs={{0,1},{1,0},{2,3},{3,2},{4,5},{5,4},{6,7},{7,6},{8,9},{9,8},{10,11... | collective-permute-start | bytes 786440 | tf_op jit(solution)/shard_map/ppermute | solution.py:52
  109.5 4.6 %copy-start = (f32[2,512,128]{2,1,0:T(8,128)S(1)}, f32[2,512,128]{2,1,0:T(8,128)}, u32[]{:S(2)}) copy-start(f32[2,512,128]{2,1,0:T(8,128)} %shard_map.62) | copy-start | bytes 1572868
  109.5 0.7 copy-start.10

commit v16 on v15

--- a/solution.py
+++ b/solution.py
@@ -144,6 +144,7 @@
     )(lax.axis_index("state").reshape(1).astype(jnp.int32), by_member, loadings)
     smoothed_parts = []
     residual_parts = []
+    fitted_parts = []
     last = [halving_stages(halves[2 * c], halves[2 * c + 1], "state") for c in range(CHUNKS)]
     kept, outgoing, pairs = last[0]
     received = lax.ppermute(outgoing, "state", pairs)
@@ -167,6 +168,8 @@
             ),
         )(decay_all, kept, received)
         gathered = lax.all_to_all(smoothed_here, "tm", split_axis=0, concat_axis=1, tiled=True)
+        if fitted_parts:
+            gathered, fitted_parts[-1] = lax.optimization_barrier((gathered, fitted_parts[-1]))
         rounded = gathered.astype(jnp.bfloat16)
         pieces = doubling_gather(rounded, "state")
         slab_hours, width, _ = rounded.shape
@@ -183,11 +186,12 @@
             ),
             scalars=1,
         )(lax.axis_index("state").reshape(1).astype(jnp.int32), loadings, *pieces)
-        fitted = jnp.transpose(fitted, (1, 0, 2))
+        fitted_parts.append(fitted)
+        smoothed_parts.append(jnp.transpose(gathered, (2, 0, 1)))
+    for chunk, fitted in enumerate(fitted_parts):
         low = chunk * members // CHUNKS
         picked = by_hour[:, :, low:low + members // CHUNKS]
-        residual_parts.append(picked.astype(jnp.float32) - fitted)
-        smoothed_parts.append(jnp.transpose(gathered, (2, 0, 1)))
+        residual_parts.append(picked.astype(jnp.float32) - jnp.transpose(fitted, (1, 0, 2)))
     return (
         jnp.concatenate(smoothed_parts, axis=2),
         jnp.concatenate(residual_parts, axis=2),

time: 118 us -> 119 us (level)
    ppermute x6, waiting for transfers between devices: 4.26 us -> 9.97 us  [doubling_gather(): pieces = pieces + [lax.ppermute(piece, axis, pairs) for piece in pieces]]
    all_to_all x2, waiting for transfers between devices: 10.1 us -> 5.24 us  [local(): lax.all_to_all(smoothed_here, 'tm', split_axis=0, concat_axis=1, tiled=True)]
    unnamed x25 -> x29, local copies, waits for them, and re-layouts: 7.12 us -> 8.22 us
  transfers between devices with their start and end apart: 14 -> 14, of which waited for: 6 -> 8; matrix products, arithmetic and copies ran while one was open for 7% -> 7% of each run, Pallas kernels for 5% -> 2%
where the time goes in v16:
time: 119 us; the launch traced here: 118 us
  waiting for transfers between devices  52.8 us (44%)
  starting transfers between devices  29 us (24%)
  Pallas kernels  16.8 us (14%)
  local copies, waits for them, and re-layouts  10.8 us (9%)
  other arithmetic  8.1 us (7%)
    all_to_all x1, waiting for transfers between devices, local(): lax.all_to_all(outgoing, 'tm', split_axis=0, concat_axis=0, tiled=True)  17.3 us
    all_to_all x2, starting transfers between devices, local(): lax.all_to_all(smoothed_here, 'tm', split_axis=0, concat_axis=1, tiled=True)  11.3 us
    ppermute x1, waiting for transfers between devices, local(): lax.ppermute(o, 'state', last[c + 1][2])  10.6 us
    ppermute x6, waiting for transfers between devices, doubling_gather(): pieces = pieces + [lax.ppermute(piece, axis, pairs) for piece in pieces]  9.97 us
    all_to_all x1, waiting for transfers between devices, local(): lax.all_to_all(masked_later, 'tm', split_axis=1, concat_axis=0, tiled=True)  9.2 us
    unnamed x29, local copies, waits for them, and re-layouts  8.22 us
    pallas_call x2, Pallas kernels, local(): vmem_call(fitted_kernel, jax.ShapeDtypeStruct((slab_hours, stations_here,...  7.69 us
    all_to_all x1, starting transfers between devices, local(): lax.all_to_all(outgoing, 'tm', split_axis=0, concat_axis=0, tiled=True)  7.25 us
  transfers between devices with their start and end apart: 14, of which 8 were waited for; matrix products, arithmetic and copies ran while one was open for 7% of the time, Pallas kernels for 2%

profile of v16, /device:TPU:0, one launch (start us, length us, event | category | flops | bytes accessed | tf_op | source)
XLA Modules:
  0.0 118.4 jit_solution(8637306132262850294)
XLA Ops:
  0.6 0.7 convert_element_type.29
  1.3 0.7 fusion.5
  2.1 1.7 %copy.37 = bf16[64,16,256]{0,2,1:T(8,128)(2,1)S(1)} copy(bf16[64,16,256]{2,1,0:T(8,128)(2,1)} %param.4) | data formatting | bytes 1048576 | tf_op args[0]
  4.4 0.9 pad_maximum_fusion.2
  5.3 7.3 %all-to-all-start = ((bf16[8,80,512]{2,1,0:T(8,128)(2,1)}), bf16[8,80,512]{2,1,0:T(8,128)(2,1)S(1)}, u32[]{:S(2)}, u32[]{:S(2)}) async-start(bf16[8,80,512]{2,1,0:T(8,128)(2,1)} %pad_maximum_fusion.2), calls=%async_computation | async-start | bytes 1310720 | tf_op jit(solution)/shard_map/all_to_all | solution.py:121
  12.6 17.3 %all-to-all-done.x_ref = bf16[8,80,512]{2,1,0:T(8,128)(2,1)S(1)} async-done(((bf16[8,80,512]{2,1,0:T(8,128)(2,1)}), bf16[8,80,512]{2,1,0:T(8,128)(2,1)S(1)}, u32[]{:S(2)}, u32[]{:S(2)}) %all-to-all-start) | async-done | bytes 655392 | tf_op jit(solution)/shard_map/all_to_all | solution.py:121
  29.9 0.8 copy-done.5
  30.7 4.8 %shard_map.59 = (f32[2,256,512]{2,1,0:T(8,128)}, f32[2,256,512]{2,1,0:T(8,128)}, f32[2,256,512]{2,1,0:T(8,128)}, f32[2,256,512]{2,1,0:T(8,128)}) custom-call(s32[1]{0:T(128)} %bitcast.10.me_ref, bf16[8,80,512]{2,1,0:T(8,128)(2,1)} %copy-done.5, bf16[512,2048]{1,0:T(8,128)(2,1)} %l_ref.5), custom_call_target="tpu_custom_call" | custom-call | flops 1073741824 | bytes 6815744 | tf_op jit(solution)/shard_map/pallas_call | solution.py:133
  36.0 1.2 copy.42
  37.2 3.6 %all-to-all-start.1 = ((bf16[64,16,256]{2,0,1:T(8,128)(2,1)}), bf16[64,16,256]{2,0,1:T(8,128)(2,1)S(1)}, u32[]{:S(2)}, u32[]{:S(2)}) async-start(bf16[64,16,256]{2,0,1:T(8,128)(2,1)} %copy.42), calls=%async_computation.1 | async-start | bytes 1048576 | tf_op jit(solution)/shard_map/all_to_all | solution.py:128
  40.8 2.4 %fusion.2 = (f32[256,512]{1,0:T(8,128)}, f32[256,512]{1,0:T(8,128)}) fusion(f32[2,256,512]{2,1,0:T(8,128)} %collective-permute-done, f32[2,256,512]{2,1,0:T(8,128)S(1)} %copy-done.2), kind=kLoop, calls=%fused_computation.8 | loop fusion | flops 262144 | bytes 3145728 | tf_op jit(solution)/shard_map/add | solution.py:40
  43.2 1.5 %collective-permute-start.1 = (f32[256,512]{1,0:T(8,128)}, f32[256,512]{1,0:T(8,128)}, u32[]{:S(2)}, u32[]{:S(2)}) collective-permute-start(f32[256,512]{1,0:T(8,128)} %get-tuple-element.38), channel_id=1, source_target_pairs={{0,2},{1,3},{2,0},{3,1},{4,6},{5,7},{6,4},{7,5},{8,10},{9,11},{10,... | collective-permute-start | bytes 1572872 | tf_op jit(solution)/shard_map/ppermute | solution.py:150
  44.7 0.8 slice_convert_fusion
  46.3 9.2 %all-to-all-done.1 = bf16[64,16,256]{2,0,1:T(8,128)(2,1)S(1)} async-done(((bf16[64,16,256]{2,0,1:T(8,128)(2,1)}), bf16[64,16,256]{2,0,1:T(8,128)(2,1)S(1)}, u32[]{:S(2)}, u32[]{:S(2)}) %all-to-all-start.1) | async-done | bytes 524320 | tf_op jit(solution)/shard_map/all_to_all | solution.py:128
  55.6 1.2 fusion
  57.2 2.2 %shard_map.60 = f32[16,16,512]{2,1,0:T(8,128)} custom-call(f32[16,512]{1,0:T(8,128)} %add.40.rate_ref, f32[16,16,512]{2,1,0:T(8,128)} %bitcast.52, f32[16,16,512]{2,1,0:T(8,128)} %bitcast.16.received_ref), custom_call_target="tpu_custom_call" | custom-call | flops 786432 | bytes 1572864 | tf_op jit(solution)/shard_map/pallas_call | solution.py:160
  59.4 5.6 %all-to-all-start.2 = ((f32[16,16,512]{2,1,0:T(8,128)}), f32[16,16,512]{2,1,0:T(8,128)S(1)}, u32[]{:S(2)}, u32[]{:S(2)}) async-start(f32[16,16,512]{2,1,0:T(8,128)} %shard_map.60), calls=%async_computation.2 | async-start | bytes 1048576 | tf_op jit(solution)/shard_map/all_to_all | solution.py:170
  65.1 1.6 %collective-permute-start.3 = (f32[256,512]{1,0:T(8,128)S(1)}, f32[256,512]{1,0:T(8,128)S(1)}, u32[]{:S(2)}, u32[]{:S(2)}) collective-permute-start(f32[256,512]{1,0:T(8,128)S(1)} %copy-done.7), channel_id=1, source_target_pairs={{0,2},{1,3},{2,0},{3,1},{4,6},{5,7},{6,4},{7,5},{8,10},{9,11},{10,... | collective-permute-start | bytes 1572872 | tf_op jit(solution)/shard_map/ppermute | solution.py:154
  66.7 10.6 %collective-permute-done.3 = f32[256,512]{1,0:T(8,128)S(1)} collective-permute-done((f32[256,512]{1,0:T(8,128)S(1)}, f32[256,512]{1,0:T(8,128)S(1)}, u32[]{:S(2)}, u32[]{:S(2)}) %collective-permute-start.3) | collective-permute-done | bytes 524320 | tf_op jit(solution)/shard_map/ppermute | solution.py:154
  77.3 0.8 copy-done.6
  78.1 2.1 %shard_map.61 = f32[16,16,512]{2,1,0:T(8,128)} custom-call(f32[16,512]{1,0:T(8,128)} %add.40.rate_ref, f32[16,16,512]{2,1,0:T(8,128)} %bitcast.56, f32[16,16,512]{2,1,0:T(8,128)} %bitcast.57), custom_call_target="tpu_custom_call" | custom-call | flops 786432 | bytes 1572864 | tf_op jit(solution)/shard_map/pallas_call | solution.py:160
  80.2 5.7 %all-to-all-start.3 = ((f32[16,16,512]{2,1,0:T(8,128)}), f32[16,16,512]{2,1,0:T(8,128)S(1)}, u32[]{:S(2)}, u32[]{:S(2)}) async-start(f32[16,16,512]{2,1,0:T(8,128)} %shard_map.61), calls=%async_computation.3 | async-start | bytes 1048576 | tf_op jit(solution)/shard_map/all_to_all | solution.py:170
  86.0 1.6 %collective-permute-start.4 = (bf16[2,128,512]{2,1,0:T(8,128)(2,1)S(1)}, bf16[2,128,512]{2,1,0:T(8,128)(2,1)S(1)}, u32[]{:S(2)}, u32[]{:S(2)}) collective-permute-start(bf16[2,128,512]{2,1,0:T(8,128)(2,1)S(1)} %bitcast_convert_fusion.refs_0_), channel_id=1, source_target_pairs={{0,2},{1,3},{2,0},{3,1},{4,6},{5,7},{6,4},{7,5},{8,10},{9,11},{10,... | collective-permute-start | bytes 786440 | tf_op jit(solution)/shard_map/ppermute | solution.py:52
  87.6 4.8 %collective-permute-done.4.refs_1_ = bf16[2,128,512]{2,1,0:T(8,128)(2,1)S(1)} collective-permute-done((bf16[2,128,512]{2,1,0:T(8,128)(2,1)S(1)}, bf16[2,128,512]{2,1,0:T(8,128)(2,1)S(1)}, u32[]{:S(2)}, u32[]{:S(2)}) %collective-permute-start.4) | collective-permute-done | bytes 262176 | tf_op jit(solution)/shard_map/ppermute | solution.py:52
  92.4 5.2 %all-to-all-done.3 = f32[16,16,512]{2,1,0:T(8,128)S(1)} async-done(((f32[16,16,512]{2,1,0:T(8,128)}), f32[16,16,512]{2,1,0:T(8,128)S(1)}, u32[]{:S(2)}, u32[]{:S(2)}) %all-to-all-start.3) | async-done | bytes 524320 | tf_op jit(solution)/shard_map/all_to_all | solution.py:170
  99.1 3.8 %shard_map.62 = f32[2,512,128]{2,1,0:T(8,128)} custom-call(s32[1]{0:T(128)} %bitcast.10.me_ref, bf16[512,2048]{1,0:T(8,128)(2,1)} %l_ref.5, bf16[2,128,512]{2,1,0:T(8,128)(2,1)} %copy-done.3, bf16[2,128,512]{2,1,0:T(8,128)(2,1)} %copy-done.8, bf16[2,128,512]{2,1,0:T(8,128)(2,1)} %copy-done.10, bf16[2,128,512]{2,1,0:T(8,128)(2,1)} %copy-done.12), custom_call_target="tpu_custom_call" | custom-call | flops 536870912 | bytes 3670016 | tf_op jit(solution)/shard_map/pallas_call | solution.py:176
  103.0 1.6 %collective-permute-start.7 = (bf16[2,128,512]{2,1,0:T(8,128)(2,1)S(1)}, bf16[2,128,512]{2,1,0:T(8,128)(2,1)S(1)}, u32[]{:S(2)}, u32[]{:S(2)}) collective-permute-start(bf16[2,128,512]{2,1,0:T(8,128)(2,1)S(1)} %convert_element_type.36.refs_0_), channel_id=1, source_target_pairs={{0,2},{1,3},{2,0},{3,1},{4,6},{5,7},{6,4},{7,5},{8,10},{9,11},{10,... | collective-permute-start | bytes 786440 | tf_op jit(solution)/shard_map/ppermute | solution.py:52
  104.6 4.8 %collective-permute-done.7.refs_1_ = bf16[2,128,512]{2,1,0:T(8,128)(2,1)S(1)} collective-permute-done((bf16[2,128,512]{2,1,0:T(8,128)(2,1)S(1)}, bf16[2,128,512]{2,1,0:T(8,128)(2,1)S(1)}, u32[]{:S(2)}, u32[]{:S(2)}) %collective-permute-start.7) | collective-permute-done | bytes 262176 | tf_op jit(solution)/shard_map/ppermute | solution.py:52
  109.5 1.3 %copy.46 = f32[512,2,256]{2,1,0:T(2,128)} copy(f32[512,2,256]{0,2,1:T(8,128)S(1)} %pad_maximum_fusion) | data formatting | bytes 2097152
  111.5 3.8 %shard_map.63 = f32[2,512,128]{2,1,0:T(8,128)} custom-call(s32[1]{0:T(128)} %bitcast.10.me_ref, bf16[512,2048]{1,0:T(8,128)(2,1)} %l_ref.5, bf16[2,128,512]{2,1,0:T(8,128)(2,1)} %copy-done.4, bf16[2,128,512]{2,1,0:T(8,128)(2,1)} %copy-done.9, bf16[2,128,512]{2,1,0:T(8,128)(2,1)} %copy-done.11, bf16[2,128,512]{2,1,0:T(8,128)(2,1)} %collective-permute-done.9.refs_3_), custom_call_target="tpu_custom_call" | custom-call | flops 536870912 | bytes 3670016 | tf_op jit(solution)/shard_map/pallas_call | solution.py:176
  115.4 1.1 bitcast_subtract_fusion.1
  116.6 1.8 %copy.47 = f32[512,2,256]{2,1,0:T(2,128)} copy(f32[512,2,256]{2,0,1:T(8,128)S(1)} %pad_maximum_fusion.1) | data formatting | bytes 2097152
  (56 shorter events, 4.8 us)
Async XLA Ops:
  5.3 24.5 %all-to-all-start = ((bf16[8,80,512]{2,1,0:T(8,128)(2,1)}), bf16[8,80,512]{2,1,0:T(8,128)(2,1)S(1)}, u32[]{:S(2)}, u32[]{:S(2)}) async-start(bf16[8,80,512]{2,1,0:T(8,128)(2,1)} %pad_maximum_fusion.2), calls=%async_computation | async-start | bytes 1310720 | tf_op jit(solution)/shard_map/all_to_all | solution.py:121
  29.9 0.8 copy-start.5
  35.5 5.3 %collective-permute-start = (f32[2,256,512]{2,1,0:T(8,128)}, f32[2,256,512]{2,1,0:T(8,128)}, u32[]{:S(2)}, u32[]{:S(2)}) collective-permute-start(f32[2,256,512]{2,1,0:T(8,128)} %get-tuple-element.18), channel_id=1, source_target_pairs={{0,1},{1,0},{2,3},{3,2},{4,5},{5,4},{6,7},{7,6},{8,9},{9,8},{10,11... | collective-permute-start | bytes 3145736 | tf_op jit(solution)/shard_map/ppermute | solution.py:38
  35.5 5.3 %copy-start.2 = (f32[2,256,512]{2,1,0:T(8,128)S(1)}, f32[2,256,512]{2,1,0:T(8,128)}, u32[]{:S(2)}) copy-start(f32[2,256,512]{2,1,0:T(8,128)} %get-tuple-element.17) | copy-start | bytes 3145732
  35.5 20.1 %collective-permute-start.2 = (f32[2,256,512]{2,1,0:T(8,128)}, f32[2,256,512]{2,1,0:T(8,128)S(1)}, u32[]{:S(2)}, u32[]{:S(2)}) collective-permute-start(f32[2,256,512]{2,1,0:T(8,128)} %get-tuple-element.20), channel_id=1, source_target_pairs={{0,1},{1,0},{2,3},{3,2},{4,5},{5,4},{6,7},{7,6},{8,9},{9,8},{10,11... | collective-permute-start | bytes 3145736 | tf_op jit(solution)/shard_map/ppermute | solution.py:38
  37.2 18.4 %all-to-all-start.1 = ((bf16[64,16,256]{2,0,1:T(8,128)(2,1)}), bf16[64,16,256]{2,0,1:T(8,128)(2,1)S(1)}, u32[]{:S(2)}, u32[]{:S(2)}) async-start(bf16[64,16,256]{2,0,1:T(8,128)(2,1)} %copy.42), calls=%async_computation.1 | async-start | bytes 1048576 | tf_op jit(solution)/shard_map/all_to_all | solution.py:128
  43.2 12.4 %copy-start.1 = (f32[2,256,512]{2,1,0:T(8,128)S(1)}, f32[2,256,512]{2,1,0:T(8,128)}, u32[]{:S(2)}) copy-start(f32[2,256,512]{2,1,0:T(8,128)} %get-tuple-element.19) | copy-start | bytes 3145732
  43.2 14.0 %collective-permute-start.1 = (f32[256,512]{1,0:T(8,128)}, f32[256,512]{1,0:T(8,128)}, u32[]{:S(2)}, u32[]{:S(2)}) collective-permute-start(f32[256,512]{1,0:T(8,128)} %get-tuple-element.38), channel_id=1, source_target_pairs={{0,2},{1,3},{2,0},{3,1},{4,6},{5,7},{6,4},{7,5},{8,10},{9,11},{10,... | collective-permute-start | bytes 1572872 | tf_op jit(solution)/shard_map/ppermute | solution.py:150
  57.2 7.8 %copy-start.7 = (f32[256,512]{1,0:T(8,128)S(1)}, f32[256,512]{1,0:T(8,128)}, u32[]{:S(2)}) copy-start(f32[256,512]{1,0:T(8,128)} %get-tuple-element.24) | copy-start | bytes 1572868
  59.4 20.8 %all-to-all-start.2 = ((f32[16,16,512]{2,1,0:T(8,128)}), f32[16,16,512]{2,1,0:T(8,128)S(1)}, u32[]{:S(2)}, u32[]{:S(2)}) async-start(f32[16,16,512]{2,1,0:T(8,128)} %shard_map.60), calls=%async_computation.2 | async-start | bytes 1048576 | tf_op jit(solution)/shard_map/all_to_all | solution.py:170
  65.1 12.2 %collective-permute-start.3 = (f32[256,512]{1,0:T(8,128)S(1)}, f32[256,512]{1,0:T(8,128)S(1)}, u32[]{:S(2)}, u32[]{:S(2)}) collective-permute-start(f32[256,512]{1,0:T(8,128)S(1)} %copy-done.7), channel_id=1, source_target_pairs={{0,2},{1,3},{2,0},{3,1},{4,6},{5,7},{6,4},{7,5},{8,10},{9,11},{10,... | collective-permute-start | bytes 1572872 | tf_op jit(solution)/shard_map/ppermute | solution.py:154
  77.3 0.8 copy-start.6
  80.2 17.4 %all-to-all-start.3 = ((f32[16,16,512]{2,1,0:T(8,128)}), f32[16,16,512]{2,1,0:T(8,128)S(1)}, u32[]{:S(2)}, u32[]{:S(2)}) async-start(f32[16,16,512]{2,1,0:T(8,128)} %shard_map.61), calls=%async_computation.3 | async-start | bytes 1048576 | tf_op jit(solution)/shard_map/all_to_all | solution.py:170
  86.0 11.8 %copy-start.3 = (bf16[2,128,512]{2,1,0:T(8,128)(2,1)}, bf16[2,128,512]{2,1,0:T(8,128)(2,1)S(1)}, u32[]{:S(2)}) copy-start(bf16[2,128,512]{2,1,0:T(8,128)(2,1)S(1)} %bitcast_convert_fusion.refs_0_) | copy-start | bytes 786436
  86.0 6.4 %collective-permute-start.4 = (bf16[2,128,512]{2,1,0:T(8,128)(2,1)S(1)}, bf16[2,128,512]{2,1,0:T(8,128)(2,1)S(1)}, u32[]{:S(2)}, u32[]{:S(2)}) collective-permute-start(bf16[2,128,512]{2,1,0:T(8,128)(2,1)S(1)} %bitcast_convert_fusion.refs_0_), channel_id=1, source_target_pairs={{0,2},{1,3},{2,0},{3,1},{4,6},{5,7},{6,4},{7,5},{8,10},{9,11},{10,... | collective-permute-start | bytes 786440 | tf_op jit(solution)/shard_map/ppermute | solution.py:52
  87.6 10.1 %collective-permute-start.5 = (bf16[2,128,512]{2,1,0:T(8,128)(2,1)S(1)}, bf16[2,128,512]{2,1,0:T(8,128)(2,1)S(1)}, u32[]{:S(2)}, u32[]{:S(2)}) collective-permute-start(bf16[2,128,512]{2,1,0:T(8,128)(2,1)S(1)} %bitcast_convert_fusion.refs_0_), channel_id=1, source_target_pairs={{0,1},{1,0},{2,3},{3,2},{4,5},{5,4},{6,7},{7,6},{8,9},{9,8},{10,11... | collective-permute-start | bytes 786440 | tf_op jit(solution)/shard_map/ppermute | solution.py:52
  92.4 5.3 %copy-start.8 = (bf16[2,128,512]{2,1,0:T(8,128)(2,1)}, bf16[2,128,512]{2,1,0:T(8,128)(2,1)S(1)}, u32[]{:S(2)}) copy-start(bf16[2,128,512]{2,1,0:T(8,128)(2,1)S(1)} %collective-permute-done.4.refs_1_) | copy-start | bytes 786436
  92.4 5.3 %collective-permute-start.6 = (bf16[2,128,512]{2,1,0:T(8,128)(2,1)S(1)}, bf16[2,128,512]{2,1,0:T(8,128)(2,1)S(1)}, u32[]{:S(2)}, u32[]{:S(2)}) collective-permute-start(bf16[2,128,512]{2,1,0:T(8,128)(2,1)S(1)} %collective-permute-done.4.refs_1_), channel_id=1, source_target_pairs={{0,1},{1,0},{2,3},{3,2},{4,5},{5,4},{6,7},{7,6},{8,9},{9,8},{10,11... | collective-permute-start | bytes 786440 | tf_op jit(solution)/shard_map/ppermute | solution.py:52
  97.7 0.7 copy-start.10
  98.4 0.7 copy-start.12
  103.0 7.8 %copy-start.4 = (bf16[2,128,512]{2,1,0:T(8,128)(2,1)}, bf16[2,128,512]{2,1,0:T(8,128)(2,1)S(1)}, u32[]{:S(2)}) copy-start(bf16[2,128,512]{2,1,0:T(8,128)(2,1)S(1)} %convert_element_type.36.refs_0_) | copy-start | bytes 786436
  103.0 6.4 %collective-permute-start.7 = (bf16[2,128,512]{2,1,0:T(8,128)(2,1)S(1)}, bf16[2,128,512]{2,1,0:T(8,128)(2,1)S(1)}, u32[]{:S(2)}, u32[]{:S(2)}) collective-permute-start(bf16[2,128,512]{2,1,0:T(8,128)(2,1)S(1)} %convert_element_type.36.refs_0_), channel_id=1, source_target_pairs={{0,2},{1,3},{2,0},{3,1},{4,6},{5,7},{6,4},{7,5},{8,10},{9,11},{10,... | collective-permute-start | bytes 786440 | tf_op jit(solution)/shard_map/ppermute | solution.py:52
  104.6 6.2 %collective-permute-start.8 = (bf16[2,128,512]{2,1,0:T(8,128)(2,1)S(1)}, bf16[2,128,512]{2,1,0:T(8,128)(2,1)S(1)}, u32[]{:S(2)}, u32[]{:S(2)}) collective-permute-start(bf16[2,128,512]{2,1,0:T(8,128)(2,1)S(1)} %convert_element_type.36.refs_0_), channel_id=1, source_target_pairs={{0,1},{1,0},{2,3},{3,2},{4,5},{5,4},{6,7},{7,6},{8,9},{9,8},{10,11... | collective-permute-start | bytes 786440 | tf_op jit(solution)/shard_map/ppermute | solution.py:52
  109.4 1.4 %copy-start.9 = (bf16[2,128,512]{2,1,0:T(8,128)(2,1)}, bf16[2,128,512]{2,1,0:T(8,128)(2,1)S(1)}, u32[]{:S(2)}) copy-start(bf16[2,128,512]{2,1,0:T(8,128)(2,1)S(1)} %collective-permute-done.7.refs_1_) | copy-start | bytes 786436
  109.4 1.7 %collective-permute-start.9 = (bf16[2,128,512]{2,1,0:T(8,128)(2,1)S(1)}, bf16[2,128,512]{2,1,0:T(8,128)(2,1)}, u32[]{:S(2)}, u32[]{:S(2)}) collective-permute-start(bf16[2,128,512]{2,1,0:T(8,128)(2,1)S(1)} %collective-permute-done.7.refs_1_), channel_id=1, source_target_pairs={{0,1},{1,0},{2,3},{3,2},{4,5},{5,4},{6,7},{7,6},{8,9},{9,8},{10,11... | collective-permute-start | bytes 786440 | tf_op jit(solution)/shard_map/ppermute | solution.py:52
  110.8 4.6 %copy-start = (f32[2,512,128]{2,1,0:T(8,128)S(1)}, f32[2,512,128]{2,1,0:T(8,128)}, u32[]{:S(2)}) copy-start(f32[2,512,128]{2,1,0:T(8,128)} %shard_map.62) | copy-start | bytes 1572868
  110.8 0.7 copy-start.11

commit v17 on v16

--- a/solution.py
+++ b/solution.py
@@ -43,14 +43,16 @@
     return keep, outgoing, pairs
 
 
-def doubling_gather(block, axis):
+def doubling_gather(block, axis, companion):
     count = lax.axis_size(axis)
     levels = count.bit_length() - 1
     pieces = [block]
     for level in reversed(range(levels)):
         pairs = [(i, i ^ (1 << level)) for i in range(count)]
         pieces = pieces + [lax.ppermute(piece, axis, pairs) for piece in pieces]
-    return pieces
+        if level == levels - 1:
+            pieces, companion = lax.optimization_barrier((pieces, companion))
+    return pieces, companion
 
 
 def fitted_kernel(me_ref, l_ref, *refs):
@@ -168,10 +170,9 @@
             ),
         )(decay_all, kept, received)
         gathered = lax.all_to_all(smoothed_here, "tm", split_axis=0, concat_axis=1, tiled=True)
-        if fitted_parts:
-            gathered, fitted_parts[-1] = lax.optimization_barrier((gathered, fitted_parts[-1]))
         rounded = gathered.astype(jnp.bfloat16)
-        pieces = doubling_gather(rounded, "state")
+        pieces, earlier = doubling_gather(rounded, "state", fitted_parts[-1:])
+        fitted_parts[-1:] = earlier
         slab_hours, width, _ = rounded.shape
         fitted = vmem_call(
             fitted_kernel,

time: 119 us -> 114 us (0.958)
  waiting for transfers between devices: 52.8 us -> 47.6 us
    ppermute x6, waiting for transfers between devices: 9.97 us -> 5.3 us  [doubling_gather(): pieces = pieces + [lax.ppermute(piece, axis, pairs) for piece in pieces]]
    unnamed x29 -> x27, local copies, waits for them, and re-layouts: 8.22 us -> 7.65 us
  transfers between devices with their start and end apart: 14 -> 14, of which waited for: 8 -> 8; matrix products, arithmetic and copies ran while one was open for 7% -> 7% of each run, Pallas kernels for 2% -> 5%
where the time goes in v17:
time: 114 us
  waiting for transfers between devices  47.6 us (42%)
  starting transfers between devices  30 us (26%)
  Pallas kernels  16.9 us (15%)
  local copies, waits for them, and re-layouts  10.2 us (9%)
  other arithmetic  8.11 us (7%)
    all_to_all x1, waiting for transfers between devices, local(): lax.all_to_all(outgoing, 'tm', split_axis=0, concat_axis=0, tiled=True)  17.3 us
    all_to_all x2, starting transfers between devices, local(): lax.all_to_all(smoothed_here, 'tm', split_axis=0, concat_axis=1, tiled=True)  11.3 us
    ppermute x1, waiting for transfers between devices, local(): lax.ppermute(o, 'state', last[c + 1][2])  10.6 us
    all_to_all x1, waiting for transfers between devices, local(): lax.all_to_all(masked_later, 'tm', split_axis=1, concat_axis=0, tiled=True)  9.18 us
    pallas_call x2, Pallas kernels, local(): vmem_call(fitted_kernel, jax.ShapeDtypeStruct((slab_hours, stations_here,...  7.71 us
    unnamed x27, local copies, waits for them, and re-layouts  7.65 us
    all_to_all x1, starting transfers between devices, local(): lax.all_to_all(outgoing, 'tm', split_axis=0, concat_axis=0, tiled=True)  7.25 us
    ppermute x6, waiting for transfers between devices, doubling_gather(): pieces = pieces + [lax.ppermute(piece, axis, pairs) for piece in pieces]  5.3 us
  transfers between devices with their start and end apart: 14, of which 8 were waited for; matrix products, arithmetic and copies ran while one was open for 7% of the time, Pallas kernels for 5%

profile of v17, /device:TPU:0, one launch (start us, length us, event | category | flops | bytes accessed | tf_op | source)
XLA Modules:
  0.0 113.7 jit_solution(762168489515323160)
XLA Ops:
  0.6 0.7 convert_element_type.29
  1.3 0.7 fusion.5
  2.1 1.7 %copy.37 = bf16[64,16,256]{0,2,1:T(8,128)(2,1)S(1)} copy(bf16[64,16,256]{2,1,0:T(8,128)(2,1)} %param.4) | data formatting | bytes 1048576 | tf_op args[0]
  4.4 0.9 pad_maximum_fusion.2
  5.3 7.3 %all-to-all-start = ((bf16[8,80,512]{2,1,0:T(8,128)(2,1)}), bf16[8,80,512]{2,1,0:T(8,128)(2,1)S(1)}, u32[]{:S(2)}, u32[]{:S(2)}) async-start(bf16[8,80,512]{2,1,0:T(8,128)(2,1)} %pad_maximum_fusion.2), calls=%async_computation | async-start | bytes 1310720 | tf_op jit(solution)/shard_map/all_to_all | solution.py:123
  12.6 17.3 %all-to-all-done.x_ref = bf16[8,80,512]{2,1,0:T(8,128)(2,1)S(1)} async-done(((bf16[8,80,512]{2,1,0:T(8,128)(2,1)}), bf16[8,80,512]{2,1,0:T(8,128)(2,1)S(1)}, u32[]{:S(2)}, u32[]{:S(2)}) %all-to-all-start) | async-done | bytes 655392 | tf_op jit(solution)/shard_map/all_to_all | solution.py:123
  29.9 0.8 copy-done.5
  30.7 4.8 %shard_map.59 = (f32[2,256,512]{2,1,0:T(8,128)}, f32[2,256,512]{2,1,0:T(8,128)}, f32[2,256,512]{2,1,0:T(8,128)}, f32[2,256,512]{2,1,0:T(8,128)}) custom-call(s32[1]{0:T(128)} %bitcast.10.me_ref, bf16[8,80,512]{2,1,0:T(8,128)(2,1)} %copy-done.5, bf16[512,2048]{1,0:T(8,128)(2,1)} %l_ref.5), custom_call_target="tpu_custom_call" | custom-call | flops 1073741824 | bytes 6815744 | tf_op jit(solution)/shard_map/pallas_call | solution.py:135
  36.0 1.2 %copy.42 = bf16[64,16,256]{2,0,1:T(8,128)(2,1)} copy(bf16[64,16,256]{0,2,1:T(8,128)(2,1)S(1)} %broadcast_multiply_fusion) | data formatting | bytes 1048576 | tf_op jit(solution)/shard_map/optimization_barrier | solution.py:129
  37.2 3.6 %all-to-all-start.1 = ((bf16[64,16,256]{2,0,1:T(8,128)(2,1)}), bf16[64,16,256]{2,0,1:T(8,128)(2,1)S(1)}, u32[]{:S(2)}, u32[]{:S(2)}) async-start(bf16[64,16,256]{2,0,1:T(8,128)(2,1)} %copy.42), calls=%async_computation.1 | async-start | bytes 1048576 | tf_op jit(solution)/shard_map/all_to_all | solution.py:130
  40.8 2.4 %fusion.2 = (f32[256,512]{1,0:T(8,128)}, f32[256,512]{1,0:T(8,128)}) fusion(f32[2,256,512]{2,1,0:T(8,128)} %collective-permute-done, f32[2,256,512]{2,1,0:T(8,128)S(1)} %copy-done.2), kind=kLoop, calls=%fused_computation.8 | loop fusion | flops 262144 | bytes 3145728 | tf_op jit(solution)/shard_map/add | solution.py:40
  43.2 1.5 %collective-permute-start.1 = (f32[256,512]{1,0:T(8,128)}, f32[256,512]{1,0:T(8,128)}, u32[]{:S(2)}, u32[]{:S(2)}) collective-permute-start(f32[256,512]{1,0:T(8,128)} %get-tuple-element.44), channel_id=1, source_target_pairs={{0,2},{1,3},{2,0},{3,1},{4,6},{5,7},{6,4},{7,5},{8,10},{9,11},{10,... | collective-permute-start | bytes 1572872 | tf_op jit(solution)/shard_map/ppermute | solution.py:152
  44.8 0.8 slice_convert_fusion
  46.4 9.2 %all-to-all-done.1 = bf16[64,16,256]{2,0,1:T(8,128)(2,1)S(1)} async-done(((bf16[64,16,256]{2,0,1:T(8,128)(2,1)}), bf16[64,16,256]{2,0,1:T(8,128)(2,1)S(1)}, u32[]{:S(2)}, u32[]{:S(2)}) %all-to-all-start.1) | async-done | bytes 524320 | tf_op jit(solution)/shard_map/all_to_all | solution.py:130
  55.6 1.2 %fusion = (f32[256,512]{1,0:T(8,128)}, f32[256,512]{1,0:T(8,128)}) fusion(f32[2,256,512]{2,1,0:T(8,128)S(1)} %collective-permute-done.2, f32[2,256,512]{2,1,0:T(8,128)S(1)} %copy-done.1), kind=kLoop, calls=%fused_computation.4 | loop fusion | flops 262144 | bytes 3145728 | tf_op jit(solution)/shard_map/add | solution.py:40
  57.2 2.2 %shard_map.60 = f32[16,16,512]{2,1,0:T(8,128)} custom-call(f32[16,512]{1,0:T(8,128)} %add.40.rate_ref, f32[16,16,512]{2,1,0:T(8,128)} %bitcast.53, f32[16,16,512]{2,1,0:T(8,128)} %bitcast.16.received_ref), custom_call_target="tpu_custom_call" | custom-call | flops 786432 | bytes 1572864 | tf_op jit(solution)/shard_map/pallas_call | solution.py:162
  59.4 5.6 %all-to-all-start.2 = ((f32[16,16,512]{2,1,0:T(8,128)}), f32[16,16,512]{2,1,0:T(8,128)S(1)}, u32[]{:S(2)}, u32[]{:S(2)}) async-start(f32[16,16,512]{2,1,0:T(8,128)} %shard_map.60), calls=%async_computation.2 | async-start | bytes 1048576 | tf_op jit(solution)/shard_map/all_to_all | solution.py:172
  65.1 1.6 %collective-permute-start.3 = (f32[256,512]{1,0:T(8,128)S(1)}, f32[256,512]{1,0:T(8,128)S(1)}, u32[]{:S(2)}, u32[]{:S(2)}) collective-permute-start(f32[256,512]{1,0:T(8,128)S(1)} %copy-done.7), channel_id=1, source_target_pairs={{0,2},{1,3},{2,0},{3,1},{4,6},{5,7},{6,4},{7,5},{8,10},{9,11},{10,... | collective-permute-start | bytes 1572872 | tf_op jit(solution)/shard_map/ppermute | solution.py:156
  66.7 10.6 %collective-permute-done.3 = f32[256,512]{1,0:T(8,128)S(1)} collective-permute-done((f32[256,512]{1,0:T(8,128)S(1)}, f32[256,512]{1,0:T(8,128)S(1)}, u32[]{:S(2)}, u32[]{:S(2)}) %collective-permute-start.3) | collective-permute-done | bytes 524320 | tf_op jit(solution)/shard_map/ppermute | solution.py:156
  77.3 0.8 copy-done.6
  78.1 2.1 %shard_map.61 = f32[16,16,512]{2,1,0:T(8,128)} custom-call(f32[16,512]{1,0:T(8,128)} %add.40.rate_ref, f32[16,16,512]{2,1,0:T(8,128)} %bitcast.57, f32[16,16,512]{2,1,0:T(8,128)} %bitcast.58), custom_call_target="tpu_custom_call" | custom-call | flops 786432 | bytes 1572864 | tf_op jit(solution)/shard_map/pallas_call | solution.py:162
  80.3 5.7 %all-to-all-start.3 = ((f32[16,16,512]{2,1,0:T(8,128)}), f32[16,16,512]{2,1,0:T(8,128)S(1)}, u32[]{:S(2)}, u32[]{:S(2)}) async-start(f32[16,16,512]{2,1,0:T(8,128)} %shard_map.61), calls=%async_computation.3 | async-start | bytes 1048576 | tf_op jit(solution)/shard_map/all_to_all | solution.py:172
  86.0 1.6 %collective-permute-start.5 = (bf16[2,128,512]{2,1,0:T(8,128)(2,1)S(1)}, bf16[2,128,512]{2,1,0:T(8,128)(2,1)S(1)}, u32[]{:S(2)}, u32[]{:S(2)}) collective-permute-start(bf16[2,128,512]{2,1,0:T(8,128)(2,1)S(1)} %bitcast_convert_fusion.refs_0_), channel_id=1, source_target_pairs={{0,2},{1,3},{2,0},{3,1},{4,6},{5,7},{6,4},{7,5},{8,10},{9,11},{10,... | collective-permute-start | bytes 786440 | tf_op jit(solution)/shard_map/ppermute | solution.py:52
  87.6 4.9 %collective-permute-done.5.refs_1_ = bf16[2,128,512]{2,1,0:T(8,128)(2,1)S(1)} collective-permute-done((bf16[2,128,512]{2,1,0:T(8,128)(2,1)S(1)}, bf16[2,128,512]{2,1,0:T(8,128)(2,1)S(1)}, u32[]{:S(2)}, u32[]{:S(2)}) %collective-permute-start.5) | collective-permute-done | bytes 262176 | tf_op jit(solution)/shard_map/ppermute | solution.py:52
  93.0 4.7 %all-to-all-done.3 = f32[16,16,512]{2,1,0:T(8,128)S(1)} async-done(((f32[16,16,512]{2,1,0:T(8,128)}), f32[16,16,512]{2,1,0:T(8,128)S(1)}, u32[]{:S(2)}, u32[]{:S(2)}) %all-to-all-start.3) | async-done | bytes 524320 | tf_op jit(solution)/shard_map/all_to_all | solution.py:172
  97.8 1.6 %collective-permute-start.4 = (bf16[2,128,512]{2,1,0:T(8,128)(2,1)S(1)}, bf16[2,128,512]{2,1,0:T(8,128)(2,1)S(1)}, u32[]{:S(2)}, u32[]{:S(2)}) collective-permute-start(bf16[2,128,512]{2,1,0:T(8,128)(2,1)S(1)} %bitcast_convert_fusion.1.refs_0_), channel_id=1, source_target_pairs={{0,2},{1,3},{2,0},{3,1},{4,6},{5,7},{6,4},{7,5},{8,10},{9,11},{10,... | collective-permute-start | bytes 786440 | tf_op jit(solution)/shard_map/ppermute | solution.py:52
  99.4 0.7 copy-done.10
  100.1 3.8 %shard_map.62 = f32[2,512,128]{2,1,0:T(8,128)} custom-call(s32[1]{0:T(128)} %bitcast.10.me_ref, bf16[512,2048]{1,0:T(8,128)(2,1)} %l_ref.5, bf16[2,128,512]{2,1,0:T(8,128)(2,1)} %copy-done.4, bf16[2,128,512]{2,1,0:T(8,128)(2,1)} %copy-done.9, bf16[2,128,512]{2,1,0:T(8,128)(2,1)} %copy-done.10, bf16[2,128,512]{2,1,0:T(8,128)(2,1)} %collective-permute-done.7.refs_3_), custom_call_target="tpu_custom_call" | custom-call | flops 536870912 | bytes 3670016 | tf_op jit(solution)/shard_map/pallas_call | solution.py:177
  104.8 1.3 %copy.46 = f32[512,2,256]{2,1,0:T(2,128)} copy(f32[512,2,256]{0,2,1:T(8,128)S(1)} %pad_maximum_fusion) | data formatting | bytes 2097152
  106.8 3.9 %shard_map.63 = f32[2,512,128]{2,1,0:T(8,128)} custom-call(s32[1]{0:T(128)} %bitcast.10.me_ref, bf16[512,2048]{1,0:T(8,128)(2,1)} %l_ref.5, bf16[2,128,512]{2,1,0:T(8,128)(2,1)} %copy-done.3, bf16[2,128,512]{2,1,0:T(8,128)(2,1)} %copy-done.8, bf16[2,128,512]{2,1,0:T(8,128)(2,1)} %copy-done.11, bf16[2,128,512]{2,1,0:T(8,128)(2,1)} %collective-permute-done.9.refs_3_), custom_call_target="tpu_custom_call" | custom-call | flops 536870912 | bytes 3670016 | tf_op jit(solution)/shard_map/pallas_call | solution.py:177
  110.7 1.1 bitcast_subtract_fusion.1
  111.9 1.8 %copy.47 = f32[512,2,256]{2,1,0:T(2,128)} copy(f32[512,2,256]{2,0,1:T(8,128)S(1)} %pad_maximum_fusion.1) | data formatting | bytes 2097152
  (54 shorter events, 4.8 us)
Async XLA Ops:
  5.3 24.5 %all-to-all-start = ((bf16[8,80,512]{2,1,0:T(8,128)(2,1)}), bf16[8,80,512]{2,1,0:T(8,128)(2,1)S(1)}, u32[]{:S(2)}, u32[]{:S(2)}) async-start(bf16[8,80,512]{2,1,0:T(8,128)(2,1)} %pad_maximum_fusion.2), calls=%async_computation | async-start | bytes 1310720 | tf_op jit(solution)/shard_map/all_to_all | solution.py:123
  29.9 0.8 copy-start.5
  35.5 5.3 %collective-permute-start = (f32[2,256,512]{2,1,0:T(8,128)}, f32[2,256,512]{2,1,0:T(8,128)}, u32[]{:S(2)}, u32[]{:S(2)}) collective-permute-start(f32[2,256,512]{2,1,0:T(8,128)} %get-tuple-element.21), channel_id=1, source_target_pairs={{0,1},{1,0},{2,3},{3,2},{4,5},{5,4},{6,7},{7,6},{8,9},{9,8},{10,11... | collective-permute-start | bytes 3145736 | tf_op jit(solution)/shard_map/ppermute | solution.py:38
  35.5 5.3 %copy-start.2 = (f32[2,256,512]{2,1,0:T(8,128)S(1)}, f32[2,256,512]{2,1,0:T(8,128)}, u32[]{:S(2)}) copy-start(f32[2,256,512]{2,1,0:T(8,128)} %get-tuple-element.20) | copy-start | bytes 3145732
  35.5 20.1 %collective-permute-start.2 = (f32[2,256,512]{2,1,0:T(8,128)}, f32[2,256,512]{2,1,0:T(8,128)S(1)}, u32[]{:S(2)}, u32[]{:S(2)}) collective-permute-start(f32[2,256,512]{2,1,0:T(8,128)} %get-tuple-element.23), channel_id=1, source_target_pairs={{0,1},{1,0},{2,3},{3,2},{4,5},{5,4},{6,7},{7,6},{8,9},{9,8},{10,11... | collective-permute-start | bytes 3145736 | tf_op jit(solution)/shard_map/ppermute | solution.py:38
  37.2 18.4 %all-to-all-start.1 = ((bf16[64,16,256]{2,0,1:T(8,128)(2,1)}), bf16[64,16,256]{2,0,1:T(8,128)(2,1)S(1)}, u32[]{:S(2)}, u32[]{:S(2)}) async-start(bf16[64,16,256]{2,0,1:T(8,128)(2,1)} %copy.42), calls=%async_computation.1 | async-start | bytes 1048576 | tf_op jit(solution)/shard_map/all_to_all | solution.py:130
  43.2 12.4 %copy-start.1 = (f32[2,256,512]{2,1,0:T(8,128)S(1)}, f32[2,256,512]{2,1,0:T(8,128)}, u32[]{:S(2)}) copy-start(f32[2,256,512]{2,1,0:T(8,128)} %get-tuple-element.22) | copy-start | bytes 3145732
  43.2 14.0 %collective-permute-start.1 = (f32[256,512]{1,0:T(8,128)}, f32[256,512]{1,0:T(8,128)}, u32[]{:S(2)}, u32[]{:S(2)}) collective-permute-start(f32[256,512]{1,0:T(8,128)} %get-tuple-element.44), channel_id=1, source_target_pairs={{0,2},{1,3},{2,0},{3,1},{4,6},{5,7},{6,4},{7,5},{8,10},{9,11},{10,... | collective-permute-start | bytes 1572872 | tf_op jit(solution)/shard_map/ppermute | solution.py:152
  57.2 7.8 %copy-start.7 = (f32[256,512]{1,0:T(8,128)S(1)}, f32[256,512]{1,0:T(8,128)}, u32[]{:S(2)}) copy-start(f32[256,512]{1,0:T(8,128)} %get-tuple-element.27) | copy-start | bytes 1572868
  59.4 20.8 %all-to-all-start.2 = ((f32[16,16,512]{2,1,0:T(8,128)}), f32[16,16,512]{2,1,0:T(8,128)S(1)}, u32[]{:S(2)}, u32[]{:S(2)}) async-start(f32[16,16,512]{2,1,0:T(8,128)} %shard_map.60), calls=%async_computation.2 | async-start | bytes 1048576 | tf_op jit(solution)/shard_map/all_to_all | solution.py:172
  65.1 12.2 %collective-permute-start.3 = (f32[256,512]{1,0:T(8,128)S(1)}, f32[256,512]{1,0:T(8,128)S(1)}, u32[]{:S(2)}, u32[]{:S(2)}) collective-permute-start(f32[256,512]{1,0:T(8,128)S(1)} %copy-done.7), channel_id=1, source_target_pairs={{0,2},{1,3},{2,0},{3,1},{4,6},{5,7},{6,4},{7,5},{8,10},{9,11},{10,... | collective-permute-start | bytes 1572872 | tf_op jit(solution)/shard_map/ppermute | solution.py:156
  77.3 0.8 copy-start.6
  80.3 17.4 %all-to-all-start.3 = ((f32[16,16,512]{2,1,0:T(8,128)}), f32[16,16,512]{2,1,0:T(8,128)S(1)}, u32[]{:S(2)}, u32[]{:S(2)}) async-start(f32[16,16,512]{2,1,0:T(8,128)} %shard_map.61), calls=%async_computation.3 | async-start | bytes 1048576 | tf_op jit(solution)/shard_map/all_to_all | solution.py:172
  86.0 13.4 %copy-start.4 = (bf16[2,128,512]{2,1,0:T(8,128)(2,1)}, bf16[2,128,512]{2,1,0:T(8,128)(2,1)S(1)}, u32[]{:S(2)}) copy-start(bf16[2,128,512]{2,1,0:T(8,128)(2,1)S(1)} %bitcast_convert_fusion.refs_0_) | copy-start | bytes 786436
  86.0 6.4 %collective-permute-start.5 = (bf16[2,128,512]{2,1,0:T(8,128)(2,1)S(1)}, bf16[2,128,512]{2,1,0:T(8,128)(2,1)S(1)}, u32[]{:S(2)}, u32[]{:S(2)}) collective-permute-start(bf16[2,128,512]{2,1,0:T(8,128)(2,1)S(1)} %bitcast_convert_fusion.refs_0_), channel_id=1, source_target_pairs={{0,2},{1,3},{2,0},{3,1},{4,6},{5,7},{6,4},{7,5},{8,10},{9,11},{10,... | collective-permute-start | bytes 786440 | tf_op jit(solution)/shard_map/ppermute | solution.py:52
  92.4 6.9 %copy-start.9 = (bf16[2,128,512]{2,1,0:T(8,128)(2,1)}, bf16[2,128,512]{2,1,0:T(8,128)(2,1)S(1)}, u32[]{:S(2)}) copy-start(bf16[2,128,512]{2,1,0:T(8,128)(2,1)S(1)} %collective-permute-done.5.refs_1_) | copy-start | bytes 786436
  92.4 6.9 %collective-permute-start.6 = (bf16[2,128,512]{2,1,0:T(8,128)(2,1)S(1)}, bf16[2,128,512]{2,1,0:T(8,128)(2,1)S(1)}, u32[]{:S(2)}, u32[]{:S(2)}) collective-permute-start(bf16[2,128,512]{2,1,0:T(8,128)(2,1)S(1)} %bitcast_convert_fusion.refs_0_), channel_id=1, source_target_pairs={{0,1},{1,0},{2,3},{3,2},{4,5},{5,4},{6,7},{7,6},{8,9},{9,8},{10,11... | collective-permute-start | bytes 786440 | tf_op jit(solution)/shard_map/ppermute | solution.py:52
  92.4 6.9 %collective-permute-start.7 = (bf16[2,128,512]{2,1,0:T(8,128)(2,1)S(1)}, bf16[2,128,512]{2,1,0:T(8,128)(2,1)}, u32[]{:S(2)}, u32[]{:S(2)}) collective-permute-start(bf16[2,128,512]{2,1,0:T(8,128)(2,1)S(1)} %collective-permute-done.5.refs_1_), channel_id=1, source_target_pairs={{0,1},{1,0},{2,3},{3,2},{4,5},{5,4},{6,7},{7,6},{8,9},{9,8},{10,11... | collective-permute-start | bytes 786440 | tf_op jit(solution)/shard_map/ppermute | solution.py:52
  97.8 6.5 %copy-start.3 = (bf16[2,128,512]{2,1,0:T(8,128)(2,1)}, bf16[2,128,512]{2,1,0:T(8,128)(2,1)S(1)}, u32[]{:S(2)}) copy-start(bf16[2,128,512]{2,1,0:T(8,128)(2,1)S(1)} %bitcast_convert_fusion.1.refs_0_) | copy-start | bytes 786436
  97.8 6.4 %collective-permute-start.4 = (bf16[2,128,512]{2,1,0:T(8,128)(2,1)S(1)}, bf16[2,128,512]{2,1,0:T(8,128)(2,1)S(1)}, u32[]{:S(2)}, u32[]{:S(2)}) collective-permute-start(bf16[2,128,512]{2,1,0:T(8,128)(2,1)S(1)} %bitcast_convert_fusion.1.refs_0_), channel_id=1, source_target_pairs={{0,2},{1,3},{2,0},{3,1},{4,6},{5,7},{6,4},{7,5},{8,10},{9,11},{10,... | collective-permute-start | bytes 786440 | tf_op jit(solution)/shard_map/ppermute | solution.py:52
  99.4 0.7 copy-start.10
  104.2 1.9 %copy-start.8 = (bf16[2,128,512]{2,1,0:T(8,128)(2,1)}, bf16[2,128,512]{2,1,0:T(8,128)(2,1)S(1)}, u32[]{:S(2)}) copy-start(bf16[2,128,512]{2,1,0:T(8,128)(2,1)S(1)} %collective-permute-done.4.refs_1_) | copy-start | bytes 786436
  104.2 1.9 %collective-permute-start.8 = (bf16[2,128,512]{2,1,0:T(8,128)(2,1)S(1)}, bf16[2,128,512]{2,1,0:T(8,128)(2,1)S(1)}, u32[]{:S(2)}, u32[]{:S(2)}) collective-permute-start(bf16[2,128,512]{2,1,0:T(8,128)(2,1)S(1)} %bitcast_convert_fusion.1.refs_0_), channel_id=1, source_target_pairs={{0,1},{1,0},{2,3},{3,2},{4,5},{5,4},{6,7},{7,6},{8,9},{9,8},{10,11... | collective-permute-start | bytes 786440 | tf_op jit(solution)/shard_map/ppermute | solution.py:52
  104.2 2.0 %collective-permute-start.9 = (bf16[2,128,512]{2,1,0:T(8,128)(2,1)S(1)}, bf16[2,128,512]{2,1,0:T(8,128)(2,1)}, u32[]{:S(2)}, u32[]{:S(2)}) collective-permute-start(bf16[2,128,512]{2,1,0:T(8,128)(2,1)S(1)} %collective-permute-done.4.refs_1_), channel_id=1, source_target_pairs={{0,1},{1,0},{2,3},{3,2},{4,5},{5,4},{6,7},{7,6},{8,9},{9,8},{10,11... | collective-permute-start | bytes 786440 | tf_op jit(solution)/shard_map/ppermute | solution.py:52
  106.1 4.6 %copy-start = (f32[2,512,128]{2,1,0:T(8,128)S(1)}, f32[2,512,128]{2,1,0:T(8,128)}, u32[]{:S(2)}) copy-start(f32[2,512,128]{2,1,0:T(8,128)} %shard_map.62) | copy-start | bytes 1572868
  106.1 0.7 copy-start.11

commit v18 on v17

--- a/solution.py
+++ b/solution.py
@@ -16,7 +16,7 @@
     levels = out_refs[0].ndim - 1
     rows, width = out_refs[0].shape[-2:]
     senders = x_ref.shape[0]
-    flipped = x_ref[:, :stations, :].reshape(senders * stations, x_ref.shape[2]).T
+    flipped = x_ref[...].reshape(senders * stations, x_ref.shape[2]).T
     for slot in range(2 ** levels):
         relative = tuple((slot >> level) & 1 for level in range(levels))
         block = 0
@@ -112,22 +112,27 @@
         masked.reshape(stations_local, hours, CHUNKS, tm_count, chunk_members),
         (3, 0, 1, 2, 4),
     ).reshape(tm_count, stations_local, hours * members_here)
+    by_member = lax.all_to_all(outgoing, "tm", split_axis=0, concat_axis=0, tiled=True)
+    stations_here = tm_count * stations_local
+    masked_later, by_member = lax.optimization_barrier((masked, by_member))
+    slab_hours, comps_here = decay.shape
     high = lax.reduce_precision(decay, exponent_bits=8, mantissa_bits=7)
     middle = lax.reduce_precision(decay - high, exponent_bits=8, mantissa_bits=7)
     low = decay - high - middle
-    pieces = jnp.stack([high, middle, low]).astype(obs.dtype).reshape(-1, hours * members_here)
-    spare = (-(stations_local + pieces.shape[0])) % 16
-    pieces = jnp.pad(pieces, ((0, spare), (0, 0)))
+    pieces = jnp.stack([high, middle, low]).astype(obs.dtype).reshape(-1, slab_hours, members)
+    piece_rows = pieces.shape[0]
+    spare = (-(stations_local + piece_rows)) % 8
+    pieces = jnp.pad(pieces, ((0, spare), (0, 0), (0, 0)))
     pieces = jnp.broadcast_to(pieces[None], (tm_count,) + pieces.shape)
-    outgoing = jnp.concatenate([outgoing, pieces], axis=1)
-    by_member = lax.all_to_all(outgoing, "tm", split_axis=0, concat_axis=0, tiled=True)
-    stations_here = tm_count * stations_local
-    slab_hours, comps_here = decay.shape
-    arrived = by_member[:, stations_local:stations_local + 3 * slab_hours * comps_here // (hours * members_here)]
+    outgoing_hours = jnp.transpose(
+        masked_later.reshape(stations_local, tm_count, slab_hours, members), (1, 0, 2, 3)
+    )
+    outgoing_hours = jnp.concatenate([outgoing_hours, pieces], axis=1)
+    by_hour = lax.all_to_all(outgoing_hours, "tm", split_axis=0, concat_axis=0, tiled=True)
+    arrived = by_hour[:, stations_local:stations_local + piece_rows]
     arrived = arrived.reshape(tm_count, 3, slab_hours, comps_here).astype(jnp.float32)
     decay_all = (arrived[:, 0] + arrived[:, 1] + arrived[:, 2]).reshape(hours, comps_here)
-    masked_later, by_member = lax.optimization_barrier((masked, by_member))
-    by_hour = lax.all_to_all(masked_later, "tm", split_axis=1, concat_axis=0, tiled=True)
+    by_hour = by_hour[:, :stations_local].reshape(stations_here, slab_hours, members)
     all_comps = loadings.shape[1]
     comps = all_comps // state_count
     rows = hours * chunk_members

time: 114 us -> 117 us (1.026)
  waiting for transfers between devices: 47.6 us -> 50.5 us
  starting transfers between devices: 30 us -> 27.9 us
  local copies, waits for them, and re-layouts: 10.2 us -> 11.6 us
    all_to_all x1, waiting for transfers between devices: 9.18 us -> 12.5 us  [local(): lax.all_to_all(outgoing_hours, 'tm', split_axis=0, concat_axis=0, tiled=T...]
    all_to_all x1, waiting for transfers between devices: 17.3 us -> 14.5 us  [local(): lax.all_to_all(outgoing, 'tm', split_axis=0, concat_axis=0, tiled=True)]
    all_to_all x2, starting transfers between devices: 11.3 us -> 9.27 us  [local(): lax.all_to_all(smoothed_here, 'tm', split_axis=0, concat_axis=1, tiled=True)]
    ppermute x1, waiting for transfers between devices: 10.6 us -> 12.1 us  [local(): lax.ppermute(o, 'state', last[c + 1][2])]
    all_to_all x2, waiting for transfers between devices: 4.73 us -> 6.05 us  [local(): lax.all_to_all(smoothed_here, 'tm', split_axis=0, concat_axis=1, tiled=True)]
    unnamed x27 -> x32, local copies, waits for them, and re-layouts: 7.65 us -> 8.44 us
  transfers between devices with their start and end apart: 14 -> 14, of which waited for: 8 -> 7; matrix products, arithmetic and copies ran while one was open for 7% -> 8% of each run, Pallas kernels for 5% -> 5%
where the time goes in v18:
time: 117 us; the launch traced here: 116 us
  waiting for transfers between devices  50.5 us (43%)
  starting transfers between devices  27.9 us (24%)
  Pallas kernels  16.8 us (14%)
  local copies, waits for them, and re-layouts  11.6 us (10%)
  other arithmetic  8.32 us (7%)
    all_to_all x1, waiting for transfers between devices, local(): lax.all_to_all(outgoing, 'tm', split_axis=0, concat_axis=0, tiled=True)  14.5 us
    all_to_all x1, waiting for transfers between devices, local(): lax.all_to_all(outgoing_hours, 'tm', split_axis=0, concat_axis=0, tiled=T...  12.5 us
    ppermute x1, waiting for transfers between devices, local(): lax.ppermute(o, 'state', last[c + 1][2])  12.1 us
    all_to_all x2, starting transfers between devices, local(): lax.all_to_all(smoothed_here, 'tm', split_axis=0, concat_axis=1, tiled=True)  9.27 us
    unnamed x32, local copies, waits for them, and re-layouts  8.44 us
    pallas_call x2, Pallas kernels, local(): vmem_call(fitted_kernel, jax.ShapeDtypeStruct((slab_hours, stations_here,...  7.71 us
    all_to_all x1, starting transfers between devices, local(): lax.all_to_all(outgoing, 'tm', split_axis=0, concat_axis=0, tiled=True)  7.25 us
    all_to_all x2, waiting for transfers between devices, local(): lax.all_to_all(smoothed_here, 'tm', split_axis=0, concat_axis=1, tiled=True)  6.05 us
  transfers between devices with their start and end apart: 14, of which 7 were waited for; matrix products, arithmetic and copies ran while one was open for 8% of the time, Pallas kernels for 5%

profile of v18, /device:TPU:0, one launch (start us, length us, event | category | flops | bytes accessed | tf_op | source)
XLA Modules:
  0.0 116.0 jit_solution(5630549595010473143)
XLA Ops:
  0.6 0.7 convert_element_type.29
  1.3 1.7 %copy.35 = bf16[64,16,256]{0,2,1:T(8,128)(2,1)S(1)} copy(bf16[64,16,256]{2,1,0:T(8,128)(2,1)} %param.4) | data formatting | bytes 1048576 | tf_op args[0]
  3.3 1.1 copy.37
  4.4 7.3 %all-to-all-start = ((bf16[8,64,512]{2,1,0:T(8,128)(2,1)}), bf16[8,64,512]{2,1,0:T(8,128)(2,1)S(1)}, u32[]{:S(2)}, u32[]{:S(2)}) async-start(bf16[8,64,512]{2,1,0:T(8,128)(2,1)} %copy.37), calls=%async_computation | async-start | bytes 1048576 | tf_op jit(solution)/shard_map/all_to_all | solution.py:115
  11.7 14.5 %all-to-all-done.x_ref = bf16[8,64,512]{2,1,0:T(8,128)(2,1)S(1)} async-done(((bf16[8,64,512]{2,1,0:T(8,128)(2,1)}), bf16[8,64,512]{2,1,0:T(8,128)(2,1)S(1)}, u32[]{:S(2)}, u32[]{:S(2)}) %all-to-all-start) | async-done | bytes 524320 | tf_op jit(solution)/shard_map/all_to_all | solution.py:115
  26.2 0.8 copy-done.7
  27.0 4.8 %shard_map.59 = (f32[2,256,512]{2,1,0:T(8,128)}, f32[2,256,512]{2,1,0:T(8,128)}, f32[2,256,512]{2,1,0:T(8,128)}, f32[2,256,512]{2,1,0:T(8,128)}) custom-call(s32[1]{0:T(128)} %bitcast.11.me_ref, bf16[8,64,512]{2,1,0:T(8,128)(2,1)} %copy-done.7, bf16[512,2048]{1,0:T(8,128)(2,1)} %l_ref.5), custom_call_target="tpu_custom_call" | custom-call | flops 1073741824 | bytes 6815744 | tf_op jit(solution)/shard_map/pallas_call | solution.py:140
  32.5 1.6 %pad_maximum_fusion.2 = bf16[8,72,2,256]{3,2,1,0:T(2,128)(2,1)} fusion(bf16[8,8,2,256]{3,2,1,0:T(2,128)(2,1)S(1)} %broadcast_in_dim.2, bf16[8,64,2,256]{3,2,1,0:T(2,128)(2,1)S(1)} %bitcast.54), kind=kLoop, calls=%fused_computation.2 | loop fusion | flops 294912 | bytes 1179648 | tf_op jit(solution)/shard_map/concatenate | solution.py:130
  34.1 3.6 %all-to-all-start.1 = ((bf16[8,72,2,256]{3,2,1,0:T(2,128)(2,1)}), bf16[8,72,2,256]{3,2,1,0:T(2,128)(2,1)S(1)}, u32[]{:S(2)}, u32[]{:S(2)}) async-start(bf16[8,72,2,256]{3,2,1,0:T(2,128)(2,1)} %pad_maximum_fusion.2), calls=%async_computation.1 | async-start | bytes 1179648 | tf_op jit(solution)/shard_map/all_to_all | solution.py:131
  38.2 2.2 %fusion.2 = (f32[256,512]{1,0:T(8,128)S(1)}, f32[256,512]{1,0:T(8,128)}) fusion(f32[2,256,512]{2,1,0:T(8,128)} %collective-permute-done, f32[2,256,512]{2,1,0:T(8,128)S(1)} %copy-done.2), kind=kLoop, calls=%fused_computation.8 | loop fusion | flops 262144 | bytes 3145728 | tf_op jit(solution)/shard_map/add | solution.py:40
  40.4 1.5 %collective-permute-start.1 = (f32[256,512]{1,0:T(8,128)S(1)}, f32[256,512]{1,0:T(8,128)S(1)}, u32[]{:S(2)}, u32[]{:S(2)}) collective-permute-start(f32[256,512]{1,0:T(8,128)S(1)} %get-tuple-element.44), channel_id=1, source_target_pairs={{0,2},{1,3},{2,0},{3,1},{4,6},{5,7},{6,4},{7,5},{8,10},{9,11},{10,... | collective-permute-start | bytes 1572872 | tf_op jit(solution)/shard_map/ppermute | solution.py:157
  41.9 12.5 %all-to-all-done.1 = bf16[8,72,2,256]{3,2,1,0:T(2,128)(2,1)S(1)} async-done(((bf16[8,72,2,256]{3,2,1,0:T(2,128)(2,1)}), bf16[8,72,2,256]{3,2,1,0:T(2,128)(2,1)S(1)}, u32[]{:S(2)}, u32[]{:S(2)}) %all-to-all-start.1) | async-done | bytes 589856 | tf_op jit(solution)/shard_map/all_to_all | solution.py:131
  55.0 0.6 add.40.rate_ref
  55.6 2.4 %fusion = (f32[256,512]{1,0:T(8,128)}, f32[256,512]{1,0:T(8,128)}) fusion(f32[2,256,512]{2,1,0:T(8,128)} %collective-permute-done.2, f32[2,256,512]{2,1,0:T(8,128)S(1)} %copy-done.1), kind=kLoop, calls=%fused_computation.4 | loop fusion | flops 262144 | bytes 3145728 | tf_op jit(solution)/shard_map/add | solution.py:40
  58.0 0.8 copy-done.5
  58.8 2.2 %shard_map.60 = f32[16,16,512]{2,1,0:T(8,128)} custom-call(f32[16,512]{1,0:T(8,128)} %add.40.rate_ref, f32[16,16,512]{2,1,0:T(8,128)} %bitcast.55, f32[16,16,512]{2,1,0:T(8,128)} %bitcast.59), custom_call_target="tpu_custom_call" | custom-call | flops 786432 | bytes 1572864 | tf_op jit(solution)/shard_map/pallas_call | solution.py:167
  61.0 3.6 %all-to-all-start.2 = ((f32[16,16,512]{2,1,0:T(8,128)}), f32[16,16,512]{2,1,0:T(8,128)S(1)}, u32[]{:S(2)}, u32[]{:S(2)}) async-start(f32[16,16,512]{2,1,0:T(8,128)} %shard_map.60), calls=%async_computation.2 | async-start | bytes 1048576 | tf_op jit(solution)/shard_map/all_to_all | solution.py:177
  64.6 1.6 %collective-permute-start.3 = (f32[256,512]{1,0:T(8,128)S(1)}, f32[256,512]{1,0:T(8,128)S(1)}, u32[]{:S(2)}, u32[]{:S(2)}) collective-permute-start(f32[256,512]{1,0:T(8,128)S(1)} %copy-done.8), channel_id=1, source_target_pairs={{0,2},{1,3},{2,0},{3,1},{4,6},{5,7},{6,4},{7,5},{8,10},{9,11},{10,... | collective-permute-start | bytes 1572872 | tf_op jit(solution)/shard_map/ppermute | solution.py:161
  66.2 12.1 %collective-permute-done.3 = f32[256,512]{1,0:T(8,128)S(1)} collective-permute-done((f32[256,512]{1,0:T(8,128)S(1)}, f32[256,512]{1,0:T(8,128)S(1)}, u32[]{:S(2)}, u32[]{:S(2)}) %collective-permute-start.3) | collective-permute-done | bytes 524320 | tf_op jit(solution)/shard_map/ppermute | solution.py:161
  78.2 0.8 copy-done.6
  79.0 2.1 %shard_map.61 = f32[16,16,512]{2,1,0:T(8,128)} custom-call(f32[16,512]{1,0:T(8,128)} %add.40.rate_ref, f32[16,16,512]{2,1,0:T(8,128)} %bitcast.58, f32[16,16,512]{2,1,0:T(8,128)} %bitcast.60), custom_call_target="tpu_custom_call" | custom-call | flops 786432 | bytes 1572864 | tf_op jit(solution)/shard_map/pallas_call | solution.py:167
  81.2 5.7 %all-to-all-start.3 = ((f32[16,16,512]{2,1,0:T(8,128)}), f32[16,16,512]{2,1,0:T(8,128)S(1)}, u32[]{:S(2)}, u32[]{:S(2)}) async-start(f32[16,16,512]{2,1,0:T(8,128)} %shard_map.61), calls=%async_computation.3 | async-start | bytes 1048576 | tf_op jit(solution)/shard_map/all_to_all | solution.py:177
  86.9 1.6 %collective-permute-start.5 = (bf16[2,128,512]{2,1,0:T(8,128)(2,1)S(1)}, bf16[2,128,512]{2,1,0:T(8,128)(2,1)S(1)}, u32[]{:S(2)}, u32[]{:S(2)}) collective-permute-start(bf16[2,128,512]{2,1,0:T(8,128)(2,1)S(1)} %bitcast_convert_fusion.refs_0_), channel_id=1, source_target_pairs={{0,2},{1,3},{2,0},{3,1},{4,6},{5,7},{6,4},{7,5},{8,10},{9,11},{10,... | collective-permute-start | bytes 786440 | tf_op jit(solution)/shard_map/ppermute | solution.py:52
  88.5 5.0 %collective-permute-done.5.refs_1_ = bf16[2,128,512]{2,1,0:T(8,128)(2,1)S(1)} collective-permute-done((bf16[2,128,512]{2,1,0:T(8,128)(2,1)S(1)}, bf16[2,128,512]{2,1,0:T(8,128)(2,1)S(1)}, u32[]{:S(2)}, u32[]{:S(2)}) %collective-permute-start.5) | collective-permute-done | bytes 262176 | tf_op jit(solution)/shard_map/ppermute | solution.py:52
  94.0 6.0 %all-to-all-done.3 = f32[16,16,512]{2,1,0:T(8,128)S(1)} async-done(((f32[16,16,512]{2,1,0:T(8,128)}), f32[16,16,512]{2,1,0:T(8,128)S(1)}, u32[]{:S(2)}, u32[]{:S(2)}) %all-to-all-start.3) | async-done | bytes 524320 | tf_op jit(solution)/shard_map/all_to_all | solution.py:177
  100.2 1.6 %collective-permute-start.4 = (bf16[2,128,512]{2,1,0:T(8,128)(2,1)S(1)}, bf16[2,128,512]{2,1,0:T(8,128)(2,1)S(1)}, u32[]{:S(2)}, u32[]{:S(2)}) collective-permute-start(bf16[2,128,512]{2,1,0:T(8,128)(2,1)S(1)} %bitcast_convert_fusion.1.refs_0_), channel_id=1, source_target_pairs={{0,2},{1,3},{2,0},{3,1},{4,6},{5,7},{6,4},{7,5},{8,10},{9,11},{10,... | collective-permute-start | bytes 786440 | tf_op jit(solution)/shard_map/ppermute | solution.py:52
  101.8 0.7 copy-done.11
  102.4 3.9 %shard_map.62 = f32[2,512,128]{2,1,0:T(8,128)} custom-call(s32[1]{0:T(128)} %bitcast.11.me_ref, bf16[512,2048]{1,0:T(8,128)(2,1)} %l_ref.5, bf16[2,128,512]{2,1,0:T(8,128)(2,1)} %copy-done.4, bf16[2,128,512]{2,1,0:T(8,128)(2,1)} %copy-done.10, bf16[2,128,512]{2,1,0:T(8,128)(2,1)} %copy-done.11, bf16[2,128,512]{2,1,0:T(8,128)(2,1)} %collective-permute-done.7.refs_3_), custom_call_target="tpu_custom_call" | custom-call | flops 536870912 | bytes 3670016 | tf_op jit(solution)/shard_map/pallas_call | solution.py:182
  107.2 1.3 %copy.44 = f32[512,2,256]{2,1,0:T(2,128)} copy(f32[512,2,256]{0,2,1:T(8,128)S(1)} %pad_maximum_fusion) | data formatting | bytes 2097152
  109.2 3.9 %shard_map.63 = f32[2,512,128]{2,1,0:T(8,128)} custom-call(s32[1]{0:T(128)} %bitcast.11.me_ref, bf16[512,2048]{1,0:T(8,128)(2,1)} %l_ref.5, bf16[2,128,512]{2,1,0:T(8,128)(2,1)} %copy-done.3, bf16[2,128,512]{2,1,0:T(8,128)(2,1)} %copy-done.9, bf16[2,128,512]{2,1,0:T(8,128)(2,1)} %copy-done.12, bf16[2,128,512]{2,1,0:T(8,128)(2,1)} %collective-permute-done.9.refs_3_), custom_call_target="tpu_custom_call" | custom-call | flops 536870912 | bytes 3670016 | tf_op jit(solution)/shard_map/pallas_call | solution.py:182
  113.1 1.1 bitcast_subtract_fusion.1
  114.3 1.8 %copy.45 = f32[512,2,256]{2,1,0:T(2,128)} copy(f32[512,2,256]{2,0,1:T(8,128)S(1)} %pad_maximum_fusion.1) | data formatting | bytes 2097152
  (60 shorter events, 4.3 us)
Async XLA Ops:
  4.4 21.7 %all-to-all-start = ((bf16[8,64,512]{2,1,0:T(8,128)(2,1)}), bf16[8,64,512]{2,1,0:T(8,128)(2,1)S(1)}, u32[]{:S(2)}, u32[]{:S(2)}) async-start(bf16[8,64,512]{2,1,0:T(8,128)(2,1)} %copy.37), calls=%async_computation | async-start | bytes 1048576 | tf_op jit(solution)/shard_map/all_to_all | solution.py:115
  11.7 20.1 %copy-start.13 = (f32[2,512]{1,0:T(2,128)S(1)}, f32[2,512]{1,0:T(2,128)}, u32[]{:S(2)}) copy-start(f32[2,512]{1,0:T(2,128)} %param.7) | copy-start | bytes 12292
  26.2 0.8 copy-start.7
  31.8 6.4 %copy-start.2 = (f32[2,256,512]{2,1,0:T(8,128)S(1)}, f32[2,256,512]{2,1,0:T(8,128)}, u32[]{:S(2)}) copy-start(f32[2,256,512]{2,1,0:T(8,128)} %get-tuple-element.20) | copy-start | bytes 3145732
  31.8 6.4 %collective-permute-start = (f32[2,256,512]{2,1,0:T(8,128)}, f32[2,256,512]{2,1,0:T(8,128)}, u32[]{:S(2)}, u32[]{:S(2)}) collective-permute-start(f32[2,256,512]{2,1,0:T(8,128)} %get-tuple-element.21), channel_id=1, source_target_pairs={{0,1},{1,0},{2,3},{3,2},{4,5},{5,4},{6,7},{7,6},{8,9},{9,8},{10,11... | collective-permute-start | bytes 3145736 | tf_op jit(solution)/shard_map/ppermute | solution.py:38
  34.1 20.3 %all-to-all-start.1 = ((bf16[8,72,2,256]{3,2,1,0:T(2,128)(2,1)}), bf16[8,72,2,256]{3,2,1,0:T(2,128)(2,1)S(1)}, u32[]{:S(2)}, u32[]{:S(2)}) async-start(bf16[8,72,2,256]{3,2,1,0:T(2,128)(2,1)} %pad_maximum_fusion.2), calls=%async_computation.1 | async-start | bytes 1179648 | tf_op jit(solution)/shard_map/all_to_all | solution.py:131
  37.7 17.9 %collective-permute-start.2 = (f32[2,256,512]{2,1,0:T(8,128)}, f32[2,256,512]{2,1,0:T(8,128)}, u32[]{:S(2)}, u32[]{:S(2)}) collective-permute-start(f32[2,256,512]{2,1,0:T(8,128)} %get-tuple-element.23), channel_id=1, source_target_pairs={{0,1},{1,0},{2,3},{3,2},{4,5},{5,4},{6,7},{7,6},{8,9},{9,8},{10,11... | collective-permute-start | bytes 3145736 | tf_op jit(solution)/shard_map/ppermute | solution.py:38
  40.4 15.2 %copy-start.1 = (f32[2,256,512]{2,1,0:T(8,128)S(1)}, f32[2,256,512]{2,1,0:T(8,128)}, u32[]{:S(2)}) copy-start(f32[2,256,512]{2,1,0:T(8,128)} %get-tuple-element.22) | copy-start | bytes 3145732
  40.4 17.6 %collective-permute-start.1 = (f32[256,512]{1,0:T(8,128)S(1)}, f32[256,512]{1,0:T(8,128)S(1)}, u32[]{:S(2)}, u32[]{:S(2)}) collective-permute-start(f32[256,512]{1,0:T(8,128)S(1)} %get-tuple-element.44), channel_id=1, source_target_pairs={{0,2},{1,3},{2,0},{3,1},{4,6},{5,7},{6,4},{7,5},{8,10},{9,11},{10,... | collective-permute-start | bytes 1572872 | tf_op jit(solution)/shard_map/ppermute | solution.py:157
  58.0 6.6 %copy-start.8 = (f32[256,512]{1,0:T(8,128)S(1)}, f32[256,512]{1,0:T(8,128)}, u32[]{:S(2)}) copy-start(f32[256,512]{1,0:T(8,128)} %get-tuple-element.27) | copy-start | bytes 1572868
  58.0 0.8 copy-start.5
  61.0 20.2 %all-to-all-start.2 = ((f32[16,16,512]{2,1,0:T(8,128)}), f32[16,16,512]{2,1,0:T(8,128)S(1)}, u32[]{:S(2)}, u32[]{:S(2)}) async-start(f32[16,16,512]{2,1,0:T(8,128)} %shard_map.60), calls=%async_computation.2 | async-start | bytes 1048576 | tf_op jit(solution)/shard_map/all_to_all | solution.py:177
  64.6 13.7 %collective-permute-start.3 = (f32[256,512]{1,0:T(8,128)S(1)}, f32[256,512]{1,0:T(8,128)S(1)}, u32[]{:S(2)}, u32[]{:S(2)}) collective-permute-start(f32[256,512]{1,0:T(8,128)S(1)} %copy-done.8), channel_id=1, source_target_pairs={{0,2},{1,3},{2,0},{3,1},{4,6},{5,7},{6,4},{7,5},{8,10},{9,11},{10,... | collective-permute-start | bytes 1572872 | tf_op jit(solution)/shard_map/ppermute | solution.py:161
  78.2 0.8 copy-start.6
  81.2 18.9 %all-to-all-start.3 = ((f32[16,16,512]{2,1,0:T(8,128)}), f32[16,16,512]{2,1,0:T(8,128)S(1)}, u32[]{:S(2)}, u32[]{:S(2)}) async-start(f32[16,16,512]{2,1,0:T(8,128)} %shard_map.61), calls=%async_computation.3 | async-start | bytes 1048576 | tf_op jit(solution)/shard_map/all_to_all | solution.py:177
  86.9 14.8 %copy-start.4 = (bf16[2,128,512]{2,1,0:T(8,128)(2,1)}, bf16[2,128,512]{2,1,0:T(8,128)(2,1)S(1)}, u32[]{:S(2)}) copy-start(bf16[2,128,512]{2,1,0:T(8,128)(2,1)S(1)} %bitcast_convert_fusion.refs_0_) | copy-start | bytes 786436
  86.9 6.6 %collective-permute-start.5 = (bf16[2,128,512]{2,1,0:T(8,128)(2,1)S(1)}, bf16[2,128,512]{2,1,0:T(8,128)(2,1)S(1)}, u32[]{:S(2)}, u32[]{:S(2)}) collective-permute-start(bf16[2,128,512]{2,1,0:T(8,128)(2,1)S(1)} %bitcast_convert_fusion.refs_0_), channel_id=1, source_target_pairs={{0,2},{1,3},{2,0},{3,1},{4,6},{5,7},{6,4},{7,5},{8,10},{9,11},{10,... | collective-permute-start | bytes 786440 | tf_op jit(solution)/shard_map/ppermute | solution.py:52
  93.5 8.3 %copy-start.10 = (bf16[2,128,512]{2,1,0:T(8,128)(2,1)}, bf16[2,128,512]{2,1,0:T(8,128)(2,1)S(1)}, u32[]{:S(2)}) copy-start(bf16[2,128,512]{2,1,0:T(8,128)(2,1)S(1)} %collective-permute-done.5.refs_1_) | copy-start | bytes 786436
  93.5 8.2 %collective-permute-start.6 = (bf16[2,128,512]{2,1,0:T(8,128)(2,1)S(1)}, bf16[2,128,512]{2,1,0:T(8,128)(2,1)S(1)}, u32[]{:S(2)}, u32[]{:S(2)}) collective-permute-start(bf16[2,128,512]{2,1,0:T(8,128)(2,1)S(1)} %bitcast_convert_fusion.refs_0_), channel_id=1, source_target_pairs={{0,1},{1,0},{2,3},{3,2},{4,5},{5,4},{6,7},{7,6},{8,9},{9,8},{10,11... | collective-permute-start | bytes 786440 | tf_op jit(solution)/shard_map/ppermute | solution.py:52
  93.5 8.2 %collective-permute-start.7 = (bf16[2,128,512]{2,1,0:T(8,128)(2,1)S(1)}, bf16[2,128,512]{2,1,0:T(8,128)(2,1)}, u32[]{:S(2)}, u32[]{:S(2)}) collective-permute-start(bf16[2,128,512]{2,1,0:T(8,128)(2,1)S(1)} %collective-permute-done.5.refs_1_), channel_id=1, source_target_pairs={{0,1},{1,0},{2,3},{3,2},{4,5},{5,4},{6,7},{7,6},{8,9},{9,8},{10,11... | collective-permute-start | bytes 786440 | tf_op jit(solution)/shard_map/ppermute | solution.py:52
  100.1 7.0 %copy-start.3 = (bf16[2,128,512]{2,1,0:T(8,128)(2,1)}, bf16[2,128,512]{2,1,0:T(8,128)(2,1)S(1)}, u32[]{:S(2)}) copy-start(bf16[2,128,512]{2,1,0:T(8,128)(2,1)S(1)} %bitcast_convert_fusion.1.refs_0_) | copy-start | bytes 786436
  100.2 6.4 %collective-permute-start.4 = (bf16[2,128,512]{2,1,0:T(8,128)(2,1)S(1)}, bf16[2,128,512]{2,1,0:T(8,128)(2,1)S(1)}, u32[]{:S(2)}, u32[]{:S(2)}) collective-permute-start(bf16[2,128,512]{2,1,0:T(8,128)(2,1)S(1)} %bitcast_convert_fusion.1.refs_0_), channel_id=1, source_target_pairs={{0,2},{1,3},{2,0},{3,1},{4,6},{5,7},{6,4},{7,5},{8,10},{9,11},{10,... | collective-permute-start | bytes 786440 | tf_op jit(solution)/shard_map/ppermute | solution.py:52
  101.7 0.7 copy-start.11
  106.6 1.9 %copy-start.9 = (bf16[2,128,512]{2,1,0:T(8,128)(2,1)}, bf16[2,128,512]{2,1,0:T(8,128)(2,1)S(1)}, u32[]{:S(2)}) copy-start(bf16[2,128,512]{2,1,0:T(8,128)(2,1)S(1)} %collective-permute-done.4.refs_1_) | copy-start | bytes 786436
  106.6 1.9 %collective-permute-start.8 = (bf16[2,128,512]{2,1,0:T(8,128)(2,1)S(1)}, bf16[2,128,512]{2,1,0:T(8,128)(2,1)S(1)}, u32[]{:S(2)}, u32[]{:S(2)}) collective-permute-start(bf16[2,128,512]{2,1,0:T(8,128)(2,1)S(1)} %bitcast_convert_fusion.1.refs_0_), channel_id=1, source_target_pairs={{0,1},{1,0},{2,3},{3,2},{4,5},{5,4},{6,7},{7,6},{8,9},{9,8},{10,11... | collective-permute-start | bytes 786440 | tf_op jit(solution)/shard_map/ppermute | solution.py:52
  106.6 2.0 %collective-permute-start.9 = (bf16[2,128,512]{2,1,0:T(8,128)(2,1)S(1)}, bf16[2,128,512]{2,1,0:T(8,128)(2,1)}, u32[]{:S(2)}, u32[]{:S(2)}) collective-permute-start(bf16[2,128,512]{2,1,0:T(8,128)(2,1)S(1)} %collective-permute-done.4.refs_1_), channel_id=1, source_target_pairs={{0,1},{1,0},{2,3},{3,2},{4,5},{5,4},{6,7},{7,6},{8,9},{9,8},{10,11... | collective-permute-start | bytes 786440 | tf_op jit(solution)/shard_map/ppermute | solution.py:52
  108.5 4.6 %copy-start = (f32[2,512,128]{2,1,0:T(8,128)S(1)}, f32[2,512,128]{2,1,0:T(8,128)}, u32[]{:S(2)}) copy-start(f32[2,512,128]{2,1,0:T(8,128)} %shard_map.62) | copy-start | bytes 1572868
  108.5 0.7 copy-start.12

commit v19 on v17

--- a/solution.py
+++ b/solution.py
@@ -112,20 +112,15 @@
         masked.reshape(stations_local, hours, CHUNKS, tm_count, chunk_members),
         (3, 0, 1, 2, 4),
     ).reshape(tm_count, stations_local, hours * members_here)
-    high = lax.reduce_precision(decay, exponent_bits=8, mantissa_bits=7)
-    middle = lax.reduce_precision(decay - high, exponent_bits=8, mantissa_bits=7)
-    low = decay - high - middle
-    pieces = jnp.stack([high, middle, low]).astype(obs.dtype).reshape(-1, hours * members_here)
-    spare = (-(stations_local + pieces.shape[0])) % 16
-    pieces = jnp.pad(pieces, ((0, spare), (0, 0)))
-    pieces = jnp.broadcast_to(pieces[None], (tm_count,) + pieces.shape)
-    outgoing = jnp.concatenate([outgoing, pieces], axis=1)
     by_member = lax.all_to_all(outgoing, "tm", split_axis=0, concat_axis=0, tiled=True)
     stations_here = tm_count * stations_local
-    slab_hours, comps_here = decay.shape
-    arrived = by_member[:, stations_local:stations_local + 3 * slab_hours * comps_here // (hours * members_here)]
-    arrived = arrived.reshape(tm_count, 3, slab_hours, comps_here).astype(jnp.float32)
-    decay_all = (arrived[:, 0] + arrived[:, 1] + arrived[:, 2]).reshape(hours, comps_here)
+    slabs, _ = doubling_gather(decay, "tm", [])
+    tm_levels = tm_count.bit_length() - 1
+    wanted = jnp.arange(tm_count) ^ lax.axis_index("tm")
+    position = jnp.zeros_like(wanted)
+    for level in range(tm_levels):
+        position = position | (((wanted >> level) & 1) << (tm_levels - 1 - level))
+    decay_all = jnp.take(jnp.stack(slabs), position, axis=0).reshape(hours, decay.shape[1])
     masked_later, by_member = lax.optimization_barrier((masked, by_member))
     by_hour = lax.all_to_all(masked_later, "tm", split_axis=1, concat_axis=0, tiled=True)
     all_comps = loadings.shape[1]

time: 114 us -> 120 us (1.053)
  starting transfers between devices: 30 us -> 38.9 us
  waiting for transfers between devices: 47.6 us -> 43.8 us
  local copies, waits for them, and re-layouts: 10.2 us -> 12 us
  other arithmetic: 8.11 us -> 6.76 us
    all_to_all x1, waiting for transfers between devices: 17.3 us -> 0.01 us  [local(): lax.all_to_all(outgoing, 'tm', split_axis=0, concat_axis=0, tiled=True)]
    ppermute x6 -> x13, waiting for transfers between devices: 5.3 us -> 17.8 us  [doubling_gather(): pieces = pieces + [lax.ppermute(piece, axis, pairs) for piece in pieces]]
    ppermute x6 -> x13, starting transfers between devices: 4.19 us -> 13.2 us  [doubling_gather(): pieces = pieces + [lax.ppermute(piece, axis, pairs) for piece in pieces]]
    ppermute x1, waiting for transfers between devices: 0.46 us -> 1.83 us  [local(): received = lax.ppermute(outgoing, 'state', pairs)]
    unnamed x27 -> x36, local copies, waits for them, and re-layouts: 7.65 us -> 8.65 us
  transfers between devices with their start and end apart: 14 -> 21, of which waited for: 8 -> 9; matrix products, arithmetic and copies ran while one was open for 7% -> 7% of each run, Pallas kernels for 5% -> 9%
where the time goes in v19:
time: 120 us; the launch traced here: 119 us
  waiting for transfers between devices  43.8 us (36%)
  starting transfers between devices  38.9 us (32%)
  Pallas kernels  16.8 us (14%)
  local copies, waits for them, and re-layouts  12 us (10%)
  other arithmetic  6.76 us (6%)
    ppermute x13, waiting for transfers between devices, doubling_gather(): pieces = pieces + [lax.ppermute(piece, axis, pairs) for piece in pieces]  17.8 us
    ppermute x13, starting transfers between devices, doubling_gather(): pieces = pieces + [lax.ppermute(piece, axis, pairs) for piece in pieces]  13.2 us
    all_to_all x2, starting transfers between devices, local(): lax.all_to_all(smoothed_here, 'tm', split_axis=0, concat_axis=1, tiled=True)  11.3 us
    ppermute x1, waiting for transfers between devices, local(): lax.ppermute(o, 'state', last[c + 1][2])  10.9 us
    unnamed x36, local copies, waits for them, and re-layouts  8.65 us
    all_to_all x1, waiting for transfers between devices, local(): lax.all_to_all(masked_later, 'tm', split_axis=1, concat_axis=0, tiled=True)  8.26 us
    pallas_call x2, Pallas kernels, local(): vmem_call(fitted_kernel, jax.ShapeDtypeStruct((slab_hours, stations_here,...  7.69 us
    all_to_all x1, starting transfers between devices, local(): lax.all_to_all(outgoing, 'tm', split_axis=0, concat_axis=0, tiled=True)  7.25 us
  transfers between devices with their start and end apart: 21, of which 9 were waited for; matrix products, arithmetic and copies ran while one was open for 7% of the time, Pallas kernels for 9%

profile of v19, /device:TPU:0, one launch (start us, length us, event | category | flops | bytes accessed | tf_op | source)
XLA Modules:
  0.0 119.1 jit_solution(8162986703554856359)
XLA Ops:
  1.3 1.7 %copy.21 = bf16[64,16,256]{0,2,1:T(8,128)(2,1)S(1)} copy(bf16[64,16,256]{2,1,0:T(8,128)(2,1)} %param.4) | data formatting | bytes 1048576 | tf_op args[0]
  3.3 1.1 copy.23
  4.5 7.3 %all-to-all-start = ((bf16[8,64,512]{2,1,0:T(8,128)(2,1)}), bf16[8,64,512]{2,1,0:T(8,128)(2,1)S(1)}, u32[]{:S(2)}, u32[]{:S(2)}) async-start(bf16[8,64,512]{2,1,0:T(8,128)(2,1)} %copy.23), calls=%async_computation | async-start | bytes 1048576 | tf_op jit(solution)/shard_map/all_to_all | solution.py:115
  11.7 2.9 %collective-permute-start = (f32[2,512]{1,0:T(2,128)S(1)}, f32[2,512]{1,0:T(2,128)S(1)}, u32[]{:S(2)}, u32[]{:S(2)}) collective-permute-start(f32[2,512]{1,0:T(2,128)S(1)} %copy-done.12), channel_id=1, source_target_pairs={{0,16},{4,20},{8,24},{12,28},{16,0},{20,4},{24,8},{28,12},{1,17},{... | collective-permute-start | bytes 12296 | tf_op jit(solution)/shard_map/ppermute | solution.py:52
  14.8 11.5 %collective-permute-done = f32[2,512]{1,0:T(2,128)S(1)} collective-permute-done((f32[2,512]{1,0:T(2,128)S(1)}, f32[2,512]{1,0:T(2,128)S(1)}, u32[]{:S(2)}, u32[]{:S(2)}) %collective-permute-start) | collective-permute-done | bytes 4128 | tf_op jit(solution)/shard_map/ppermute | solution.py:52
  26.4 1.5 %collective-permute-start.3 = (f32[2,512]{1,0:T(2,128)S(1)}, f32[2,512]{1,0:T(2,128)S(1)}, u32[]{:S(2)}, u32[]{:S(2)}) collective-permute-start(f32[2,512]{1,0:T(2,128)S(1)} %copy-done.12), channel_id=1, source_target_pairs={{0,4},{4,0},{8,12},{12,8},{16,20},{20,16},{24,28},{28,24},{1,5},{5... | collective-permute-start | bytes 12296 | tf_op jit(solution)/shard_map/ppermute | solution.py:52
  28.4 2.0 %collective-permute-start.2 = (f32[2,512]{1,0:T(2,128)S(1)}, f32[2,512]{1,0:T(2,128)S(1)}, u32[]{:S(2)}, u32[]{:S(2)}) collective-permute-start(f32[2,512]{1,0:T(2,128)S(1)} %collective-permute-done), channel_id=1, source_target_pairs={{0,8},{4,12},{8,0},{12,4},{16,24},{20,28},{24,16},{28,20},{1,9},{5... | collective-permute-start | bytes 12296 | tf_op jit(solution)/shard_map/ppermute | solution.py:52
  30.4 1.0 collective-permute-done.1
  32.0 1.5 %collective-permute-start.6 = (f32[2,512]{1,0:T(2,128)S(1)}, f32[2,512]{1,0:T(2,128)S(1)}, u32[]{:S(2)}, u32[]{:S(2)}) collective-permute-start(f32[2,512]{1,0:T(2,128)S(1)} %collective-permute-done.2), channel_id=1, source_target_pairs={{0,4},{4,0},{8,12},{12,8},{16,20},{20,16},{24,28},{28,24},{1,5},{5... | collective-permute-start | bytes 12296 | tf_op jit(solution)/shard_map/ppermute | solution.py:52
  34.3 4.8 %shard_map.59 = (f32[2,256,512]{2,1,0:T(8,128)}, f32[2,256,512]{2,1,0:T(8,128)}, f32[2,256,512]{2,1,0:T(8,128)}, f32[2,256,512]{2,1,0:T(8,128)}) custom-call(s32[1]{0:T(128)} %bitcast.15.me_ref, bf16[8,64,512]{2,1,0:T(8,128)(2,1)} %copy-done.6, bf16[512,2048]{1,0:T(8,128)(2,1)} %l_ref.5), custom_call_target="tpu_custom_call" | custom-call | flops 1073741824 | bytes 6815744 | tf_op jit(solution)/shard_map/pallas_call | solution.py:130
  39.7 1.1 copy.24
  40.8 3.5 %all-to-all-start.1 = ((bf16[64,16,256]{2,0,1:T(8,128)(2,1)}), bf16[64,16,256]{2,0,1:T(8,128)(2,1)S(1)}, u32[]{:S(2)}, u32[]{:S(2)}) async-start(bf16[64,16,256]{2,0,1:T(8,128)(2,1)} %copy.24), calls=%async_computation.1 | async-start | bytes 1048576 | tf_op jit(solution)/shard_map/all_to_all | solution.py:125
  45.3 2.8 %fusion.2 = (f32[256,512]{1,0:T(8,128)}, f32[256,512]{1,0:T(8,128)}) fusion(f32[2,256,512]{2,1,0:T(8,128)} %copy-done.2, f32[2,256,512]{2,1,0:T(8,128)} %get-tuple-element.24), kind=kLoop, calls=%fused_computation.8 | loop fusion | flops 262144 | bytes 3145728 | tf_op jit(solution)/shard_map/add | solution.py:40
  48.1 1.5 %collective-permute-start.8 = (f32[256,512]{1,0:T(8,128)}, f32[256,512]{1,0:T(8,128)}, u32[]{:S(2)}, u32[]{:S(2)}) collective-permute-start(f32[256,512]{1,0:T(8,128)} %get-tuple-element.46), channel_id=1, source_target_pairs={{0,2},{1,3},{2,0},{3,1},{4,6},{5,7},{6,4},{7,5},{8,10},{9,11},{10,... | collective-permute-start | bytes 1572872 | tf_op jit(solution)/shard_map/ppermute | solution.py:147
  50.9 8.3 %all-to-all-done.1 = bf16[64,16,256]{2,0,1:T(8,128)(2,1)S(1)} async-done(((bf16[64,16,256]{2,0,1:T(8,128)(2,1)}), bf16[64,16,256]{2,0,1:T(8,128)(2,1)S(1)}, u32[]{:S(2)}, u32[]{:S(2)}) %all-to-all-start.1) | async-done | bytes 524320 | tf_op jit(solution)/shard_map/all_to_all | solution.py:125
  59.2 1.2 fusion
  60.4 1.8 %collective-permute-done.8 = f32[256,512]{1,0:T(8,128)} collective-permute-done((f32[256,512]{1,0:T(8,128)}, f32[256,512]{1,0:T(8,128)}, u32[]{:S(2)}, u32[]{:S(2)}) %collective-permute-start.8) | collective-permute-done | bytes 524320 | tf_op jit(solution)/shard_map/ppermute | solution.py:147
  62.3 2.2 %shard_map.60 = f32[16,16,512]{2,1,0:T(8,128)} custom-call(f32[16,512]{1,0:T(8,128)} %broadcast_select_fusion.rate_ref, f32[16,16,512]{2,1,0:T(8,128)} %bitcast.63, f32[16,16,512]{2,1,0:T(8,128)} %bitcast.21.received_ref), custom_call_target="tpu_custom_call" | custom-call | flops 786432 | bytes 1572864 | tf_op jit(solution)/shard_map/pallas_call | solution.py:157
  64.4 5.6 %all-to-all-start.2 = ((f32[16,16,512]{2,1,0:T(8,128)}), f32[16,16,512]{2,1,0:T(8,128)S(1)}, u32[]{:S(2)}, u32[]{:S(2)}) async-start(f32[16,16,512]{2,1,0:T(8,128)} %shard_map.60), calls=%async_computation.2 | async-start | bytes 1048576 | tf_op jit(solution)/shard_map/all_to_all | solution.py:167
  70.1 1.6 %collective-permute-start.10 = (f32[256,512]{1,0:T(8,128)S(1)}, f32[256,512]{1,0:T(8,128)S(1)}, u32[]{:S(2)}, u32[]{:S(2)}) collective-permute-start(f32[256,512]{1,0:T(8,128)S(1)} %copy-done.7), channel_id=1, source_target_pairs={{0,2},{1,3},{2,0},{3,1},{4,6},{5,7},{6,4},{7,5},{8,10},{9,11},{10,... | collective-permute-start | bytes 1572872 | tf_op jit(solution)/shard_map/ppermute | solution.py:151
  71.7 10.9 %collective-permute-done.10 = f32[256,512]{1,0:T(8,128)S(1)} collective-permute-done((f32[256,512]{1,0:T(8,128)S(1)}, f32[256,512]{1,0:T(8,128)S(1)}, u32[]{:S(2)}, u32[]{:S(2)}) %collective-permute-start.10) | collective-permute-done | bytes 524320 | tf_op jit(solution)/shard_map/ppermute | solution.py:151
  83.3 2.1 %shard_map.61 = f32[16,16,512]{2,1,0:T(8,128)} custom-call(f32[16,512]{1,0:T(8,128)} %broadcast_select_fusion.rate_ref, f32[16,16,512]{2,1,0:T(8,128)} %bitcast.66, f32[16,16,512]{2,1,0:T(8,128)} %bitcast.67), custom_call_target="tpu_custom_call" | custom-call | flops 786432 | bytes 1572864 | tf_op jit(solution)/shard_map/pallas_call | solution.py:157
  85.5 5.7 %all-to-all-start.3 = ((f32[16,16,512]{2,1,0:T(8,128)}), f32[16,16,512]{2,1,0:T(8,128)S(1)}, u32[]{:S(2)}, u32[]{:S(2)}) async-start(f32[16,16,512]{2,1,0:T(8,128)} %shard_map.61), calls=%async_computation.3 | async-start | bytes 1048576 | tf_op jit(solution)/shard_map/all_to_all | solution.py:167
  91.2 1.6 %collective-permute-start.12 = (bf16[2,128,512]{2,1,0:T(8,128)(2,1)S(1)}, bf16[2,128,512]{2,1,0:T(8,128)(2,1)S(1)}, u32[]{:S(2)}, u32[]{:S(2)}) collective-permute-start(bf16[2,128,512]{2,1,0:T(8,128)(2,1)S(1)} %bitcast_convert_fusion.refs_0_), channel_id=1, source_target_pairs={{0,2},{1,3},{2,0},{3,1},{4,6},{5,7},{6,4},{7,5},{8,10},{9,11},{10,... | collective-permute-start | bytes 786440 | tf_op jit(solution)/shard_map/ppermute | solution.py:52
  92.8 4.9 %collective-permute-done.12.refs_1_ = bf16[2,128,512]{2,1,0:T(8,128)(2,1)S(1)} collective-permute-done((bf16[2,128,512]{2,1,0:T(8,128)(2,1)S(1)}, bf16[2,128,512]{2,1,0:T(8,128)(2,1)S(1)}, u32[]{:S(2)}, u32[]{:S(2)}) %collective-permute-start.12) | collective-permute-done | bytes 262176 | tf_op jit(solution)/shard_map/ppermute | solution.py:52
  98.2 5.0 %all-to-all-done.3 = f32[16,16,512]{2,1,0:T(8,128)S(1)} async-done(((f32[16,16,512]{2,1,0:T(8,128)}), f32[16,16,512]{2,1,0:T(8,128)S(1)}, u32[]{:S(2)}, u32[]{:S(2)}) %all-to-all-start.3) | async-done | bytes 524320 | tf_op jit(solution)/shard_map/all_to_all | solution.py:167
  103.2 1.6 %collective-permute-start.11 = (bf16[2,128,512]{2,1,0:T(8,128)(2,1)S(1)}, bf16[2,128,512]{2,1,0:T(8,128)(2,1)S(1)}, u32[]{:S(2)}, u32[]{:S(2)}) collective-permute-start(bf16[2,128,512]{2,1,0:T(8,128)(2,1)S(1)} %bitcast_convert_fusion.1.refs_0_), channel_id=1, source_target_pairs={{0,2},{1,3},{2,0},{3,1},{4,6},{5,7},{6,4},{7,5},{8,10},{9,11},{10,... | collective-permute-start | bytes 786440 | tf_op jit(solution)/shard_map/ppermute | solution.py:52
  105.5 3.9 %shard_map.62 = f32[2,512,128]{2,1,0:T(8,128)} custom-call(s32[1]{0:T(128)} %bitcast.15.me_ref, bf16[512,2048]{1,0:T(8,128)(2,1)} %l_ref.5, bf16[2,128,512]{2,1,0:T(8,128)(2,1)} %copy-done.4, bf16[2,128,512]{2,1,0:T(8,128)(2,1)} %copy-done.9, bf16[2,128,512]{2,1,0:T(8,128)(2,1)} %copy-done.10, bf16[2,128,512]{2,1,0:T(8,128)(2,1)} %collective-permute-done.14.refs_3_), custom_call_target="tpu_custom_call" | custom-call | flops 536870912 | bytes 3670016 | tf_op jit(solution)/shard_map/pallas_call | solution.py:172
  110.3 1.3 %copy.28 = f32[512,2,256]{2,1,0:T(2,128)} copy(f32[512,2,256]{0,2,1:T(8,128)S(1)} %pad_maximum_fusion) | data formatting | bytes 2097152
  112.3 3.8 %shard_map.63 = f32[2,512,128]{2,1,0:T(8,128)} custom-call(s32[1]{0:T(128)} %bitcast.15.me_ref, bf16[512,2048]{1,0:T(8,128)(2,1)} %l_ref.5, bf16[2,128,512]{2,1,0:T(8,128)(2,1)} %copy-done.3, bf16[2,128,512]{2,1,0:T(8,128)(2,1)} %copy-done.8, bf16[2,128,512]{2,1,0:T(8,128)(2,1)} %copy-done.11, bf16[2,128,512]{2,1,0:T(8,128)(2,1)} %collective-permute-done.16.refs_3_), custom_call_target="tpu_custom_call" | custom-call | flops 536870912 | bytes 3670016 | tf_op jit(solution)/shard_map/pallas_call | solution.py:172
  116.1 1.1 bitcast_subtract_fusion.1
  117.3 1.8 %copy.29 = f32[512,2,256]{2,1,0:T(2,128)} copy(f32[512,2,256]{2,0,1:T(8,128)S(1)} %pad_maximum_fusion.1) | data formatting | bytes 2097152
  (75 shorter events, 9.8 us)
Async XLA Ops:
  3.1 8.6 %copy-start.12 = (f32[2,512]{1,0:T(2,128)S(1)}, f32[2,512]{1,0:T(2,128)}, u32[]{:S(2)}) copy-start(f32[2,512]{1,0:T(2,128)} %param.7) | copy-start | bytes 12292
  4.5 29.0 %all-to-all-start = ((bf16[8,64,512]{2,1,0:T(8,128)(2,1)}), bf16[8,64,512]{2,1,0:T(8,128)(2,1)S(1)}, u32[]{:S(2)}, u32[]{:S(2)}) async-start(bf16[8,64,512]{2,1,0:T(8,128)(2,1)} %copy.23), calls=%async_computation | async-start | bytes 1048576 | tf_op jit(solution)/shard_map/all_to_all | solution.py:115
  11.7 14.7 %collective-permute-start = (f32[2,512]{1,0:T(2,128)S(1)}, f32[2,512]{1,0:T(2,128)S(1)}, u32[]{:S(2)}, u32[]{:S(2)}) collective-permute-start(f32[2,512]{1,0:T(2,128)S(1)} %copy-done.12), channel_id=1, source_target_pairs={{0,16},{4,20},{8,24},{12,28},{16,0},{20,4},{24,8},{28,12},{1,17},{... | collective-permute-start | bytes 12296 | tf_op jit(solution)/shard_map/ppermute | solution.py:52
  26.4 12.7 %collective-permute-start.3 = (f32[2,512]{1,0:T(2,128)S(1)}, f32[2,512]{1,0:T(2,128)S(1)}, u32[]{:S(2)}, u32[]{:S(2)}) collective-permute-start(f32[2,512]{1,0:T(2,128)S(1)} %copy-done.12), channel_id=1, source_target_pairs={{0,4},{4,0},{8,12},{12,8},{16,20},{20,16},{24,28},{28,24},{1,5},{5... | collective-permute-start | bytes 12296 | tf_op jit(solution)/shard_map/ppermute | solution.py:52
  27.8 3.6 %collective-permute-start.1 = (f32[2,512]{1,0:T(2,128)S(1)}, f32[2,512]{1,0:T(2,128)S(1)}, u32[]{:S(2)}, u32[]{:S(2)}) collective-permute-start(f32[2,512]{1,0:T(2,128)S(1)} %copy-done.12), channel_id=1, source_target_pairs={{0,8},{4,12},{8,0},{12,4},{16,24},{20,28},{24,16},{28,20},{1,9},{5... | collective-permute-start | bytes 12296 | tf_op jit(solution)/shard_map/ppermute | solution.py:52
  27.8 11.8 %collective-permute-start.4 = (f32[2,512]{1,0:T(2,128)S(1)}, f32[2,512]{1,0:T(2,128)S(1)}, u32[]{:S(2)}, u32[]{:S(2)}) collective-permute-start(f32[2,512]{1,0:T(2,128)S(1)} %collective-permute-done), channel_id=1, source_target_pairs={{0,4},{4,0},{8,12},{12,8},{16,20},{20,16},{24,28},{28,24},{1,5},{5... | collective-permute-start | bytes 12296 | tf_op jit(solution)/shard_map/ppermute | solution.py:52
  28.4 3.6 %collective-permute-start.2 = (f32[2,512]{1,0:T(2,128)S(1)}, f32[2,512]{1,0:T(2,128)S(1)}, u32[]{:S(2)}, u32[]{:S(2)}) collective-permute-start(f32[2,512]{1,0:T(2,128)S(1)} %collective-permute-done), channel_id=1, source_target_pairs={{0,8},{4,12},{8,0},{12,4},{16,24},{20,28},{24,16},{28,20},{1,9},{5... | collective-permute-start | bytes 12296 | tf_op jit(solution)/shard_map/ppermute | solution.py:52
  31.4 12.9 %collective-permute-start.5 = (f32[2,512]{1,0:T(2,128)S(1)}, f32[2,512]{1,0:T(2,128)S(1)}, u32[]{:S(2)}, u32[]{:S(2)}) collective-permute-start(f32[2,512]{1,0:T(2,128)S(1)} %collective-permute-done.1), channel_id=1, source_target_pairs={{0,4},{4,0},{8,12},{12,8},{16,20},{20,16},{24,28},{28,24},{1,5},{5... | collective-permute-start | bytes 12296 | tf_op jit(solution)/shard_map/ppermute | solution.py:52
  32.0 17.6 %collective-permute-start.6 = (f32[2,512]{1,0:T(2,128)S(1)}, f32[2,512]{1,0:T(2,128)S(1)}, u32[]{:S(2)}, u32[]{:S(2)}) collective-permute-start(f32[2,512]{1,0:T(2,128)S(1)} %collective-permute-done.2), channel_id=1, source_target_pairs={{0,4},{4,0},{8,12},{12,8},{16,20},{20,16},{24,28},{28,24},{1,5},{5... | collective-permute-start | bytes 12296 | tf_op jit(solution)/shard_map/ppermute | solution.py:52
  33.5 0.8 copy-start.6
  39.1 5.3 %collective-permute-start.7 = (f32[2,256,512]{2,1,0:T(8,128)}, f32[2,256,512]{2,1,0:T(8,128)S(1)}, u32[]{:S(2)}, u32[]{:S(2)}) collective-permute-start(f32[2,256,512]{2,1,0:T(8,128)} %get-tuple-element.25), channel_id=1, source_target_pairs={{0,1},{1,0},{2,3},{3,2},{4,5},{5,4},{6,7},{7,6},{8,9},{9,8},{10,11... | collective-permute-start | bytes 3145736 | tf_op jit(solution)/shard_map/ppermute | solution.py:38
  39.1 20.1 %collective-permute-start.9 = (f32[2,256,512]{2,1,0:T(8,128)}, f32[2,256,512]{2,1,0:T(8,128)S(1)}, u32[]{:S(2)}, u32[]{:S(2)}) collective-permute-start(f32[2,256,512]{2,1,0:T(8,128)} %get-tuple-element.27), channel_id=1, source_target_pairs={{0,1},{1,0},{2,3},{3,2},{4,5},{5,4},{6,7},{7,6},{8,9},{9,8},{10,11... | collective-permute-start | bytes 3145736 | tf_op jit(solution)/shard_map/ppermute | solution.py:38
  40.8 18.4 %all-to-all-start.1 = ((bf16[64,16,256]{2,0,1:T(8,128)(2,1)}), bf16[64,16,256]{2,0,1:T(8,128)(2,1)S(1)}, u32[]{:S(2)}, u32[]{:S(2)}) async-start(bf16[64,16,256]{2,0,1:T(8,128)(2,1)} %copy.24), calls=%async_computation.1 | async-start | bytes 1048576 | tf_op jit(solution)/shard_map/all_to_all | solution.py:125
  44.3 1.0 copy-start.2
  45.3 13.9 %copy-start.1 = (f32[2,256,512]{2,1,0:T(8,128)S(1)}, f32[2,256,512]{2,1,0:T(8,128)}, u32[]{:S(2)}) copy-start(f32[2,256,512]{2,1,0:T(8,128)} %get-tuple-element.26) | copy-start | bytes 3145732
  48.1 14.2 %collective-permute-start.8 = (f32[256,512]{1,0:T(8,128)}, f32[256,512]{1,0:T(8,128)}, u32[]{:S(2)}, u32[]{:S(2)}) collective-permute-start(f32[256,512]{1,0:T(8,128)} %get-tuple-element.46), channel_id=1, source_target_pairs={{0,2},{1,3},{2,0},{3,1},{4,6},{5,7},{6,4},{7,5},{8,10},{9,11},{10,... | collective-permute-start | bytes 1572872 | tf_op jit(solution)/shard_map/ppermute | solution.py:147
  60.4 9.6 %copy-start.7 = (f32[256,512]{1,0:T(8,128)S(1)}, f32[256,512]{1,0:T(8,128)}, u32[]{:S(2)}) copy-start(f32[256,512]{1,0:T(8,128)} %get-tuple-element.31) | copy-start | bytes 1572868
  64.4 21.0 %all-to-all-start.2 = ((f32[16,16,512]{2,1,0:T(8,128)}), f32[16,16,512]{2,1,0:T(8,128)S(1)}, u32[]{:S(2)}, u32[]{:S(2)}) async-start(f32[16,16,512]{2,1,0:T(8,128)} %shard_map.60), calls=%async_computation.2 | async-start | bytes 1048576 | tf_op jit(solution)/shard_map/all_to_all | solution.py:167
  70.1 12.5 %collective-permute-start.10 = (f32[256,512]{1,0:T(8,128)S(1)}, f32[256,512]{1,0:T(8,128)S(1)}, u32[]{:S(2)}, u32[]{:S(2)}) collective-permute-start(f32[256,512]{1,0:T(8,128)S(1)} %copy-done.7), channel_id=1, source_target_pairs={{0,2},{1,3},{2,0},{3,1},{4,6},{5,7},{6,4},{7,5},{8,10},{9,11},{10,... | collective-permute-start | bytes 1572872 | tf_op jit(solution)/shard_map/ppermute | solution.py:151
  82.5 0.8 copy-start.5
  85.5 17.7 %all-to-all-start.3 = ((f32[16,16,512]{2,1,0:T(8,128)}), f32[16,16,512]{2,1,0:T(8,128)S(1)}, u32[]{:S(2)}, u32[]{:S(2)}) async-start(f32[16,16,512]{2,1,0:T(8,128)} %shard_map.61), calls=%async_computation.3 | async-start | bytes 1048576 | tf_op jit(solution)/shard_map/all_to_all | solution.py:167
  91.2 13.6 %copy-start.4 = (bf16[2,128,512]{2,1,0:T(8,128)(2,1)}, bf16[2,128,512]{2,1,0:T(8,128)(2,1)S(1)}, u32[]{:S(2)}) copy-start(bf16[2,128,512]{2,1,0:T(8,128)(2,1)S(1)} %bitcast_convert_fusion.refs_0_) | copy-start | bytes 786436
  91.2 6.4 %collective-permute-start.12 = (bf16[2,128,512]{2,1,0:T(8,128)(2,1)S(1)}, bf16[2,128,512]{2,1,0:T(8,128)(2,1)S(1)}, u32[]{:S(2)}, u32[]{:S(2)}) collective-permute-start(bf16[2,128,512]{2,1,0:T(8,128)(2,1)S(1)} %bitcast_convert_fusion.refs_0_), channel_id=1, source_target_pairs={{0,2},{1,3},{2,0},{3,1},{4,6},{5,7},{6,4},{7,5},{8,10},{9,11},{10,... | collective-permute-start | bytes 786440 | tf_op jit(solution)/shard_map/ppermute | solution.py:52
  97.7 7.2 %copy-start.9 = (bf16[2,128,512]{2,1,0:T(8,128)(2,1)}, bf16[2,128,512]{2,1,0:T(8,128)(2,1)S(1)}, u32[]{:S(2)}) copy-start(bf16[2,128,512]{2,1,0:T(8,128)(2,1)S(1)} %collective-permute-done.12.refs_1_) | copy-start | bytes 786436
  97.7 7.2 %collective-permute-start.13 = (bf16[2,128,512]{2,1,0:T(8,128)(2,1)S(1)}, bf16[2,128,512]{2,1,0:T(8,128)(2,1)S(1)}, u32[]{:S(2)}, u32[]{:S(2)}) collective-permute-start(bf16[2,128,512]{2,1,0:T(8,128)(2,1)S(1)} %bitcast_convert_fusion.refs_0_), channel_id=1, source_target_pairs={{0,1},{1,0},{2,3},{3,2},{4,5},{5,4},{6,7},{7,6},{8,9},{9,8},{10,11... | collective-permute-start | bytes 786440 | tf_op jit(solution)/shard_map/ppermute | solution.py:52
  97.7 7.2 %collective-permute-start.14 = (bf16[2,128,512]{2,1,0:T(8,128)(2,1)S(1)}, bf16[2,128,512]{2,1,0:T(8,128)(2,1)}, u32[]{:S(2)}, u32[]{:S(2)}) collective-permute-start(bf16[2,128,512]{2,1,0:T(8,128)(2,1)S(1)} %collective-permute-done.12.refs_1_), channel_id=1, source_target_pairs={{0,1},{1,0},{2,3},{3,2},{4,5},{5,4},{6,7},{7,6},{8,9},{9,8},{10,11... | collective-permute-start | bytes 786440 | tf_op jit(solution)/shard_map/ppermute | solution.py:52
  103.2 7.0 %copy-start.3 = (bf16[2,128,512]{2,1,0:T(8,128)(2,1)}, bf16[2,128,512]{2,1,0:T(8,128)(2,1)S(1)}, u32[]{:S(2)}) copy-start(bf16[2,128,512]{2,1,0:T(8,128)(2,1)S(1)} %bitcast_convert_fusion.1.refs_0_) | copy-start | bytes 786436
  103.2 6.4 %collective-permute-start.11 = (bf16[2,128,512]{2,1,0:T(8,128)(2,1)S(1)}, bf16[2,128,512]{2,1,0:T(8,128)(2,1)S(1)}, u32[]{:S(2)}, u32[]{:S(2)}) collective-permute-start(bf16[2,128,512]{2,1,0:T(8,128)(2,1)S(1)} %bitcast_convert_fusion.1.refs_0_), channel_id=1, source_target_pairs={{0,2},{1,3},{2,0},{3,1},{4,6},{5,7},{6,4},{7,5},{8,10},{9,11},{10,... | collective-permute-start | bytes 786440 | tf_op jit(solution)/shard_map/ppermute | solution.py:52
  109.7 1.9 %copy-start.8 = (bf16[2,128,512]{2,1,0:T(8,128)(2,1)}, bf16[2,128,512]{2,1,0:T(8,128)(2,1)S(1)}, u32[]{:S(2)}) copy-start(bf16[2,128,512]{2,1,0:T(8,128)(2,1)S(1)} %collective-permute-done.11.refs_1_) | copy-start | bytes 786436
  109.7 1.9 %collective-permute-start.15 = (bf16[2,128,512]{2,1,0:T(8,128)(2,1)S(1)}, bf16[2,128,512]{2,1,0:T(8,128)(2,1)S(1)}, u32[]{:S(2)}, u32[]{:S(2)}) collective-permute-start(bf16[2,128,512]{2,1,0:T(8,128)(2,1)S(1)} %bitcast_convert_fusion.1.refs_0_), channel_id=1, source_target_pairs={{0,1},{1,0},{2,3},{3,2},{4,5},{5,4},{6,7},{7,6},{8,9},{9,8},{10,11... | collective-permute-start | bytes 786440 | tf_op jit(solution)/shard_map/ppermute | solution.py:52
  109.7 2.0 %collective-permute-start.16 = (bf16[2,128,512]{2,1,0:T(8,128)(2,1)S(1)}, bf16[2,128,512]{2,1,0:T(8,128)(2,1)}, u32[]{:S(2)}, u32[]{:S(2)}) collective-permute-start(bf16[2,128,512]{2,1,0:T(8,128)(2,1)S(1)} %collective-permute-done.11.refs_1_), channel_id=1, source_target_pairs={{0,1},{1,0},{2,3},{3,2},{4,5},{5,4},{6,7},{7,6},{8,9},{9,8},{10,11... | collective-permute-start | bytes 786440 | tf_op jit(solution)/shard_map/ppermute | solution.py:52
  111.6 4.5 %copy-start = (f32[2,512,128]{2,1,0:T(8,128)S(1)}, f32[2,512,128]{2,1,0:T(8,128)}, u32[]{:S(2)}) copy-start(f32[2,512,128]{2,1,0:T(8,128)} %shard_map.62) | copy-start | bytes 1572868
  (2 other events, 1.4 us)

commit v20 on v17

--- a/solution.py
+++ b/solution.py
@@ -56,24 +56,26 @@
 
 
 def fitted_kernel(me_ref, l_ref, *refs):
-    *piece_refs, out_ref = refs
+    *piece_refs, observed_ref, out_ref = refs
     me = me_ref[0]
     levels = len(piece_refs).bit_length() - 1
-    width = piece_refs[0].shape[-1]
-    for hour in range(out_ref.shape[0]):
-        total = None
-        for position, piece_ref in enumerate(piece_refs):
-            flipped = 0
-            for level in range(levels):
-                flipped |= ((position >> level) & 1) << (levels - 1 - level)
-            block = me ^ flipped
-            columns = l_ref[:, pl.ds(pl.multiple_of(block * width, width), width)]
-            part = lax.dot_general(
-                columns, piece_ref[hour], (((1,), (1,)), ((), ())),
-                preferred_element_type=jnp.float32,
-            )
-            total = part if total is None else total + part
-        out_ref[hour] = total
+    hours, members, width = piece_refs[0].shape
+    total = None
+    for position, piece_ref in enumerate(piece_refs):
+        flipped = 0
+        for level in range(levels):
+            flipped |= ((position >> level) & 1) << (levels - 1 - level)
+        block = me ^ flipped
+        columns = l_ref[:, pl.ds(pl.multiple_of(block * width, width), width)]
+        piece = piece_ref[...].reshape(hours * members, width)
+        part = lax.dot_general(
+            columns, piece, (((1,), (1,)), ((), ())),
+            preferred_element_type=jnp.float32,
+        )
+        total = part if total is None else total + part
+    for hour in range(hours):
+        observed = observed_ref[hour].astype(jnp.float32)
+        out_ref[hour] = observed - total[:, hour * members:(hour + 1) * members]
 
 
 def recurrence_kernel(rate_ref, keep_ref, received_ref, out_ref):
@@ -174,10 +176,12 @@
         pieces, earlier = doubling_gather(rounded, "state", fitted_parts[-1:])
         fitted_parts[-1:] = earlier
         slab_hours, width, _ = rounded.shape
+        low = chunk * members // CHUNKS
+        observed = jnp.transpose(by_hour[:, :, low:low + members // CHUNKS], (1, 0, 2))
         fitted = vmem_call(
             fitted_kernel,
             jax.ShapeDtypeStruct((slab_hours, stations_here, width), jnp.float32),
-            1 + len(pieces),
+            2 + len(pieces),
             pl.CostEstimate(
                 flops=2 * stations_here * slab_hours * width * all_comps,
                 bytes_accessed=2 * stations_here * all_comps
@@ -186,13 +190,11 @@
                 transcendentals=0,
             ),
             scalars=1,
-        )(lax.axis_index("state").reshape(1).astype(jnp.int32), loadings, *pieces)
+        )(lax.axis_index("state").reshape(1).astype(jnp.int32), loadings, *pieces, observed)
         fitted_parts.append(fitted)
         smoothed_parts.append(jnp.transpose(gathered, (2, 0, 1)))
-    for chunk, fitted in enumerate(fitted_parts):
-        low = chunk * members // CHUNKS
-        picked = by_hour[:, :, low:low + members // CHUNKS]
-        residual_parts.append(picked.astype(jnp.float32) - jnp.transpose(fitted, (1, 0, 2)))
+    for residual in fitted_parts:
+        residual_parts.append(jnp.transpose(residual, (1, 0, 2)))
     return (
         jnp.concatenate(smoothed_parts, axis=2),
         jnp.concatenate(residual_parts, axis=2),

time: 114 us -> 116 us (1.018)
  waiting for transfers between devices: 47.6 us -> 50.5 us
  local copies, waits for them, and re-layouts: 10.2 us -> 12.1 us
  starting transfers between devices: 30 us -> 28.2 us
    all_to_all x2, starting transfers between devices: 11.3 us -> 9.48 us  [local(): lax.all_to_all(smoothed_here, 'tm', split_axis=0, concat_axis=1, tiled=True)]
    ppermute x1, waiting for transfers between devices: 10.6 us -> 11.9 us  [local(): lax.ppermute(o, 'state', last[c + 1][2])]
    all_to_all x2, waiting for transfers between devices: 4.73 us -> 6 us  [local(): lax.all_to_all(smoothed_here, 'tm', split_axis=0, concat_axis=1, tiled=True)]
    all_to_all x1, waiting for transfers between devices: 9.18 us -> 10.4 us  [local(): lax.all_to_all(masked_later, 'tm', split_axis=1, concat_axis=0, tiled=True)]
    unnamed x27 -> x29, local copies, waits for them, and re-layouts: 7.65 us -> 8.74 us
  transfers between devices with their start and end apart: 14 -> 14, of which waited for: 8 -> 5; matrix products, arithmetic and copies ran while one was open for 7% -> 7% of each run, Pallas kernels for 5% -> 5%
where the time goes in v20:
time: 116 us
  waiting for transfers between devices  50.5 us (44%)
  starting transfers between devices  28.2 us (24%)
  Pallas kernels  16 us (14%)
  local copies, waits for them, and re-layouts  12.1 us (10%)
  other arithmetic  7.85 us (7%)
    all_to_all x1, waiting for transfers between devices, local(): lax.all_to_all(outgoing, 'tm', split_axis=0, concat_axis=0, tiled=True)  17.3 us
    ppermute x1, waiting for transfers between devices, local(): lax.ppermute(o, 'state', last[c + 1][2])  11.9 us
    all_to_all x1, waiting for transfers between devices, local(): lax.all_to_all(masked_later, 'tm', split_axis=1, concat_axis=0, tiled=True)  10.4 us
    all_to_all x2, starting transfers between devices, local(): lax.all_to_all(smoothed_here, 'tm', split_axis=0, concat_axis=1, tiled=True)  9.48 us
    unnamed x29, local copies, waits for them, and re-layouts  8.74 us
    all_to_all x1, starting transfers between devices, local(): lax.all_to_all(outgoing, 'tm', split_axis=0, concat_axis=0, tiled=True)  7.25 us
    pallas_call x2, Pallas kernels, local(): vmem_call(fitted_kernel, jax.ShapeDtypeStruct((slab_hours, stations_here,...  6.93 us
    all_to_all x2, waiting for transfers between devices, local(): lax.all_to_all(smoothed_here, 'tm', split_axis=0, concat_axis=1, tiled=True)  6 us
  transfers between devices with their start and end apart: 14, of which 5 were waited for; matrix products, arithmetic and copies ran while one was open for 7% of the time, Pallas kernels for 5%

profile of v20, /device:TPU:0, one launch (start us, length us, event | category | flops | bytes accessed | tf_op | source)
XLA Modules:
  0.0 115.5 jit_solution(4631585206255463256)
XLA Ops:
  0.6 0.7 convert_element_type.23
  2.1 1.7 %copy.37 = bf16[64,16,256]{0,2,1:T(8,128)(2,1)S(1)} copy(bf16[64,16,256]{2,1,0:T(8,128)(2,1)} %param.4) | data formatting | bytes 1048576 | tf_op args[0]
  4.4 0.9 pad_maximum_fusion.2
  5.3 7.3 %all-to-all-start = ((bf16[8,80,512]{2,1,0:T(8,128)(2,1)}), bf16[8,80,512]{2,1,0:T(8,128)(2,1)S(1)}, u32[]{:S(2)}, u32[]{:S(2)}) async-start(bf16[8,80,512]{2,1,0:T(8,128)(2,1)} %pad_maximum_fusion.2), calls=%async_computation | async-start | bytes 1310720 | tf_op jit(solution)/shard_map/all_to_all | solution.py:125
  12.6 17.3 %all-to-all-done.x_ref = bf16[8,80,512]{2,1,0:T(8,128)(2,1)S(1)} async-done(((bf16[8,80,512]{2,1,0:T(8,128)(2,1)}), bf16[8,80,512]{2,1,0:T(8,128)(2,1)S(1)}, u32[]{:S(2)}, u32[]{:S(2)}) %all-to-all-start) | async-done | bytes 655392 | tf_op jit(solution)/shard_map/all_to_all | solution.py:125
  29.9 0.8 copy-done.5
  30.7 4.8 %shard_map.59 = (f32[2,256,512]{2,1,0:T(8,128)}, f32[2,256,512]{2,1,0:T(8,128)}, f32[2,256,512]{2,1,0:T(8,128)}, f32[2,256,512]{2,1,0:T(8,128)}) custom-call(s32[1]{0:T(128)} %bitcast.10.me_ref, bf16[8,80,512]{2,1,0:T(8,128)(2,1)} %copy-done.5, bf16[512,2048]{1,0:T(8,128)(2,1)} %l_ref.5), custom_call_target="tpu_custom_call" | custom-call | flops 1073741824 | bytes 6815744 | tf_op jit(solution)/shard_map/pallas_call | solution.py:137
  36.0 1.1 copy.42
  37.2 3.6 %all-to-all-start.1 = ((bf16[64,16,256]{2,0,1:T(8,128)(2,1)}), bf16[64,16,256]{2,0,1:T(8,128)(2,1)S(1)}, u32[]{:S(2)}, u32[]{:S(2)}) async-start(bf16[64,16,256]{2,0,1:T(8,128)(2,1)} %copy.42), calls=%async_computation.1 | async-start | bytes 1048576 | tf_op jit(solution)/shard_map/all_to_all | solution.py:132
  40.8 1.2 %fusion.2 = (f32[256,512]{1,0:T(8,128)}, f32[256,512]{1,0:T(8,128)}) fusion(f32[2,256,512]{2,1,0:T(8,128)S(1)} %collective-permute-done, f32[2,256,512]{2,1,0:T(8,128)S(1)} %copy-done.2), kind=kLoop, calls=%fused_computation.8 | loop fusion | flops 262144 | bytes 3145728 | tf_op jit(solution)/shard_map/add | solution.py:40
  42.0 1.5 %collective-permute-start.1 = (f32[256,512]{1,0:T(8,128)}, f32[256,512]{1,0:T(8,128)S(1)}, u32[]{:S(2)}, u32[]{:S(2)}) collective-permute-start(f32[256,512]{1,0:T(8,128)} %get-tuple-element.44), channel_id=1, source_target_pairs={{0,2},{1,3},{2,0},{3,1},{4,6},{5,7},{6,4},{7,5},{8,10},{9,11},{10,... | collective-permute-start | bytes 1572872 | tf_op jit(solution)/shard_map/ppermute | solution.py:154
  43.5 0.8 slice_convert_fusion
  45.1 10.4 %all-to-all-done.1 = bf16[64,16,256]{2,0,1:T(8,128)(2,1)S(1)} async-done(((bf16[64,16,256]{2,0,1:T(8,128)(2,1)}), bf16[64,16,256]{2,0,1:T(8,128)(2,1)S(1)}, u32[]{:S(2)}, u32[]{:S(2)}) %all-to-all-start.1) | async-done | bytes 524320 | tf_op jit(solution)/shard_map/all_to_all | solution.py:132
  55.6 2.2 %fusion = (f32[256,512]{1,0:T(8,128)S(1)}, f32[256,512]{1,0:T(8,128)}) fusion(f32[2,256,512]{2,1,0:T(8,128)} %collective-permute-done.2, f32[2,256,512]{2,1,0:T(8,128)S(1)} %copy-done.1), kind=kLoop, calls=%fused_computation.4 | loop fusion | flops 262144 | bytes 3145728 | tf_op jit(solution)/shard_map/add | solution.py:40
  57.8 0.8 copy-done.6
  58.6 2.2 %shard_map.60 = f32[16,16,512]{2,1,0:T(8,128)} custom-call(f32[16,512]{1,0:T(8,128)} %add.40.rate_ref, f32[16,16,512]{2,1,0:T(8,128)} %bitcast.55, f32[16,16,512]{2,1,0:T(8,128)} %bitcast.62), custom_call_target="tpu_custom_call" | custom-call | flops 786432 | bytes 1572864 | tf_op jit(solution)/shard_map/pallas_call | solution.py:164
  60.7 3.8 %all-to-all-start.2 = ((f32[16,16,512]{2,1,0:T(8,128)}), f32[16,16,512]{2,1,0:T(8,128)S(1)}, u32[]{:S(2)}, u32[]{:S(2)}) async-start(f32[16,16,512]{2,1,0:T(8,128)} %shard_map.60), calls=%async_computation.2 | async-start | bytes 1048576 | tf_op jit(solution)/shard_map/all_to_all | solution.py:174
  64.5 1.5 %collective-permute-start.3 = (f32[256,512]{1,0:T(8,128)S(1)}, f32[256,512]{1,0:T(8,128)S(1)}, u32[]{:S(2)}, u32[]{:S(2)}) collective-permute-start(f32[256,512]{1,0:T(8,128)S(1)} %get-tuple-element.27), channel_id=1, source_target_pairs={{0,2},{1,3},{2,0},{3,1},{4,6},{5,7},{6,4},{7,5},{8,10},{9,11},{10,... | collective-permute-start | bytes 1572872 | tf_op jit(solution)/shard_map/ppermute | solution.py:158
  66.0 11.9 %collective-permute-done.3 = f32[256,512]{1,0:T(8,128)S(1)} collective-permute-done((f32[256,512]{1,0:T(8,128)S(1)}, f32[256,512]{1,0:T(8,128)S(1)}, u32[]{:S(2)}, u32[]{:S(2)}) %collective-permute-start.3) | collective-permute-done | bytes 524320 | tf_op jit(solution)/shard_map/ppermute | solution.py:158
  77.9 0.8 copy-done.7
  78.7 2.1 %shard_map.61 = f32[16,16,512]{2,1,0:T(8,128)} custom-call(f32[16,512]{1,0:T(8,128)} %add.40.rate_ref, f32[16,16,512]{2,1,0:T(8,128)} %bitcast.60, f32[16,16,512]{2,1,0:T(8,128)} %bitcast.63), custom_call_target="tpu_custom_call" | custom-call | flops 786432 | bytes 1572864 | tf_op jit(solution)/shard_map/pallas_call | solution.py:164
  80.8 5.7 %all-to-all-start.3 = ((f32[16,16,512]{2,1,0:T(8,128)}), f32[16,16,512]{2,1,0:T(8,128)S(1)}, u32[]{:S(2)}, u32[]{:S(2)}) async-start(f32[16,16,512]{2,1,0:T(8,128)} %shard_map.61), calls=%async_computation.3 | async-start | bytes 1048576 | tf_op jit(solution)/shard_map/all_to_all | solution.py:174
  86.7 1.6 %collective-permute-start.5 = (bf16[2,128,512]{2,1,0:T(8,128)(2,1)S(1)}, bf16[2,128,512]{2,1,0:T(8,128)(2,1)S(1)}, u32[]{:S(2)}, u32[]{:S(2)}) collective-permute-start(bf16[2,128,512]{2,1,0:T(8,128)(2,1)S(1)} %bitcast_convert_fusion.refs_0_), channel_id=1, source_target_pairs={{0,2},{1,3},{2,0},{3,1},{4,6},{5,7},{6,4},{7,5},{8,10},{9,11},{10,... | collective-permute-start | bytes 786440 | tf_op jit(solution)/shard_map/ppermute | solution.py:52
  88.2 4.9 %collective-permute-done.5.refs_1_ = bf16[2,128,512]{2,1,0:T(8,128)(2,1)S(1)} collective-permute-done((bf16[2,128,512]{2,1,0:T(8,128)(2,1)S(1)}, bf16[2,128,512]{2,1,0:T(8,128)(2,1)S(1)}, u32[]{:S(2)}, u32[]{:S(2)}) %collective-permute-start.5) | collective-permute-done | bytes 262176 | tf_op jit(solution)/shard_map/ppermute | solution.py:52
  93.6 6.0 %all-to-all-done.3 = f32[16,16,512]{2,1,0:T(8,128)S(1)} async-done(((f32[16,16,512]{2,1,0:T(8,128)}), f32[16,16,512]{2,1,0:T(8,128)S(1)}, u32[]{:S(2)}, u32[]{:S(2)}) %all-to-all-start.3) | async-done | bytes 524320 | tf_op jit(solution)/shard_map/all_to_all | solution.py:174
  99.7 1.6 %collective-permute-start.4 = (bf16[2,128,512]{2,1,0:T(8,128)(2,1)S(1)}, bf16[2,128,512]{2,1,0:T(8,128)(2,1)S(1)}, u32[]{:S(2)}, u32[]{:S(2)}) collective-permute-start(bf16[2,128,512]{2,1,0:T(8,128)(2,1)S(1)} %bitcast_convert_fusion.1.refs_0_), channel_id=1, source_target_pairs={{0,2},{1,3},{2,0},{3,1},{4,6},{5,7},{6,4},{7,5},{8,10},{9,11},{10,... | collective-permute-start | bytes 786440 | tf_op jit(solution)/shard_map/ppermute | solution.py:52
  101.3 0.9 slice_bitcast_fusion
  102.9 3.4 %shard_map.62 = f32[2,512,128]{2,1,0:T(8,128)} custom-call(s32[1]{0:T(128)} %bitcast.10.me_ref, bf16[512,2048]{1,0:T(8,128)(2,1)} %l_ref.5, bf16[2,128,512]{2,1,0:T(8,128)(2,1)} %copy-done.4, bf16[2,128,512]{2,1,0:T(8,128)(2,1)} %copy-done.9, bf16[2,128,512]{2,1,0:T(8,128)(2,1)} %copy-done.10, bf16[2,128,512]{2,1,0:T(8,128)(2,1)} %collective-permute-done.7.refs_3_, ...), custom_call_target="tpu_custom_call" | custom-call | flops 536870912 | bytes 3670016 | tf_op jit(solution)/shard_map/pallas_call | solution.py:181
  107.0 1.3 %copy.46 = f32[512,2,256]{2,1,0:T(2,128)} copy(f32[512,2,256]{0,2,1:T(8,128)S(1)} %pad_maximum_fusion) | data formatting | bytes 2097152
  109.1 3.5 %shard_map.63 = f32[2,512,128]{2,1,0:T(8,128)} custom-call(s32[1]{0:T(128)} %bitcast.10.me_ref, bf16[512,2048]{1,0:T(8,128)(2,1)} %l_ref.5, bf16[2,128,512]{2,1,0:T(8,128)(2,1)} %copy-done.3, bf16[2,128,512]{2,1,0:T(8,128)(2,1)} %copy-done.8, bf16[2,128,512]{2,1,0:T(8,128)(2,1)} %copy-done.11, bf16[2,128,512]{2,1,0:T(8,128)(2,1)} %copy-done.12, ...), custom_call_target="tpu_custom_call" | custom-call | flops 536870912 | bytes 3670016 | tf_op jit(solution)/shard_map/pallas_call | solution.py:181
  112.6 1.1 pad_maximum_fusion.1
  113.7 1.8 %copy.47 = f32[512,2,256]{2,1,0:T(2,128)} copy(f32[512,2,256]{2,0,1:T(8,128)S(1)} %pad_maximum_fusion.1) | data formatting | bytes 2097152
  (56 shorter events, 5.5 us)
Async XLA Ops:
  5.3 24.5 %all-to-all-start = ((bf16[8,80,512]{2,1,0:T(8,128)(2,1)}), bf16[8,80,512]{2,1,0:T(8,128)(2,1)S(1)}, u32[]{:S(2)}, u32[]{:S(2)}) async-start(bf16[8,80,512]{2,1,0:T(8,128)(2,1)} %pad_maximum_fusion.2), calls=%async_computation | async-start | bytes 1310720 | tf_op jit(solution)/shard_map/all_to_all | solution.py:125
  29.9 0.8 copy-start.5
  35.5 5.3 %collective-permute-start = (f32[2,256,512]{2,1,0:T(8,128)}, f32[2,256,512]{2,1,0:T(8,128)S(1)}, u32[]{:S(2)}, u32[]{:S(2)}) collective-permute-start(f32[2,256,512]{2,1,0:T(8,128)} %get-tuple-element.21), channel_id=1, source_target_pairs={{0,1},{1,0},{2,3},{3,2},{4,5},{5,4},{6,7},{7,6},{8,9},{9,8},{10,11... | collective-permute-start | bytes 3145736 | tf_op jit(solution)/shard_map/ppermute | solution.py:38
  35.5 5.3 %copy-start.2 = (f32[2,256,512]{2,1,0:T(8,128)S(1)}, f32[2,256,512]{2,1,0:T(8,128)}, u32[]{:S(2)}) copy-start(f32[2,256,512]{2,1,0:T(8,128)} %get-tuple-element.20) | copy-start | bytes 3145732
  35.5 20.0 %collective-permute-start.2 = (f32[2,256,512]{2,1,0:T(8,128)}, f32[2,256,512]{2,1,0:T(8,128)}, u32[]{:S(2)}, u32[]{:S(2)}) collective-permute-start(f32[2,256,512]{2,1,0:T(8,128)} %get-tuple-element.23), channel_id=1, source_target_pairs={{0,1},{1,0},{2,3},{3,2},{4,5},{5,4},{6,7},{7,6},{8,9},{9,8},{10,11... | collective-permute-start | bytes 3145736 | tf_op jit(solution)/shard_map/ppermute | solution.py:38
  37.2 18.4 %all-to-all-start.1 = ((bf16[64,16,256]{2,0,1:T(8,128)(2,1)}), bf16[64,16,256]{2,0,1:T(8,128)(2,1)S(1)}, u32[]{:S(2)}, u32[]{:S(2)}) async-start(bf16[64,16,256]{2,0,1:T(8,128)(2,1)} %copy.42), calls=%async_computation.1 | async-start | bytes 1048576 | tf_op jit(solution)/shard_map/all_to_all | solution.py:132
  42.0 13.6 %copy-start.1 = (f32[2,256,512]{2,1,0:T(8,128)S(1)}, f32[2,256,512]{2,1,0:T(8,128)}, u32[]{:S(2)}) copy-start(f32[2,256,512]{2,1,0:T(8,128)} %get-tuple-element.22) | copy-start | bytes 3145732
  42.0 15.8 %collective-permute-start.1 = (f32[256,512]{1,0:T(8,128)}, f32[256,512]{1,0:T(8,128)S(1)}, u32[]{:S(2)}, u32[]{:S(2)}) collective-permute-start(f32[256,512]{1,0:T(8,128)} %get-tuple-element.44), channel_id=1, source_target_pairs={{0,2},{1,3},{2,0},{3,1},{4,6},{5,7},{6,4},{7,5},{8,10},{9,11},{10,... | collective-permute-start | bytes 1572872 | tf_op jit(solution)/shard_map/ppermute | solution.py:154
  57.8 0.8 copy-start.6
  60.7 20.1 %all-to-all-start.2 = ((f32[16,16,512]{2,1,0:T(8,128)}), f32[16,16,512]{2,1,0:T(8,128)S(1)}, u32[]{:S(2)}, u32[]{:S(2)}) async-start(f32[16,16,512]{2,1,0:T(8,128)} %shard_map.60), calls=%async_computation.2 | async-start | bytes 1048576 | tf_op jit(solution)/shard_map/all_to_all | solution.py:174
  64.5 13.4 %collective-permute-start.3 = (f32[256,512]{1,0:T(8,128)S(1)}, f32[256,512]{1,0:T(8,128)S(1)}, u32[]{:S(2)}, u32[]{:S(2)}) collective-permute-start(f32[256,512]{1,0:T(8,128)S(1)} %get-tuple-element.27), channel_id=1, source_target_pairs={{0,2},{1,3},{2,0},{3,1},{4,6},{5,7},{6,4},{7,5},{8,10},{9,11},{10,... | collective-permute-start | bytes 1572872 | tf_op jit(solution)/shard_map/ppermute | solution.py:158
  77.9 0.8 copy-start.7
  80.8 18.8 %all-to-all-start.3 = ((f32[16,16,512]{2,1,0:T(8,128)}), f32[16,16,512]{2,1,0:T(8,128)S(1)}, u32[]{:S(2)}, u32[]{:S(2)}) async-start(f32[16,16,512]{2,1,0:T(8,128)} %shard_map.61), calls=%async_computation.3 | async-start | bytes 1048576 | tf_op jit(solution)/shard_map/all_to_all | solution.py:174
  86.6 15.5 %copy-start.4 = (bf16[2,128,512]{2,1,0:T(8,128)(2,1)}, bf16[2,128,512]{2,1,0:T(8,128)(2,1)S(1)}, u32[]{:S(2)}) copy-start(bf16[2,128,512]{2,1,0:T(8,128)(2,1)S(1)} %bitcast_convert_fusion.refs_0_) | copy-start | bytes 786436
  86.7 6.4 %collective-permute-start.5 = (bf16[2,128,512]{2,1,0:T(8,128)(2,1)S(1)}, bf16[2,128,512]{2,1,0:T(8,128)(2,1)S(1)}, u32[]{:S(2)}, u32[]{:S(2)}) collective-permute-start(bf16[2,128,512]{2,1,0:T(8,128)(2,1)S(1)} %bitcast_convert_fusion.refs_0_), channel_id=1, source_target_pairs={{0,2},{1,3},{2,0},{3,1},{4,6},{5,7},{6,4},{7,5},{8,10},{9,11},{10,... | collective-permute-start | bytes 786440 | tf_op jit(solution)/shard_map/ppermute | solution.py:52
  93.1 9.1 %copy-start.9 = (bf16[2,128,512]{2,1,0:T(8,128)(2,1)}, bf16[2,128,512]{2,1,0:T(8,128)(2,1)S(1)}, u32[]{:S(2)}) copy-start(bf16[2,128,512]{2,1,0:T(8,128)(2,1)S(1)} %collective-permute-done.5.refs_1_) | copy-start | bytes 786436
  93.1 9.1 %collective-permute-start.6 = (bf16[2,128,512]{2,1,0:T(8,128)(2,1)S(1)}, bf16[2,128,512]{2,1,0:T(8,128)(2,1)S(1)}, u32[]{:S(2)}, u32[]{:S(2)}) collective-permute-start(bf16[2,128,512]{2,1,0:T(8,128)(2,1)S(1)} %bitcast_convert_fusion.refs_0_), channel_id=1, source_target_pairs={{0,1},{1,0},{2,3},{3,2},{4,5},{5,4},{6,7},{7,6},{8,9},{9,8},{10,11... | collective-permute-start | bytes 786440 | tf_op jit(solution)/shard_map/ppermute | solution.py:52
  93.1 9.1 %collective-permute-start.7 = (bf16[2,128,512]{2,1,0:T(8,128)(2,1)S(1)}, bf16[2,128,512]{2,1,0:T(8,128)(2,1)}, u32[]{:S(2)}, u32[]{:S(2)}) collective-permute-start(bf16[2,128,512]{2,1,0:T(8,128)(2,1)S(1)} %collective-permute-done.5.refs_1_), channel_id=1, source_target_pairs={{0,1},{1,0},{2,3},{3,2},{4,5},{5,4},{6,7},{7,6},{8,9},{9,8},{10,11... | collective-permute-start | bytes 786440 | tf_op jit(solution)/shard_map/ppermute | solution.py:52
  99.7 6.6 %copy-start.3 = (bf16[2,128,512]{2,1,0:T(8,128)(2,1)}, bf16[2,128,512]{2,1,0:T(8,128)(2,1)S(1)}, u32[]{:S(2)}) copy-start(bf16[2,128,512]{2,1,0:T(8,128)(2,1)S(1)} %bitcast_convert_fusion.1.refs_0_) | copy-start | bytes 786436
  99.7 6.6 %collective-permute-start.4 = (bf16[2,128,512]{2,1,0:T(8,128)(2,1)S(1)}, bf16[2,128,512]{2,1,0:T(8,128)(2,1)S(1)}, u32[]{:S(2)}, u32[]{:S(2)}) collective-permute-start(bf16[2,128,512]{2,1,0:T(8,128)(2,1)S(1)} %bitcast_convert_fusion.1.refs_0_), channel_id=1, source_target_pairs={{0,2},{1,3},{2,0},{3,1},{4,6},{5,7},{6,4},{7,5},{8,10},{9,11},{10,... | collective-permute-start | bytes 786440 | tf_op jit(solution)/shard_map/ppermute | solution.py:52
  102.2 0.7 copy-start.10
  106.3 2.0 %copy-start.8 = (bf16[2,128,512]{2,1,0:T(8,128)(2,1)}, bf16[2,128,512]{2,1,0:T(8,128)(2,1)S(1)}, u32[]{:S(2)}) copy-start(bf16[2,128,512]{2,1,0:T(8,128)(2,1)S(1)} %collective-permute-done.4.refs_1_) | copy-start | bytes 786436
  106.3 2.0 %collective-permute-start.8 = (bf16[2,128,512]{2,1,0:T(8,128)(2,1)S(1)}, bf16[2,128,512]{2,1,0:T(8,128)(2,1)S(1)}, u32[]{:S(2)}, u32[]{:S(2)}) collective-permute-start(bf16[2,128,512]{2,1,0:T(8,128)(2,1)S(1)} %bitcast_convert_fusion.1.refs_0_), channel_id=1, source_target_pairs={{0,1},{1,0},{2,3},{3,2},{4,5},{5,4},{6,7},{7,6},{8,9},{9,8},{10,11... | collective-permute-start | bytes 786440 | tf_op jit(solution)/shard_map/ppermute | solution.py:52
  106.4 1.9 %collective-permute-start.9 = (bf16[2,128,512]{2,1,0:T(8,128)(2,1)S(1)}, bf16[2,128,512]{2,1,0:T(8,128)(2,1)S(1)}, u32[]{:S(2)}, u32[]{:S(2)}) collective-permute-start(bf16[2,128,512]{2,1,0:T(8,128)(2,1)S(1)} %collective-permute-done.4.refs_1_), channel_id=1, source_target_pairs={{0,1},{1,0},{2,3},{3,2},{4,5},{5,4},{6,7},{7,6},{8,9},{9,8},{10,11... | collective-permute-start | bytes 786440 | tf_op jit(solution)/shard_map/ppermute | solution.py:52
  108.3 0.7 copy-start.11
  108.3 0.8 copy-start.12
  109.1 3.5 %copy-start = (f32[2,512,128]{2,1,0:T(8,128)S(1)}, f32[2,512,128]{2,1,0:T(8,128)}, u32[]{:S(2)}) copy-start(f32[2,512,128]{2,1,0:T(8,128)} %shard_map.62) | copy-start | bytes 1572868

commit v21 on v17

--- a/solution.py
+++ b/solution.py
@@ -7,7 +7,7 @@
 from jax.experimental.pallas import tpu as pltpu
 from jax.sharding import PartitionSpec as P
 
-CHUNKS = 2
+CHUNKS = 4
 
 
 def information_kernel(hours, stations, me_ref, x_ref, l_ref, *out_refs):

time: 114 us -> 141 us (1.24)
  starting transfers between devices: 30 us -> 45.8 us
  Pallas kernels: 16.9 us -> 27.3 us
  waiting for transfers between devices: 47.6 us -> 41.1 us
  local copies, waits for them, and re-layouts: 10.2 us -> 16.1 us
    all_to_all x2 -> x4, starting transfers between devices: 11.3 us -> 21.2 us  [local(): lax.all_to_all(smoothed_here, 'tm', split_axis=0, concat_axis=1, tiled=True)]
    pallas_call x2 -> x4, Pallas kernels: 7.71 us -> 15.1 us  [local(): vmem_call(fitted_kernel, jax.ShapeDtypeStruct((slab_hours, stations_here,...]
    unnamed x27 -> x59, local copies, waits for them, and re-layouts: 7.65 us -> 13.5 us
    ppermute x6 -> x12, waiting for transfers between devices: 5.3 us -> 0.21 us  [doubling_gather(): pieces = pieces + [lax.ppermute(piece, axis, pairs) for piece in pieces]]
    ppermute x1 -> x3, waiting for transfers between devices: 10.6 us -> 15.7 us  [local(): lax.ppermute(o, 'state', last[c + 1][2])]
    all_to_all x2 -> x4, waiting for transfers between devices: 4.73 us -> 0.01 us  [local(): lax.all_to_all(smoothed_here, 'tm', split_axis=0, concat_axis=1, tiled=True)]
    pallas_call x2 -> x4, Pallas kernels: 4.34 us -> 7.33 us  [local(): vmem_call(recurrence_kernel, jax.ShapeDtypeStruct(kept.shape, jnp.float32...]
    ppermute x1 -> x3, starting transfers between devices: 1.58 us -> 4.56 us  [local(): lax.ppermute(o, 'state', last[c + 1][2])]
  transfers between devices with their start and end apart: 14 -> 26, of which waited for: 8 -> 6; matrix products, arithmetic and copies ran while one was open for 7% -> 5% of each run, Pallas kernels for 5% -> 12%
where the time goes in v21:
time: 141 us; the launch traced here: 139 us
  starting transfers between devices  45.8 us (32%)
  waiting for transfers between devices  41.1 us (29%)
  Pallas kernels  27.3 us (19%)
  local copies, waits for them, and re-layouts  16.1 us (11%)
  other arithmetic  8.16 us (6%)
    all_to_all x4, starting transfers between devices, local(): lax.all_to_all(smoothed_here, 'tm', split_axis=0, concat_axis=1, tiled=True)  21.2 us
    all_to_all x1, waiting for transfers between devices, local(): lax.all_to_all(outgoing, 'tm', split_axis=0, concat_axis=0, tiled=True)  17.3 us
    ppermute x3, waiting for transfers between devices, local(): lax.ppermute(o, 'state', last[c + 1][2])  15.7 us
    pallas_call x4, Pallas kernels, local(): vmem_call(fitted_kernel, jax.ShapeDtypeStruct((slab_hours, stations_here,...  15.1 us
    unnamed x59, local copies, waits for them, and re-layouts  13.5 us
    all_to_all x1, waiting for transfers between devices, local(): lax.all_to_all(masked_later, 'tm', split_axis=1, concat_axis=0, tiled=True)  7.92 us
    pallas_call x4, Pallas kernels, local(): vmem_call(recurrence_kernel, jax.ShapeDtypeStruct(kept.shape, jnp.float32...  7.33 us
    all_to_all x1, starting transfers between devices, local(): lax.all_to_all(outgoing, 'tm', split_axis=0, concat_axis=0, tiled=True)  7.25 us
  transfers between devices with their start and end apart: 26, of which 6 were waited for; matrix products, arithmetic and copies ran while one was open for 5% of the time, Pallas kernels for 12%

profile of v21, /device:TPU:0, one launch (start us, length us, event | category | flops | bytes accessed | tf_op | source)
XLA Modules:
  0.0 139.5 jit_solution(6949478072827509025)
XLA Ops:
  2.1 1.7 %copy.43 = bf16[64,16,256]{0,2,1:T(8,128)(2,1)S(1)} copy(bf16[64,16,256]{2,1,0:T(8,128)(2,1)} %param.4) | data formatting | bytes 1048576 | tf_op args[0]
  4.4 0.9 pad_maximum_fusion.2
  5.3 7.3 %all-to-all-start = ((bf16[8,80,512]{2,1,0:T(8,128)(2,1)}), bf16[8,80,512]{2,1,0:T(8,128)(2,1)S(1)}, u32[]{:S(2)}, u32[]{:S(2)}) async-start(bf16[8,80,512]{2,1,0:T(8,128)(2,1)} %pad_maximum_fusion.2), calls=%async_computation | async-start | bytes 1310720 | tf_op jit(solution)/shard_map/all_to_all | solution.py:123
  12.6 17.3 %all-to-all-done.x_ref = bf16[8,80,512]{2,1,0:T(8,128)(2,1)S(1)} async-done(((bf16[8,80,512]{2,1,0:T(8,128)(2,1)}), bf16[8,80,512]{2,1,0:T(8,128)(2,1)S(1)}, u32[]{:S(2)}, u32[]{:S(2)}) %all-to-all-start) | async-done | bytes 655392 | tf_op jit(solution)/shard_map/all_to_all | solution.py:123
  30.7 4.9 %shard_map.59 = (f32[2,128,512]{2,1,0:T(8,128)}, f32[2,128,512]{2,1,0:T(8,128)}, f32[2,128,512]{2,1,0:T(8,128)}, f32[2,128,512]{2,1,0:T(8,128)}, f32[2,128,512]{...) custom-call(s32[1]{0:T(128)} %bitcast.10.me_ref, ...), custom_call_target="tpu_custom_call" | custom-call | flops 1073741824 | bytes 6815744 | tf_op jit(solution)/shard_map/pallas_call | solution.py:135
  35.6 1.1 copy.48
  36.7 3.6 %all-to-all-start.1 = ((bf16[64,16,256]{2,0,1:T(8,128)(2,1)}), bf16[64,16,256]{2,0,1:T(8,128)(2,1)S(1)}, u32[]{:S(2)}, u32[]{:S(2)}) async-start(bf16[64,16,256]{2,0,1:T(8,128)(2,1)} %copy.48), calls=%async_computation.1 | async-start | bytes 1048576 | tf_op jit(solution)/shard_map/all_to_all | solution.py:130
  43.8 1.5 %collective-permute-start.1 = (f32[128,512]{1,0:T(8,128)S(1)}, f32[128,512]{1,0:T(8,128)S(1)}, u32[]{:S(2)}, u32[]{:S(2)}) collective-permute-start(f32[128,512]{1,0:T(8,128)S(1)} %get-tuple-element.76), channel_id=1, source_target_pairs={{0,2},{1,3},{2,0},{3,1},{4,6},{5,7},{6,4},{7,5},{8,10},{9,11},{10,... | collective-permute-start | bytes 786440 | tf_op jit(solution)/shard_map/ppermute | solution.py:152
  47.7 7.9 %all-to-all-done.1 = bf16[64,16,256]{2,0,1:T(8,128)(2,1)S(1)} async-done(((bf16[64,16,256]{2,0,1:T(8,128)(2,1)}), bf16[64,16,256]{2,0,1:T(8,128)(2,1)S(1)}, u32[]{:S(2)}, u32[]{:S(2)}) %all-to-all-start.1) | async-done | bytes 524320 | tf_op jit(solution)/shard_map/all_to_all | solution.py:130
  56.3 1.8 %shard_map.60 = f32[16,8,512]{2,1,0:T(8,128)} custom-call(f32[16,512]{1,0:T(8,128)} %add.64.rate_ref, f32[16,8,512]{2,1,0:T(8,128)} %bitcast.105, f32[16,8,512]{2,1,0:T(8,128)} %bitcast.123), custom_call_target="tpu_custom_call" | custom-call | flops 393216 | bytes 786432 | tf_op jit(solution)/shard_map/pallas_call | solution.py:162
  58.2 3.6 %all-to-all-start.2 = ((f32[16,8,512]{2,1,0:T(8,128)}), f32[16,8,512]{2,1,0:T(8,128)S(1)}, u32[]{:S(2)}, u32[]{:S(2)}) async-start(f32[16,8,512]{2,1,0:T(8,128)} %shard_map.60), calls=%async_computation.2 | async-start | bytes 524288 | tf_op jit(solution)/shard_map/all_to_all | solution.py:172
  61.8 1.5 %collective-permute-start.5 = (f32[128,512]{1,0:T(8,128)S(1)}, f32[128,512]{1,0:T(8,128)S(1)}, u32[]{:S(2)}, u32[]{:S(2)}) collective-permute-start(f32[128,512]{1,0:T(8,128)S(1)} %get-tuple-element.45), channel_id=1, source_target_pairs={{0,2},{1,3},{2,0},{3,1},{4,6},{5,7},{6,4},{7,5},{8,10},{9,11},{10,... | collective-permute-start | bytes 786440 | tf_op jit(solution)/shard_map/ppermute | solution.py:156
  63.3 6.5 %collective-permute-done.5 = f32[128,512]{1,0:T(8,128)S(1)} collective-permute-done((f32[128,512]{1,0:T(8,128)S(1)}, f32[128,512]{1,0:T(8,128)S(1)}, u32[]{:S(2)}, u32[]{:S(2)}) %collective-permute-start.5) | collective-permute-done | bytes 262176 | tf_op jit(solution)/shard_map/ppermute | solution.py:156
  70.5 1.8 %shard_map.61 = f32[16,8,512]{2,1,0:T(8,128)} custom-call(f32[16,512]{1,0:T(8,128)} %add.64.rate_ref, f32[16,8,512]{2,1,0:T(8,128)} %bitcast.104, f32[16,8,512]{2,1,0:T(8,128)} %bitcast.125), custom_call_target="tpu_custom_call" | custom-call | flops 393216 | bytes 786432 | tf_op jit(solution)/shard_map/pallas_call | solution.py:162
  72.3 5.7 %all-to-all-start.3 = ((f32[16,8,512]{2,1,0:T(8,128)}), f32[16,8,512]{2,1,0:T(8,128)S(1)}, u32[]{:S(2)}, u32[]{:S(2)}) async-start(f32[16,8,512]{2,1,0:T(8,128)} %shard_map.61), calls=%async_computation.3 | async-start | bytes 524288 | tf_op jit(solution)/shard_map/all_to_all | solution.py:172
  78.0 1.5 %collective-permute-start.6 = (f32[128,512]{1,0:T(8,128)S(1)}, f32[128,512]{1,0:T(8,128)S(1)}, u32[]{:S(2)}, u32[]{:S(2)}) collective-permute-start(f32[128,512]{1,0:T(8,128)S(1)} %get-tuple-element.47), channel_id=1, source_target_pairs={{0,2},{1,3},{2,0},{3,1},{4,6},{5,7},{6,4},{7,5},{8,10},{9,11},{10,... | collective-permute-start | bytes 786440 | tf_op jit(solution)/shard_map/ppermute | solution.py:156
  79.6 5.0 %collective-permute-done.6 = f32[128,512]{1,0:T(8,128)S(1)} collective-permute-done((f32[128,512]{1,0:T(8,128)S(1)}, f32[128,512]{1,0:T(8,128)S(1)}, u32[]{:S(2)}, u32[]{:S(2)}) %collective-permute-start.6) | collective-permute-done | bytes 262176 | tf_op jit(solution)/shard_map/ppermute | solution.py:156
  85.2 1.8 %shard_map.62 = f32[16,8,512]{2,1,0:T(8,128)} custom-call(f32[16,512]{1,0:T(8,128)} %add.64.rate_ref, f32[16,8,512]{2,1,0:T(8,128)} %bitcast.103, f32[16,8,512]{2,1,0:T(8,128)} %bitcast.126), custom_call_target="tpu_custom_call" | custom-call | flops 393216 | bytes 786432 | tf_op jit(solution)/shard_map/pallas_call | solution.py:162
  87.1 5.9 %all-to-all-start.4 = ((f32[16,8,512]{2,1,0:T(8,128)}), f32[16,8,512]{2,1,0:T(8,128)S(1)}, u32[]{:S(2)}, u32[]{:S(2)}) async-start(f32[16,8,512]{2,1,0:T(8,128)} %shard_map.62), calls=%async_computation.4 | async-start | bytes 524288 | tf_op jit(solution)/shard_map/all_to_all | solution.py:172
  93.0 1.5 %collective-permute-start.7 = (f32[128,512]{1,0:T(8,128)S(1)}, f32[128,512]{1,0:T(8,128)S(1)}, u32[]{:S(2)}, u32[]{:S(2)}) collective-permute-start(f32[128,512]{1,0:T(8,128)S(1)} %get-tuple-element.49), channel_id=1, source_target_pairs={{0,2},{1,3},{2,0},{3,1},{4,6},{5,7},{6,4},{7,5},{8,10},{9,11},{10,... | collective-permute-start | bytes 786440 | tf_op jit(solution)/shard_map/ppermute | solution.py:156
  95.1 4.2 %collective-permute-done.7 = f32[128,512]{1,0:T(8,128)S(1)} collective-permute-done((f32[128,512]{1,0:T(8,128)S(1)}, f32[128,512]{1,0:T(8,128)S(1)}, u32[]{:S(2)}, u32[]{:S(2)}) %collective-permute-start.7) | collective-permute-done | bytes 262176 | tf_op jit(solution)/shard_map/ppermute | solution.py:156
  100.0 1.8 %shard_map.63 = f32[16,8,512]{2,1,0:T(8,128)} custom-call(f32[16,512]{1,0:T(8,128)} %add.64.rate_ref, f32[16,8,512]{2,1,0:T(8,128)} %bitcast.102, f32[16,8,512]{2,1,0:T(8,128)} %bitcast.124), custom_call_target="tpu_custom_call" | custom-call | flops 393216 | bytes 786432 | tf_op jit(solution)/shard_map/pallas_call | solution.py:162
  101.9 6.0 %all-to-all-start.5 = ((f32[16,8,512]{2,1,0:T(8,128)}), f32[16,8,512]{2,1,0:T(8,128)S(1)}, u32[]{:S(2)}, u32[]{:S(2)}) async-start(f32[16,8,512]{2,1,0:T(8,128)} %shard_map.63), calls=%async_computation.5 | async-start | bytes 524288 | tf_op jit(solution)/shard_map/all_to_all | solution.py:172
  108.5 1.6 %collective-permute-start.8 = (bf16[2,64,512]{2,1,0:T(8,128)(2,1)S(1)}, bf16[2,64,512]{2,1,0:T(8,128)(2,1)S(1)}, u32[]{:S(2)}, u32[]{:S(2)}) collective-permute-start(bf16[2,64,512]{2,1,0:T(8,128)(2,1)S(1)} %bitcast.119), channel_id=1, source_target_pairs={{0,2},{1,3},{2,0},{3,1},{4,6},{5,7},{6,4},{7,5},{8,10},{9,11},{10,... | collective-permute-start | bytes 393224 | tf_op jit(solution)/shard_map/ppermute | solution.py:52
  111.4 3.8 %shard_map.64 = f32[2,512,64]{2,1,0:T(8,128)} custom-call(s32[1]{0:T(128)} %bitcast.10.me_ref, bf16[512,2048]{1,0:T(8,128)(2,1)} %l_ref.9, bf16[2,64,512]{2,1,0:T(8,128)(2,1)} %bitcast.118, bf16[2,64,512]{2,1,0:T(8,128)(2,1)} %copy-done.18, bf16[2,64,512]{2,1,0:T(8,128)(2,1)} %copy-done.23, bf16[2,64,512]{2,1,0:T(8,128)(2,1)} %copy-done.26), custom_call_target="tpu_custom_call" | custom-call | flops 268435456 | bytes 2883584 | tf_op jit(solution)/shard_map/pallas_call | solution.py:177
  117.9 3.8 %shard_map.65 = f32[2,512,64]{2,1,0:T(8,128)} custom-call(s32[1]{0:T(128)} %bitcast.10.me_ref, bf16[512,2048]{1,0:T(8,128)(2,1)} %l_ref.9, bf16[2,64,512]{2,1,0:T(8,128)(2,1)} %bitcast.121, bf16[2,64,512]{2,1,0:T(8,128)(2,1)} %copy-done.19, bf16[2,64,512]{2,1,0:T(8,128)(2,1)} %copy-done.24, bf16[2,64,512]{2,1,0:T(8,128)(2,1)} %copy-done.27), custom_call_target="tpu_custom_call" | custom-call | flops 268435456 | bytes 2883584 | tf_op jit(solution)/shard_map/pallas_call | solution.py:177
  122.3 1.4 collective-permute-start.15
  125.1 3.8 %shard_map.66 = f32[2,512,64]{2,1,0:T(8,128)} custom-call(s32[1]{0:T(128)} %bitcast.10.me_ref, bf16[512,2048]{1,0:T(8,128)(2,1)} %l_ref.9, bf16[2,64,512]{2,1,0:T(8,128)(2,1)} %bitcast.112, bf16[2,64,512]{2,1,0:T(8,128)(2,1)} %copy-done.16, bf16[2,64,512]{2,1,0:T(8,128)(2,1)} %copy-done.20, bf16[2,64,512]{2,1,0:T(8,128)(2,1)} %copy-done.21), custom_call_target="tpu_custom_call" | custom-call | flops 268435456 | bytes 2883584 | tf_op jit(solution)/shard_map/pallas_call | solution.py:177
  129.5 1.3 copy.54
  132.2 3.8 %shard_map.67 = f32[2,512,64]{2,1,0:T(8,128)} custom-call(s32[1]{0:T(128)} %bitcast.10.me_ref, bf16[512,2048]{1,0:T(8,128)(2,1)} %l_ref.9, bf16[2,64,512]{2,1,0:T(8,128)(2,1)} %bitcast.115, bf16[2,64,512]{2,1,0:T(8,128)(2,1)} %copy-done.17, bf16[2,64,512]{2,1,0:T(8,128)(2,1)} %copy-done.22, bf16[2,64,512]{2,1,0:T(8,128)(2,1)} %copy-done.25), custom_call_target="tpu_custom_call" | custom-call | flops 268435456 | bytes 2883584 | tf_op jit(solution)/shard_map/pallas_call | solution.py:177
  135.9 1.3 bitcast_subtract_fusion.3
  137.7 1.8 %copy.55 = f32[512,2,256]{2,1,0:T(2,128)} copy(f32[512,2,256]{2,0,1:T(8,128)S(1)} %pad_maximum_fusion.1) | data formatting | bytes 2097152
  (120 shorter events, 21.1 us)
Async XLA Ops:
  5.3 24.5 %all-to-all-start = ((bf16[8,80,512]{2,1,0:T(8,128)(2,1)}), bf16[8,80,512]{2,1,0:T(8,128)(2,1)S(1)}, u32[]{:S(2)}, u32[]{:S(2)}) async-start(bf16[8,80,512]{2,1,0:T(8,128)(2,1)} %pad_maximum_fusion.2), calls=%async_computation | async-start | bytes 1310720 | tf_op jit(solution)/shard_map/all_to_all | solution.py:123
  35.6 7.4 %copy-start.7 = (f32[2,128,512]{2,1,0:T(8,128)S(1)}, f32[2,128,512]{2,1,0:T(8,128)}, u32[]{:S(2)}) copy-start(f32[2,128,512]{2,1,0:T(8,128)} %get-tuple-element.34) | copy-start | bytes 1572868
  35.6 7.4 %collective-permute-start = (f32[2,128,512]{2,1,0:T(8,128)}, f32[2,128,512]{2,1,0:T(8,128)S(1)}, u32[]{:S(2)}, u32[]{:S(2)}) collective-permute-start(f32[2,128,512]{2,1,0:T(8,128)} %get-tuple-element.35), channel_id=1, source_target_pairs={{0,1},{1,0},{2,3},{3,2},{4,5},{5,4},{6,7},{7,6},{8,9},{9,8},{10,11... | collective-permute-start | bytes 1572872 | tf_op jit(solution)/shard_map/ppermute | solution.py:38
  36.7 18.9 %all-to-all-start.1 = ((bf16[64,16,256]{2,0,1:T(8,128)(2,1)}), bf16[64,16,256]{2,0,1:T(8,128)(2,1)S(1)}, u32[]{:S(2)}, u32[]{:S(2)}) async-start(bf16[64,16,256]{2,0,1:T(8,128)(2,1)} %copy.48), calls=%async_computation.1 | async-start | bytes 1048576 | tf_op jit(solution)/shard_map/all_to_all | solution.py:130
  40.4 4.9 %collective-permute-start.2 = (f32[2,128,512]{2,1,0:T(8,128)}, f32[2,128,512]{2,1,0:T(8,128)S(1)}, u32[]{:S(2)}, u32[]{:S(2)}) collective-permute-start(f32[2,128,512]{2,1,0:T(8,128)} %get-tuple-element.37), channel_id=1, source_target_pairs={{0,1},{1,0},{2,3},{3,2},{4,5},{5,4},{6,7},{7,6},{8,9},{9,8},{10,11... | collective-permute-start | bytes 1572872 | tf_op jit(solution)/shard_map/ppermute | solution.py:38
  41.7 4.4 %collective-permute-start.3 = (f32[2,128,512]{2,1,0:T(8,128)}, f32[2,128,512]{2,1,0:T(8,128)S(1)}, u32[]{:S(2)}, u32[]{:S(2)}) collective-permute-start(f32[2,128,512]{2,1,0:T(8,128)} %get-tuple-element.39), channel_id=1, source_target_pairs={{0,1},{1,0},{2,3},{3,2},{4,5},{5,4},{6,7},{7,6},{8,9},{9,8},{10,11... | collective-permute-start | bytes 1572872 | tf_op jit(solution)/shard_map/ppermute | solution.py:38
  42.7 4.2 %collective-permute-start.4 = (f32[2,128,512]{2,1,0:T(8,128)}, f32[2,128,512]{2,1,0:T(8,128)S(1)}, u32[]{:S(2)}, u32[]{:S(2)}) collective-permute-start(f32[2,128,512]{2,1,0:T(8,128)} %get-tuple-element.41), channel_id=1, source_target_pairs={{0,1},{1,0},{2,3},{3,2},{4,5},{5,4},{6,7},{7,6},{8,9},{9,8},{10,11... | collective-permute-start | bytes 1572872 | tf_op jit(solution)/shard_map/ppermute | solution.py:38
  43.8 11.9 %collective-permute-start.1 = (f32[128,512]{1,0:T(8,128)S(1)}, f32[128,512]{1,0:T(8,128)S(1)}, u32[]{:S(2)}, u32[]{:S(2)}) collective-permute-start(f32[128,512]{1,0:T(8,128)S(1)} %get-tuple-element.76), channel_id=1, source_target_pairs={{0,2},{1,3},{2,0},{3,1},{4,6},{5,7},{6,4},{7,5},{8,10},{9,11},{10,... | collective-permute-start | bytes 786440 | tf_op jit(solution)/shard_map/ppermute | solution.py:152
  58.2 14.1 %all-to-all-start.2 = ((f32[16,8,512]{2,1,0:T(8,128)}), f32[16,8,512]{2,1,0:T(8,128)S(1)}, u32[]{:S(2)}, u32[]{:S(2)}) async-start(f32[16,8,512]{2,1,0:T(8,128)} %shard_map.60), calls=%async_computation.2 | async-start | bytes 524288 | tf_op jit(solution)/shard_map/all_to_all | solution.py:172
  61.8 8.0 %collective-permute-start.5 = (f32[128,512]{1,0:T(8,128)S(1)}, f32[128,512]{1,0:T(8,128)S(1)}, u32[]{:S(2)}, u32[]{:S(2)}) collective-permute-start(f32[128,512]{1,0:T(8,128)S(1)} %get-tuple-element.45), channel_id=1, source_target_pairs={{0,2},{1,3},{2,0},{3,1},{4,6},{5,7},{6,4},{7,5},{8,10},{9,11},{10,... | collective-permute-start | bytes 786440 | tf_op jit(solution)/shard_map/ppermute | solution.py:156
  72.3 14.8 %all-to-all-start.3 = ((f32[16,8,512]{2,1,0:T(8,128)}), f32[16,8,512]{2,1,0:T(8,128)S(1)}, u32[]{:S(2)}, u32[]{:S(2)}) async-start(f32[16,8,512]{2,1,0:T(8,128)} %shard_map.61), calls=%async_computation.3 | async-start | bytes 524288 | tf_op jit(solution)/shard_map/all_to_all | solution.py:172
  78.0 6.5 %collective-permute-start.6 = (f32[128,512]{1,0:T(8,128)S(1)}, f32[128,512]{1,0:T(8,128)S(1)}, u32[]{:S(2)}, u32[]{:S(2)}) collective-permute-start(f32[128,512]{1,0:T(8,128)S(1)} %get-tuple-element.47), channel_id=1, source_target_pairs={{0,2},{1,3},{2,0},{3,1},{4,6},{5,7},{6,4},{7,5},{8,10},{9,11},{10,... | collective-permute-start | bytes 786440 | tf_op jit(solution)/shard_map/ppermute | solution.py:156
  87.1 14.8 %all-to-all-start.4 = ((f32[16,8,512]{2,1,0:T(8,128)}), f32[16,8,512]{2,1,0:T(8,128)S(1)}, u32[]{:S(2)}, u32[]{:S(2)}) async-start(f32[16,8,512]{2,1,0:T(8,128)} %shard_map.62), calls=%async_computation.4 | async-start | bytes 524288 | tf_op jit(solution)/shard_map/all_to_all | solution.py:172
  93.0 6.4 %collective-permute-start.7 = (f32[128,512]{1,0:T(8,128)S(1)}, f32[128,512]{1,0:T(8,128)S(1)}, u32[]{:S(2)}, u32[]{:S(2)}) collective-permute-start(f32[128,512]{1,0:T(8,128)S(1)} %get-tuple-element.49), channel_id=1, source_target_pairs={{0,2},{1,3},{2,0},{3,1},{4,6},{5,7},{6,4},{7,5},{8,10},{9,11},{10,... | collective-permute-start | bytes 786440 | tf_op jit(solution)/shard_map/ppermute | solution.py:156
  94.5 15.6 %copy-start.10 = (bf16[8,2,8,512]{3,2,0,1:T(8,128)(2,1)}, bf16[8,2,8,512]{3,2,0,1:T(8,128)(2,1)S(1)}, u32[]{:S(2)}) copy-start(bf16[8,2,8,512]{3,2,0,1:T(8,128)(2,1)S(1)} %copy.66) | copy-start | bytes 393220
  94.5 13.4 %collective-permute-start.9 = (bf16[2,64,512]{2,1,0:T(8,128)(2,1)S(1)}, bf16[2,64,512]{2,1,0:T(8,128)(2,1)S(1)}, u32[]{:S(2)}, u32[]{:S(2)}) collective-permute-start(bf16[2,64,512]{2,1,0:T(8,128)(2,1)S(1)} %bitcast.116), channel_id=1, source_target_pairs={{0,2},{1,3},{2,0},{3,1},{4,6},{5,7},{6,4},{7,5},{8,10},{9,11},{10,... | collective-permute-start | bytes 393224 | tf_op jit(solution)/shard_map/ppermute | solution.py:52
  101.9 20.4 %all-to-all-start.5 = ((f32[16,8,512]{2,1,0:T(8,128)}), f32[16,8,512]{2,1,0:T(8,128)S(1)}, u32[]{:S(2)}, u32[]{:S(2)}) async-start(f32[16,8,512]{2,1,0:T(8,128)} %shard_map.63), calls=%async_computation.5 | async-start | bytes 524288 | tf_op jit(solution)/shard_map/all_to_all | solution.py:172
  107.9 2.2 %collective-permute-start.10 = (bf16[2,64,512]{2,1,0:T(8,128)(2,1)S(1)}, bf16[2,64,512]{2,1,0:T(8,128)(2,1)S(1)}, u32[]{:S(2)}, u32[]{:S(2)}) collective-permute-start(bf16[2,64,512]{2,1,0:T(8,128)(2,1)S(1)} %bitcast.117), channel_id=1, source_target_pairs={{0,1},{1,0},{2,3},{3,2},{4,5},{5,4},{6,7},{7,6},{8,9},{9,8},{10,11... | collective-permute-start | bytes 393224 | tf_op jit(solution)/shard_map/ppermute | solution.py:52
  108.0 2.1 %collective-permute-start.11 = (bf16[2,64,512]{2,1,0:T(8,128)(2,1)S(1)}, bf16[2,64,512]{2,1,0:T(8,128)(2,1)S(1)}, u32[]{:S(2)}, u32[]{:S(2)}) collective-permute-start(bf16[2,64,512]{2,1,0:T(8,128)(2,1)S(1)} %collective-permute-done.9.refs_1_), channel_id=1, source_target_pairs={{0,1},{1,0},{2,3},{3,2},{4,5},{5,4},{6,7},{7,6},{8,9},{9,8},{10,11... | collective-permute-start | bytes 393224 | tf_op jit(solution)/shard_map/ppermute | solution.py:52
  108.5 6.7 %copy-start.11 = (bf16[8,2,8,512]{3,2,0,1:T(8,128)(2,1)}, bf16[8,2,8,512]{3,2,0,1:T(8,128)(2,1)S(1)}, u32[]{:S(2)}) copy-start(bf16[8,2,8,512]{3,2,0,1:T(8,128)(2,1)S(1)} %copy.67) | copy-start | bytes 393220
  108.5 6.7 %collective-permute-start.8 = (bf16[2,64,512]{2,1,0:T(8,128)(2,1)S(1)}, bf16[2,64,512]{2,1,0:T(8,128)(2,1)S(1)}, u32[]{:S(2)}, u32[]{:S(2)}) collective-permute-start(bf16[2,64,512]{2,1,0:T(8,128)(2,1)S(1)} %bitcast.119), channel_id=1, source_target_pairs={{0,2},{1,3},{2,0},{3,1},{4,6},{5,7},{6,4},{7,5},{8,10},{9,11},{10,... | collective-permute-start | bytes 393224 | tf_op jit(solution)/shard_map/ppermute | solution.py:52
  115.2 1.4 %collective-permute-start.13 = (bf16[2,64,512]{2,1,0:T(8,128)(2,1)S(1)}, bf16[2,64,512]{2,1,0:T(8,128)(2,1)S(1)}, u32[]{:S(2)}, u32[]{:S(2)}) collective-permute-start(bf16[2,64,512]{2,1,0:T(8,128)(2,1)S(1)} %bitcast.120), channel_id=1, source_target_pairs={{0,1},{1,0},{2,3},{3,2},{4,5},{5,4},{6,7},{7,6},{8,9},{9,8},{10,11... | collective-permute-start | bytes 393224 | tf_op jit(solution)/shard_map/ppermute | solution.py:52
  115.3 1.5 %collective-permute-start.14 = (bf16[2,64,512]{2,1,0:T(8,128)(2,1)S(1)}, bf16[2,64,512]{2,1,0:T(8,128)(2,1)S(1)}, u32[]{:S(2)}, u32[]{:S(2)}) collective-permute-start(bf16[2,64,512]{2,1,0:T(8,128)(2,1)S(1)} %collective-permute-done.8.refs_1_), channel_id=1, source_target_pairs={{0,1},{1,0},{2,3},{3,2},{4,5},{5,4},{6,7},{7,6},{8,9},{9,8},{10,11... | collective-permute-start | bytes 393224 | tf_op jit(solution)/shard_map/ppermute | solution.py:52
  115.8 5.9 %copy-start.8 = (bf16[8,2,8,512]{3,2,0,1:T(8,128)(2,1)}, bf16[8,2,8,512]{3,2,0,1:T(8,128)(2,1)S(1)}, u32[]{:S(2)}) copy-start(bf16[8,2,8,512]{3,2,0,1:T(8,128)(2,1)S(1)} %copy.65) | copy-start | bytes 393220
  115.8 5.9 %collective-permute-start.12 = (bf16[2,64,512]{2,1,0:T(8,128)(2,1)S(1)}, bf16[2,64,512]{2,1,0:T(8,128)(2,1)S(1)}, u32[]{:S(2)}, u32[]{:S(2)}) collective-permute-start(bf16[2,64,512]{2,1,0:T(8,128)(2,1)S(1)} %bitcast.110), channel_id=1, source_target_pairs={{0,2},{1,3},{2,0},{3,1},{4,6},{5,7},{6,4},{7,5},{8,10},{9,11},{10,... | collective-permute-start | bytes 393224 | tf_op jit(solution)/shard_map/ppermute | solution.py:52
  121.7 2.1 %collective-permute-start.16 = (bf16[2,64,512]{2,1,0:T(8,128)(2,1)S(1)}, bf16[2,64,512]{2,1,0:T(8,128)(2,1)S(1)}, u32[]{:S(2)}, u32[]{:S(2)}) collective-permute-start(bf16[2,64,512]{2,1,0:T(8,128)(2,1)S(1)} %bitcast.111), channel_id=1, source_target_pairs={{0,1},{1,0},{2,3},{3,2},{4,5},{5,4},{6,7},{7,6},{8,9},{9,8},{10,11... | collective-permute-start | bytes 393224 | tf_op jit(solution)/shard_map/ppermute | solution.py:52
  121.9 1.9 %collective-permute-start.17 = (bf16[2,64,512]{2,1,0:T(8,128)(2,1)S(1)}, bf16[2,64,512]{2,1,0:T(8,128)(2,1)S(1)}, u32[]{:S(2)}, u32[]{:S(2)}) collective-permute-start(bf16[2,64,512]{2,1,0:T(8,128)(2,1)S(1)} %collective-permute-done.12.refs_1_), channel_id=1, source_target_pairs={{0,1},{1,0},{2,3},{3,2},{4,5},{5,4},{6,7},{7,6},{8,9},{9,8},{10,11... | collective-permute-start | bytes 393224 | tf_op jit(solution)/shard_map/ppermute | solution.py:52
  122.3 6.6 %copy-start.9 = (bf16[8,2,8,512]{3,2,0,1:T(8,128)(2,1)}, bf16[8,2,8,512]{3,2,0,1:T(8,128)(2,1)S(1)}, u32[]{:S(2)}) copy-start(bf16[8,2,8,512]{3,2,0,1:T(8,128)(2,1)S(1)} %copy.64) | copy-start | bytes 393220
  122.3 6.5 %collective-permute-start.15 = (bf16[2,64,512]{2,1,0:T(8,128)(2,1)S(1)}, bf16[2,64,512]{2,1,0:T(8,128)(2,1)S(1)}, u32[]{:S(2)}, u32[]{:S(2)}) collective-permute-start(bf16[2,64,512]{2,1,0:T(8,128)(2,1)S(1)} %bitcast.113), channel_id=1, source_target_pairs={{0,2},{1,3},{2,0},{3,1},{4,6},{5,7},{6,4},{7,5},{8,10},{9,11},{10,... | collective-permute-start | bytes 393224 | tf_op jit(solution)/shard_map/ppermute | solution.py:52
  128.9 2.0 %collective-permute-start.18 = (bf16[2,64,512]{2,1,0:T(8,128)(2,1)S(1)}, bf16[2,64,512]{2,1,0:T(8,128)(2,1)S(1)}, u32[]{:S(2)}, u32[]{:S(2)}) collective-permute-start(bf16[2,64,512]{2,1,0:T(8,128)(2,1)S(1)} %bitcast.114), channel_id=1, source_target_pairs={{0,1},{1,0},{2,3},{3,2},{4,5},{5,4},{6,7},{7,6},{8,9},{9,8},{10,11... | collective-permute-start | bytes 393224 | tf_op jit(solution)/shard_map/ppermute | solution.py:52
  128.9 1.9 %collective-permute-start.19 = (bf16[2,64,512]{2,1,0:T(8,128)(2,1)S(1)}, bf16[2,64,512]{2,1,0:T(8,128)(2,1)S(1)}, u32[]{:S(2)}, u32[]{:S(2)}) collective-permute-start(bf16[2,64,512]{2,1,0:T(8,128)(2,1)S(1)} %collective-permute-done.15.refs_1_), channel_id=1, source_target_pairs={{0,1},{1,0},{2,3},{3,2},{4,5},{5,4},{6,7},{7,6},{8,9},{9,8},{10,11... | collective-permute-start | bytes 393224 | tf_op jit(solution)/shard_map/ppermute | solution.py:52
  130.8 5.1 %copy-start.2 = (f32[2,512,64]{2,1,0:T(8,128)S(1)}, f32[2,512,64]{2,1,0:T(8,128)}, u32[]{:S(2)}) copy-start(f32[2,512,64]{2,1,0:T(8,128)} %shard_map.66) | copy-start | bytes 786436
  (22 other events, 36.6 us)

commit v22 on v17

--- a/solution.py
+++ b/solution.py
@@ -10,20 +10,21 @@
 CHUNKS = 2
 
 
-def information_kernel(hours, stations, me_ref, x_ref, l_ref, *out_refs):
+def information_kernel(hours, stations, me_ref, x_ref, l_ref, *refs):
+    *out_refs, total_ref = refs
     me = me_ref[0]
     chunks = len(out_refs) // 2
     levels = out_refs[0].ndim - 1
     rows, width = out_refs[0].shape[-2:]
     senders = x_ref.shape[0]
     flipped = x_ref[:, :stations, :].reshape(senders * stations, x_ref.shape[2]).T
+    total_ref[...] = jnp.dot(flipped, l_ref[...], preferred_element_type=jnp.float32)
     for slot in range(2 ** levels):
         relative = tuple((slot >> level) & 1 for level in range(levels))
         block = 0
         for level in range(levels):
             block = block + ((relative[level] ^ ((me >> level) & 1) ^ 1) << level)
-        columns = l_ref[:, pl.ds(pl.multiple_of(block * width, width), width)]
-        total = jnp.dot(flipped, columns, preferred_element_type=jnp.float32)
+        total = total_ref[:, pl.ds(pl.multiple_of(block * width, width), width)]
         total = total.reshape(hours, chunks, rows // hours, width)
         for chunk in range(chunks):
             target = out_refs[2 * chunk + relative[0]]
@@ -89,10 +90,11 @@
         out_ref[hour] = state
 
 
-def vmem_call(kernel, out_shape, count, cost, scalars=0):
+def vmem_call(kernel, out_shape, count, cost, scalars=0, scratch=()):
     return pl.pallas_call(
         kernel,
         out_shape=out_shape,
+        scratch_shapes=list(scratch),
         in_specs=[pl.BlockSpec(memory_space=pltpu.SMEM)] * scalars
         + [pl.BlockSpec(memory_space=pltpu.VMEM)] * count,
         out_specs=jax.tree.map(lambda _: pl.BlockSpec(memory_space=pltpu.VMEM), out_shape),
@@ -143,6 +145,7 @@
             transcendentals=0,
         ),
         scalars=1,
+        scratch=[pltpu.VMEM((hours * members_here, all_comps), jnp.float32)],
     )(lax.axis_index("state").reshape(1).astype(jnp.int32), by_member, loadings)
     smoothed_parts = []
     residual_parts = []

time: 114 us -> 115 us (level)
  no operation moved by 1% of the time
where the time goes in v22:
time: 115 us; the launch traced here: 114 us
  waiting for transfers between devices  47.6 us (41%)
  starting transfers between devices  30 us (26%)
  Pallas kernels  17.2 us (15%)
  local copies, waits for them, and re-layouts  10.2 us (9%)
  other arithmetic  8.11 us (7%)
    all_to_all x1, waiting for transfers between devices, local(): lax.all_to_all(outgoing, 'tm', split_axis=0, concat_axis=0, tiled=True)  17.3 us
    all_to_all x2, starting transfers between devices, local(): lax.all_to_all(smoothed_here, 'tm', split_axis=0, concat_axis=1, tiled=True)  11.3 us
    ppermute x1, waiting for transfers between devices, local(): lax.ppermute(o, 'state', last[c + 1][2])  10.6 us
    all_to_all x1, waiting for transfers between devices, local(): lax.all_to_all(masked_later, 'tm', split_axis=1, concat_axis=0, tiled=True)  9.18 us
    pallas_call x2, Pallas kernels, local(): vmem_call(fitted_kernel, jax.ShapeDtypeStruct((slab_hours, stations_here,...  7.71 us
    unnamed x27, local copies, waits for them, and re-layouts  7.65 us
    all_to_all x1, starting transfers between devices, local(): lax.all_to_all(outgoing, 'tm', split_axis=0, concat_axis=0, tiled=True)  7.25 us
    ppermute x6, waiting for transfers between devices, doubling_gather(): pieces = pieces + [lax.ppermute(piece, axis, pairs) for piece in pieces]  5.3 us
  transfers between devices with their start and end apart: 14, of which 8 were waited for; matrix products, arithmetic and copies ran while one was open for 7% of the time, Pallas kernels for 5%

profile of v22, /device:TPU:0, one launch (start us, length us, event | category | flops | bytes accessed | tf_op | source)
XLA Modules:
  0.0 114.0 jit_solution(10335797878355599969)
XLA Ops:
  0.6 0.7 convert_element_type.29
  1.3 0.7 fusion.5
  2.1 1.7 %copy.37 = bf16[64,16,256]{0,2,1:T(8,128)(2,1)S(1)} copy(bf16[64,16,256]{2,1,0:T(8,128)(2,1)} %param.4) | data formatting | bytes 1048576 | tf_op args[0]
  4.4 0.9 pad_maximum_fusion.2
  5.3 7.3 %all-to-all-start = ((bf16[8,80,512]{2,1,0:T(8,128)(2,1)}), bf16[8,80,512]{2,1,0:T(8,128)(2,1)S(1)}, u32[]{:S(2)}, u32[]{:S(2)}) async-start(bf16[8,80,512]{2,1,0:T(8,128)(2,1)} %pad_maximum_fusion.2), calls=%async_computation | async-start | bytes 1310720 | tf_op jit(solution)/shard_map/all_to_all | solution.py:125
  12.6 17.3 %all-to-all-done.x_ref = bf16[8,80,512]{2,1,0:T(8,128)(2,1)S(1)} async-done(((bf16[8,80,512]{2,1,0:T(8,128)(2,1)}), bf16[8,80,512]{2,1,0:T(8,128)(2,1)S(1)}, u32[]{:S(2)}, u32[]{:S(2)}) %all-to-all-start) | async-done | bytes 655392 | tf_op jit(solution)/shard_map/all_to_all | solution.py:125
  29.9 0.8 copy-done.5
  30.7 5.2 %shard_map.59 = (f32[2,256,512]{2,1,0:T(8,128)}, f32[2,256,512]{2,1,0:T(8,128)}, f32[2,256,512]{2,1,0:T(8,128)}, f32[2,256,512]{2,1,0:T(8,128)}) custom-call(s32[1]{0:T(128)} %bitcast.10.me_ref, bf16[8,80,512]{2,1,0:T(8,128)(2,1)} %copy-done.5, bf16[512,2048]{1,0:T(8,128)(2,1)} %l_ref.5), custom_call_target="tpu_custom_call" | custom-call | flops 1073741824 | bytes 6815744 | tf_op jit(solution)/shard_map/pallas_call | solution.py:137
  36.4 1.2 %copy.42 = bf16[64,16,256]{2,0,1:T(8,128)(2,1)} copy(bf16[64,16,256]{0,2,1:T(8,128)(2,1)S(1)} %broadcast_multiply_fusion) | data formatting | bytes 1048576 | tf_op jit(solution)/shard_map/optimization_barrier | solution.py:131
  37.5 3.6 %all-to-all-start.1 = ((bf16[64,16,256]{2,0,1:T(8,128)(2,1)}), bf16[64,16,256]{2,0,1:T(8,128)(2,1)S(1)}, u32[]{:S(2)}, u32[]{:S(2)}) async-start(bf16[64,16,256]{2,0,1:T(8,128)(2,1)} %copy.42), calls=%async_computation.1 | async-start | bytes 1048576 | tf_op jit(solution)/shard_map/all_to_all | solution.py:132
  41.2 2.4 %fusion.2 = (f32[256,512]{1,0:T(8,128)}, f32[256,512]{1,0:T(8,128)}) fusion(f32[2,256,512]{2,1,0:T(8,128)} %collective-permute-done, f32[2,256,512]{2,1,0:T(8,128)S(1)} %copy-done.2), kind=kLoop, calls=%fused_computation.8 | loop fusion | flops 262144 | bytes 3145728 | tf_op jit(solution)/shard_map/add | solution.py:41
  43.6 1.5 %collective-permute-start.1 = (f32[256,512]{1,0:T(8,128)}, f32[256,512]{1,0:T(8,128)}, u32[]{:S(2)}, u32[]{:S(2)}) collective-permute-start(f32[256,512]{1,0:T(8,128)} %get-tuple-element.44), channel_id=1, source_target_pairs={{0,2},{1,3},{2,0},{3,1},{4,6},{5,7},{6,4},{7,5},{8,10},{9,11},{10,... | collective-permute-start | bytes 1572872 | tf_op jit(solution)/shard_map/ppermute | solution.py:155
  45.1 0.8 slice_convert_fusion
  46.7 9.2 %all-to-all-done.1 = bf16[64,16,256]{2,0,1:T(8,128)(2,1)S(1)} async-done(((bf16[64,16,256]{2,0,1:T(8,128)(2,1)}), bf16[64,16,256]{2,0,1:T(8,128)(2,1)S(1)}, u32[]{:S(2)}, u32[]{:S(2)}) %all-to-all-start.1) | async-done | bytes 524320 | tf_op jit(solution)/shard_map/all_to_all | solution.py:132
  56.0 1.2 %fusion = (f32[256,512]{1,0:T(8,128)}, f32[256,512]{1,0:T(8,128)}) fusion(f32[2,256,512]{2,1,0:T(8,128)S(1)} %collective-permute-done.2, f32[2,256,512]{2,1,0:T(8,128)S(1)} %copy-done.1), kind=kLoop, calls=%fused_computation.4 | loop fusion | flops 262144 | bytes 3145728 | tf_op jit(solution)/shard_map/add | solution.py:41
  57.6 2.2 %shard_map.60 = f32[16,16,512]{2,1,0:T(8,128)} custom-call(f32[16,512]{1,0:T(8,128)} %add.40.rate_ref, f32[16,16,512]{2,1,0:T(8,128)} %bitcast.53, f32[16,16,512]{2,1,0:T(8,128)} %bitcast.16.received_ref), custom_call_target="tpu_custom_call" | custom-call | flops 786432 | bytes 1572864 | tf_op jit(solution)/shard_map/pallas_call | solution.py:165
  59.8 5.6 %all-to-all-start.2 = ((f32[16,16,512]{2,1,0:T(8,128)}), f32[16,16,512]{2,1,0:T(8,128)S(1)}, u32[]{:S(2)}, u32[]{:S(2)}) async-start(f32[16,16,512]{2,1,0:T(8,128)} %shard_map.60), calls=%async_computation.2 | async-start | bytes 1048576 | tf_op jit(solution)/shard_map/all_to_all | solution.py:175
  65.5 1.6 %collective-permute-start.3 = (f32[256,512]{1,0:T(8,128)S(1)}, f32[256,512]{1,0:T(8,128)S(1)}, u32[]{:S(2)}, u32[]{:S(2)}) collective-permute-start(f32[256,512]{1,0:T(8,128)S(1)} %copy-done.7), channel_id=1, source_target_pairs={{0,2},{1,3},{2,0},{3,1},{4,6},{5,7},{6,4},{7,5},{8,10},{9,11},{10,... | collective-permute-start | bytes 1572872 | tf_op jit(solution)/shard_map/ppermute | solution.py:159
  67.0 10.6 %collective-permute-done.3 = f32[256,512]{1,0:T(8,128)S(1)} collective-permute-done((f32[256,512]{1,0:T(8,128)S(1)}, f32[256,512]{1,0:T(8,128)S(1)}, u32[]{:S(2)}, u32[]{:S(2)}) %collective-permute-start.3) | collective-permute-done | bytes 524320 | tf_op jit(solution)/shard_map/ppermute | solution.py:159
  77.7 0.8 copy-done.6
  78.5 2.1 %shard_map.61 = f32[16,16,512]{2,1,0:T(8,128)} custom-call(f32[16,512]{1,0:T(8,128)} %add.40.rate_ref, f32[16,16,512]{2,1,0:T(8,128)} %bitcast.57, f32[16,16,512]{2,1,0:T(8,128)} %bitcast.58), custom_call_target="tpu_custom_call" | custom-call | flops 786432 | bytes 1572864 | tf_op jit(solution)/shard_map/pallas_call | solution.py:165
  80.6 5.7 %all-to-all-start.3 = ((f32[16,16,512]{2,1,0:T(8,128)}), f32[16,16,512]{2,1,0:T(8,128)S(1)}, u32[]{:S(2)}, u32[]{:S(2)}) async-start(f32[16,16,512]{2,1,0:T(8,128)} %shard_map.61), calls=%async_computation.3 | async-start | bytes 1048576 | tf_op jit(solution)/shard_map/all_to_all | solution.py:175
  86.4 1.6 %collective-permute-start.5 = (bf16[2,128,512]{2,1,0:T(8,128)(2,1)S(1)}, bf16[2,128,512]{2,1,0:T(8,128)(2,1)S(1)}, u32[]{:S(2)}, u32[]{:S(2)}) collective-permute-start(bf16[2,128,512]{2,1,0:T(8,128)(2,1)S(1)} %bitcast_convert_fusion.refs_0_), channel_id=1, source_target_pairs={{0,2},{1,3},{2,0},{3,1},{4,6},{5,7},{6,4},{7,5},{8,10},{9,11},{10,... | collective-permute-start | bytes 786440 | tf_op jit(solution)/shard_map/ppermute | solution.py:53
  87.9 4.9 %collective-permute-done.5.refs_1_ = bf16[2,128,512]{2,1,0:T(8,128)(2,1)S(1)} collective-permute-done((bf16[2,128,512]{2,1,0:T(8,128)(2,1)S(1)}, bf16[2,128,512]{2,1,0:T(8,128)(2,1)S(1)}, u32[]{:S(2)}, u32[]{:S(2)}) %collective-permute-start.5) | collective-permute-done | bytes 262176 | tf_op jit(solution)/shard_map/ppermute | solution.py:53
  93.3 4.7 %all-to-all-done.3 = f32[16,16,512]{2,1,0:T(8,128)S(1)} async-done(((f32[16,16,512]{2,1,0:T(8,128)}), f32[16,16,512]{2,1,0:T(8,128)S(1)}, u32[]{:S(2)}, u32[]{:S(2)}) %all-to-all-start.3) | async-done | bytes 524320 | tf_op jit(solution)/shard_map/all_to_all | solution.py:175
  98.1 1.6 %collective-permute-start.4 = (bf16[2,128,512]{2,1,0:T(8,128)(2,1)S(1)}, bf16[2,128,512]{2,1,0:T(8,128)(2,1)S(1)}, u32[]{:S(2)}, u32[]{:S(2)}) collective-permute-start(bf16[2,128,512]{2,1,0:T(8,128)(2,1)S(1)} %bitcast_convert_fusion.1.refs_0_), channel_id=1, source_target_pairs={{0,2},{1,3},{2,0},{3,1},{4,6},{5,7},{6,4},{7,5},{8,10},{9,11},{10,... | collective-permute-start | bytes 786440 | tf_op jit(solution)/shard_map/ppermute | solution.py:53
  99.7 0.7 copy-done.10
  100.4 3.9 %shard_map.62 = f32[2,512,128]{2,1,0:T(8,128)} custom-call(s32[1]{0:T(128)} %bitcast.10.me_ref, bf16[512,2048]{1,0:T(8,128)(2,1)} %l_ref.5, bf16[2,128,512]{2,1,0:T(8,128)(2,1)} %copy-done.4, bf16[2,128,512]{2,1,0:T(8,128)(2,1)} %copy-done.9, bf16[2,128,512]{2,1,0:T(8,128)(2,1)} %copy-done.10, bf16[2,128,512]{2,1,0:T(8,128)(2,1)} %collective-permute-done.7.refs_3_), custom_call_target="tpu_custom_call" | custom-call | flops 536870912 | bytes 3670016 | tf_op jit(solution)/shard_map/pallas_call | solution.py:180
  105.2 1.3 %copy.46 = f32[512,2,256]{2,1,0:T(2,128)} copy(f32[512,2,256]{0,2,1:T(8,128)S(1)} %pad_maximum_fusion) | data formatting | bytes 2097152
  107.2 3.9 %shard_map.63 = f32[2,512,128]{2,1,0:T(8,128)} custom-call(s32[1]{0:T(128)} %bitcast.10.me_ref, bf16[512,2048]{1,0:T(8,128)(2,1)} %l_ref.5, bf16[2,128,512]{2,1,0:T(8,128)(2,1)} %copy-done.3, bf16[2,128,512]{2,1,0:T(8,128)(2,1)} %copy-done.8, bf16[2,128,512]{2,1,0:T(8,128)(2,1)} %copy-done.11, bf16[2,128,512]{2,1,0:T(8,128)(2,1)} %collective-permute-done.9.refs_3_), custom_call_target="tpu_custom_call" | custom-call | flops 536870912 | bytes 3670016 | tf_op jit(solution)/shard_map/pallas_call | solution.py:180
  111.0 1.1 bitcast_subtract_fusion.1
  112.2 1.8 %copy.47 = f32[512,2,256]{2,1,0:T(2,128)} copy(f32[512,2,256]{2,0,1:T(8,128)S(1)} %pad_maximum_fusion.1) | data formatting | bytes 2097152
  (54 shorter events, 4.8 us)
Async XLA Ops:
  5.3 24.5 %all-to-all-start = ((bf16[8,80,512]{2,1,0:T(8,128)(2,1)}), bf16[8,80,512]{2,1,0:T(8,128)(2,1)S(1)}, u32[]{:S(2)}, u32[]{:S(2)}) async-start(bf16[8,80,512]{2,1,0:T(8,128)(2,1)} %pad_maximum_fusion.2), calls=%async_computation | async-start | bytes 1310720 | tf_op jit(solution)/shard_map/all_to_all | solution.py:125
  29.9 0.8 copy-start.5
  35.9 5.3 %collective-permute-start = (f32[2,256,512]{2,1,0:T(8,128)}, f32[2,256,512]{2,1,0:T(8,128)}, u32[]{:S(2)}, u32[]{:S(2)}) collective-permute-start(f32[2,256,512]{2,1,0:T(8,128)} %get-tuple-element.21), channel_id=1, source_target_pairs={{0,1},{1,0},{2,3},{3,2},{4,5},{5,4},{6,7},{7,6},{8,9},{9,8},{10,11... | collective-permute-start | bytes 3145736 | tf_op jit(solution)/shard_map/ppermute | solution.py:39
  35.9 5.3 %copy-start.2 = (f32[2,256,512]{2,1,0:T(8,128)S(1)}, f32[2,256,512]{2,1,0:T(8,128)}, u32[]{:S(2)}) copy-start(f32[2,256,512]{2,1,0:T(8,128)} %get-tuple-element.20) | copy-start | bytes 3145732
  35.9 20.1 %collective-permute-start.2 = (f32[2,256,512]{2,1,0:T(8,128)}, f32[2,256,512]{2,1,0:T(8,128)S(1)}, u32[]{:S(2)}, u32[]{:S(2)}) collective-permute-start(f32[2,256,512]{2,1,0:T(8,128)} %get-tuple-element.23), channel_id=1, source_target_pairs={{0,1},{1,0},{2,3},{3,2},{4,5},{5,4},{6,7},{7,6},{8,9},{9,8},{10,11... | collective-permute-start | bytes 3145736 | tf_op jit(solution)/shard_map/ppermute | solution.py:39
  37.5 18.4 %all-to-all-start.1 = ((bf16[64,16,256]{2,0,1:T(8,128)(2,1)}), bf16[64,16,256]{2,0,1:T(8,128)(2,1)S(1)}, u32[]{:S(2)}, u32[]{:S(2)}) async-start(bf16[64,16,256]{2,0,1:T(8,128)(2,1)} %copy.42), calls=%async_computation.1 | async-start | bytes 1048576 | tf_op jit(solution)/shard_map/all_to_all | solution.py:132
  43.6 12.4 %copy-start.1 = (f32[2,256,512]{2,1,0:T(8,128)S(1)}, f32[2,256,512]{2,1,0:T(8,128)}, u32[]{:S(2)}) copy-start(f32[2,256,512]{2,1,0:T(8,128)} %get-tuple-element.22) | copy-start | bytes 3145732
  43.6 14.0 %collective-permute-start.1 = (f32[256,512]{1,0:T(8,128)}, f32[256,512]{1,0:T(8,128)}, u32[]{:S(2)}, u32[]{:S(2)}) collective-permute-start(f32[256,512]{1,0:T(8,128)} %get-tuple-element.44), channel_id=1, source_target_pairs={{0,2},{1,3},{2,0},{3,1},{4,6},{5,7},{6,4},{7,5},{8,10},{9,11},{10,... | collective-permute-start | bytes 1572872 | tf_op jit(solution)/shard_map/ppermute | solution.py:155
  57.6 7.8 %copy-start.7 = (f32[256,512]{1,0:T(8,128)S(1)}, f32[256,512]{1,0:T(8,128)}, u32[]{:S(2)}) copy-start(f32[256,512]{1,0:T(8,128)} %get-tuple-element.27) | copy-start | bytes 1572868
  59.8 20.8 %all-to-all-start.2 = ((f32[16,16,512]{2,1,0:T(8,128)}), f32[16,16,512]{2,1,0:T(8,128)S(1)}, u32[]{:S(2)}, u32[]{:S(2)}) async-start(f32[16,16,512]{2,1,0:T(8,128)} %shard_map.60), calls=%async_computation.2 | async-start | bytes 1048576 | tf_op jit(solution)/shard_map/all_to_all | solution.py:175
  65.5 12.2 %collective-permute-start.3 = (f32[256,512]{1,0:T(8,128)S(1)}, f32[256,512]{1,0:T(8,128)S(1)}, u32[]{:S(2)}, u32[]{:S(2)}) collective-permute-start(f32[256,512]{1,0:T(8,128)S(1)} %copy-done.7), channel_id=1, source_target_pairs={{0,2},{1,3},{2,0},{3,1},{4,6},{5,7},{6,4},{7,5},{8,10},{9,11},{10,... | collective-permute-start | bytes 1572872 | tf_op jit(solution)/shard_map/ppermute | solution.py:159
  77.7 0.8 copy-start.6
  80.6 17.4 %all-to-all-start.3 = ((f32[16,16,512]{2,1,0:T(8,128)}), f32[16,16,512]{2,1,0:T(8,128)S(1)}, u32[]{:S(2)}, u32[]{:S(2)}) async-start(f32[16,16,512]{2,1,0:T(8,128)} %shard_map.61), calls=%async_computation.3 | async-start | bytes 1048576 | tf_op jit(solution)/shard_map/all_to_all | solution.py:175
  86.3 13.4 %copy-start.4 = (bf16[2,128,512]{2,1,0:T(8,128)(2,1)}, bf16[2,128,512]{2,1,0:T(8,128)(2,1)S(1)}, u32[]{:S(2)}) copy-start(bf16[2,128,512]{2,1,0:T(8,128)(2,1)S(1)} %bitcast_convert_fusion.refs_0_) | copy-start | bytes 786436
  86.4 6.4 %collective-permute-start.5 = (bf16[2,128,512]{2,1,0:T(8,128)(2,1)S(1)}, bf16[2,128,512]{2,1,0:T(8,128)(2,1)S(1)}, u32[]{:S(2)}, u32[]{:S(2)}) collective-permute-start(bf16[2,128,512]{2,1,0:T(8,128)(2,1)S(1)} %bitcast_convert_fusion.refs_0_), channel_id=1, source_target_pairs={{0,2},{1,3},{2,0},{3,1},{4,6},{5,7},{6,4},{7,5},{8,10},{9,11},{10,... | collective-permute-start | bytes 786440 | tf_op jit(solution)/shard_map/ppermute | solution.py:53
  92.8 6.9 %copy-start.9 = (bf16[2,128,512]{2,1,0:T(8,128)(2,1)}, bf16[2,128,512]{2,1,0:T(8,128)(2,1)S(1)}, u32[]{:S(2)}) copy-start(bf16[2,128,512]{2,1,0:T(8,128)(2,1)S(1)} %collective-permute-done.5.refs_1_) | copy-start | bytes 786436
  92.8 6.9 %collective-permute-start.6 = (bf16[2,128,512]{2,1,0:T(8,128)(2,1)S(1)}, bf16[2,128,512]{2,1,0:T(8,128)(2,1)S(1)}, u32[]{:S(2)}, u32[]{:S(2)}) collective-permute-start(bf16[2,128,512]{2,1,0:T(8,128)(2,1)S(1)} %bitcast_convert_fusion.refs_0_), channel_id=1, source_target_pairs={{0,1},{1,0},{2,3},{3,2},{4,5},{5,4},{6,7},{7,6},{8,9},{9,8},{10,11... | collective-permute-start | bytes 786440 | tf_op jit(solution)/shard_map/ppermute | solution.py:53
  92.8 6.9 %collective-permute-start.7 = (bf16[2,128,512]{2,1,0:T(8,128)(2,1)S(1)}, bf16[2,128,512]{2,1,0:T(8,128)(2,1)}, u32[]{:S(2)}, u32[]{:S(2)}) collective-permute-start(bf16[2,128,512]{2,1,0:T(8,128)(2,1)S(1)} %collective-permute-done.5.refs_1_), channel_id=1, source_target_pairs={{0,1},{1,0},{2,3},{3,2},{4,5},{5,4},{6,7},{7,6},{8,9},{9,8},{10,11... | collective-permute-start | bytes 786440 | tf_op jit(solution)/shard_map/ppermute | solution.py:53
  98.1 6.5 %copy-start.3 = (bf16[2,128,512]{2,1,0:T(8,128)(2,1)}, bf16[2,128,512]{2,1,0:T(8,128)(2,1)S(1)}, u32[]{:S(2)}) copy-start(bf16[2,128,512]{2,1,0:T(8,128)(2,1)S(1)} %bitcast_convert_fusion.1.refs_0_) | copy-start | bytes 786436
  98.1 6.4 %collective-permute-start.4 = (bf16[2,128,512]{2,1,0:T(8,128)(2,1)S(1)}, bf16[2,128,512]{2,1,0:T(8,128)(2,1)S(1)}, u32[]{:S(2)}, u32[]{:S(2)}) collective-permute-start(bf16[2,128,512]{2,1,0:T(8,128)(2,1)S(1)} %bitcast_convert_fusion.1.refs_0_), channel_id=1, source_target_pairs={{0,2},{1,3},{2,0},{3,1},{4,6},{5,7},{6,4},{7,5},{8,10},{9,11},{10,... | collective-permute-start | bytes 786440 | tf_op jit(solution)/shard_map/ppermute | solution.py:53
  99.7 0.7 copy-start.10
  104.6 1.9 %copy-start.8 = (bf16[2,128,512]{2,1,0:T(8,128)(2,1)}, bf16[2,128,512]{2,1,0:T(8,128)(2,1)S(1)}, u32[]{:S(2)}) copy-start(bf16[2,128,512]{2,1,0:T(8,128)(2,1)S(1)} %collective-permute-done.4.refs_1_) | copy-start | bytes 786436
  104.6 1.9 %collective-permute-start.8 = (bf16[2,128,512]{2,1,0:T(8,128)(2,1)S(1)}, bf16[2,128,512]{2,1,0:T(8,128)(2,1)S(1)}, u32[]{:S(2)}, u32[]{:S(2)}) collective-permute-start(bf16[2,128,512]{2,1,0:T(8,128)(2,1)S(1)} %bitcast_convert_fusion.1.refs_0_), channel_id=1, source_target_pairs={{0,1},{1,0},{2,3},{3,2},{4,5},{5,4},{6,7},{7,6},{8,9},{9,8},{10,11... | collective-permute-start | bytes 786440 | tf_op jit(solution)/shard_map/ppermute | solution.py:53
  104.6 2.0 %collective-permute-start.9 = (bf16[2,128,512]{2,1,0:T(8,128)(2,1)S(1)}, bf16[2,128,512]{2,1,0:T(8,128)(2,1)}, u32[]{:S(2)}, u32[]{:S(2)}) collective-permute-start(bf16[2,128,512]{2,1,0:T(8,128)(2,1)S(1)} %collective-permute-done.4.refs_1_), channel_id=1, source_target_pairs={{0,1},{1,0},{2,3},{3,2},{4,5},{5,4},{6,7},{7,6},{8,9},{9,8},{10,11... | collective-permute-start | bytes 786440 | tf_op jit(solution)/shard_map/ppermute | solution.py:53
  106.5 4.6 %copy-start = (f32[2,512,128]{2,1,0:T(8,128)S(1)}, f32[2,512,128]{2,1,0:T(8,128)}, u32[]{:S(2)}) copy-start(f32[2,512,128]{2,1,0:T(8,128)} %shard_map.62) | copy-start | bytes 1572868
  106.5 0.7 copy-start.11

commit v23 on v17

--- a/solution.py
+++ b/solution.py
@@ -116,7 +116,7 @@
     middle = lax.reduce_precision(decay - high, exponent_bits=8, mantissa_bits=7)
     low = decay - high - middle
     pieces = jnp.stack([high, middle, low]).astype(obs.dtype).reshape(-1, hours * members_here)
-    spare = (-(stations_local + pieces.shape[0])) % 16
+    spare = (-(stations_local + pieces.shape[0])) % 8
     pieces = jnp.pad(pieces, ((0, spare), (0, 0)))
     pieces = jnp.broadcast_to(pieces[None], (tm_count,) + pieces.shape)
     outgoing = jnp.concatenate([outgoing, pieces], axis=1)

time: 114 us -> 113 us (level)
  waiting for transfers between devices: 47.6 us -> 46.2 us
    all_to_all x1, waiting for transfers between devices: 17.3 us -> 15.9 us  [local(): lax.all_to_all(outgoing, 'tm', split_axis=0, concat_axis=0, tiled=True)]
where the time goes in v23:
time: 113 us; the launch traced here: 112 us
  waiting for transfers between devices  46.2 us (41%)
  starting transfers between devices  30 us (27%)
  Pallas kernels  16.8 us (15%)
  local copies, waits for them, and re-layouts  10.2 us (9%)
  other arithmetic  8.1 us (7%)
    all_to_all x1, waiting for transfers between devices, local(): lax.all_to_all(outgoing, 'tm', split_axis=0, concat_axis=0, tiled=True)  15.9 us
    all_to_all x2, starting transfers between devices, local(): lax.all_to_all(smoothed_here, 'tm', split_axis=0, concat_axis=1, tiled=True)  11.3 us
    ppermute x1, waiting for transfers between devices, local(): lax.ppermute(o, 'state', last[c + 1][2])  10.6 us
    all_to_all x1, waiting for transfers between devices, local(): lax.all_to_all(masked_later, 'tm', split_axis=1, concat_axis=0, tiled=True)  9.16 us
    pallas_call x2, Pallas kernels, local(): vmem_call(fitted_kernel, jax.ShapeDtypeStruct((slab_hours, stations_here,...  7.7 us
    unnamed x27, local copies, waits for them, and re-layouts  7.63 us
    all_to_all x1, starting transfers between devices, local(): lax.all_to_all(outgoing, 'tm', split_axis=0, concat_axis=0, tiled=True)  7.25 us
    ppermute x6, waiting for transfers between devices, doubling_gather(): pieces = pieces + [lax.ppermute(piece, axis, pairs) for piece in pieces]  5.28 us
  transfers between devices with their start and end apart: 14, of which 8 were waited for; matrix products, arithmetic and copies ran while one was open for 7% of the time, Pallas kernels for 5%

profile of v23, /device:TPU:0, one launch (start us, length us, event | category | flops | bytes accessed | tf_op | source)
XLA Modules:
  0.0 112.2 jit_solution(8980060786842114272)
XLA Ops:
  0.6 0.7 convert_element_type.29
  1.3 0.7 fusion.5
  2.1 1.7 %copy.37 = bf16[64,16,256]{0,2,1:T(8,128)(2,1)S(1)} copy(bf16[64,16,256]{2,1,0:T(8,128)(2,1)} %param.4) | data formatting | bytes 1048576 | tf_op args[0]
  4.4 0.9 pad_maximum_fusion.2
  5.3 7.3 %all-to-all-start = ((bf16[8,72,512]{2,1,0:T(8,128)(2,1)}), bf16[8,72,512]{2,1,0:T(8,128)(2,1)S(1)}, u32[]{:S(2)}, u32[]{:S(2)}) async-start(bf16[8,72,512]{2,1,0:T(8,128)(2,1)} %pad_maximum_fusion.2), calls=%async_computation | async-start | bytes 1179648 | tf_op jit(solution)/shard_map/all_to_all | solution.py:123
  12.5 15.9 %all-to-all-done.x_ref = bf16[8,72,512]{2,1,0:T(8,128)(2,1)S(1)} async-done(((bf16[8,72,512]{2,1,0:T(8,128)(2,1)}), bf16[8,72,512]{2,1,0:T(8,128)(2,1)S(1)}, u32[]{:S(2)}, u32[]{:S(2)}) %all-to-all-start) | async-done | bytes 589856 | tf_op jit(solution)/shard_map/all_to_all | solution.py:123
  28.4 0.8 copy-done.5
  29.2 4.8 %shard_map.59 = (f32[2,256,512]{2,1,0:T(8,128)}, f32[2,256,512]{2,1,0:T(8,128)}, f32[2,256,512]{2,1,0:T(8,128)}, f32[2,256,512]{2,1,0:T(8,128)}) custom-call(s32[1]{0:T(128)} %bitcast.10.me_ref, bf16[8,72,512]{2,1,0:T(8,128)(2,1)} %copy-done.5, bf16[512,2048]{1,0:T(8,128)(2,1)} %l_ref.5), custom_call_target="tpu_custom_call" | custom-call | flops 1073741824 | bytes 6815744 | tf_op jit(solution)/shard_map/pallas_call | solution.py:135
  34.6 1.1 %copy.42 = bf16[64,16,256]{2,0,1:T(8,128)(2,1)} copy(bf16[64,16,256]{0,2,1:T(8,128)(2,1)S(1)} %broadcast_multiply_fusion) | data formatting | bytes 1048576 | tf_op jit(solution)/shard_map/optimization_barrier | solution.py:129
  35.7 3.6 %all-to-all-start.1 = ((bf16[64,16,256]{2,0,1:T(8,128)(2,1)}), bf16[64,16,256]{2,0,1:T(8,128)(2,1)S(1)}, u32[]{:S(2)}, u32[]{:S(2)}) async-start(bf16[64,16,256]{2,0,1:T(8,128)(2,1)} %copy.42), calls=%async_computation.1 | async-start | bytes 1048576 | tf_op jit(solution)/shard_map/all_to_all | solution.py:130
  39.3 2.4 %fusion.2 = (f32[256,512]{1,0:T(8,128)}, f32[256,512]{1,0:T(8,128)}) fusion(f32[2,256,512]{2,1,0:T(8,128)} %collective-permute-done, f32[2,256,512]{2,1,0:T(8,128)S(1)} %copy-done.2), kind=kLoop, calls=%fused_computation.8 | loop fusion | flops 262144 | bytes 3145728 | tf_op jit(solution)/shard_map/add | solution.py:40
  41.7 1.5 %collective-permute-start.1 = (f32[256,512]{1,0:T(8,128)}, f32[256,512]{1,0:T(8,128)}, u32[]{:S(2)}, u32[]{:S(2)}) collective-permute-start(f32[256,512]{1,0:T(8,128)} %get-tuple-element.44), channel_id=1, source_target_pairs={{0,2},{1,3},{2,0},{3,1},{4,6},{5,7},{6,4},{7,5},{8,10},{9,11},{10,... | collective-permute-start | bytes 1572872 | tf_op jit(solution)/shard_map/ppermute | solution.py:152
  43.3 0.8 slice_convert_fusion
  44.9 9.2 %all-to-all-done.1 = bf16[64,16,256]{2,0,1:T(8,128)(2,1)S(1)} async-done(((bf16[64,16,256]{2,0,1:T(8,128)(2,1)}), bf16[64,16,256]{2,0,1:T(8,128)(2,1)S(1)}, u32[]{:S(2)}, u32[]{:S(2)}) %all-to-all-start.1) | async-done | bytes 524320 | tf_op jit(solution)/shard_map/all_to_all | solution.py:130
  54.1 1.2 %fusion = (f32[256,512]{1,0:T(8,128)}, f32[256,512]{1,0:T(8,128)}) fusion(f32[2,256,512]{2,1,0:T(8,128)S(1)} %collective-permute-done.2, f32[2,256,512]{2,1,0:T(8,128)S(1)} %copy-done.1), kind=kLoop, calls=%fused_computation.4 | loop fusion | flops 262144 | bytes 3145728 | tf_op jit(solution)/shard_map/add | solution.py:40
  55.8 2.2 %shard_map.60 = f32[16,16,512]{2,1,0:T(8,128)} custom-call(f32[16,512]{1,0:T(8,128)} %add.40.rate_ref, f32[16,16,512]{2,1,0:T(8,128)} %bitcast.53, f32[16,16,512]{2,1,0:T(8,128)} %bitcast.16.received_ref), custom_call_target="tpu_custom_call" | custom-call | flops 786432 | bytes 1572864 | tf_op jit(solution)/shard_map/pallas_call | solution.py:162
  58.0 5.6 %all-to-all-start.2 = ((f32[16,16,512]{2,1,0:T(8,128)}), f32[16,16,512]{2,1,0:T(8,128)S(1)}, u32[]{:S(2)}, u32[]{:S(2)}) async-start(f32[16,16,512]{2,1,0:T(8,128)} %shard_map.60), calls=%async_computation.2 | async-start | bytes 1048576 | tf_op jit(solution)/shard_map/all_to_all | solution.py:172
  63.6 1.6 %collective-permute-start.3 = (f32[256,512]{1,0:T(8,128)S(1)}, f32[256,512]{1,0:T(8,128)S(1)}, u32[]{:S(2)}, u32[]{:S(2)}) collective-permute-start(f32[256,512]{1,0:T(8,128)S(1)} %copy-done.7), channel_id=1, source_target_pairs={{0,2},{1,3},{2,0},{3,1},{4,6},{5,7},{6,4},{7,5},{8,10},{9,11},{10,... | collective-permute-start | bytes 1572872 | tf_op jit(solution)/shard_map/ppermute | solution.py:156
  65.2 10.6 %collective-permute-done.3 = f32[256,512]{1,0:T(8,128)S(1)} collective-permute-done((f32[256,512]{1,0:T(8,128)S(1)}, f32[256,512]{1,0:T(8,128)S(1)}, u32[]{:S(2)}, u32[]{:S(2)}) %collective-permute-start.3) | collective-permute-done | bytes 524320 | tf_op jit(solution)/shard_map/ppermute | solution.py:156
  75.8 0.8 copy-done.6
  76.6 2.1 %shard_map.61 = f32[16,16,512]{2,1,0:T(8,128)} custom-call(f32[16,512]{1,0:T(8,128)} %add.40.rate_ref, f32[16,16,512]{2,1,0:T(8,128)} %bitcast.57, f32[16,16,512]{2,1,0:T(8,128)} %bitcast.58), custom_call_target="tpu_custom_call" | custom-call | flops 786432 | bytes 1572864 | tf_op jit(solution)/shard_map/pallas_call | solution.py:162
  78.8 5.7 %all-to-all-start.3 = ((f32[16,16,512]{2,1,0:T(8,128)}), f32[16,16,512]{2,1,0:T(8,128)S(1)}, u32[]{:S(2)}, u32[]{:S(2)}) async-start(f32[16,16,512]{2,1,0:T(8,128)} %shard_map.61), calls=%async_computation.3 | async-start | bytes 1048576 | tf_op jit(solution)/shard_map/all_to_all | solution.py:172
  84.5 1.6 %collective-permute-start.5 = (bf16[2,128,512]{2,1,0:T(8,128)(2,1)S(1)}, bf16[2,128,512]{2,1,0:T(8,128)(2,1)S(1)}, u32[]{:S(2)}, u32[]{:S(2)}) collective-permute-start(bf16[2,128,512]{2,1,0:T(8,128)(2,1)S(1)} %bitcast_convert_fusion.refs_0_), channel_id=1, source_target_pairs={{0,2},{1,3},{2,0},{3,1},{4,6},{5,7},{6,4},{7,5},{8,10},{9,11},{10,... | collective-permute-start | bytes 786440 | tf_op jit(solution)/shard_map/ppermute | solution.py:52
  86.1 4.8 %collective-permute-done.5.refs_1_ = bf16[2,128,512]{2,1,0:T(8,128)(2,1)S(1)} collective-permute-done((bf16[2,128,512]{2,1,0:T(8,128)(2,1)S(1)}, bf16[2,128,512]{2,1,0:T(8,128)(2,1)S(1)}, u32[]{:S(2)}, u32[]{:S(2)}) %collective-permute-start.5) | collective-permute-done | bytes 262176 | tf_op jit(solution)/shard_map/ppermute | solution.py:52
  91.5 4.7 %all-to-all-done.3 = f32[16,16,512]{2,1,0:T(8,128)S(1)} async-done(((f32[16,16,512]{2,1,0:T(8,128)}), f32[16,16,512]{2,1,0:T(8,128)S(1)}, u32[]{:S(2)}, u32[]{:S(2)}) %all-to-all-start.3) | async-done | bytes 524320 | tf_op jit(solution)/shard_map/all_to_all | solution.py:172
  96.3 1.6 %collective-permute-start.4 = (bf16[2,128,512]{2,1,0:T(8,128)(2,1)S(1)}, bf16[2,128,512]{2,1,0:T(8,128)(2,1)S(1)}, u32[]{:S(2)}, u32[]{:S(2)}) collective-permute-start(bf16[2,128,512]{2,1,0:T(8,128)(2,1)S(1)} %bitcast_convert_fusion.1.refs_0_), channel_id=1, source_target_pairs={{0,2},{1,3},{2,0},{3,1},{4,6},{5,7},{6,4},{7,5},{8,10},{9,11},{10,... | collective-permute-start | bytes 786440 | tf_op jit(solution)/shard_map/ppermute | solution.py:52
  97.9 0.7 copy-done.10
  98.6 3.9 %shard_map.62 = f32[2,512,128]{2,1,0:T(8,128)} custom-call(s32[1]{0:T(128)} %bitcast.10.me_ref, bf16[512,2048]{1,0:T(8,128)(2,1)} %l_ref.5, bf16[2,128,512]{2,1,0:T(8,128)(2,1)} %copy-done.4, bf16[2,128,512]{2,1,0:T(8,128)(2,1)} %copy-done.9, bf16[2,128,512]{2,1,0:T(8,128)(2,1)} %copy-done.10, bf16[2,128,512]{2,1,0:T(8,128)(2,1)} %collective-permute-done.7.refs_3_), custom_call_target="tpu_custom_call" | custom-call | flops 536870912 | bytes 3670016 | tf_op jit(solution)/shard_map/pallas_call | solution.py:177
  103.3 1.3 %copy.46 = f32[512,2,256]{2,1,0:T(2,128)} copy(f32[512,2,256]{0,2,1:T(8,128)S(1)} %pad_maximum_fusion) | data formatting | bytes 2097152
  105.3 3.9 %shard_map.63 = f32[2,512,128]{2,1,0:T(8,128)} custom-call(s32[1]{0:T(128)} %bitcast.10.me_ref, bf16[512,2048]{1,0:T(8,128)(2,1)} %l_ref.5, bf16[2,128,512]{2,1,0:T(8,128)(2,1)} %copy-done.3, bf16[2,128,512]{2,1,0:T(8,128)(2,1)} %copy-done.8, bf16[2,128,512]{2,1,0:T(8,128)(2,1)} %copy-done.11, bf16[2,128,512]{2,1,0:T(8,128)(2,1)} %collective-permute-done.9.refs_3_), custom_call_target="tpu_custom_call" | custom-call | flops 536870912 | bytes 3670016 | tf_op jit(solution)/shard_map/pallas_call | solution.py:177
  109.2 1.1 %bitcast_subtract_fusion.1 = (f32[512,2,128]{2,0,1:T(8,128)S(1)}, f32[512,2,128]{2,0,1:T(8,128)S(1)}) fusion(f32[2,512,128]{2,1,0:T(8,128)S(1)} %copy-done, bf16[512,2,256]{2,0,1:T(8,128)(2,1)S(1)} %bitcast.52, f32[2,512,128]{2,1,0:T(8,128)} %shard_map.63), kind=kLoop, calls=%fused_computation.12 | loop fusion | flops 524288 | bytes 2621440 | tf_op jit(solution)/shard_map/sub | solution.py:195
  110.4 1.8 %copy.47 = f32[512,2,256]{2,1,0:T(2,128)} copy(f32[512,2,256]{2,0,1:T(8,128)S(1)} %pad_maximum_fusion.1) | data formatting | bytes 2097152
  (54 shorter events, 4.8 us)
Async XLA Ops:
  5.3 23.1 %all-to-all-start = ((bf16[8,72,512]{2,1,0:T(8,128)(2,1)}), bf16[8,72,512]{2,1,0:T(8,128)(2,1)S(1)}, u32[]{:S(2)}, u32[]{:S(2)}) async-start(bf16[8,72,512]{2,1,0:T(8,128)(2,1)} %pad_maximum_fusion.2), calls=%async_computation | async-start | bytes 1179648 | tf_op jit(solution)/shard_map/all_to_all | solution.py:123
  28.4 0.8 copy-start.5
  34.0 5.3 %collective-permute-start = (f32[2,256,512]{2,1,0:T(8,128)}, f32[2,256,512]{2,1,0:T(8,128)}, u32[]{:S(2)}, u32[]{:S(2)}) collective-permute-start(f32[2,256,512]{2,1,0:T(8,128)} %get-tuple-element.21), channel_id=1, source_target_pairs={{0,1},{1,0},{2,3},{3,2},{4,5},{5,4},{6,7},{7,6},{8,9},{9,8},{10,11... | collective-permute-start | bytes 3145736 | tf_op jit(solution)/shard_map/ppermute | solution.py:38
  34.0 5.3 %copy-start.2 = (f32[2,256,512]{2,1,0:T(8,128)S(1)}, f32[2,256,512]{2,1,0:T(8,128)}, u32[]{:S(2)}) copy-start(f32[2,256,512]{2,1,0:T(8,128)} %get-tuple-element.20) | copy-start | bytes 3145732
  34.0 20.0 %collective-permute-start.2 = (f32[2,256,512]{2,1,0:T(8,128)}, f32[2,256,512]{2,1,0:T(8,128)S(1)}, u32[]{:S(2)}, u32[]{:S(2)}) collective-permute-start(f32[2,256,512]{2,1,0:T(8,128)} %get-tuple-element.23), channel_id=1, source_target_pairs={{0,1},{1,0},{2,3},{3,2},{4,5},{5,4},{6,7},{7,6},{8,9},{9,8},{10,11... | collective-permute-start | bytes 3145736 | tf_op jit(solution)/shard_map/ppermute | solution.py:38
  35.7 18.4 %all-to-all-start.1 = ((bf16[64,16,256]{2,0,1:T(8,128)(2,1)}), bf16[64,16,256]{2,0,1:T(8,128)(2,1)S(1)}, u32[]{:S(2)}, u32[]{:S(2)}) async-start(bf16[64,16,256]{2,0,1:T(8,128)(2,1)} %copy.42), calls=%async_computation.1 | async-start | bytes 1048576 | tf_op jit(solution)/shard_map/all_to_all | solution.py:130
  41.7 12.4 %copy-start.1 = (f32[2,256,512]{2,1,0:T(8,128)S(1)}, f32[2,256,512]{2,1,0:T(8,128)}, u32[]{:S(2)}) copy-start(f32[2,256,512]{2,1,0:T(8,128)} %get-tuple-element.22) | copy-start | bytes 3145732
  41.7 14.0 %collective-permute-start.1 = (f32[256,512]{1,0:T(8,128)}, f32[256,512]{1,0:T(8,128)}, u32[]{:S(2)}, u32[]{:S(2)}) collective-permute-start(f32[256,512]{1,0:T(8,128)} %get-tuple-element.44), channel_id=1, source_target_pairs={{0,2},{1,3},{2,0},{3,1},{4,6},{5,7},{6,4},{7,5},{8,10},{9,11},{10,... | collective-permute-start | bytes 1572872 | tf_op jit(solution)/shard_map/ppermute | solution.py:152
  55.8 7.8 %copy-start.7 = (f32[256,512]{1,0:T(8,128)S(1)}, f32[256,512]{1,0:T(8,128)}, u32[]{:S(2)}) copy-start(f32[256,512]{1,0:T(8,128)} %get-tuple-element.27) | copy-start | bytes 1572868
  58.0 20.8 %all-to-all-start.2 = ((f32[16,16,512]{2,1,0:T(8,128)}), f32[16,16,512]{2,1,0:T(8,128)S(1)}, u32[]{:S(2)}, u32[]{:S(2)}) async-start(f32[16,16,512]{2,1,0:T(8,128)} %shard_map.60), calls=%async_computation.2 | async-start | bytes 1048576 | tf_op jit(solution)/shard_map/all_to_all | solution.py:172
  63.6 12.2 %collective-permute-start.3 = (f32[256,512]{1,0:T(8,128)S(1)}, f32[256,512]{1,0:T(8,128)S(1)}, u32[]{:S(2)}, u32[]{:S(2)}) collective-permute-start(f32[256,512]{1,0:T(8,128)S(1)} %copy-done.7), channel_id=1, source_target_pairs={{0,2},{1,3},{2,0},{3,1},{4,6},{5,7},{6,4},{7,5},{8,10},{9,11},{10,... | collective-permute-start | bytes 1572872 | tf_op jit(solution)/shard_map/ppermute | solution.py:156
  75.8 0.8 copy-start.6
  78.8 17.4 %all-to-all-start.3 = ((f32[16,16,512]{2,1,0:T(8,128)}), f32[16,16,512]{2,1,0:T(8,128)S(1)}, u32[]{:S(2)}, u32[]{:S(2)}) async-start(f32[16,16,512]{2,1,0:T(8,128)} %shard_map.61), calls=%async_computation.3 | async-start | bytes 1048576 | tf_op jit(solution)/shard_map/all_to_all | solution.py:172
  84.5 13.4 %copy-start.4 = (bf16[2,128,512]{2,1,0:T(8,128)(2,1)}, bf16[2,128,512]{2,1,0:T(8,128)(2,1)S(1)}, u32[]{:S(2)}) copy-start(bf16[2,128,512]{2,1,0:T(8,128)(2,1)S(1)} %bitcast_convert_fusion.refs_0_) | copy-start | bytes 786436
  84.5 6.4 %collective-permute-start.5 = (bf16[2,128,512]{2,1,0:T(8,128)(2,1)S(1)}, bf16[2,128,512]{2,1,0:T(8,128)(2,1)S(1)}, u32[]{:S(2)}, u32[]{:S(2)}) collective-permute-start(bf16[2,128,512]{2,1,0:T(8,128)(2,1)S(1)} %bitcast_convert_fusion.refs_0_), channel_id=1, source_target_pairs={{0,2},{1,3},{2,0},{3,1},{4,6},{5,7},{6,4},{7,5},{8,10},{9,11},{10,... | collective-permute-start | bytes 786440 | tf_op jit(solution)/shard_map/ppermute | solution.py:52
  91.0 7.0 %copy-start.9 = (bf16[2,128,512]{2,1,0:T(8,128)(2,1)}, bf16[2,128,512]{2,1,0:T(8,128)(2,1)S(1)}, u32[]{:S(2)}) copy-start(bf16[2,128,512]{2,1,0:T(8,128)(2,1)S(1)} %collective-permute-done.5.refs_1_) | copy-start | bytes 786436
  91.0 6.9 %collective-permute-start.6 = (bf16[2,128,512]{2,1,0:T(8,128)(2,1)S(1)}, bf16[2,128,512]{2,1,0:T(8,128)(2,1)S(1)}, u32[]{:S(2)}, u32[]{:S(2)}) collective-permute-start(bf16[2,128,512]{2,1,0:T(8,128)(2,1)S(1)} %bitcast_convert_fusion.refs_0_), channel_id=1, source_target_pairs={{0,1},{1,0},{2,3},{3,2},{4,5},{5,4},{6,7},{7,6},{8,9},{9,8},{10,11... | collective-permute-start | bytes 786440 | tf_op jit(solution)/shard_map/ppermute | solution.py:52
  91.0 6.9 %collective-permute-start.7 = (bf16[2,128,512]{2,1,0:T(8,128)(2,1)S(1)}, bf16[2,128,512]{2,1,0:T(8,128)(2,1)}, u32[]{:S(2)}, u32[]{:S(2)}) collective-permute-start(bf16[2,128,512]{2,1,0:T(8,128)(2,1)S(1)} %collective-permute-done.5.refs_1_), channel_id=1, source_target_pairs={{0,1},{1,0},{2,3},{3,2},{4,5},{5,4},{6,7},{7,6},{8,9},{9,8},{10,11... | collective-permute-start | bytes 786440 | tf_op jit(solution)/shard_map/ppermute | solution.py:52
  96.3 6.5 %copy-start.3 = (bf16[2,128,512]{2,1,0:T(8,128)(2,1)}, bf16[2,128,512]{2,1,0:T(8,128)(2,1)S(1)}, u32[]{:S(2)}) copy-start(bf16[2,128,512]{2,1,0:T(8,128)(2,1)S(1)} %bitcast_convert_fusion.1.refs_0_) | copy-start | bytes 786436
  96.3 6.4 %collective-permute-start.4 = (bf16[2,128,512]{2,1,0:T(8,128)(2,1)S(1)}, bf16[2,128,512]{2,1,0:T(8,128)(2,1)S(1)}, u32[]{:S(2)}, u32[]{:S(2)}) collective-permute-start(bf16[2,128,512]{2,1,0:T(8,128)(2,1)S(1)} %bitcast_convert_fusion.1.refs_0_), channel_id=1, source_target_pairs={{0,2},{1,3},{2,0},{3,1},{4,6},{5,7},{6,4},{7,5},{8,10},{9,11},{10,... | collective-permute-start | bytes 786440 | tf_op jit(solution)/shard_map/ppermute | solution.py:52
  97.9 0.7 copy-start.10
  102.7 1.9 %copy-start.8 = (bf16[2,128,512]{2,1,0:T(8,128)(2,1)}, bf16[2,128,512]{2,1,0:T(8,128)(2,1)S(1)}, u32[]{:S(2)}) copy-start(bf16[2,128,512]{2,1,0:T(8,128)(2,1)S(1)} %collective-permute-done.4.refs_1_) | copy-start | bytes 786436
  102.7 1.9 %collective-permute-start.8 = (bf16[2,128,512]{2,1,0:T(8,128)(2,1)S(1)}, bf16[2,128,512]{2,1,0:T(8,128)(2,1)S(1)}, u32[]{:S(2)}, u32[]{:S(2)}) collective-permute-start(bf16[2,128,512]{2,1,0:T(8,128)(2,1)S(1)} %bitcast_convert_fusion.1.refs_0_), channel_id=1, source_target_pairs={{0,1},{1,0},{2,3},{3,2},{4,5},{5,4},{6,7},{7,6},{8,9},{9,8},{10,11... | collective-permute-start | bytes 786440 | tf_op jit(solution)/shard_map/ppermute | solution.py:52
  102.7 2.0 %collective-permute-start.9 = (bf16[2,128,512]{2,1,0:T(8,128)(2,1)S(1)}, bf16[2,128,512]{2,1,0:T(8,128)(2,1)}, u32[]{:S(2)}, u32[]{:S(2)}) collective-permute-start(bf16[2,128,512]{2,1,0:T(8,128)(2,1)S(1)} %collective-permute-done.4.refs_1_), channel_id=1, source_target_pairs={{0,1},{1,0},{2,3},{3,2},{4,5},{5,4},{6,7},{7,6},{8,9},{9,8},{10,11... | collective-permute-start | bytes 786440 | tf_op jit(solution)/shard_map/ppermute | solution.py:52
  104.6 4.6 %copy-start = (f32[2,512,128]{2,1,0:T(8,128)S(1)}, f32[2,512,128]{2,1,0:T(8,128)}, u32[]{:S(2)}) copy-start(f32[2,512,128]{2,1,0:T(8,128)} %shard_map.62) | copy-start | bytes 1572868
  104.6 0.7 copy-start.11

commit v24 on v20

--- a/solution.py
+++ b/solution.py
@@ -56,10 +56,11 @@
 
 
 def fitted_kernel(me_ref, l_ref, *refs):
-    *piece_refs, observed_ref, out_ref = refs
+    *piece_refs, out_ref = refs
     me = me_ref[0]
     levels = len(piece_refs).bit_length() - 1
-    hours, members, width = piece_refs[0].shape
+    width = piece_refs[0].shape[-1]
+    hours, members, _ = piece_refs[0].shape
     total = None
     for position, piece_ref in enumerate(piece_refs):
         flipped = 0
@@ -74,8 +75,7 @@
         )
         total = part if total is None else total + part
     for hour in range(hours):
-        observed = observed_ref[hour].astype(jnp.float32)
-        out_ref[hour] = observed - total[:, hour * members:(hour + 1) * members]
+        out_ref[hour] = total[:, hour * members:(hour + 1) * members]
 
 
 def recurrence_kernel(rate_ref, keep_ref, received_ref, out_ref):
@@ -118,7 +118,7 @@
     middle = lax.reduce_precision(decay - high, exponent_bits=8, mantissa_bits=7)
     low = decay - high - middle
     pieces = jnp.stack([high, middle, low]).astype(obs.dtype).reshape(-1, hours * members_here)
-    spare = (-(stations_local + pieces.shape[0])) % 16
+    spare = (-(stations_local + pieces.shape[0])) % 8
     pieces = jnp.pad(pieces, ((0, spare), (0, 0)))
     pieces = jnp.broadcast_to(pieces[None], (tm_count,) + pieces.shape)
     outgoing = jnp.concatenate([outgoing, pieces], axis=1)
@@ -176,12 +176,10 @@
         pieces, earlier = doubling_gather(rounded, "state", fitted_parts[-1:])
         fitted_parts[-1:] = earlier
         slab_hours, width, _ = rounded.shape
-        low = chunk * members // CHUNKS
-        observed = jnp.transpose(by_hour[:, :, low:low + members // CHUNKS], (1, 0, 2))
         fitted = vmem_call(
             fitted_kernel,
             jax.ShapeDtypeStruct((slab_hours, stations_here, width), jnp.float32),
-            2 + len(pieces),
+            1 + len(pieces),
             pl.CostEstimate(
                 flops=2 * stations_here * slab_hours * width * all_comps,
                 bytes_accessed=2 * stations_here * all_comps
@@ -190,11 +188,13 @@
                 transcendentals=0,
             ),
             scalars=1,
-        )(lax.axis_index("state").reshape(1).astype(jnp.int32), loadings, *pieces, observed)
+        )(lax.axis_index("state").reshape(1).astype(jnp.int32), loadings, *pieces)
         fitted_parts.append(fitted)
         smoothed_parts.append(jnp.transpose(gathered, (2, 0, 1)))
-    for residual in fitted_parts:
-        residual_parts.append(jnp.transpose(residual, (1, 0, 2)))
+    for chunk, fitted in enumerate(fitted_parts):
+        low = chunk * members // CHUNKS
+        picked = by_hour[:, :, low:low + members // CHUNKS]
+        residual_parts.append(picked.astype(jnp.float32) - jnp.transpose(fitted, (1, 0, 2)))
     return (
         jnp.concatenate(smoothed_parts, axis=2),
         jnp.concatenate(residual_parts, axis=2),

time: 116 us -> 112 us (0.966)
  waiting for transfers between devices: 50.5 us -> 46.7 us
  local copies, waits for them, and re-layouts: 12.1 us -> 10.2 us
  starting transfers between devices: 28.2 us -> 30 us
    all_to_all x2, starting transfers between devices: 9.48 us -> 11.3 us  [local(): lax.all_to_all(smoothed_here, 'tm', split_axis=0, concat_axis=1, tiled=True)]
    all_to_all x1, waiting for transfers between devices: 17.3 us -> 15.9 us  [local(): lax.all_to_all(outgoing, 'tm', split_axis=0, concat_axis=0, tiled=True)]
    ppermute x1, waiting for transfers between devices: 11.9 us -> 10.6 us  [local(): lax.ppermute(o, 'state', last[c + 1][2])]
    all_to_all x2, waiting for transfers between devices: 6 us -> 4.73 us  [local(): lax.all_to_all(smoothed_here, 'tm', split_axis=0, concat_axis=1, tiled=True)]
    all_to_all x1, waiting for transfers between devices: 10.4 us -> 9.16 us  [local(): lax.all_to_all(masked_later, 'tm', split_axis=1, concat_axis=0, tiled=True)]
    unnamed x29 -> x27, local copies, waits for them, and re-layouts: 8.74 us -> 7.63 us
  transfers between devices with their start and end apart: 14 -> 14, of which waited for: 5 -> 8; matrix products, arithmetic and copies ran while one was open for 7% -> 7% of each run, Pallas kernels for 5% -> 5%
where the time goes in v24:
time: 112 us
  waiting for transfers between devices  46.7 us (42%)
  starting transfers between devices  30 us (27%)
  Pallas kernels  15.8 us (14%)
  local copies, waits for them, and re-layouts  10.2 us (9%)
  other arithmetic  8.1 us (7%)
    all_to_all x1, waiting for transfers between devices, local(): lax.all_to_all(outgoing, 'tm', split_axis=0, concat_axis=0, tiled=True)  15.9 us
    all_to_all x2, starting transfers between devices, local(): lax.all_to_all(smoothed_here, 'tm', split_axis=0, concat_axis=1, tiled=True)  11.3 us
    ppermute x1, waiting for transfers between devices, local(): lax.ppermute(o, 'state', last[c + 1][2])  10.6 us
    all_to_all x1, waiting for transfers between devices, local(): lax.all_to_all(masked_later, 'tm', split_axis=1, concat_axis=0, tiled=True)  9.16 us
    unnamed x27, local copies, waits for them, and re-layouts  7.63 us
    all_to_all x1, starting transfers between devices, local(): lax.all_to_all(outgoing, 'tm', split_axis=0, concat_axis=0, tiled=True)  7.25 us
    pallas_call x2, Pallas kernels, local(): vmem_call(fitted_kernel, jax.ShapeDtypeStruct((slab_hours, stations_here,...  6.71 us
    ppermute x6, waiting for transfers between devices, doubling_gather(): pieces = pieces + [lax.ppermute(piece, axis, pairs) for piece in pieces]  5.78 us
  transfers between devices with their start and end apart: 14, of which 8 were waited for; matrix products, arithmetic and copies ran while one was open for 7% of the time, Pallas kernels for 5%

profile of v24, /device:TPU:0, one launch (start us, length us, event | category | flops | bytes accessed | tf_op | source)
XLA Modules:
  0.0 111.7 jit_solution(1567331763907951796)
XLA Ops:
  0.6 0.7 convert_element_type.29
  1.3 0.7 fusion.5
  2.1 1.7 %copy.37 = bf16[64,16,256]{0,2,1:T(8,128)(2,1)S(1)} copy(bf16[64,16,256]{2,1,0:T(8,128)(2,1)} %param.4) | data formatting | bytes 1048576 | tf_op args[0]
  4.4 0.9 pad_maximum_fusion.2
  5.3 7.3 %all-to-all-start = ((bf16[8,72,512]{2,1,0:T(8,128)(2,1)}), bf16[8,72,512]{2,1,0:T(8,128)(2,1)S(1)}, u32[]{:S(2)}, u32[]{:S(2)}) async-start(bf16[8,72,512]{2,1,0:T(8,128)(2,1)} %pad_maximum_fusion.2), calls=%async_computation | async-start | bytes 1179648 | tf_op jit(solution)/shard_map/all_to_all | solution.py:125
  12.5 15.9 %all-to-all-done.x_ref = bf16[8,72,512]{2,1,0:T(8,128)(2,1)S(1)} async-done(((bf16[8,72,512]{2,1,0:T(8,128)(2,1)}), bf16[8,72,512]{2,1,0:T(8,128)(2,1)S(1)}, u32[]{:S(2)}, u32[]{:S(2)}) %all-to-all-start) | async-done | bytes 589856 | tf_op jit(solution)/shard_map/all_to_all | solution.py:125
  28.4 0.8 copy-done.5
  29.2 4.8 %shard_map.59 = (f32[2,256,512]{2,1,0:T(8,128)}, f32[2,256,512]{2,1,0:T(8,128)}, f32[2,256,512]{2,1,0:T(8,128)}, f32[2,256,512]{2,1,0:T(8,128)}) custom-call(s32[1]{0:T(128)} %bitcast.10.me_ref, bf16[8,72,512]{2,1,0:T(8,128)(2,1)} %copy-done.5, bf16[512,2048]{1,0:T(8,128)(2,1)} %l_ref.5), custom_call_target="tpu_custom_call" | custom-call | flops 1073741824 | bytes 6815744 | tf_op jit(solution)/shard_map/pallas_call | solution.py:137
  34.6 1.1 %copy.42 = bf16[64,16,256]{2,0,1:T(8,128)(2,1)} copy(bf16[64,16,256]{0,2,1:T(8,128)(2,1)S(1)} %broadcast_multiply_fusion) | data formatting | bytes 1048576 | tf_op jit(solution)/shard_map/optimization_barrier | solution.py:131
  35.7 3.6 %all-to-all-start.1 = ((bf16[64,16,256]{2,0,1:T(8,128)(2,1)}), bf16[64,16,256]{2,0,1:T(8,128)(2,1)S(1)}, u32[]{:S(2)}, u32[]{:S(2)}) async-start(bf16[64,16,256]{2,0,1:T(8,128)(2,1)} %copy.42), calls=%async_computation.1 | async-start | bytes 1048576 | tf_op jit(solution)/shard_map/all_to_all | solution.py:132
  39.3 2.4 %fusion.2 = (f32[256,512]{1,0:T(8,128)}, f32[256,512]{1,0:T(8,128)}) fusion(f32[2,256,512]{2,1,0:T(8,128)} %collective-permute-done, f32[2,256,512]{2,1,0:T(8,128)S(1)} %copy-done.2), kind=kLoop, calls=%fused_computation.8 | loop fusion | flops 262144 | bytes 3145728 | tf_op jit(solution)/shard_map/add | solution.py:40
  41.7 1.5 %collective-permute-start.1 = (f32[256,512]{1,0:T(8,128)}, f32[256,512]{1,0:T(8,128)}, u32[]{:S(2)}, u32[]{:S(2)}) collective-permute-start(f32[256,512]{1,0:T(8,128)} %get-tuple-element.44), channel_id=1, source_target_pairs={{0,2},{1,3},{2,0},{3,1},{4,6},{5,7},{6,4},{7,5},{8,10},{9,11},{10,... | collective-permute-start | bytes 1572872 | tf_op jit(solution)/shard_map/ppermute | solution.py:154
  43.3 0.8 slice_convert_fusion
  44.9 9.2 %all-to-all-done.1 = bf16[64,16,256]{2,0,1:T(8,128)(2,1)S(1)} async-done(((bf16[64,16,256]{2,0,1:T(8,128)(2,1)}), bf16[64,16,256]{2,0,1:T(8,128)(2,1)S(1)}, u32[]{:S(2)}, u32[]{:S(2)}) %all-to-all-start.1) | async-done | bytes 524320 | tf_op jit(solution)/shard_map/all_to_all | solution.py:132
  54.1 1.2 %fusion = (f32[256,512]{1,0:T(8,128)}, f32[256,512]{1,0:T(8,128)}) fusion(f32[2,256,512]{2,1,0:T(8,128)S(1)} %collective-permute-done.2, f32[2,256,512]{2,1,0:T(8,128)S(1)} %copy-done.1), kind=kLoop, calls=%fused_computation.4 | loop fusion | flops 262144 | bytes 3145728 | tf_op jit(solution)/shard_map/add | solution.py:40
  55.8 2.2 %shard_map.60 = f32[16,16,512]{2,1,0:T(8,128)} custom-call(f32[16,512]{1,0:T(8,128)} %add.40.rate_ref, f32[16,16,512]{2,1,0:T(8,128)} %bitcast.53, f32[16,16,512]{2,1,0:T(8,128)} %bitcast.16.received_ref), custom_call_target="tpu_custom_call" | custom-call | flops 786432 | bytes 1572864 | tf_op jit(solution)/shard_map/pallas_call | solution.py:164
  58.0 5.6 %all-to-all-start.2 = ((f32[16,16,512]{2,1,0:T(8,128)}), f32[16,16,512]{2,1,0:T(8,128)S(1)}, u32[]{:S(2)}, u32[]{:S(2)}) async-start(f32[16,16,512]{2,1,0:T(8,128)} %shard_map.60), calls=%async_computation.2 | async-start | bytes 1048576 | tf_op jit(solution)/shard_map/all_to_all | solution.py:174
  63.6 1.6 %collective-permute-start.3 = (f32[256,512]{1,0:T(8,128)S(1)}, f32[256,512]{1,0:T(8,128)S(1)}, u32[]{:S(2)}, u32[]{:S(2)}) collective-permute-start(f32[256,512]{1,0:T(8,128)S(1)} %copy-done.7), channel_id=1, source_target_pairs={{0,2},{1,3},{2,0},{3,1},{4,6},{5,7},{6,4},{7,5},{8,10},{9,11},{10,... | collective-permute-start | bytes 1572872 | tf_op jit(solution)/shard_map/ppermute | solution.py:158
  65.2 10.6 %collective-permute-done.3 = f32[256,512]{1,0:T(8,128)S(1)} collective-permute-done((f32[256,512]{1,0:T(8,128)S(1)}, f32[256,512]{1,0:T(8,128)S(1)}, u32[]{:S(2)}, u32[]{:S(2)}) %collective-permute-start.3) | collective-permute-done | bytes 524320 | tf_op jit(solution)/shard_map/ppermute | solution.py:158
  75.8 0.8 copy-done.6
  76.6 2.1 %shard_map.61 = f32[16,16,512]{2,1,0:T(8,128)} custom-call(f32[16,512]{1,0:T(8,128)} %add.40.rate_ref, f32[16,16,512]{2,1,0:T(8,128)} %bitcast.57, f32[16,16,512]{2,1,0:T(8,128)} %bitcast.58), custom_call_target="tpu_custom_call" | custom-call | flops 786432 | bytes 1572864 | tf_op jit(solution)/shard_map/pallas_call | solution.py:164
  78.8 5.7 %all-to-all-start.3 = ((f32[16,16,512]{2,1,0:T(8,128)}), f32[16,16,512]{2,1,0:T(8,128)S(1)}, u32[]{:S(2)}, u32[]{:S(2)}) async-start(f32[16,16,512]{2,1,0:T(8,128)} %shard_map.61), calls=%async_computation.3 | async-start | bytes 1048576 | tf_op jit(solution)/shard_map/all_to_all | solution.py:174
  84.5 1.6 %collective-permute-start.5 = (bf16[2,128,512]{2,1,0:T(8,128)(2,1)S(1)}, bf16[2,128,512]{2,1,0:T(8,128)(2,1)S(1)}, u32[]{:S(2)}, u32[]{:S(2)}) collective-permute-start(bf16[2,128,512]{2,1,0:T(8,128)(2,1)S(1)} %bitcast_convert_fusion.refs_0_), channel_id=1, source_target_pairs={{0,2},{1,3},{2,0},{3,1},{4,6},{5,7},{6,4},{7,5},{8,10},{9,11},{10,... | collective-permute-start | bytes 786440 | tf_op jit(solution)/shard_map/ppermute | solution.py:52
  86.1 4.8 %collective-permute-done.5.refs_1_ = bf16[2,128,512]{2,1,0:T(8,128)(2,1)S(1)} collective-permute-done((bf16[2,128,512]{2,1,0:T(8,128)(2,1)S(1)}, bf16[2,128,512]{2,1,0:T(8,128)(2,1)S(1)}, u32[]{:S(2)}, u32[]{:S(2)}) %collective-permute-start.5) | collective-permute-done | bytes 262176 | tf_op jit(solution)/shard_map/ppermute | solution.py:52
  91.5 4.7 %all-to-all-done.3 = f32[16,16,512]{2,1,0:T(8,128)S(1)} async-done(((f32[16,16,512]{2,1,0:T(8,128)}), f32[16,16,512]{2,1,0:T(8,128)S(1)}, u32[]{:S(2)}, u32[]{:S(2)}) %all-to-all-start.3) | async-done | bytes 524320 | tf_op jit(solution)/shard_map/all_to_all | solution.py:174
  96.3 1.6 %collective-permute-start.4 = (bf16[2,128,512]{2,1,0:T(8,128)(2,1)S(1)}, bf16[2,128,512]{2,1,0:T(8,128)(2,1)S(1)}, u32[]{:S(2)}, u32[]{:S(2)}) collective-permute-start(bf16[2,128,512]{2,1,0:T(8,128)(2,1)S(1)} %bitcast_convert_fusion.1.refs_0_), channel_id=1, source_target_pairs={{0,2},{1,3},{2,0},{3,1},{4,6},{5,7},{6,4},{7,5},{8,10},{9,11},{10,... | collective-permute-start | bytes 786440 | tf_op jit(solution)/shard_map/ppermute | solution.py:52
  98.6 3.4 %shard_map.62 = f32[2,512,128]{2,1,0:T(8,128)} custom-call(s32[1]{0:T(128)} %bitcast.10.me_ref, bf16[512,2048]{1,0:T(8,128)(2,1)} %l_ref.5, bf16[2,128,512]{2,1,0:T(8,128)(2,1)} %copy-done.4, bf16[2,128,512]{2,1,0:T(8,128)(2,1)} %copy-done.9, bf16[2,128,512]{2,1,0:T(8,128)(2,1)} %copy-done.10, bf16[2,128,512]{2,1,0:T(8,128)(2,1)} %collective-permute-done.7.refs_3_), custom_call_target="tpu_custom_call" | custom-call | flops 536870912 | bytes 3670016 | tf_op jit(solution)/shard_map/pallas_call | solution.py:179
  101.9 0.8 collective-permute-done.4.refs_1_
  103.3 1.3 %copy.46 = f32[512,2,256]{2,1,0:T(2,128)} copy(f32[512,2,256]{0,2,1:T(8,128)S(1)} %pad_maximum_fusion) | data formatting | bytes 2097152
  105.3 3.4 %shard_map.63 = f32[2,512,128]{2,1,0:T(8,128)} custom-call(s32[1]{0:T(128)} %bitcast.10.me_ref, bf16[512,2048]{1,0:T(8,128)(2,1)} %l_ref.5, bf16[2,128,512]{2,1,0:T(8,128)(2,1)} %copy-done.3, bf16[2,128,512]{2,1,0:T(8,128)(2,1)} %copy-done.8, bf16[2,128,512]{2,1,0:T(8,128)(2,1)} %copy-done.11, bf16[2,128,512]{2,1,0:T(8,128)(2,1)} %collective-permute-done.9.refs_3_), custom_call_target="tpu_custom_call" | custom-call | flops 536870912 | bytes 3670016 | tf_op jit(solution)/shard_map/pallas_call | solution.py:179
  108.7 1.1 %bitcast_subtract_fusion.1 = (f32[512,2,128]{2,0,1:T(8,128)S(1)}, f32[512,2,128]{2,0,1:T(8,128)S(1)}) fusion(f32[2,512,128]{2,1,0:T(8,128)S(1)} %copy-done, bf16[512,2,256]{2,0,1:T(8,128)(2,1)S(1)} %bitcast.52, f32[2,512,128]{2,1,0:T(8,128)} %shard_map.63), kind=kLoop, calls=%fused_computation.12 | loop fusion | flops 524288 | bytes 2621440 | tf_op jit(solution)/shard_map/sub | solution.py:197
  109.9 1.8 %copy.47 = f32[512,2,256]{2,1,0:T(2,128)} copy(f32[512,2,256]{2,0,1:T(8,128)S(1)} %pad_maximum_fusion.1) | data formatting | bytes 2097152
  (54 shorter events, 5.1 us)
Async XLA Ops:
  5.3 23.1 %all-to-all-start = ((bf16[8,72,512]{2,1,0:T(8,128)(2,1)}), bf16[8,72,512]{2,1,0:T(8,128)(2,1)S(1)}, u32[]{:S(2)}, u32[]{:S(2)}) async-start(bf16[8,72,512]{2,1,0:T(8,128)(2,1)} %pad_maximum_fusion.2), calls=%async_computation | async-start | bytes 1179648 | tf_op jit(solution)/shard_map/all_to_all | solution.py:125
  28.4 0.8 copy-start.5
  34.0 5.3 %collective-permute-start = (f32[2,256,512]{2,1,0:T(8,128)}, f32[2,256,512]{2,1,0:T(8,128)}, u32[]{:S(2)}, u32[]{:S(2)}) collective-permute-start(f32[2,256,512]{2,1,0:T(8,128)} %get-tuple-element.21), channel_id=1, source_target_pairs={{0,1},{1,0},{2,3},{3,2},{4,5},{5,4},{6,7},{7,6},{8,9},{9,8},{10,11... | collective-permute-start | bytes 3145736 | tf_op jit(solution)/shard_map/ppermute | solution.py:38
  34.0 5.3 %copy-start.2 = (f32[2,256,512]{2,1,0:T(8,128)S(1)}, f32[2,256,512]{2,1,0:T(8,128)}, u32[]{:S(2)}) copy-start(f32[2,256,512]{2,1,0:T(8,128)} %get-tuple-element.20) | copy-start | bytes 3145732
  34.0 20.0 %collective-permute-start.2 = (f32[2,256,512]{2,1,0:T(8,128)}, f32[2,256,512]{2,1,0:T(8,128)S(1)}, u32[]{:S(2)}, u32[]{:S(2)}) collective-permute-start(f32[2,256,512]{2,1,0:T(8,128)} %get-tuple-element.23), channel_id=1, source_target_pairs={{0,1},{1,0},{2,3},{3,2},{4,5},{5,4},{6,7},{7,6},{8,9},{9,8},{10,11... | collective-permute-start | bytes 3145736 | tf_op jit(solution)/shard_map/ppermute | solution.py:38
  35.7 18.4 %all-to-all-start.1 = ((bf16[64,16,256]{2,0,1:T(8,128)(2,1)}), bf16[64,16,256]{2,0,1:T(8,128)(2,1)S(1)}, u32[]{:S(2)}, u32[]{:S(2)}) async-start(bf16[64,16,256]{2,0,1:T(8,128)(2,1)} %copy.42), calls=%async_computation.1 | async-start | bytes 1048576 | tf_op jit(solution)/shard_map/all_to_all | solution.py:132
  41.7 12.4 %copy-start.1 = (f32[2,256,512]{2,1,0:T(8,128)S(1)}, f32[2,256,512]{2,1,0:T(8,128)}, u32[]{:S(2)}) copy-start(f32[2,256,512]{2,1,0:T(8,128)} %get-tuple-element.22) | copy-start | bytes 3145732
  41.7 14.0 %collective-permute-start.1 = (f32[256,512]{1,0:T(8,128)}, f32[256,512]{1,0:T(8,128)}, u32[]{:S(2)}, u32[]{:S(2)}) collective-permute-start(f32[256,512]{1,0:T(8,128)} %get-tuple-element.44), channel_id=1, source_target_pairs={{0,2},{1,3},{2,0},{3,1},{4,6},{5,7},{6,4},{7,5},{8,10},{9,11},{10,... | collective-permute-start | bytes 1572872 | tf_op jit(solution)/shard_map/ppermute | solution.py:154
  55.8 7.8 %copy-start.7 = (f32[256,512]{1,0:T(8,128)S(1)}, f32[256,512]{1,0:T(8,128)}, u32[]{:S(2)}) copy-start(f32[256,512]{1,0:T(8,128)} %get-tuple-element.27) | copy-start | bytes 1572868
  58.0 20.8 %all-to-all-start.2 = ((f32[16,16,512]{2,1,0:T(8,128)}), f32[16,16,512]{2,1,0:T(8,128)S(1)}, u32[]{:S(2)}, u32[]{:S(2)}) async-start(f32[16,16,512]{2,1,0:T(8,128)} %shard_map.60), calls=%async_computation.2 | async-start | bytes 1048576 | tf_op jit(solution)/shard_map/all_to_all | solution.py:174
  63.6 12.2 %collective-permute-start.3 = (f32[256,512]{1,0:T(8,128)S(1)}, f32[256,512]{1,0:T(8,128)S(1)}, u32[]{:S(2)}, u32[]{:S(2)}) collective-permute-start(f32[256,512]{1,0:T(8,128)S(1)} %copy-done.7), channel_id=1, source_target_pairs={{0,2},{1,3},{2,0},{3,1},{4,6},{5,7},{6,4},{7,5},{8,10},{9,11},{10,... | collective-permute-start | bytes 1572872 | tf_op jit(solution)/shard_map/ppermute | solution.py:158
  75.8 0.8 copy-start.6
  78.8 17.4 %all-to-all-start.3 = ((f32[16,16,512]{2,1,0:T(8,128)}), f32[16,16,512]{2,1,0:T(8,128)S(1)}, u32[]{:S(2)}, u32[]{:S(2)}) async-start(f32[16,16,512]{2,1,0:T(8,128)} %shard_map.61), calls=%async_computation.3 | async-start | bytes 1048576 | tf_op jit(solution)/shard_map/all_to_all | solution.py:174
  84.5 13.4 %copy-start.4 = (bf16[2,128,512]{2,1,0:T(8,128)(2,1)}, bf16[2,128,512]{2,1,0:T(8,128)(2,1)S(1)}, u32[]{:S(2)}) copy-start(bf16[2,128,512]{2,1,0:T(8,128)(2,1)S(1)} %bitcast_convert_fusion.refs_0_) | copy-start | bytes 786436
  84.5 6.4 %collective-permute-start.5 = (bf16[2,128,512]{2,1,0:T(8,128)(2,1)S(1)}, bf16[2,128,512]{2,1,0:T(8,128)(2,1)S(1)}, u32[]{:S(2)}, u32[]{:S(2)}) collective-permute-start(bf16[2,128,512]{2,1,0:T(8,128)(2,1)S(1)} %bitcast_convert_fusion.refs_0_), channel_id=1, source_target_pairs={{0,2},{1,3},{2,0},{3,1},{4,6},{5,7},{6,4},{7,5},{8,10},{9,11},{10,... | collective-permute-start | bytes 786440 | tf_op jit(solution)/shard_map/ppermute | solution.py:52
  91.0 7.0 %copy-start.9 = (bf16[2,128,512]{2,1,0:T(8,128)(2,1)}, bf16[2,128,512]{2,1,0:T(8,128)(2,1)S(1)}, u32[]{:S(2)}) copy-start(bf16[2,128,512]{2,1,0:T(8,128)(2,1)S(1)} %collective-permute-done.5.refs_1_) | copy-start | bytes 786436
  91.0 6.9 %collective-permute-start.6 = (bf16[2,128,512]{2,1,0:T(8,128)(2,1)S(1)}, bf16[2,128,512]{2,1,0:T(8,128)(2,1)S(1)}, u32[]{:S(2)}, u32[]{:S(2)}) collective-permute-start(bf16[2,128,512]{2,1,0:T(8,128)(2,1)S(1)} %bitcast_convert_fusion.refs_0_), channel_id=1, source_target_pairs={{0,1},{1,0},{2,3},{3,2},{4,5},{5,4},{6,7},{7,6},{8,9},{9,8},{10,11... | collective-permute-start | bytes 786440 | tf_op jit(solution)/shard_map/ppermute | solution.py:52
  91.0 6.9 %collective-permute-start.7 = (bf16[2,128,512]{2,1,0:T(8,128)(2,1)S(1)}, bf16[2,128,512]{2,1,0:T(8,128)(2,1)}, u32[]{:S(2)}, u32[]{:S(2)}) collective-permute-start(bf16[2,128,512]{2,1,0:T(8,128)(2,1)S(1)} %collective-permute-done.5.refs_1_), channel_id=1, source_target_pairs={{0,1},{1,0},{2,3},{3,2},{4,5},{5,4},{6,7},{7,6},{8,9},{9,8},{10,11... | collective-permute-start | bytes 786440 | tf_op jit(solution)/shard_map/ppermute | solution.py:52
  96.3 6.5 %copy-start.3 = (bf16[2,128,512]{2,1,0:T(8,128)(2,1)}, bf16[2,128,512]{2,1,0:T(8,128)(2,1)S(1)}, u32[]{:S(2)}) copy-start(bf16[2,128,512]{2,1,0:T(8,128)(2,1)S(1)} %bitcast_convert_fusion.1.refs_0_) | copy-start | bytes 786436
  96.3 6.4 %collective-permute-start.4 = (bf16[2,128,512]{2,1,0:T(8,128)(2,1)S(1)}, bf16[2,128,512]{2,1,0:T(8,128)(2,1)S(1)}, u32[]{:S(2)}, u32[]{:S(2)}) collective-permute-start(bf16[2,128,512]{2,1,0:T(8,128)(2,1)S(1)} %bitcast_convert_fusion.1.refs_0_), channel_id=1, source_target_pairs={{0,2},{1,3},{2,0},{3,1},{4,6},{5,7},{6,4},{7,5},{8,10},{9,11},{10,... | collective-permute-start | bytes 786440 | tf_op jit(solution)/shard_map/ppermute | solution.py:52
  97.9 0.7 copy-start.10
  102.7 1.9 %copy-start.8 = (bf16[2,128,512]{2,1,0:T(8,128)(2,1)}, bf16[2,128,512]{2,1,0:T(8,128)(2,1)S(1)}, u32[]{:S(2)}) copy-start(bf16[2,128,512]{2,1,0:T(8,128)(2,1)S(1)} %collective-permute-done.4.refs_1_) | copy-start | bytes 786436
  102.7 1.9 %collective-permute-start.8 = (bf16[2,128,512]{2,1,0:T(8,128)(2,1)S(1)}, bf16[2,128,512]{2,1,0:T(8,128)(2,1)S(1)}, u32[]{:S(2)}, u32[]{:S(2)}) collective-permute-start(bf16[2,128,512]{2,1,0:T(8,128)(2,1)S(1)} %bitcast_convert_fusion.1.refs_0_), channel_id=1, source_target_pairs={{0,1},{1,0},{2,3},{3,2},{4,5},{5,4},{6,7},{7,6},{8,9},{9,8},{10,11... | collective-permute-start | bytes 786440 | tf_op jit(solution)/shard_map/ppermute | solution.py:52
  102.7 2.0 %collective-permute-start.9 = (bf16[2,128,512]{2,1,0:T(8,128)(2,1)S(1)}, bf16[2,128,512]{2,1,0:T(8,128)(2,1)}, u32[]{:S(2)}, u32[]{:S(2)}) collective-permute-start(bf16[2,128,512]{2,1,0:T(8,128)(2,1)S(1)} %collective-permute-done.4.refs_1_), channel_id=1, source_target_pairs={{0,1},{1,0},{2,3},{3,2},{4,5},{5,4},{6,7},{7,6},{8,9},{9,8},{10,11... | collective-permute-start | bytes 786440 | tf_op jit(solution)/shard_map/ppermute | solution.py:52
  104.6 4.1 %copy-start = (f32[2,512,128]{2,1,0:T(8,128)S(1)}, f32[2,512,128]{2,1,0:T(8,128)}, u32[]{:S(2)}) copy-start(f32[2,512,128]{2,1,0:T(8,128)} %shard_map.62) | copy-start | bytes 1572868
  104.6 0.7 copy-start.11

commit v25 on v24

--- a/solution.py
+++ b/solution.py
@@ -34,13 +34,19 @@
     count = lax.axis_size(axis)
     level = 0
     pairs = [(i, i ^ 1) for i in range(count)]
+    parts = (keep,)
     while keep.ndim > 2:
         received = lax.ppermute(outgoing, axis, pairs)
         level += 1
         outgoing = keep[0] + received[0]
-        keep = keep[1] + received[1]
+        if keep.ndim == 3:
+            parts = (keep[1], received[1])
+            keep = keep[1]
+        else:
+            keep = keep[1] + received[1]
+            parts = (keep,)
         pairs = [(i, i ^ (1 << level)) for i in range(count)]
-    return keep, outgoing, pairs
+    return parts, outgoing, pairs
 
 
 def doubling_gather(block, axis, companion):
@@ -78,11 +84,15 @@
         out_ref[hour] = total[:, hour * members:(hour + 1) * members]
 
 
-def recurrence_kernel(rate_ref, keep_ref, received_ref, out_ref):
+def recurrence_kernel(rate_ref, *refs):
+    *addend_refs, out_ref = refs
     hours = out_ref.shape[0]
     state = jnp.zeros(out_ref.shape[1:], jnp.float32)
     for hour in range(hours):
-        state = rate_ref[pl.ds(hour, 1), :] * state + (keep_ref[hour] + received_ref[hour])
+        information = addend_refs[0][hour]
+        for addend_ref in addend_refs[1:]:
+            information = information + addend_ref[hour]
+        state = rate_ref[pl.ds(hour, 1), :] * state + information
         out_ref[hour] = state
     state = jnp.zeros(out_ref.shape[1:], jnp.float32)
     for hour in reversed(range(hours)):
@@ -159,18 +169,17 @@
     ]
     for chunk in range(CHUNKS):
         kept, received = addends[chunk]
-        kept = kept.reshape(hours, chunk_members, comps)
-        received = received.reshape(hours, chunk_members, comps)
+        parts = [a.reshape(hours, chunk_members, comps) for a in kept + (received,)]
         smoothed_here = vmem_call(
             recurrence_kernel,
-            jax.ShapeDtypeStruct(kept.shape, jnp.float32),
-            3,
+            jax.ShapeDtypeStruct(parts[0].shape, jnp.float32),
+            1 + len(parts),
             pl.CostEstimate(
                 flops=6 * hours * chunk_members * comps,
                 bytes_accessed=12 * hours * chunk_members * comps,
                 transcendentals=0,
             ),
-        )(decay_all, kept, received)
+        )(decay_all, *parts)
         gathered = lax.all_to_all(smoothed_here, "tm", split_axis=0, concat_axis=1, tiled=True)
         rounded = gathered.astype(jnp.bfloat16)
         pieces, earlier = doubling_gather(rounded, "state", fitted_parts[-1:])

time: 112 us -> 113 us (level)
    unnamed x27 -> x25, local copies, waits for them, and re-layouts: 7.63 us -> 7.64 us
where the time goes in v25:
time: 113 us; the launch traced here: 112 us
  waiting for transfers between devices  46.7 us (41%)
  starting transfers between devices  30 us (27%)
  Pallas kernels  16.1 us (14%)
  local copies, waits for them, and re-layouts  10.2 us (9%)
  other arithmetic  8.13 us (7%)
    all_to_all x1, waiting for transfers between devices, local(): lax.all_to_all(outgoing, 'tm', split_axis=0, concat_axis=0, tiled=True)  15.9 us
    all_to_all x2, starting transfers between devices, local(): lax.all_to_all(smoothed_here, 'tm', split_axis=0, concat_axis=1, tiled=True)  11.4 us
    ppermute x1, waiting for transfers between devices, local(): lax.ppermute(o, 'state', last[c + 1][2])  10.6 us
    all_to_all x1, waiting for transfers between devices, local(): lax.all_to_all(masked_later, 'tm', split_axis=1, concat_axis=0, tiled=True)  9.16 us
    unnamed x25, local copies, waits for them, and re-layouts  7.64 us
    all_to_all x1, starting transfers between devices, local(): lax.all_to_all(outgoing, 'tm', split_axis=0, concat_axis=0, tiled=True)  7.25 us
    pallas_call x2, Pallas kernels, local(): vmem_call(fitted_kernel, jax.ShapeDtypeStruct((slab_hours, stations_here,...  6.71 us
    ppermute x6, waiting for transfers between devices, doubling_gather(): pieces = pieces + [lax.ppermute(piece, axis, pairs) for piece in pieces]  5.82 us
  transfers between devices with their start and end apart: 14, of which 8 were waited for; matrix products, arithmetic and copies ran while one was open for 7% of the time, Pallas kernels for 5%

profile of v25, /device:TPU:0, one launch (start us, length us, event | category | flops | bytes accessed | tf_op | source)
XLA Modules:
  0.0 112.0 jit_solution(17141050122277557234)
XLA Ops:
  0.6 0.7 convert_element_type.29
  1.3 0.7 fusion.3
  2.1 1.7 %copy.37 = bf16[64,16,256]{0,2,1:T(8,128)(2,1)S(1)} copy(bf16[64,16,256]{2,1,0:T(8,128)(2,1)} %param.4) | data formatting | bytes 1048576 | tf_op args[0]
  4.4 0.9 pad_maximum_fusion.2
  5.3 7.3 %all-to-all-start = ((bf16[8,72,512]{2,1,0:T(8,128)(2,1)}), bf16[8,72,512]{2,1,0:T(8,128)(2,1)S(1)}, u32[]{:S(2)}, u32[]{:S(2)}) async-start(bf16[8,72,512]{2,1,0:T(8,128)(2,1)} %pad_maximum_fusion.2), calls=%async_computation | async-start | bytes 1179648 | tf_op jit(solution)/shard_map/all_to_all | solution.py:135
  12.5 15.9 %all-to-all-done.x_ref = bf16[8,72,512]{2,1,0:T(8,128)(2,1)S(1)} async-done(((bf16[8,72,512]{2,1,0:T(8,128)(2,1)}), bf16[8,72,512]{2,1,0:T(8,128)(2,1)S(1)}, u32[]{:S(2)}, u32[]{:S(2)}) %all-to-all-start) | async-done | bytes 589856 | tf_op jit(solution)/shard_map/all_to_all | solution.py:135
  28.4 0.8 copy-done.5
  29.2 4.8 %shard_map.59 = (f32[2,256,512]{2,1,0:T(8,128)}, f32[2,256,512]{2,1,0:T(8,128)}, f32[2,256,512]{2,1,0:T(8,128)}, f32[2,256,512]{2,1,0:T(8,128)}) custom-call(s32[1]{0:T(128)} %bitcast.10.me_ref, bf16[8,72,512]{2,1,0:T(8,128)(2,1)} %copy-done.5, bf16[512,2048]{1,0:T(8,128)(2,1)} %l_ref.5), custom_call_target="tpu_custom_call" | custom-call | flops 1073741824 | bytes 6815744 | tf_op jit(solution)/shard_map/pallas_call | solution.py:147
  34.6 1.1 copy.42
  35.7 3.6 %all-to-all-start.1 = ((bf16[64,16,256]{2,0,1:T(8,128)(2,1)}), bf16[64,16,256]{2,0,1:T(8,128)(2,1)S(1)}, u32[]{:S(2)}, u32[]{:S(2)}) async-start(bf16[64,16,256]{2,0,1:T(8,128)(2,1)} %copy.42), calls=%async_computation.1 | async-start | bytes 1048576 | tf_op jit(solution)/shard_map/all_to_all | solution.py:142
  39.3 2.4 %fusion.1 = (f32[256,512]{1,0:T(8,128)}, f32[256,512]{1,0:T(8,128)}, f32[256,512]{1,0:T(8,128)}) fusion(f32[2,256,512]{2,1,0:T(8,128)} %collective-permute-done, f32[2,256,512]{2,1,0:T(8,128)S(1)} %copy-done.2), kind=kLoop, calls=%fused_computation.7 | loop fusion | flops 131072 | bytes 3670016 | tf_op jit(solution)/shard_map/add | solution.py:41
  41.7 1.5 %collective-permute-start.1 = (f32[256,512]{1,0:T(8,128)}, f32[256,512]{1,0:T(8,128)}, u32[]{:S(2)}, u32[]{:S(2)}) collective-permute-start(f32[256,512]{1,0:T(8,128)} %get-tuple-element.49), channel_id=1, source_target_pairs={{0,2},{1,3},{2,0},{3,1},{4,6},{5,7},{6,4},{7,5},{8,10},{9,11},{10,... | collective-permute-start | bytes 1572872 | tf_op jit(solution)/shard_map/ppermute | solution.py:164
  43.3 0.8 slice_convert_fusion
  44.9 9.2 %all-to-all-done.1 = bf16[64,16,256]{2,0,1:T(8,128)(2,1)S(1)} async-done(((bf16[64,16,256]{2,0,1:T(8,128)(2,1)}), bf16[64,16,256]{2,0,1:T(8,128)(2,1)S(1)}, u32[]{:S(2)}, u32[]{:S(2)}) %all-to-all-start.1) | async-done | bytes 524320 | tf_op jit(solution)/shard_map/all_to_all | solution.py:142
  54.1 1.2 %fusion = (f32[256,512]{1,0:T(8,128)S(1)}, f32[256,512]{1,0:T(8,128)}, f32[256,512]{1,0:T(8,128)}) fusion(f32[2,256,512]{2,1,0:T(8,128)S(1)} %collective-permute-done.2, f32[2,256,512]{2,1,0:T(8,128)S(1)} %copy-done.1), kind=kLoop, calls=%fused_computation.4 | loop fusion | flops 131072 | bytes 3670016 | tf_op jit(solution)/shard_map/add | solution.py:41
  55.8 2.3 %shard_map.60 = f32[16,16,512]{2,1,0:T(8,128)} custom-call(f32[16,512]{1,0:T(8,128)} %add.28.rate_ref, f32[16,16,512]{2,1,0:T(8,128)} %bitcast.59, f32[16,16,512]{2,1,0:T(8,128)} %bitcast.60, f32[16,16,512]{2,1,0:T(8,128)} %bitcast.19.refs_2_), custom_call_target="tpu_custom_call" | custom-call | flops 786432 | bytes 1572864 | tf_op jit(solution)/shard_map/pallas_call | solution.py:173
  58.1 5.6 %all-to-all-start.2 = ((f32[16,16,512]{2,1,0:T(8,128)}), f32[16,16,512]{2,1,0:T(8,128)S(1)}, u32[]{:S(2)}, u32[]{:S(2)}) async-start(f32[16,16,512]{2,1,0:T(8,128)} %shard_map.60), calls=%async_computation.2 | async-start | bytes 1048576 | tf_op jit(solution)/shard_map/all_to_all | solution.py:183
  63.7 1.5 %collective-permute-start.3 = (f32[256,512]{1,0:T(8,128)S(1)}, f32[256,512]{1,0:T(8,128)S(1)}, u32[]{:S(2)}, u32[]{:S(2)}) collective-permute-start(f32[256,512]{1,0:T(8,128)S(1)} %get-tuple-element.31), channel_id=1, source_target_pairs={{0,2},{1,3},{2,0},{3,1},{4,6},{5,7},{6,4},{7,5},{8,10},{9,11},{10,... | collective-permute-start | bytes 1572872 | tf_op jit(solution)/shard_map/ppermute | solution.py:168
  65.2 10.6 %collective-permute-done.3 = f32[256,512]{1,0:T(8,128)S(1)} collective-permute-done((f32[256,512]{1,0:T(8,128)S(1)}, f32[256,512]{1,0:T(8,128)S(1)}, u32[]{:S(2)}, u32[]{:S(2)}) %collective-permute-start.3) | collective-permute-done | bytes 524320 | tf_op jit(solution)/shard_map/ppermute | solution.py:168
  75.9 0.8 copy-done.6
  76.7 2.3 %shard_map.61 = f32[16,16,512]{2,1,0:T(8,128)} custom-call(f32[16,512]{1,0:T(8,128)} %add.28.rate_ref, f32[16,16,512]{2,1,0:T(8,128)} %bitcast.62, f32[16,16,512]{2,1,0:T(8,128)} %bitcast.63, f32[16,16,512]{2,1,0:T(8,128)} %bitcast.66), custom_call_target="tpu_custom_call" | custom-call | flops 786432 | bytes 1572864 | tf_op jit(solution)/shard_map/pallas_call | solution.py:173
  79.0 5.7 %all-to-all-start.3 = ((f32[16,16,512]{2,1,0:T(8,128)}), f32[16,16,512]{2,1,0:T(8,128)S(1)}, u32[]{:S(2)}, u32[]{:S(2)}) async-start(f32[16,16,512]{2,1,0:T(8,128)} %shard_map.61), calls=%async_computation.3 | async-start | bytes 1048576 | tf_op jit(solution)/shard_map/all_to_all | solution.py:183
  84.8 1.6 %collective-permute-start.5 = (bf16[2,128,512]{2,1,0:T(8,128)(2,1)S(1)}, bf16[2,128,512]{2,1,0:T(8,128)(2,1)S(1)}, u32[]{:S(2)}, u32[]{:S(2)}) collective-permute-start(bf16[2,128,512]{2,1,0:T(8,128)(2,1)S(1)} %bitcast_convert_fusion.refs_0_), channel_id=1, source_target_pairs={{0,2},{1,3},{2,0},{3,1},{4,6},{5,7},{6,4},{7,5},{8,10},{9,11},{10,... | collective-permute-start | bytes 786440 | tf_op jit(solution)/shard_map/ppermute | solution.py:58
  86.4 4.9 %collective-permute-done.5.refs_1_ = bf16[2,128,512]{2,1,0:T(8,128)(2,1)S(1)} collective-permute-done((bf16[2,128,512]{2,1,0:T(8,128)(2,1)S(1)}, bf16[2,128,512]{2,1,0:T(8,128)(2,1)S(1)}, u32[]{:S(2)}, u32[]{:S(2)}) %collective-permute-start.5) | collective-permute-done | bytes 262176 | tf_op jit(solution)/shard_map/ppermute | solution.py:58
  91.8 4.7 %all-to-all-done.3 = f32[16,16,512]{2,1,0:T(8,128)S(1)} async-done(((f32[16,16,512]{2,1,0:T(8,128)}), f32[16,16,512]{2,1,0:T(8,128)S(1)}, u32[]{:S(2)}, u32[]{:S(2)}) %all-to-all-start.3) | async-done | bytes 524320 | tf_op jit(solution)/shard_map/all_to_all | solution.py:183
  96.6 1.6 %collective-permute-start.4 = (bf16[2,128,512]{2,1,0:T(8,128)(2,1)S(1)}, bf16[2,128,512]{2,1,0:T(8,128)(2,1)S(1)}, u32[]{:S(2)}, u32[]{:S(2)}) collective-permute-start(bf16[2,128,512]{2,1,0:T(8,128)(2,1)S(1)} %bitcast_convert_fusion.1.refs_0_), channel_id=1, source_target_pairs={{0,2},{1,3},{2,0},{3,1},{4,6},{5,7},{6,4},{7,5},{8,10},{9,11},{10,... | collective-permute-start | bytes 786440 | tf_op jit(solution)/shard_map/ppermute | solution.py:58
  98.9 3.4 %shard_map.62 = f32[2,512,128]{2,1,0:T(8,128)} custom-call(s32[1]{0:T(128)} %bitcast.10.me_ref, bf16[512,2048]{1,0:T(8,128)(2,1)} %l_ref.5, bf16[2,128,512]{2,1,0:T(8,128)(2,1)} %copy-done.4, bf16[2,128,512]{2,1,0:T(8,128)(2,1)} %copy-done.8, bf16[2,128,512]{2,1,0:T(8,128)(2,1)} %copy-done.9, bf16[2,128,512]{2,1,0:T(8,128)(2,1)} %collective-permute-done.7.refs_3_), custom_call_target="tpu_custom_call" | custom-call | flops 536870912 | bytes 3670016 | tf_op jit(solution)/shard_map/pallas_call | solution.py:188
  102.2 0.8 collective-permute-done.4.refs_1_
  103.6 1.3 %copy.46 = f32[512,2,256]{2,1,0:T(2,128)} copy(f32[512,2,256]{0,2,1:T(8,128)S(1)} %pad_maximum_fusion) | data formatting | bytes 2097152
  105.7 3.4 %shard_map.63 = f32[2,512,128]{2,1,0:T(8,128)} custom-call(s32[1]{0:T(128)} %bitcast.10.me_ref, bf16[512,2048]{1,0:T(8,128)(2,1)} %l_ref.5, bf16[2,128,512]{2,1,0:T(8,128)(2,1)} %copy-done.3, bf16[2,128,512]{2,1,0:T(8,128)(2,1)} %copy-done.7, bf16[2,128,512]{2,1,0:T(8,128)(2,1)} %copy-done.10, bf16[2,128,512]{2,1,0:T(8,128)(2,1)} %collective-permute-done.9.refs_3_), custom_call_target="tpu_custom_call" | custom-call | flops 536870912 | bytes 3670016 | tf_op jit(solution)/shard_map/pallas_call | solution.py:188
  109.0 1.1 %bitcast_subtract_fusion.1 = (f32[512,2,128]{2,0,1:T(8,128)S(1)}, f32[512,2,128]{2,0,1:T(8,128)S(1)}) fusion(f32[2,512,128]{2,1,0:T(8,128)S(1)} %copy-done, bf16[512,2,256]{2,0,1:T(8,128)(2,1)S(1)} %bitcast.58, f32[2,512,128]{2,1,0:T(8,128)} %shard_map.63), kind=kLoop, calls=%fused_computation.10 | loop fusion | flops 524288 | bytes 2621440 | tf_op jit(solution)/shard_map/sub | solution.py:206
  110.2 1.8 %copy.47 = f32[512,2,256]{2,1,0:T(2,128)} copy(f32[512,2,256]{2,0,1:T(8,128)S(1)} %pad_maximum_fusion.1) | data formatting | bytes 2097152
  (52 shorter events, 5.1 us)
Async XLA Ops:
  5.3 23.1 %all-to-all-start = ((bf16[8,72,512]{2,1,0:T(8,128)(2,1)}), bf16[8,72,512]{2,1,0:T(8,128)(2,1)S(1)}, u32[]{:S(2)}, u32[]{:S(2)}) async-start(bf16[8,72,512]{2,1,0:T(8,128)(2,1)} %pad_maximum_fusion.2), calls=%async_computation | async-start | bytes 1179648 | tf_op jit(solution)/shard_map/all_to_all | solution.py:135
  28.4 0.8 copy-start.5
  34.0 5.3 %collective-permute-start = (f32[2,256,512]{2,1,0:T(8,128)}, f32[2,256,512]{2,1,0:T(8,128)}, u32[]{:S(2)}, u32[]{:S(2)}) collective-permute-start(f32[2,256,512]{2,1,0:T(8,128)} %get-tuple-element.23), channel_id=1, source_target_pairs={{0,1},{1,0},{2,3},{3,2},{4,5},{5,4},{6,7},{7,6},{8,9},{9,8},{10,11... | collective-permute-start | bytes 3145736 | tf_op jit(solution)/shard_map/ppermute | solution.py:39
  34.0 5.3 %copy-start.2 = (f32[2,256,512]{2,1,0:T(8,128)S(1)}, f32[2,256,512]{2,1,0:T(8,128)}, u32[]{:S(2)}) copy-start(f32[2,256,512]{2,1,0:T(8,128)} %get-tuple-element.22) | copy-start | bytes 3145732
  34.1 20.0 %collective-permute-start.2 = (f32[2,256,512]{2,1,0:T(8,128)}, f32[2,256,512]{2,1,0:T(8,128)S(1)}, u32[]{:S(2)}, u32[]{:S(2)}) collective-permute-start(f32[2,256,512]{2,1,0:T(8,128)} %get-tuple-element.25), channel_id=1, source_target_pairs={{0,1},{1,0},{2,3},{3,2},{4,5},{5,4},{6,7},{7,6},{8,9},{9,8},{10,11... | collective-permute-start | bytes 3145736 | tf_op jit(solution)/shard_map/ppermute | solution.py:39
  35.7 18.4 %all-to-all-start.1 = ((bf16[64,16,256]{2,0,1:T(8,128)(2,1)}), bf16[64,16,256]{2,0,1:T(8,128)(2,1)S(1)}, u32[]{:S(2)}, u32[]{:S(2)}) async-start(bf16[64,16,256]{2,0,1:T(8,128)(2,1)} %copy.42), calls=%async_computation.1 | async-start | bytes 1048576 | tf_op jit(solution)/shard_map/all_to_all | solution.py:142
  41.7 12.3 %copy-start.1 = (f32[2,256,512]{2,1,0:T(8,128)S(1)}, f32[2,256,512]{2,1,0:T(8,128)}, u32[]{:S(2)}) copy-start(f32[2,256,512]{2,1,0:T(8,128)} %get-tuple-element.24) | copy-start | bytes 3145732
  41.7 14.0 %collective-permute-start.1 = (f32[256,512]{1,0:T(8,128)}, f32[256,512]{1,0:T(8,128)}, u32[]{:S(2)}, u32[]{:S(2)}) collective-permute-start(f32[256,512]{1,0:T(8,128)} %get-tuple-element.49), channel_id=1, source_target_pairs={{0,2},{1,3},{2,0},{3,1},{4,6},{5,7},{6,4},{7,5},{8,10},{9,11},{10,... | collective-permute-start | bytes 1572872 | tf_op jit(solution)/shard_map/ppermute | solution.py:164
  58.1 20.9 %all-to-all-start.2 = ((f32[16,16,512]{2,1,0:T(8,128)}), f32[16,16,512]{2,1,0:T(8,128)S(1)}, u32[]{:S(2)}, u32[]{:S(2)}) async-start(f32[16,16,512]{2,1,0:T(8,128)} %shard_map.60), calls=%async_computation.2 | async-start | bytes 1048576 | tf_op jit(solution)/shard_map/all_to_all | solution.py:183
  63.7 12.2 %collective-permute-start.3 = (f32[256,512]{1,0:T(8,128)S(1)}, f32[256,512]{1,0:T(8,128)S(1)}, u32[]{:S(2)}, u32[]{:S(2)}) collective-permute-start(f32[256,512]{1,0:T(8,128)S(1)} %get-tuple-element.31), channel_id=1, source_target_pairs={{0,2},{1,3},{2,0},{3,1},{4,6},{5,7},{6,4},{7,5},{8,10},{9,11},{10,... | collective-permute-start | bytes 1572872 | tf_op jit(solution)/shard_map/ppermute | solution.py:168
  75.9 0.8 copy-start.6
  79.0 17.5 %all-to-all-start.3 = ((f32[16,16,512]{2,1,0:T(8,128)}), f32[16,16,512]{2,1,0:T(8,128)S(1)}, u32[]{:S(2)}, u32[]{:S(2)}) async-start(f32[16,16,512]{2,1,0:T(8,128)} %shard_map.61), calls=%async_computation.3 | async-start | bytes 1048576 | tf_op jit(solution)/shard_map/all_to_all | solution.py:183
  84.8 13.4 %copy-start.4 = (bf16[2,128,512]{2,1,0:T(8,128)(2,1)}, bf16[2,128,512]{2,1,0:T(8,128)(2,1)S(1)}, u32[]{:S(2)}) copy-start(bf16[2,128,512]{2,1,0:T(8,128)(2,1)S(1)} %bitcast_convert_fusion.refs_0_) | copy-start | bytes 786436
  84.8 6.4 %collective-permute-start.5 = (bf16[2,128,512]{2,1,0:T(8,128)(2,1)S(1)}, bf16[2,128,512]{2,1,0:T(8,128)(2,1)S(1)}, u32[]{:S(2)}, u32[]{:S(2)}) collective-permute-start(bf16[2,128,512]{2,1,0:T(8,128)(2,1)S(1)} %bitcast_convert_fusion.refs_0_), channel_id=1, source_target_pairs={{0,2},{1,3},{2,0},{3,1},{4,6},{5,7},{6,4},{7,5},{8,10},{9,11},{10,... | collective-permute-start | bytes 786440 | tf_op jit(solution)/shard_map/ppermute | solution.py:58
  91.3 6.9 %copy-start.8 = (bf16[2,128,512]{2,1,0:T(8,128)(2,1)}, bf16[2,128,512]{2,1,0:T(8,128)(2,1)S(1)}, u32[]{:S(2)}) copy-start(bf16[2,128,512]{2,1,0:T(8,128)(2,1)S(1)} %collective-permute-done.5.refs_1_) | copy-start | bytes 786436
  91.3 6.9 %collective-permute-start.6 = (bf16[2,128,512]{2,1,0:T(8,128)(2,1)S(1)}, bf16[2,128,512]{2,1,0:T(8,128)(2,1)S(1)}, u32[]{:S(2)}, u32[]{:S(2)}) collective-permute-start(bf16[2,128,512]{2,1,0:T(8,128)(2,1)S(1)} %bitcast_convert_fusion.refs_0_), channel_id=1, source_target_pairs={{0,1},{1,0},{2,3},{3,2},{4,5},{5,4},{6,7},{7,6},{8,9},{9,8},{10,11... | collective-permute-start | bytes 786440 | tf_op jit(solution)/shard_map/ppermute | solution.py:58
  91.3 6.9 %collective-permute-start.7 = (bf16[2,128,512]{2,1,0:T(8,128)(2,1)S(1)}, bf16[2,128,512]{2,1,0:T(8,128)(2,1)}, u32[]{:S(2)}, u32[]{:S(2)}) collective-permute-start(bf16[2,128,512]{2,1,0:T(8,128)(2,1)S(1)} %collective-permute-done.5.refs_1_), channel_id=1, source_target_pairs={{0,1},{1,0},{2,3},{3,2},{4,5},{5,4},{6,7},{7,6},{8,9},{9,8},{10,11... | collective-permute-start | bytes 786440 | tf_op jit(solution)/shard_map/ppermute | solution.py:58
  96.6 6.5 %copy-start.3 = (bf16[2,128,512]{2,1,0:T(8,128)(2,1)}, bf16[2,128,512]{2,1,0:T(8,128)(2,1)S(1)}, u32[]{:S(2)}) copy-start(bf16[2,128,512]{2,1,0:T(8,128)(2,1)S(1)} %bitcast_convert_fusion.1.refs_0_) | copy-start | bytes 786436
  96.6 6.4 %collective-permute-start.4 = (bf16[2,128,512]{2,1,0:T(8,128)(2,1)S(1)}, bf16[2,128,512]{2,1,0:T(8,128)(2,1)S(1)}, u32[]{:S(2)}, u32[]{:S(2)}) collective-permute-start(bf16[2,128,512]{2,1,0:T(8,128)(2,1)S(1)} %bitcast_convert_fusion.1.refs_0_), channel_id=1, source_target_pairs={{0,2},{1,3},{2,0},{3,1},{4,6},{5,7},{6,4},{7,5},{8,10},{9,11},{10,... | collective-permute-start | bytes 786440 | tf_op jit(solution)/shard_map/ppermute | solution.py:58
  98.2 0.7 copy-start.9
  103.1 1.9 %copy-start.7 = (bf16[2,128,512]{2,1,0:T(8,128)(2,1)}, bf16[2,128,512]{2,1,0:T(8,128)(2,1)S(1)}, u32[]{:S(2)}) copy-start(bf16[2,128,512]{2,1,0:T(8,128)(2,1)S(1)} %collective-permute-done.4.refs_1_) | copy-start | bytes 786436
  103.1 1.9 %collective-permute-start.8 = (bf16[2,128,512]{2,1,0:T(8,128)(2,1)S(1)}, bf16[2,128,512]{2,1,0:T(8,128)(2,1)S(1)}, u32[]{:S(2)}, u32[]{:S(2)}) collective-permute-start(bf16[2,128,512]{2,1,0:T(8,128)(2,1)S(1)} %bitcast_convert_fusion.1.refs_0_), channel_id=1, source_target_pairs={{0,1},{1,0},{2,3},{3,2},{4,5},{5,4},{6,7},{7,6},{8,9},{9,8},{10,11... | collective-permute-start | bytes 786440 | tf_op jit(solution)/shard_map/ppermute | solution.py:58
  103.1 2.0 %collective-permute-start.9 = (bf16[2,128,512]{2,1,0:T(8,128)(2,1)S(1)}, bf16[2,128,512]{2,1,0:T(8,128)(2,1)}, u32[]{:S(2)}, u32[]{:S(2)}) collective-permute-start(bf16[2,128,512]{2,1,0:T(8,128)(2,1)S(1)} %collective-permute-done.4.refs_1_), channel_id=1, source_target_pairs={{0,1},{1,0},{2,3},{3,2},{4,5},{5,4},{6,7},{7,6},{8,9},{9,8},{10,11... | collective-permute-start | bytes 786440 | tf_op jit(solution)/shard_map/ppermute | solution.py:58
  104.9 4.1 %copy-start = (f32[2,512,128]{2,1,0:T(8,128)S(1)}, f32[2,512,128]{2,1,0:T(8,128)}, u32[]{:S(2)}) copy-start(f32[2,512,128]{2,1,0:T(8,128)} %shard_map.62) | copy-start | bytes 1572868
  105.0 0.7 copy-start.10

commit v26 on v24

--- a/solution.py
+++ b/solution.py
@@ -75,7 +75,7 @@
         )
         total = part if total is None else total + part
     for hour in range(hours):
-        out_ref[hour] = total[:, hour * members:(hour + 1) * members]
+        out_ref[:, hour, :] = total[:, hour * members:(hour + 1) * members]
 
 
 def recurrence_kernel(rate_ref, keep_ref, received_ref, out_ref):
@@ -178,7 +178,7 @@
         slab_hours, width, _ = rounded.shape
         fitted = vmem_call(
             fitted_kernel,
-            jax.ShapeDtypeStruct((slab_hours, stations_here, width), jnp.float32),
+            jax.ShapeDtypeStruct((stations_here, slab_hours, width), jnp.float32),
             1 + len(pieces),
             pl.CostEstimate(
                 flops=2 * stations_here * slab_hours * width * all_comps,
@@ -194,7 +194,7 @@
     for chunk, fitted in enumerate(fitted_parts):
         low = chunk * members // CHUNKS
         picked = by_hour[:, :, low:low + members // CHUNKS]
-        residual_parts.append(picked.astype(jnp.float32) - jnp.transpose(fitted, (1, 0, 2)))
+        residual_parts.append(picked.astype(jnp.float32) - fitted)
     return (
         jnp.concatenate(smoothed_parts, axis=2),
         jnp.concatenate(residual_parts, axis=2),

time: 112 us -> 113 us (level)
  other arithmetic: 8.1 us -> 9.93 us
  local copies, waits for them, and re-layouts: 10.2 us -> 8.92 us
    unnamed x27 -> x26, local copies, waits for them, and re-layouts: 7.63 us -> 5.85 us
    concatenate x1, other arithmetic: 0.07 us -> 1.45 us  [local(): jnp.concatenate(residual_parts, axis=2)]
  transfers between devices with their start and end apart: 14 -> 14, of which waited for: 8 -> 7; matrix products, arithmetic and copies ran while one was open for 7% -> 7% of each run, Pallas kernels for 5% -> 5%
where the time goes in v26:
time: 113 us; the launch traced here: 112 us
  waiting for transfers between devices  46 us (41%)
  starting transfers between devices  30 us (27%)
  Pallas kernels  16.2 us (14%)
  other arithmetic  9.93 us (9%)
  local copies, waits for them, and re-layouts  8.92 us (8%)
    all_to_all x1, waiting for transfers between devices, local(): lax.all_to_all(outgoing, 'tm', split_axis=0, concat_axis=0, tiled=True)  15.9 us
    all_to_all x2, starting transfers between devices, local(): lax.all_to_all(smoothed_here, 'tm', split_axis=0, concat_axis=1, tiled=True)  11.3 us
    ppermute x1, waiting for transfers between devices, local(): lax.ppermute(o, 'state', last[c + 1][2])  10.6 us
    all_to_all x1, waiting for transfers between devices, local(): lax.all_to_all(masked_later, 'tm', split_axis=1, concat_axis=0, tiled=True)  9.16 us
    all_to_all x1, starting transfers between devices, local(): lax.all_to_all(outgoing, 'tm', split_axis=0, concat_axis=0, tiled=True)  7.25 us
    pallas_call x2, Pallas kernels, local(): vmem_call(fitted_kernel, jax.ShapeDtypeStruct((stations_here, slab_hours,...  7.09 us
    unnamed x26, local copies, waits for them, and re-layouts  5.85 us
    ppermute x6, waiting for transfers between devices, doubling_gather(): pieces = pieces + [lax.ppermute(piece, axis, pairs) for piece in pieces]  5.59 us
  transfers between devices with their start and end apart: 14, of which 7 were waited for; matrix products, arithmetic and copies ran while one was open for 7% of the time, Pallas kernels for 5%

profile of v26, /device:TPU:0, one launch (start us, length us, event | category | flops | bytes accessed | tf_op | source)
XLA Modules:
  0.0 111.9 jit_solution(6191017633712186359)
XLA Ops:
  0.6 0.7 convert_element_type.29
  1.3 0.7 fusion.5
  2.1 1.7 %copy.34 = bf16[64,16,256]{0,2,1:T(8,128)(2,1)S(1)} copy(bf16[64,16,256]{2,1,0:T(8,128)(2,1)} %param.4) | data formatting | bytes 1048576 | tf_op args[0]
  4.4 0.9 pad_maximum_fusion.2
  5.3 7.3 %all-to-all-start = ((bf16[8,72,512]{2,1,0:T(8,128)(2,1)}), bf16[8,72,512]{2,1,0:T(8,128)(2,1)S(1)}, u32[]{:S(2)}, u32[]{:S(2)}) async-start(bf16[8,72,512]{2,1,0:T(8,128)(2,1)} %pad_maximum_fusion.2), calls=%async_computation | async-start | bytes 1179648 | tf_op jit(solution)/shard_map/all_to_all | solution.py:125
  12.5 15.9 %all-to-all-done.x_ref = bf16[8,72,512]{2,1,0:T(8,128)(2,1)S(1)} async-done(((bf16[8,72,512]{2,1,0:T(8,128)(2,1)}), bf16[8,72,512]{2,1,0:T(8,128)(2,1)S(1)}, u32[]{:S(2)}, u32[]{:S(2)}) %all-to-all-start) | async-done | bytes 589856 | tf_op jit(solution)/shard_map/all_to_all | solution.py:125
  28.4 0.8 copy-done.5
  29.2 4.8 %shard_map.59 = (f32[2,256,512]{2,1,0:T(8,128)}, f32[2,256,512]{2,1,0:T(8,128)}, f32[2,256,512]{2,1,0:T(8,128)}, f32[2,256,512]{2,1,0:T(8,128)}) custom-call(s32[1]{0:T(128)} %bitcast.10.me_ref, bf16[8,72,512]{2,1,0:T(8,128)(2,1)} %copy-done.5, bf16[512,2048]{1,0:T(8,128)(2,1)} %l_ref.5), custom_call_target="tpu_custom_call" | custom-call | flops 1073741824 | bytes 6815744 | tf_op jit(solution)/shard_map/pallas_call | solution.py:137
  34.6 1.1 %copy.39 = bf16[64,16,256]{2,0,1:T(8,128)(2,1)} copy(bf16[64,16,256]{0,2,1:T(8,128)(2,1)S(1)} %broadcast_multiply_fusion) | data formatting | bytes 1048576 | tf_op jit(solution)/shard_map/optimization_barrier | solution.py:131
  35.7 3.6 %all-to-all-start.1 = ((bf16[64,16,256]{2,0,1:T(8,128)(2,1)}), bf16[64,16,256]{2,0,1:T(8,128)(2,1)S(1)}, u32[]{:S(2)}, u32[]{:S(2)}) async-start(bf16[64,16,256]{2,0,1:T(8,128)(2,1)} %copy.39), calls=%async_computation.1 | async-start | bytes 1048576 | tf_op jit(solution)/shard_map/all_to_all | solution.py:132
  39.3 2.4 %fusion.2 = (f32[256,512]{1,0:T(8,128)}, f32[256,512]{1,0:T(8,128)}) fusion(f32[2,256,512]{2,1,0:T(8,128)} %collective-permute-done, f32[2,256,512]{2,1,0:T(8,128)S(1)} %copy-done.2), kind=kLoop, calls=%fused_computation.8 | loop fusion | flops 262144 | bytes 3145728 | tf_op jit(solution)/shard_map/add | solution.py:40
  41.7 1.5 %collective-permute-start.1 = (f32[256,512]{1,0:T(8,128)}, f32[256,512]{1,0:T(8,128)}, u32[]{:S(2)}, u32[]{:S(2)}) collective-permute-start(f32[256,512]{1,0:T(8,128)} %get-tuple-element.44), channel_id=1, source_target_pairs={{0,2},{1,3},{2,0},{3,1},{4,6},{5,7},{6,4},{7,5},{8,10},{9,11},{10,... | collective-permute-start | bytes 1572872 | tf_op jit(solution)/shard_map/ppermute | solution.py:154
  43.3 0.8 slice_convert_fusion
  44.9 9.2 %all-to-all-done.1 = bf16[64,16,256]{2,0,1:T(8,128)(2,1)S(1)} async-done(((bf16[64,16,256]{2,0,1:T(8,128)(2,1)}), bf16[64,16,256]{2,0,1:T(8,128)(2,1)S(1)}, u32[]{:S(2)}, u32[]{:S(2)}) %all-to-all-start.1) | async-done | bytes 524320 | tf_op jit(solution)/shard_map/all_to_all | solution.py:132
  54.6 1.2 %fusion = (f32[256,512]{1,0:T(8,128)}, f32[256,512]{1,0:T(8,128)}) fusion(f32[2,256,512]{2,1,0:T(8,128)S(1)} %collective-permute-done.2, f32[2,256,512]{2,1,0:T(8,128)S(1)} %copy-done.1), kind=kLoop, calls=%fused_computation.4 | loop fusion | flops 262144 | bytes 3145728 | tf_op jit(solution)/shard_map/add | solution.py:40
  55.8 2.2 %shard_map.60 = f32[16,16,512]{2,1,0:T(8,128)} custom-call(f32[16,512]{1,0:T(8,128)} %add.40.rate_ref, f32[16,16,512]{2,1,0:T(8,128)} %bitcast.49, f32[16,16,512]{2,1,0:T(8,128)} %bitcast.16.received_ref), custom_call_target="tpu_custom_call" | custom-call | flops 786432 | bytes 1572864 | tf_op jit(solution)/shard_map/pallas_call | solution.py:164
  58.0 5.6 %all-to-all-start.2 = ((f32[16,16,512]{2,1,0:T(8,128)}), f32[16,16,512]{2,1,0:T(8,128)S(1)}, u32[]{:S(2)}, u32[]{:S(2)}) async-start(f32[16,16,512]{2,1,0:T(8,128)} %shard_map.60), calls=%async_computation.2 | async-start | bytes 1048576 | tf_op jit(solution)/shard_map/all_to_all | solution.py:174
  63.6 1.6 %collective-permute-start.3 = (f32[256,512]{1,0:T(8,128)S(1)}, f32[256,512]{1,0:T(8,128)S(1)}, u32[]{:S(2)}, u32[]{:S(2)}) collective-permute-start(f32[256,512]{1,0:T(8,128)S(1)} %copy-done.7), channel_id=1, source_target_pairs={{0,2},{1,3},{2,0},{3,1},{4,6},{5,7},{6,4},{7,5},{8,10},{9,11},{10,... | collective-permute-start | bytes 1572872 | tf_op jit(solution)/shard_map/ppermute | solution.py:158
  65.2 10.6 %collective-permute-done.3 = f32[256,512]{1,0:T(8,128)S(1)} collective-permute-done((f32[256,512]{1,0:T(8,128)S(1)}, f32[256,512]{1,0:T(8,128)S(1)}, u32[]{:S(2)}, u32[]{:S(2)}) %collective-permute-start.3) | collective-permute-done | bytes 524320 | tf_op jit(solution)/shard_map/ppermute | solution.py:158
  75.8 0.8 copy-done.6
  76.6 2.1 %shard_map.61 = f32[16,16,512]{2,1,0:T(8,128)} custom-call(f32[16,512]{1,0:T(8,128)} %add.40.rate_ref, f32[16,16,512]{2,1,0:T(8,128)} %bitcast.53, f32[16,16,512]{2,1,0:T(8,128)} %bitcast.54), custom_call_target="tpu_custom_call" | custom-call | flops 786432 | bytes 1572864 | tf_op jit(solution)/shard_map/pallas_call | solution.py:164
  78.8 5.7 %all-to-all-start.3 = ((f32[16,16,512]{2,1,0:T(8,128)}), f32[16,16,512]{2,1,0:T(8,128)S(1)}, u32[]{:S(2)}, u32[]{:S(2)}) async-start(f32[16,16,512]{2,1,0:T(8,128)} %shard_map.61), calls=%async_computation.3 | async-start | bytes 1048576 | tf_op jit(solution)/shard_map/all_to_all | solution.py:174
  84.5 1.6 %collective-permute-start.5 = (bf16[2,128,512]{2,1,0:T(8,128)(2,1)S(1)}, bf16[2,128,512]{2,1,0:T(8,128)(2,1)S(1)}, u32[]{:S(2)}, u32[]{:S(2)}) collective-permute-start(bf16[2,128,512]{2,1,0:T(8,128)(2,1)S(1)} %bitcast_convert_fusion.refs_0_), channel_id=1, source_target_pairs={{0,2},{1,3},{2,0},{3,1},{4,6},{5,7},{6,4},{7,5},{8,10},{9,11},{10,... | collective-permute-start | bytes 786440 | tf_op jit(solution)/shard_map/ppermute | solution.py:52
  86.1 4.8 %collective-permute-done.5.refs_1_ = bf16[2,128,512]{2,1,0:T(8,128)(2,1)S(1)} collective-permute-done((bf16[2,128,512]{2,1,0:T(8,128)(2,1)S(1)}, bf16[2,128,512]{2,1,0:T(8,128)(2,1)S(1)}, u32[]{:S(2)}, u32[]{:S(2)}) %collective-permute-start.5) | collective-permute-done | bytes 262176 | tf_op jit(solution)/shard_map/ppermute | solution.py:52
  91.5 4.7 %all-to-all-done.3 = f32[16,16,512]{2,1,0:T(8,128)S(1)} async-done(((f32[16,16,512]{2,1,0:T(8,128)}), f32[16,16,512]{2,1,0:T(8,128)S(1)}, u32[]{:S(2)}, u32[]{:S(2)}) %all-to-all-start.3) | async-done | bytes 524320 | tf_op jit(solution)/shard_map/all_to_all | solution.py:174
  96.3 1.6 %collective-permute-start.4 = (bf16[2,128,512]{2,1,0:T(8,128)(2,1)S(1)}, bf16[2,128,512]{2,1,0:T(8,128)(2,1)S(1)}, u32[]{:S(2)}, u32[]{:S(2)}) collective-permute-start(bf16[2,128,512]{2,1,0:T(8,128)(2,1)S(1)} %bitcast_convert_fusion.1.refs_0_), channel_id=1, source_target_pairs={{0,2},{1,3},{2,0},{3,1},{4,6},{5,7},{6,4},{7,5},{8,10},{9,11},{10,... | collective-permute-start | bytes 786440 | tf_op jit(solution)/shard_map/ppermute | solution.py:52
  97.9 0.7 copy-done.10
  98.6 3.5 %shard_map.62 = f32[512,2,128]{2,1,0:T(2,128)} custom-call(s32[1]{0:T(128)} %bitcast.10.me_ref, bf16[512,2048]{1,0:T(8,128)(2,1)} %l_ref.5, bf16[2,128,512]{2,1,0:T(8,128)(2,1)} %copy-done.4, bf16[2,128,512]{2,1,0:T(8,128)(2,1)} %copy-done.9, bf16[2,128,512]{2,1,0:T(8,128)(2,1)} %copy-done.10, bf16[2,128,512]{2,1,0:T(8,128)(2,1)} %collective-permute-done.7.refs_3_), custom_call_target="tpu_custom_call" | custom-call | flops 536870912 | bytes 3670016 | tf_op jit(solution)/shard_map/pallas_call | solution.py:179
  103.3 1.3 %copy.43 = f32[512,2,256]{2,1,0:T(2,128)} copy(f32[512,2,256]{0,2,1:T(8,128)S(1)} %pad_maximum_fusion) | data formatting | bytes 2097152
  105.3 3.5 %shard_map.63 = f32[512,2,128]{2,1,0:T(2,128)} custom-call(s32[1]{0:T(128)} %bitcast.10.me_ref, bf16[512,2048]{1,0:T(8,128)(2,1)} %l_ref.5, bf16[2,128,512]{2,1,0:T(8,128)(2,1)} %copy-done.3, bf16[2,128,512]{2,1,0:T(8,128)(2,1)} %copy-done.8, bf16[2,128,512]{2,1,0:T(8,128)(2,1)} %copy-done.11, bf16[2,128,512]{2,1,0:T(8,128)(2,1)} %collective-permute-done.9.refs_3_), custom_call_target="tpu_custom_call" | custom-call | flops 536870912 | bytes 3670016 | tf_op jit(solution)/shard_map/pallas_call | solution.py:179
  108.9 1.6 %convert_subtract_fusion.1 = (f32[512,2,128]{2,1,0:T(2,128)S(1)}, f32[512,2,128]{2,1,0:T(2,128)S(1)}) fusion(f32[512,2,128]{2,1,0:T(2,128)S(1)} %copy-done, bf16[512,2,256]{2,1,0:T(2,128)(2,1)S(1)} %bitcast.48, f32[512,2,128]{2,1,0:T(2,128)} %shard_map.63), kind=kLoop, calls=%fused_computation.14 | loop fusion | flops 524288 | bytes 2621440 | tf_op jit(solution)/shard_map/sub | solution.py:197
  110.5 1.5 %pad_maximum_fusion.1 = f32[512,2,256]{2,1,0:T(2,128)} fusion(f32[512,2,128]{2,1,0:T(2,128)S(1)} %get-tuple-element.47, f32[512,2,128]{2,1,0:T(2,128)S(1)} %get-tuple-element.46), kind=kLoop, calls=%fused_computation.1 | loop fusion | flops 262144 | bytes 2097152 | tf_op jit(solution)/shard_map/concatenate | solution.py:200
  (53 shorter events, 5.0 us)
Async XLA Ops:
  5.3 23.1 %all-to-all-start = ((bf16[8,72,512]{2,1,0:T(8,128)(2,1)}), bf16[8,72,512]{2,1,0:T(8,128)(2,1)S(1)}, u32[]{:S(2)}, u32[]{:S(2)}) async-start(bf16[8,72,512]{2,1,0:T(8,128)(2,1)} %pad_maximum_fusion.2), calls=%async_computation | async-start | bytes 1179648 | tf_op jit(solution)/shard_map/all_to_all | solution.py:125
  28.4 0.8 copy-start.5
  34.0 5.3 %collective-permute-start = (f32[2,256,512]{2,1,0:T(8,128)}, f32[2,256,512]{2,1,0:T(8,128)}, u32[]{:S(2)}, u32[]{:S(2)}) collective-permute-start(f32[2,256,512]{2,1,0:T(8,128)} %get-tuple-element.21), channel_id=1, source_target_pairs={{0,1},{1,0},{2,3},{3,2},{4,5},{5,4},{6,7},{7,6},{8,9},{9,8},{10,11... | collective-permute-start | bytes 3145736 | tf_op jit(solution)/shard_map/ppermute | solution.py:38
  34.0 5.3 %copy-start.2 = (f32[2,256,512]{2,1,0:T(8,128)S(1)}, f32[2,256,512]{2,1,0:T(8,128)}, u32[]{:S(2)}) copy-start(f32[2,256,512]{2,1,0:T(8,128)} %get-tuple-element.20) | copy-start | bytes 3145732
  34.0 20.5 %collective-permute-start.2 = (f32[2,256,512]{2,1,0:T(8,128)}, f32[2,256,512]{2,1,0:T(8,128)S(1)}, u32[]{:S(2)}, u32[]{:S(2)}) collective-permute-start(f32[2,256,512]{2,1,0:T(8,128)} %get-tuple-element.23), channel_id=1, source_target_pairs={{0,1},{1,0},{2,3},{3,2},{4,5},{5,4},{6,7},{7,6},{8,9},{9,8},{10,11... | collective-permute-start | bytes 3145736 | tf_op jit(solution)/shard_map/ppermute | solution.py:38
  35.7 18.4 %all-to-all-start.1 = ((bf16[64,16,256]{2,0,1:T(8,128)(2,1)}), bf16[64,16,256]{2,0,1:T(8,128)(2,1)S(1)}, u32[]{:S(2)}, u32[]{:S(2)}) async-start(bf16[64,16,256]{2,0,1:T(8,128)(2,1)} %copy.39), calls=%async_computation.1 | async-start | bytes 1048576 | tf_op jit(solution)/shard_map/all_to_all | solution.py:132
  41.7 12.9 %copy-start.1 = (f32[2,256,512]{2,1,0:T(8,128)S(1)}, f32[2,256,512]{2,1,0:T(8,128)}, u32[]{:S(2)}) copy-start(f32[2,256,512]{2,1,0:T(8,128)} %get-tuple-element.22) | copy-start | bytes 3145732
  41.7 14.0 %collective-permute-start.1 = (f32[256,512]{1,0:T(8,128)}, f32[256,512]{1,0:T(8,128)}, u32[]{:S(2)}, u32[]{:S(2)}) collective-permute-start(f32[256,512]{1,0:T(8,128)} %get-tuple-element.44), channel_id=1, source_target_pairs={{0,2},{1,3},{2,0},{3,1},{4,6},{5,7},{6,4},{7,5},{8,10},{9,11},{10,... | collective-permute-start | bytes 1572872 | tf_op jit(solution)/shard_map/ppermute | solution.py:154
  55.8 7.8 %copy-start.7 = (f32[256,512]{1,0:T(8,128)S(1)}, f32[256,512]{1,0:T(8,128)}, u32[]{:S(2)}) copy-start(f32[256,512]{1,0:T(8,128)} %get-tuple-element.27) | copy-start | bytes 1572868
  58.0 20.8 %all-to-all-start.2 = ((f32[16,16,512]{2,1,0:T(8,128)}), f32[16,16,512]{2,1,0:T(8,128)S(1)}, u32[]{:S(2)}, u32[]{:S(2)}) async-start(f32[16,16,512]{2,1,0:T(8,128)} %shard_map.60), calls=%async_computation.2 | async-start | bytes 1048576 | tf_op jit(solution)/shard_map/all_to_all | solution.py:174
  63.6 12.2 %collective-permute-start.3 = (f32[256,512]{1,0:T(8,128)S(1)}, f32[256,512]{1,0:T(8,128)S(1)}, u32[]{:S(2)}, u32[]{:S(2)}) collective-permute-start(f32[256,512]{1,0:T(8,128)S(1)} %copy-done.7), channel_id=1, source_target_pairs={{0,2},{1,3},{2,0},{3,1},{4,6},{5,7},{6,4},{7,5},{8,10},{9,11},{10,... | collective-permute-start | bytes 1572872 | tf_op jit(solution)/shard_map/ppermute | solution.py:158
  75.8 0.8 copy-start.6
  78.8 17.4 %all-to-all-start.3 = ((f32[16,16,512]{2,1,0:T(8,128)}), f32[16,16,512]{2,1,0:T(8,128)S(1)}, u32[]{:S(2)}, u32[]{:S(2)}) async-start(f32[16,16,512]{2,1,0:T(8,128)} %shard_map.61), calls=%async_computation.3 | async-start | bytes 1048576 | tf_op jit(solution)/shard_map/all_to_all | solution.py:174
  84.5 13.4 %copy-start.4 = (bf16[2,128,512]{2,1,0:T(8,128)(2,1)}, bf16[2,128,512]{2,1,0:T(8,128)(2,1)S(1)}, u32[]{:S(2)}) copy-start(bf16[2,128,512]{2,1,0:T(8,128)(2,1)S(1)} %bitcast_convert_fusion.refs_0_) | copy-start | bytes 786436
  84.5 6.4 %collective-permute-start.5 = (bf16[2,128,512]{2,1,0:T(8,128)(2,1)S(1)}, bf16[2,128,512]{2,1,0:T(8,128)(2,1)S(1)}, u32[]{:S(2)}, u32[]{:S(2)}) collective-permute-start(bf16[2,128,512]{2,1,0:T(8,128)(2,1)S(1)} %bitcast_convert_fusion.refs_0_), channel_id=1, source_target_pairs={{0,2},{1,3},{2,0},{3,1},{4,6},{5,7},{6,4},{7,5},{8,10},{9,11},{10,... | collective-permute-start | bytes 786440 | tf_op jit(solution)/shard_map/ppermute | solution.py:52
  91.0 7.0 %copy-start.9 = (bf16[2,128,512]{2,1,0:T(8,128)(2,1)}, bf16[2,128,512]{2,1,0:T(8,128)(2,1)S(1)}, u32[]{:S(2)}) copy-start(bf16[2,128,512]{2,1,0:T(8,128)(2,1)S(1)} %collective-permute-done.5.refs_1_) | copy-start | bytes 786436
  91.0 6.9 %collective-permute-start.6 = (bf16[2,128,512]{2,1,0:T(8,128)(2,1)S(1)}, bf16[2,128,512]{2,1,0:T(8,128)(2,1)S(1)}, u32[]{:S(2)}, u32[]{:S(2)}) collective-permute-start(bf16[2,128,512]{2,1,0:T(8,128)(2,1)S(1)} %bitcast_convert_fusion.refs_0_), channel_id=1, source_target_pairs={{0,1},{1,0},{2,3},{3,2},{4,5},{5,4},{6,7},{7,6},{8,9},{9,8},{10,11... | collective-permute-start | bytes 786440 | tf_op jit(solution)/shard_map/ppermute | solution.py:52
  91.0 6.9 %collective-permute-start.7 = (bf16[2,128,512]{2,1,0:T(8,128)(2,1)S(1)}, bf16[2,128,512]{2,1,0:T(8,128)(2,1)}, u32[]{:S(2)}, u32[]{:S(2)}) collective-permute-start(bf16[2,128,512]{2,1,0:T(8,128)(2,1)S(1)} %collective-permute-done.5.refs_1_), channel_id=1, source_target_pairs={{0,1},{1,0},{2,3},{3,2},{4,5},{5,4},{6,7},{7,6},{8,9},{9,8},{10,11... | collective-permute-start | bytes 786440 | tf_op jit(solution)/shard_map/ppermute | solution.py:52
  96.3 6.5 %copy-start.3 = (bf16[2,128,512]{2,1,0:T(8,128)(2,1)}, bf16[2,128,512]{2,1,0:T(8,128)(2,1)S(1)}, u32[]{:S(2)}) copy-start(bf16[2,128,512]{2,1,0:T(8,128)(2,1)S(1)} %bitcast_convert_fusion.1.refs_0_) | copy-start | bytes 786436
  96.3 6.4 %collective-permute-start.4 = (bf16[2,128,512]{2,1,0:T(8,128)(2,1)S(1)}, bf16[2,128,512]{2,1,0:T(8,128)(2,1)S(1)}, u32[]{:S(2)}, u32[]{:S(2)}) collective-permute-start(bf16[2,128,512]{2,1,0:T(8,128)(2,1)S(1)} %bitcast_convert_fusion.1.refs_0_), channel_id=1, source_target_pairs={{0,2},{1,3},{2,0},{3,1},{4,6},{5,7},{6,4},{7,5},{8,10},{9,11},{10,... | collective-permute-start | bytes 786440 | tf_op jit(solution)/shard_map/ppermute | solution.py:52
  97.9 0.7 copy-start.10
  102.7 1.9 %copy-start.8 = (bf16[2,128,512]{2,1,0:T(8,128)(2,1)}, bf16[2,128,512]{2,1,0:T(8,128)(2,1)S(1)}, u32[]{:S(2)}) copy-start(bf16[2,128,512]{2,1,0:T(8,128)(2,1)S(1)} %collective-permute-done.4.refs_1_) | copy-start | bytes 786436
  102.7 1.9 %collective-permute-start.8 = (bf16[2,128,512]{2,1,0:T(8,128)(2,1)S(1)}, bf16[2,128,512]{2,1,0:T(8,128)(2,1)S(1)}, u32[]{:S(2)}, u32[]{:S(2)}) collective-permute-start(bf16[2,128,512]{2,1,0:T(8,128)(2,1)S(1)} %bitcast_convert_fusion.1.refs_0_), channel_id=1, source_target_pairs={{0,1},{1,0},{2,3},{3,2},{4,5},{5,4},{6,7},{7,6},{8,9},{9,8},{10,11... | collective-permute-start | bytes 786440 | tf_op jit(solution)/shard_map/ppermute | solution.py:52
  102.7 2.0 %collective-permute-start.9 = (bf16[2,128,512]{2,1,0:T(8,128)(2,1)S(1)}, bf16[2,128,512]{2,1,0:T(8,128)(2,1)}, u32[]{:S(2)}, u32[]{:S(2)}) collective-permute-start(bf16[2,128,512]{2,1,0:T(8,128)(2,1)S(1)} %collective-permute-done.4.refs_1_), channel_id=1, source_target_pairs={{0,1},{1,0},{2,3},{3,2},{4,5},{5,4},{6,7},{7,6},{8,9},{9,8},{10,11... | collective-permute-start | bytes 786440 | tf_op jit(solution)/shard_map/ppermute | solution.py:52
  104.6 4.3 %copy-start = (f32[512,2,128]{2,1,0:T(2,128)S(1)}, f32[512,2,128]{2,1,0:T(2,128)}, u32[]{:S(2)}) copy-start(f32[512,2,128]{2,1,0:T(2,128)} %shard_map.62) | copy-start | bytes 1572868
  104.6 0.7 copy-start.11

commit v27 on v26

--- a/solution.py
+++ b/solution.py
@@ -55,12 +55,14 @@
     return pieces, companion
 
 
-def fitted_kernel(me_ref, l_ref, *refs):
-    *piece_refs, out_ref = refs
+def fitted_kernel(chunk, count, me_ref, l_ref, *refs):
+    piece_refs = refs[:count]
+    observed_ref = refs[count]
+    earlier_ref = refs[count + 1] if chunk else None
+    out_ref = refs[-1]
     me = me_ref[0]
     levels = len(piece_refs).bit_length() - 1
-    width = piece_refs[0].shape[-1]
-    hours, members, _ = piece_refs[0].shape
+    hours, members, width = piece_refs[0].shape
     total = None
     for position, piece_ref in enumerate(piece_refs):
         flipped = 0
@@ -74,8 +76,14 @@
             preferred_element_type=jnp.float32,
         )
         total = part if total is None else total + part
+    low = chunk * members
+    if chunk:
+        out_ref[:, :, :low] = earlier_ref[:, :, :low]
     for hour in range(hours):
-        out_ref[:, hour, :] = total[:, hour * members:(hour + 1) * members]
+        observed = observed_ref[:, hour, low:low + members].astype(jnp.float32)
+        out_ref[:, hour, low:low + members] = (
+            observed - total[:, hour * members:(hour + 1) * members]
+        )
 
 
 def recurrence_kernel(rate_ref, keep_ref, received_ref, out_ref):
@@ -176,28 +184,28 @@
         pieces, earlier = doubling_gather(rounded, "state", fitted_parts[-1:])
         fitted_parts[-1:] = earlier
         slab_hours, width, _ = rounded.shape
-        fitted = vmem_call(
-            fitted_kernel,
-            jax.ShapeDtypeStruct((stations_here, slab_hours, width), jnp.float32),
-            1 + len(pieces),
-            pl.CostEstimate(
+        extra = [fitted_parts[-1]] if fitted_parts else []
+        fitted = pl.pallas_call(
+            functools.partial(fitted_kernel, chunk, len(pieces)),
+            out_shape=jax.ShapeDtypeStruct(by_hour.shape, jnp.float32),
+            in_specs=[pl.BlockSpec(memory_space=pltpu.SMEM)]
+            + [pl.BlockSpec(memory_space=pltpu.VMEM)] * (2 + len(pieces) + len(extra)),
+            out_specs=pl.BlockSpec(memory_space=pltpu.VMEM),
+            input_output_aliases={3 + len(pieces): 0} if extra else {},
+            cost_estimate=pl.CostEstimate(
                 flops=2 * stations_here * slab_hours * width * all_comps,
                 bytes_accessed=2 * stations_here * all_comps
                 + 2 * slab_hours * width * all_comps
                 + 4 * slab_hours * stations_here * width,
                 transcendentals=0,
             ),
-            scalars=1,
-        )(lax.axis_index("state").reshape(1).astype(jnp.int32), loadings, *pieces)
+        )(lax.axis_index("state").reshape(1).astype(jnp.int32), loadings, *pieces, by_hour, *extra)
         fitted_parts.append(fitted)
         smoothed_parts.append(jnp.transpose(gathered, (2, 0, 1)))
-    for chunk, fitted in enumerate(fitted_parts):
-        low = chunk * members // CHUNKS
-        picked = by_hour[:, :, low:low + members // CHUNKS]
-        residual_parts.append(picked.astype(jnp.float32) - fitted)
+
     return (
         jnp.concatenate(smoothed_parts, axis=2),
-        jnp.concatenate(residual_parts, axis=2),
+        fitted_parts[-1],
     )
 
 

time: 113 us -> 114 us (level)
  local copies, waits for them, and re-layouts: 8.92 us -> 12.1 us
  other arithmetic: 9.93 us -> 6.89 us
  Pallas kernels: 16.2 us -> 18.2 us
    unnamed x26 -> x30, local copies, waits for them, and re-layouts: 5.85 us -> 8.2 us
    pallas_call x2, Pallas kernels: 7.09 us -> 9.05 us  [local(): pl.pallas_call(functools.partial(fitted_kernel, chunk, len(pieces)), out_...]
    sub x1 -> x0, other arithmetic: 1.58 us -> none  [local(): residual_parts.append(picked.astype(jnp.float32) - fitted)]
    concatenate x2 -> x1, other arithmetic: 1.52 us -> 0.07 us  [local(): return (jnp.concatenate(smoothed_parts, axis=2), fitted_parts[-1])]
  transfers between devices with their start and end apart: 14 -> 14, of which waited for: 7 -> 5; matrix products, arithmetic and copies ran while one was open for 7% -> 8% of each run, Pallas kernels for 5% -> 6%
where the time goes in v27:
time: 114 us; the launch traced here: 113 us
  waiting for transfers between devices  45.9 us (40%)
  starting transfers between devices  29.1 us (26%)
  Pallas kernels  18.2 us (16%)
  local copies, waits for them, and re-layouts  12.1 us (11%)
  other arithmetic  6.89 us (6%)
    all_to_all x1, waiting for transfers between devices, local(): lax.all_to_all(outgoing, 'tm', split_axis=0, concat_axis=0, tiled=True)  15.9 us
    ppermute x1, waiting for transfers between devices, local(): lax.ppermute(o, 'state', last[c + 1][2])  10.9 us
    all_to_all x2, starting transfers between devices, local(): lax.all_to_all(smoothed_here, 'tm', split_axis=0, concat_axis=1, tiled=True)  10.4 us
    all_to_all x1, waiting for transfers between devices, local(): lax.all_to_all(masked_later, 'tm', split_axis=1, concat_axis=0, tiled=True)  9.18 us
    pallas_call x2, Pallas kernels, local(): pl.pallas_call(functools.partial(fitted_kernel, chunk, len(pieces)), out_...  9.05 us
    unnamed x30, local copies, waits for them, and re-layouts  8.2 us
    all_to_all x1, starting transfers between devices, local(): lax.all_to_all(outgoing, 'tm', split_axis=0, concat_axis=0, tiled=True)  7.25 us
    all_to_all x2, waiting for transfers between devices, local(): lax.all_to_all(smoothed_here, 'tm', split_axis=0, concat_axis=1, tiled=True)  5.04 us
  transfers between devices with their start and end apart: 14, of which 5 were waited for; matrix products, arithmetic and copies ran while one was open for 8% of the time, Pallas kernels for 6%

profile of v27, /device:TPU:0, one launch (start us, length us, event | category | flops | bytes accessed | tf_op | source)
XLA Modules:
  0.0 113.0 jit_solution(16431269679216637602)
XLA Ops:
  0.6 0.7 convert_element_type.23
  2.1 1.7 %copy.35 = bf16[64,16,256]{0,2,1:T(8,128)(2,1)S(1)} copy(bf16[64,16,256]{2,1,0:T(8,128)(2,1)} %param.4) | data formatting | bytes 1048576 | tf_op args[0]
  4.4 0.9 pad_maximum_fusion.1
  5.3 7.3 %all-to-all-start = ((bf16[8,72,512]{2,1,0:T(8,128)(2,1)}), bf16[8,72,512]{2,1,0:T(8,128)(2,1)S(1)}, u32[]{:S(2)}, u32[]{:S(2)}) async-start(bf16[8,72,512]{2,1,0:T(8,128)(2,1)} %pad_maximum_fusion.1), calls=%async_computation | async-start | bytes 1179648 | tf_op jit(solution)/shard_map/all_to_all | solution.py:133
  12.5 15.9 %all-to-all-done.x_ref = bf16[8,72,512]{2,1,0:T(8,128)(2,1)S(1)} async-done(((bf16[8,72,512]{2,1,0:T(8,128)(2,1)}), bf16[8,72,512]{2,1,0:T(8,128)(2,1)S(1)}, u32[]{:S(2)}, u32[]{:S(2)}) %all-to-all-start) | async-done | bytes 589856 | tf_op jit(solution)/shard_map/all_to_all | solution.py:133
  28.4 0.8 copy-done.4
  29.2 4.8 %shard_map.59 = (f32[2,256,512]{2,1,0:T(8,128)}, f32[2,256,512]{2,1,0:T(8,128)}, f32[2,256,512]{2,1,0:T(8,128)}, f32[2,256,512]{2,1,0:T(8,128)}) custom-call(s32[1]{0:T(128)} %bitcast.10.me_ref, bf16[8,72,512]{2,1,0:T(8,128)(2,1)} %copy-done.4, bf16[512,2048]{1,0:T(8,128)(2,1)} %l_ref.5), custom_call_target="tpu_custom_call" | custom-call | flops 1073741824 | bytes 6815744 | tf_op jit(solution)/shard_map/pallas_call | solution.py:145
  34.5 1.1 %copy.40 = bf16[64,16,256]{2,0,1:T(8,128)(2,1)} copy(bf16[64,16,256]{0,2,1:T(8,128)(2,1)S(1)} %broadcast_multiply_fusion) | data formatting | bytes 1048576 | tf_op jit(solution)/shard_map/optimization_barrier | solution.py:139
  35.7 3.6 %all-to-all-start.1 = ((bf16[64,16,256]{2,0,1:T(8,128)(2,1)}), bf16[64,16,256]{2,0,1:T(8,128)(2,1)S(1)}, u32[]{:S(2)}, u32[]{:S(2)}) async-start(bf16[64,16,256]{2,0,1:T(8,128)(2,1)} %copy.40), calls=%async_computation.1 | async-start | bytes 1048576 | tf_op jit(solution)/shard_map/all_to_all | solution.py:140
  39.3 2.4 %fusion.2 = (f32[256,512]{1,0:T(8,128)}, f32[256,512]{1,0:T(8,128)}) fusion(f32[2,256,512]{2,1,0:T(8,128)} %collective-permute-done, f32[2,256,512]{2,1,0:T(8,128)S(1)} %copy-done.1), kind=kLoop, calls=%fused_computation.7 | loop fusion | flops 262144 | bytes 3145728 | tf_op jit(solution)/shard_map/add | solution.py:40
  41.7 1.5 %collective-permute-start.1 = (f32[256,512]{1,0:T(8,128)}, f32[256,512]{1,0:T(8,128)S(1)}, u32[]{:S(2)}, u32[]{:S(2)}) collective-permute-start(f32[256,512]{1,0:T(8,128)} %get-tuple-element.44), channel_id=1, source_target_pairs={{0,2},{1,3},{2,0},{3,1},{4,6},{5,7},{6,4},{7,5},{8,10},{9,11},{10,... | collective-permute-start | bytes 1572872 | tf_op jit(solution)/shard_map/ppermute | solution.py:162
  43.3 0.8 slice_convert_fusion
  44.9 9.2 %all-to-all-done.1 = bf16[64,16,256]{2,0,1:T(8,128)(2,1)S(1)} async-done(((bf16[64,16,256]{2,0,1:T(8,128)(2,1)}), bf16[64,16,256]{2,0,1:T(8,128)(2,1)S(1)}, u32[]{:S(2)}, u32[]{:S(2)}) %all-to-all-start.1) | async-done | bytes 524320 | tf_op jit(solution)/shard_map/all_to_all | solution.py:140
  54.0 1.4 %copy.41 = bf16[64,8,2,256]{3,2,0,1:T(2,128)(2,1)} copy(bf16[64,8,2,256]{3,0,2,1:T(8,128)(2,1)S(1)} %bitcast.51) | data formatting | bytes 1048576 | tf_op jit(solution)/shard_map/all_to_all | solution.py:140
  55.4 1.2 %fusion = (f32[256,512]{1,0:T(8,128)}, f32[256,512]{1,0:T(8,128)}) fusion(f32[2,256,512]{2,1,0:T(8,128)S(1)} %collective-permute-done.2, f32[2,256,512]{2,1,0:T(8,128)S(1)} %copy-done), kind=kLoop, calls=%fused_computation.3 | loop fusion | flops 262144 | bytes 3145728 | tf_op jit(solution)/shard_map/add | solution.py:40
  56.6 0.8 copy-done.5
  57.4 2.2 %shard_map.60 = f32[16,16,512]{2,1,0:T(8,128)} custom-call(f32[16,512]{1,0:T(8,128)} %add.40.rate_ref, f32[16,16,512]{2,1,0:T(8,128)} %bitcast.50, f32[16,16,512]{2,1,0:T(8,128)} %bitcast.55), custom_call_target="tpu_custom_call" | custom-call | flops 786432 | bytes 1572864 | tf_op jit(solution)/shard_map/pallas_call | solution.py:172
  59.6 4.7 %all-to-all-start.2 = ((f32[16,16,512]{2,1,0:T(8,128)}), f32[16,16,512]{2,1,0:T(8,128)S(1)}, u32[]{:S(2)}, u32[]{:S(2)}) async-start(f32[16,16,512]{2,1,0:T(8,128)} %shard_map.60), calls=%async_computation.2 | async-start | bytes 1048576 | tf_op jit(solution)/shard_map/all_to_all | solution.py:182
  64.3 1.6 %collective-permute-start.3 = (f32[256,512]{1,0:T(8,128)S(1)}, f32[256,512]{1,0:T(8,128)S(1)}, u32[]{:S(2)}, u32[]{:S(2)}) collective-permute-start(f32[256,512]{1,0:T(8,128)S(1)} %copy-done.7), channel_id=1, source_target_pairs={{0,2},{1,3},{2,0},{3,1},{4,6},{5,7},{6,4},{7,5},{8,10},{9,11},{10,... | collective-permute-start | bytes 1572872 | tf_op jit(solution)/shard_map/ppermute | solution.py:166
  65.9 10.9 %collective-permute-done.3 = f32[256,512]{1,0:T(8,128)S(1)} collective-permute-done((f32[256,512]{1,0:T(8,128)S(1)}, f32[256,512]{1,0:T(8,128)S(1)}, u32[]{:S(2)}, u32[]{:S(2)}) %collective-permute-start.3) | collective-permute-done | bytes 524320 | tf_op jit(solution)/shard_map/ppermute | solution.py:166
  76.8 0.8 copy-done.6
  77.6 2.1 %shard_map.61 = f32[16,16,512]{2,1,0:T(8,128)} custom-call(f32[16,512]{1,0:T(8,128)} %add.40.rate_ref, f32[16,16,512]{2,1,0:T(8,128)} %bitcast.54, f32[16,16,512]{2,1,0:T(8,128)} %bitcast.56), custom_call_target="tpu_custom_call" | custom-call | flops 786432 | bytes 1572864 | tf_op jit(solution)/shard_map/pallas_call | solution.py:172
  79.7 5.7 %all-to-all-start.3 = ((f32[16,16,512]{2,1,0:T(8,128)}), f32[16,16,512]{2,1,0:T(8,128)S(1)}, u32[]{:S(2)}, u32[]{:S(2)}) async-start(f32[16,16,512]{2,1,0:T(8,128)} %shard_map.61), calls=%async_computation.3 | async-start | bytes 1048576 | tf_op jit(solution)/shard_map/all_to_all | solution.py:182
  85.5 1.6 %collective-permute-start.5 = (bf16[2,128,512]{2,1,0:T(8,128)(2,1)S(1)}, bf16[2,128,512]{2,1,0:T(8,128)(2,1)S(1)}, u32[]{:S(2)}, u32[]{:S(2)}) collective-permute-start(bf16[2,128,512]{2,1,0:T(8,128)(2,1)S(1)} %bitcast_convert_fusion.refs_0_), channel_id=1, source_target_pairs={{0,2},{1,3},{2,0},{3,1},{4,6},{5,7},{6,4},{7,5},{8,10},{9,11},{10,... | collective-permute-start | bytes 786440 | tf_op jit(solution)/shard_map/ppermute | solution.py:52
  87.1 4.9 %collective-permute-done.5.refs_1_ = bf16[2,128,512]{2,1,0:T(8,128)(2,1)S(1)} collective-permute-done((bf16[2,128,512]{2,1,0:T(8,128)(2,1)S(1)}, bf16[2,128,512]{2,1,0:T(8,128)(2,1)S(1)}, u32[]{:S(2)}, u32[]{:S(2)}) %collective-permute-start.5) | collective-permute-done | bytes 262176 | tf_op jit(solution)/shard_map/ppermute | solution.py:52
  92.4 5.0 %all-to-all-done.3 = f32[16,16,512]{2,1,0:T(8,128)S(1)} async-done(((f32[16,16,512]{2,1,0:T(8,128)}), f32[16,16,512]{2,1,0:T(8,128)S(1)}, u32[]{:S(2)}, u32[]{:S(2)}) %all-to-all-start.3) | async-done | bytes 524320 | tf_op jit(solution)/shard_map/all_to_all | solution.py:182
  97.6 1.6 %collective-permute-start.4 = (bf16[2,128,512]{2,1,0:T(8,128)(2,1)S(1)}, bf16[2,128,512]{2,1,0:T(8,128)(2,1)S(1)}, u32[]{:S(2)}, u32[]{:S(2)}) collective-permute-start(bf16[2,128,512]{2,1,0:T(8,128)(2,1)S(1)} %bitcast_convert_fusion.1.refs_0_), channel_id=1, source_target_pairs={{0,2},{1,3},{2,0},{3,1},{4,6},{5,7},{6,4},{7,5},{8,10},{9,11},{10,... | collective-permute-start | bytes 786440 | tf_op jit(solution)/shard_map/ppermute | solution.py:52
  99.9 0.7 copy-done.11
  100.6 4.3 %shard_map.62.refs_5_ = f32[512,2,256]{2,1,0:T(2,128)} custom-call(s32[1]{0:T(128)} %bitcast.10.me_ref, bf16[512,2048]{1,0:T(8,128)(2,1)} %l_ref.5, bf16[2,128,512]{2,1,0:T(8,128)(2,1)} %copy-done.3, bf16[2,128,512]{2,1,0:T(8,128)(2,1)} %copy-done.9, bf16[2,128,512]{2,1,0:T(8,128)(2,1)} %copy-done.10, bf16[2,128,512]{2,1,0:T(8,128)(2,1)} %copy-done.11, ...), custom_call_target="tpu_custom_call" | custom-call | flops 536870912 | bytes 3670016 | tf_op jit(solution)/shard_map/pallas_call | solution.py:188
  105.5 1.3 %copy.44 = f32[512,2,256]{2,1,0:T(2,128)} copy(f32[512,2,256]{0,2,1:T(8,128)S(1)} %pad_maximum_fusion) | data formatting | bytes 2097152
  107.5 0.7 copy-done.13
  108.2 4.8 %shard_map.63 = f32[512,2,256]{2,1,0:T(2,128)} custom-call(s32[1]{0:T(128)} %bitcast.10.me_ref, bf16[512,2048]{1,0:T(8,128)(2,1)} %l_ref.5, bf16[2,128,512]{2,1,0:T(8,128)(2,1)} %copy-done.2, bf16[2,128,512]{2,1,0:T(8,128)(2,1)} %copy-done.8, bf16[2,128,512]{2,1,0:T(8,128)(2,1)} %copy-done.12, ...), custom_call_target="tpu_custom_call", output_to_operand_aliasing={{}: (7, {})} | custom-call | flops 536870912 | bytes 3670016 | tf_op jit(solution)/shard_map/pallas_call | solution.py:188
  (55 shorter events, 5.3 us)
Async XLA Ops:
  5.3 23.1 %all-to-all-start = ((bf16[8,72,512]{2,1,0:T(8,128)(2,1)}), bf16[8,72,512]{2,1,0:T(8,128)(2,1)S(1)}, u32[]{:S(2)}, u32[]{:S(2)}) async-start(bf16[8,72,512]{2,1,0:T(8,128)(2,1)} %pad_maximum_fusion.1), calls=%async_computation | async-start | bytes 1179648 | tf_op jit(solution)/shard_map/all_to_all | solution.py:133
  28.4 0.8 copy-start.4
  34.0 5.3 %collective-permute-start = (f32[2,256,512]{2,1,0:T(8,128)}, f32[2,256,512]{2,1,0:T(8,128)}, u32[]{:S(2)}, u32[]{:S(2)}) collective-permute-start(f32[2,256,512]{2,1,0:T(8,128)} %get-tuple-element.21), channel_id=1, source_target_pairs={{0,1},{1,0},{2,3},{3,2},{4,5},{5,4},{6,7},{7,6},{8,9},{9,8},{10,11... | collective-permute-start | bytes 3145736 | tf_op jit(solution)/shard_map/ppermute | solution.py:38
  34.0 5.3 %copy-start.1 = (f32[2,256,512]{2,1,0:T(8,128)S(1)}, f32[2,256,512]{2,1,0:T(8,128)}, u32[]{:S(2)}) copy-start(f32[2,256,512]{2,1,0:T(8,128)} %get-tuple-element.20) | copy-start | bytes 3145732
  34.0 21.4 %collective-permute-start.2 = (f32[2,256,512]{2,1,0:T(8,128)}, f32[2,256,512]{2,1,0:T(8,128)S(1)}, u32[]{:S(2)}, u32[]{:S(2)}) collective-permute-start(f32[2,256,512]{2,1,0:T(8,128)} %get-tuple-element.23), channel_id=1, source_target_pairs={{0,1},{1,0},{2,3},{3,2},{4,5},{5,4},{6,7},{7,6},{8,9},{9,8},{10,11... | collective-permute-start | bytes 3145736 | tf_op jit(solution)/shard_map/ppermute | solution.py:38
  35.7 18.4 %all-to-all-start.1 = ((bf16[64,16,256]{2,0,1:T(8,128)(2,1)}), bf16[64,16,256]{2,0,1:T(8,128)(2,1)S(1)}, u32[]{:S(2)}, u32[]{:S(2)}) async-start(bf16[64,16,256]{2,0,1:T(8,128)(2,1)} %copy.40), calls=%async_computation.1 | async-start | bytes 1048576 | tf_op jit(solution)/shard_map/all_to_all | solution.py:140
  41.7 13.7 %copy-start = (f32[2,256,512]{2,1,0:T(8,128)S(1)}, f32[2,256,512]{2,1,0:T(8,128)}, u32[]{:S(2)}) copy-start(f32[2,256,512]{2,1,0:T(8,128)} %get-tuple-element.22) | copy-start | bytes 3145732
  41.7 14.8 %collective-permute-start.1 = (f32[256,512]{1,0:T(8,128)}, f32[256,512]{1,0:T(8,128)S(1)}, u32[]{:S(2)}, u32[]{:S(2)}) collective-permute-start(f32[256,512]{1,0:T(8,128)} %get-tuple-element.44), channel_id=1, source_target_pairs={{0,2},{1,3},{2,0},{3,1},{4,6},{5,7},{6,4},{7,5},{8,10},{9,11},{10,... | collective-permute-start | bytes 1572872 | tf_op jit(solution)/shard_map/ppermute | solution.py:162
  56.6 0.8 copy-start.5
  57.4 6.9 %copy-start.7 = (f32[256,512]{1,0:T(8,128)S(1)}, f32[256,512]{1,0:T(8,128)}, u32[]{:S(2)}) copy-start(f32[256,512]{1,0:T(8,128)} %get-tuple-element.27) | copy-start | bytes 1572868
  59.6 20.2 %all-to-all-start.2 = ((f32[16,16,512]{2,1,0:T(8,128)}), f32[16,16,512]{2,1,0:T(8,128)S(1)}, u32[]{:S(2)}, u32[]{:S(2)}) async-start(f32[16,16,512]{2,1,0:T(8,128)} %shard_map.60), calls=%async_computation.2 | async-start | bytes 1048576 | tf_op jit(solution)/shard_map/all_to_all | solution.py:182
  64.3 12.5 %collective-permute-start.3 = (f32[256,512]{1,0:T(8,128)S(1)}, f32[256,512]{1,0:T(8,128)S(1)}, u32[]{:S(2)}, u32[]{:S(2)}) collective-permute-start(f32[256,512]{1,0:T(8,128)S(1)} %copy-done.7), channel_id=1, source_target_pairs={{0,2},{1,3},{2,0},{3,1},{4,6},{5,7},{6,4},{7,5},{8,10},{9,11},{10,... | collective-permute-start | bytes 1572872 | tf_op jit(solution)/shard_map/ppermute | solution.py:166
  76.8 0.8 copy-start.6
  79.7 17.7 %all-to-all-start.3 = ((f32[16,16,512]{2,1,0:T(8,128)}), f32[16,16,512]{2,1,0:T(8,128)S(1)}, u32[]{:S(2)}, u32[]{:S(2)}) async-start(f32[16,16,512]{2,1,0:T(8,128)} %shard_map.61), calls=%async_computation.3 | async-start | bytes 1048576 | tf_op jit(solution)/shard_map/all_to_all | solution.py:182
  85.5 13.7 %copy-start.3 = (bf16[2,128,512]{2,1,0:T(8,128)(2,1)}, bf16[2,128,512]{2,1,0:T(8,128)(2,1)S(1)}, u32[]{:S(2)}) copy-start(bf16[2,128,512]{2,1,0:T(8,128)(2,1)S(1)} %bitcast_convert_fusion.refs_0_) | copy-start | bytes 786436
  85.5 6.4 %collective-permute-start.5 = (bf16[2,128,512]{2,1,0:T(8,128)(2,1)S(1)}, bf16[2,128,512]{2,1,0:T(8,128)(2,1)S(1)}, u32[]{:S(2)}, u32[]{:S(2)}) collective-permute-start(bf16[2,128,512]{2,1,0:T(8,128)(2,1)S(1)} %bitcast_convert_fusion.refs_0_), channel_id=1, source_target_pairs={{0,2},{1,3},{2,0},{3,1},{4,6},{5,7},{6,4},{7,5},{8,10},{9,11},{10,... | collective-permute-start | bytes 786440 | tf_op jit(solution)/shard_map/ppermute | solution.py:52
  91.9 7.3 %copy-start.9 = (bf16[2,128,512]{2,1,0:T(8,128)(2,1)}, bf16[2,128,512]{2,1,0:T(8,128)(2,1)S(1)}, u32[]{:S(2)}) copy-start(bf16[2,128,512]{2,1,0:T(8,128)(2,1)S(1)} %collective-permute-done.5.refs_1_) | copy-start | bytes 786436
  91.9 7.2 %collective-permute-start.6 = (bf16[2,128,512]{2,1,0:T(8,128)(2,1)S(1)}, bf16[2,128,512]{2,1,0:T(8,128)(2,1)S(1)}, u32[]{:S(2)}, u32[]{:S(2)}) collective-permute-start(bf16[2,128,512]{2,1,0:T(8,128)(2,1)S(1)} %bitcast_convert_fusion.refs_0_), channel_id=1, source_target_pairs={{0,1},{1,0},{2,3},{3,2},{4,5},{5,4},{6,7},{7,6},{8,9},{9,8},{10,11... | collective-permute-start | bytes 786440 | tf_op jit(solution)/shard_map/ppermute | solution.py:52
  91.9 7.2 %collective-permute-start.7 = (bf16[2,128,512]{2,1,0:T(8,128)(2,1)S(1)}, bf16[2,128,512]{2,1,0:T(8,128)(2,1)S(1)}, u32[]{:S(2)}, u32[]{:S(2)}) collective-permute-start(bf16[2,128,512]{2,1,0:T(8,128)(2,1)S(1)} %collective-permute-done.5.refs_1_), channel_id=1, source_target_pairs={{0,1},{1,0},{2,3},{3,2},{4,5},{5,4},{6,7},{7,6},{8,9},{9,8},{10,11... | collective-permute-start | bytes 786440 | tf_op jit(solution)/shard_map/ppermute | solution.py:52
  97.6 7.3 %copy-start.2 = (bf16[2,128,512]{2,1,0:T(8,128)(2,1)}, bf16[2,128,512]{2,1,0:T(8,128)(2,1)S(1)}, u32[]{:S(2)}) copy-start(bf16[2,128,512]{2,1,0:T(8,128)(2,1)S(1)} %bitcast_convert_fusion.1.refs_0_) | copy-start | bytes 786436
  97.6 7.3 %collective-permute-start.4 = (bf16[2,128,512]{2,1,0:T(8,128)(2,1)S(1)}, bf16[2,128,512]{2,1,0:T(8,128)(2,1)S(1)}, u32[]{:S(2)}, u32[]{:S(2)}) collective-permute-start(bf16[2,128,512]{2,1,0:T(8,128)(2,1)S(1)} %bitcast_convert_fusion.1.refs_0_), channel_id=1, source_target_pairs={{0,2},{1,3},{2,0},{3,1},{4,6},{5,7},{6,4},{7,5},{8,10},{9,11},{10,... | collective-permute-start | bytes 786440 | tf_op jit(solution)/shard_map/ppermute | solution.py:52
  99.2 0.7 copy-start.10
  99.9 0.7 copy-start.11
  104.9 2.0 %copy-start.8 = (bf16[2,128,512]{2,1,0:T(8,128)(2,1)}, bf16[2,128,512]{2,1,0:T(8,128)(2,1)S(1)}, u32[]{:S(2)}) copy-start(bf16[2,128,512]{2,1,0:T(8,128)(2,1)S(1)} %collective-permute-done.4.refs_1_) | copy-start | bytes 786436
  104.9 2.0 %collective-permute-start.8 = (bf16[2,128,512]{2,1,0:T(8,128)(2,1)S(1)}, bf16[2,128,512]{2,1,0:T(8,128)(2,1)S(1)}, u32[]{:S(2)}, u32[]{:S(2)}) collective-permute-start(bf16[2,128,512]{2,1,0:T(8,128)(2,1)S(1)} %bitcast_convert_fusion.1.refs_0_), channel_id=1, source_target_pairs={{0,1},{1,0},{2,3},{3,2},{4,5},{5,4},{6,7},{7,6},{8,9},{9,8},{10,11... | collective-permute-start | bytes 786440 | tf_op jit(solution)/shard_map/ppermute | solution.py:52
  104.9 1.9 %collective-permute-start.9 = (bf16[2,128,512]{2,1,0:T(8,128)(2,1)S(1)}, bf16[2,128,512]{2,1,0:T(8,128)(2,1)S(1)}, u32[]{:S(2)}, u32[]{:S(2)}) collective-permute-start(bf16[2,128,512]{2,1,0:T(8,128)(2,1)S(1)} %collective-permute-done.4.refs_1_), channel_id=1, source_target_pairs={{0,1},{1,0},{2,3},{3,2},{4,5},{5,4},{6,7},{7,6},{8,9},{9,8},{10,11... | collective-permute-start | bytes 786440 | tf_op jit(solution)/shard_map/ppermute | solution.py:52
  106.8 0.7 copy-start.12
  107.5 0.7 copy-start.13
